TPU v7x, 512 devices: a whole 4x4x16 slice. The times are simulated.
512 devices in a mesh: section: 32 (over z_lo, y, core), seq: 16 (over x, z_hi).
Axes of the slice: x: 4, y: 4, z: 16 (z_hi: 4, z_lo: 4; z = z_hi * 4 + z_lo), core: 2. Of those that a mesh axis runs over, the one named last changes fastest.
Arguments:
- up_activation: bfloat16 [32, 2048, 4096], P('section', 'seq'), as said below
- saved_projections: bfloat16 [32, 2048, 768], P('section', 'seq'), as said below
- up_cotangent: bfloat16 [32, 2048, 4096], P('section', 'seq'), may hold values from -6 to 6
- up_input_weight: bfloat16 [32, 4096, 768], P('section', 'seq'), may hold values from -0.09375 to 0.09375
- up_output_weight: bfloat16 [32, 512, 4096], P('section', None, 'seq'), may hold values from -0.25 to 0.25
- upward_gain: float32 [32, 4096], P('section'), may hold values from 0.5 to 1.5
- accum_input: bfloat16 [32, 4096, 768], P('section', 'seq'), may hold values from -48 to 48
- doc_starts: int32 [32, 2048], P('section', 'seq'), may hold values from 0 to 2047, as said below
Outputs:
- upward_grad: bfloat16 [32, 2048, 4096], P('section', 'seq')
- project_grads: bfloat16 [32, 4096, 768], P('section', 'seq')
Inputs may be any that keep to these rules, and one draw needn't show every extreme that they name: doc_starts[s, t] is the position of the first token of the document holding token t: it is 0 at t = 0, equals t or doc_starts[s, t - 1] elsewhere, and the last token of every micro-batch starts a document. `up_activation`: saved inputs of the upward layers. `saved_projections`: saved queries, keys and values of the upward layers.
All inputs are finite; a program needn't handle non-finite values.
Results may differ from a plain program's by a relative error of at most 0.014.
Values may be sent and summed in bfloat16 or wider, within the bound.
No kernel may reach another device: no remote copies, remote signals or barrier semaphores. Data moves between devices by JAX's collectives and lax.ppermute only.
A program may use at most 64 MiB of HBM per device.

v0:
```python
import jax
import jax.numpy as jnp
from jax import lax
from jax.sharding import PartitionSpec as P

HEAD = 128
GROUP = 4


def shifted(value, axis, steps):
    count = lax.axis_size(axis)
    initial, last = (max(0, -steps), min(count, count - steps))
    return lax.ppermute(value, axis, [(source, source + steps) for source in range(initial, last)])


def from_partner(x, axis, stride):
    return lax.ppermute(x, axis, [(i, i ^ 1 << stride) for i in range(lax.axis_size(axis))])


def contract_last(left, right):
    return lax.dot_general(
        left, right, (((1,), (1,)), ((), ())), preferred_element_type=jnp.float32
    )


def contract_first(left, right):
    return lax.dot_general(
        left, right, (((0,), (0,)), ((), ())), preferred_element_type=jnp.float32
    )


def normalize(values, gain):
    floats = values.astype(jnp.float32)
    inverse = lax.rsqrt(jnp.mean(floats * floats, axis=-1, keepdims=True) + 1e-05)
    unit = floats * inverse
    return (unit, inverse, unit * gain)


def per_device(
    up_activation,
    saved_projections,
    up_cotangent,
    up_input_weight,
    up_output_weight,
    upward_gain,
    accum_input,
    doc_starts,
):
    factor = HEAD ** (-0.5)
    width = GROUP * HEAD
    count = up_activation.shape[1]
    first = lax.axis_index("seq") * count
    saved = saved_projections[0]
    cotangent = up_cotangent[0]
    unit_up, inverse_up, normed_up = normalize(up_activation[0], upward_gain[0])
    hidden = normed_up.astype(jnp.bfloat16)
    key_value = lax.all_gather(saved[:, width:], "seq", axis=0, tiled=True)
    keys = key_value[:, :HEAD]
    values = key_value[:, HEAD:]
    query = saved[:, :width].reshape(count, GROUP, HEAD)
    hidden_cols = lax.all_to_all(hidden, "seq", split_axis=1, concat_axis=0, tiled=True)
    block = cotangent
    attn_grad = contract_last(
        block, lax.all_gather(up_output_weight[0], "seq", axis=1, tiled=True)
    ).astype(jnp.bfloat16)
    positions = first + jnp.arange(count, dtype=jnp.int32)
    key_positions = jnp.arange(keys.shape[0], dtype=jnp.int32)
    starts = doc_starts[0]
    visible = (key_positions[None, :] <= positions[:, None]) & (
        key_positions[None, :] >= starts[:, None]
    )
    scores = jnp.einsum("tgh,jh->tgj", query, keys, preferred_element_type=jnp.float32) * factor
    scores = jnp.where(visible[:, None, :], scores, -1e30)
    top = jnp.max(scores, axis=-1, keepdims=True)
    exps = jnp.where(visible[:, None, :], jnp.exp(scores - top), 0.0)
    probs = exps / jnp.sum(exps, axis=-1, keepdims=True)
    weights = probs.astype(jnp.bfloat16)
    grad_heads = attn_grad.reshape(count, GROUP, HEAD)
    prob_grad = jnp.einsum("tgh,jh->tgj", grad_heads, values, preferred_element_type=jnp.float32)
    inner = jnp.sum(probs * prob_grad, axis=-1, keepdims=True)
    score_grad = (probs * (prob_grad - inner) * factor).astype(jnp.bfloat16)
    query_grad = (
        jnp.einsum("tgj,jh->tgh", score_grad, keys, preferred_element_type=jnp.float32)
        .astype(jnp.bfloat16)
        .reshape(count, width)
    )
    key_part = jnp.einsum("tgj,tgh->jh", score_grad, query, preferred_element_type=jnp.float32)
    value_part = jnp.einsum("tgj,tgh->jh", weights, grad_heads, preferred_element_type=jnp.float32)
    key_total, value_total = (
        lax.psum(key_part.astype(jnp.bfloat16), "seq").astype(jnp.float32),
        lax.psum(value_part.astype(jnp.bfloat16), "seq").astype(jnp.float32),
    )
    kv_grad = jnp.concatenate(
        [key_total.astype(jnp.bfloat16), value_total.astype(jnp.bfloat16)], axis=1
    )
    query_all = lax.all_gather(query_grad, "seq", axis=0, tiled=True)
    grad_all = jnp.concatenate([query_all, kv_grad], axis=1)
    input_term = contract_first(hidden_cols, grad_all).astype(jnp.bfloat16)
    block = contract_last(grad_all, up_input_weight[0])
    hidden_grad = lax.all_to_all(block, "seq", split_axis=0, concat_axis=1, tiled=True)
    scaled = hidden_grad * upward_gain[0]
    input_grad = cotangent.astype(jnp.float32) + inverse_up * (
        scaled - unit_up * jnp.mean(scaled * unit_up, axis=-1, keepdims=True)
    )
    moved_grad = shifted(input_grad.astype(jnp.bfloat16), "section", 1)
    sections = lax.axis_size("section")
    mirror_input = input_term
    for bit in range(sections.bit_length() - 1):
        mirror_input = from_partner(mirror_input, "section", bit)
    project_grads = (accum_input[0].astype(jnp.float32) + mirror_input.astype(jnp.float32)).astype(
        jnp.bfloat16
    )
    return (moved_grad[None], project_grads[None])


def solution(mesh):
    return jax.shard_map(
        per_device,
        mesh=mesh,
        in_specs=(
            P("section", "seq", None),
            P("section", "seq", None),
            P("section", "seq", None),
            P("section", "seq", None),
            P("section", None, "seq"),
            P("section", None),
            P("section", "seq", None),
            P("section", "seq"),
        ),
        out_specs=(P("section", "seq", None), P("section", "seq", None)),
        check_vma=False,
    )
```

profile of v0, /device:TPU:25, one launch (start us, length us, event | category | flops | bytes accessed | tf_op | source)
XLA Modules:
  0.0 827.4 jit_solution(4818707884297721254)
XLA Ops:
  7.2 0.0 copy-start
  7.2 0.0 all-gather.5.cloned.1.call-start
  7.2 1.5 slice.17
  8.7 0.0 all-gather.5.cloned.1.call-update
  8.8 0.0 all-gather.9.cloned.1.call-start
  8.8 0.7 all-gather.9.cloned.1.call-update
  9.5 0.0 all-reduce.3.cloned.1.call-start
  9.6 1.1 fusion.37
  10.7 0.0 copy-start.1
  10.7 82.6 %all-gather.5.cloned.1.call-done = bf16[2048,256]{1,0:T(8,128)(2,1)} async-done(((bf16[128,256]{1,0:T(8,128)(2,1)}), bf16[2048,256]{1,0:T(8,128)(2,1)}) %all-gather.5.cloned.1.call-update) | async-done | bytes 1048592 | tf_op jit(solution)/shard_map/all_gather | solution.py:57
  93.3 5.0 fusion.64
  98.4 136.5 %all-gather.9.cloned.1.call-done = bf16[1,512,4096]{2,1,0:T(8,128)(2,1)} async-done(((bf16[1,512,256]{2,1,0:T(8,128)(2,1)}), bf16[1,512,4096]{2,1,0:T(8,128)(2,1)}) %all-gather.9.cloned.1.call-update) | async-done | bytes 4194320 | tf_op jit(solution)/shard_map/all_gather | solution.py:64
  234.9 0.0 copy-done.1
  234.9 3.9 fusion.33
  238.8 0.0 copy-done.9
  238.8 0.0 copy-start.6
  238.8 1.8 fusion.9
  240.5 0.0 copy-done.6
  240.5 2.7 fusion.41
  243.2 0.0 copy-done.8
  243.2 8.2 fusion.8
  251.4 0.0 all-reduce.3.cloned.1.call-update
  251.4 0.0 all-gather.7.cloned.1.call-start
  251.5 9.2 %fusion.27 = bf16[128,4,128]{0,2,1:T(8,128)(2,1)} fusion(f32[128,4,2048]{2,0,1:T(8,128)} %fusion.41, bf16[2048,256]{1,0:T(8,128)(2,1)S(1)} %copy-done.6, f32[128,4,2048]{2,0,1:T(8,128)} %get-tuple-element.9, f32[128,4]{0,1:T(4,128)S(1)} %get-tuple-element.8), kind=kOutput, calls=%fused_computation.35 | convolution fusion | flops 275843584 | bytes 17436672 | tf_op jit(solution)/shard_map/tgj,jh->tgh/dot_general | solution.py:83
  260.7 0.0 all-gather.7.cloned.1.call-update
  260.7 195.4 %all-reduce.3.cloned.1.call-done = (bf16[2048,128]{1,0:T(8,128)(2,1)}, bf16[2048,128]{1,0:T(8,128)(2,1)}) async-done(((bf16[2048,128]{1,0:T(8,128)(2,1)}, bf16[2048,128]{1,0:T(8,128)(2,1)}), (bf16[2048,128]{1,0:T(8,128)(2,1)}, bf16[2048,128]{1,0:T(8,128)(2,1)})) %all-reduce.3.cloned.1.call-update) | async-done | bytes 1048592 | tf_op jit(solution)/shard_map/psum | solution.py:91
  456.1 2.0 copy.29
  458.2 2.0 copy.30
  460.2 102.7 %all-gather.7.cloned.1.call-done = bf16[2048,512]{0,1:T(8,128)(2,1)} async-done(((bf16[128,512]{0,1:T(8,128)(2,1)}), bf16[2048,512]{0,1:T(8,128)(2,1)}) %all-gather.7.cloned.1.call-update) | async-done | bytes 2097168 | tf_op jit(solution)/shard_map/all_gather | solution.py:96
  562.9 2.0 pad_maximum_fusion
  565.0 2.8 copy.31
  567.8 4.2 fusion.43
  572.1 10.1 %all-to-all-start = ((f32[16,128,256]{2,1,0:T(8,128)}), f32[16,128,256]{2,1,0:T(8,128)S(1)}, u32[]{:S(2)}, u32[]{:S(2)}) async-start(f32[16,128,256]{2,1,0:T(8,128)} %fusion.43), calls=%async_computation | async-start | bytes 4194304 | tf_op jit(solution)/shard_map/all_to_all | solution.py:100
  582.2 1.6 copy.21
  583.8 1.6 copy.33
  585.5 0.6 broadcast.82
  586.0 1.3 reduce.4
  587.4 1.3 mul.85
  588.7 0.6 fusion.19
  589.2 0.5 add_rsqrt_fusion
  589.8 73.2 %all-to-all-done = f32[16,128,256]{2,1,0:T(8,128)S(1)} async-done(((f32[16,128,256]{2,1,0:T(8,128)}), f32[16,128,256]{2,1,0:T(8,128)S(1)}, u32[]{:S(2)}, u32[]{:S(2)}) %all-to-all-start) | async-done | bytes 2097184 | tf_op jit(solution)/shard_map/all_to_all | solution.py:100
  662.9 3.1 multiply_convert_fusion.1
  666.0 76.9 %all_to_all.32 = bf16[128,16,256]{2,0,1:T(8,128)(2,1)S(1)} all-to-all(bf16[128,16,256]{2,0,1:T(8,128)(2,1)S(1)} %get-tuple-element.6), channel_id=1, replica_groups=mesh['section'=32,'seq'=16] {'seq'}, dimensions={1} | all-to-all | bytes 2097152 | tf_op jit(solution)/shard_map/all_to_all | solution.py:61
  742.9 0.0 copy-done.2
  742.9 0.0 copy-done.4
  742.9 1.0 convolution_convert_fusion
  743.9 5.6 collective-permute-start.1
  749.5 1.5 collective-permute-done.1
  751.0 1.9 collective-permute-start.2
  752.9 2.3 copy.20
  755.2 1.8 copy.32
  757.0 0.7 broadcast_multiply_fusion
  757.8 5.8 collective-permute-done.2
  763.5 1.9 collective-permute-start.3
  765.4 2.3 fusion.18
  767.7 1.9 collective-permute-start
  769.7 6.8 collective-permute-done.3
  776.5 8.9 %collective-permute-start.4 = (bf16[256,768]{1,0:T(8,128)(2,1)S(1)}, bf16[256,768]{1,0:T(8,128)(2,1)S(1)}, u32[]{:S(2)}, u32[]{:S(2)}) collective-permute-start(bf16[256,768]{1,0:T(8,128)(2,1)S(1)} %collective-permute-done.3), channel_id=1, source_target_pairs={{0,128},{16,144},{32,160},{48,176},{64,192},{80,208},{96,224},{112... | collective-permute-start | bytes 1179656 | tf_op jit(solution)/shard_map/ppermute | solution.py:17
  785.4 6.4 collective-permute-done.4
  791.8 11.7 %collective-permute-start.5 = (bf16[256,768]{1,0:T(8,128)(2,1)S(1)}, bf16[256,768]{1,0:T(8,128)(2,1)S(1)}, u32[]{:S(2)}, u32[]{:S(2)}) collective-permute-start(bf16[256,768]{1,0:T(8,128)(2,1)S(1)} %collective-permute-done.4), channel_id=1, source_target_pairs={{0,256},{16,272},{32,288},{48,304},{64,320},{80,336},{96,352},{112... | collective-permute-start | bytes 1179656 | tf_op jit(solution)/shard_map/ppermute | solution.py:17
  803.5 0.0 collective-permute-done
  803.5 1.3 copy.34
  804.8 15.2 %collective-permute-done.5 = bf16[256,768]{1,0:T(8,128)(2,1)S(1)} collective-permute-done((bf16[256,768]{1,0:T(8,128)(2,1)S(1)}, bf16[256,768]{1,0:T(8,128)(2,1)S(1)}, u32[]{:S(2)}, u32[]{:S(2)}) %collective-permute-start.5) | collective-permute-done | bytes 393248 | tf_op jit(solution)/shard_map/ppermute | solution.py:17
  820.1 0.8 fusion.42
  (12 shorter events, 0.0 us)
Async XLA Ops:
  7.2 560.7 %copy-start = (bf16[1,256,768]{2,1,0:T(8,128)(2,1)S(1)}, bf16[1,256,768]{2,1,0:T(8,128)(2,1)}, u32[]{:S(2)}) copy-start(bf16[1,256,768]{2,1,0:T(8,128)(2,1)} %param.11) | copy-start | bytes 1179652
  7.2 86.2 %all-gather.5.cloned.1.call-start = ((), (), s32[]{:S(2)}) async-start(), calls=%async_computation.2 | async-start | bytes 1114112 | tf_op jit(solution)/shard_map/all_gather | solution.py:57
  8.8 226.1 %all-gather.9.cloned.1.call-start = ((), (), s32[]{:S(2)}) async-start(), calls=%async_computation.4 | async-start | bytes 4456448 | tf_op jit(solution)/shard_map/all_gather | solution.py:64
  9.5 446.6 %all-reduce.3.cloned.1.call-start = ((), (), s32[]{:S(2)}) async-start(), calls=%async_computation.5 | async-start | bytes 2097152 | tf_op jit(solution)/shard_map/psum | solution.py:91
  10.7 224.2 %copy-start.1 = (bf16[1,128,4096]{2,1,0:T(8,128)(2,1)S(1)}, bf16[1,128,4096]{2,1,0:T(8,128)(2,1)}, u32[]{:S(2)}) copy-start(bf16[1,128,4096]{2,1,0:T(8,128)(2,1)} %param.10) | copy-start | bytes 3145732
  234.9 3.9 copy-start.9
  238.8 1.8 copy-start.6
  240.5 2.7 copy-start.8
  251.4 311.5 %all-gather.7.cloned.1.call-start = ((), (), s32[]{:S(2)}) async-start(), calls=%async_computation.3 | async-start | bytes 2228224 | tf_op jit(solution)/shard_map/all_gather | solution.py:96
  572.1 14.0 %copy-start.7 = (f32[1,4096]{1,0:T(1,128)S(1)}, f32[1,4096]{1,0:T(1,128)}, u32[]{:S(2)}) copy-start(f32[1,4096]{1,0:T(1,128)} %param.13) | copy-start | bytes 49156
  572.1 90.9 %all-to-all-start = ((f32[16,128,256]{2,1,0:T(8,128)}), f32[16,128,256]{2,1,0:T(8,128)S(1)}, u32[]{:S(2)}, u32[]{:S(2)}) async-start(f32[16,128,256]{2,1,0:T(8,128)} %fusion.43), calls=%async_computation | async-start | bytes 4194304 | tf_op jit(solution)/shard_map/all_to_all | solution.py:100
  662.9 80.0 %copy-start.2 = (bf16[2048,512]{0,1:T(8,128)(2,1)S(1)}, bf16[2048,512]{0,1:T(8,128)(2,1)}, u32[]{:S(2)}) copy-start(bf16[2048,512]{0,1:T(8,128)(2,1)} %all-gather.7.cloned.1.call-done) | copy-start | bytes 6291460
  662.9 80.0 %copy-start.3 = (bf16[2048,128]{0,1:T(8,128)(2,1)S(1)}, bf16[2048,128]{0,1:T(8,128)(2,1)}, u32[]{:S(2)}) copy-start(bf16[2048,128]{0,1:T(8,128)(2,1)} %copy.29) | copy-start | bytes 1572868
  662.9 80.0 %copy-start.4 = (bf16[2048,128]{0,1:T(8,128)(2,1)S(1)}, bf16[2048,128]{0,1:T(8,128)(2,1)}, u32[]{:S(2)}) copy-start(bf16[2048,128]{0,1:T(8,128)(2,1)} %copy.30) | copy-start | bytes 1572868
  743.9 7.1 collective-permute-start.1
  751.0 12.5 %collective-permute-start.2 = (bf16[256,768]{1,0:T(8,128)(2,1)}, bf16[256,768]{1,0:T(8,128)(2,1)}, u32[]{:S(2)}, u32[]{:S(2)}) collective-permute-start(bf16[256,768]{1,0:T(8,128)(2,1)} %collective-permute-done.1), channel_id=1, source_target_pairs={{0,32},{16,48},{32,0},{48,16},{64,96},{80,112},{96,64},{112,80},{1... | collective-permute-start | bytes 1179656 | tf_op jit(solution)/shard_map/ppermute | solution.py:17
  757.0 63.1 %copy-start.5 = (bf16[1,256,768]{2,1,0:T(8,128)(2,1)S(1)}, bf16[1,256,768]{2,1,0:T(8,128)(2,1)}, u32[]{:S(2)}) copy-start(bf16[1,256,768]{2,1,0:T(8,128)(2,1)} %param.14) | copy-start | bytes 1179652
  763.5 13.0 %collective-permute-start.3 = (bf16[256,768]{1,0:T(8,128)(2,1)}, bf16[256,768]{1,0:T(8,128)(2,1)S(1)}, u32[]{:S(2)}, u32[]{:S(2)}) collective-permute-start(bf16[256,768]{1,0:T(8,128)(2,1)} %collective-permute-done.2), channel_id=1, source_target_pairs={{0,64},{16,80},{32,96},{48,112},{64,0},{80,16},{96,32},{112,48},{1... | collective-permute-start | bytes 1179656 | tf_op jit(solution)/shard_map/ppermute | solution.py:17
  767.7 35.8 %collective-permute-start = (bf16[128,4096]{0,1:T(8,128)(2,1)S(1)}, bf16[128,4096]{0,1:T(8,128)(2,1)S(1)}, u32[]{:S(2)}, u32[]{:S(2)}) collective-permute-start(bf16[128,4096]{0,1:T(8,128)(2,1)S(1)} %fusion.18), channel_id=1, source_target_pairs={{0,16},{16,32},{32,48},{48,64},{64,80},{80,96},{96,112},{112,128},... | collective-permute-start | bytes 3145736 | tf_op jit(solution)/shard_map/ppermute | solution.py:13
  776.5 15.3 %collective-permute-start.4 = (bf16[256,768]{1,0:T(8,128)(2,1)S(1)}, bf16[256,768]{1,0:T(8,128)(2,1)S(1)}, u32[]{:S(2)}, u32[]{:S(2)}) collective-permute-start(bf16[256,768]{1,0:T(8,128)(2,1)S(1)} %collective-permute-done.3), channel_id=1, source_target_pairs={{0,128},{16,144},{32,160},{48,176},{64,192},{80,208},{96,224},{112... | collective-permute-start | bytes 1179656 | tf_op jit(solution)/shard_map/ppermute | solution.py:17
  791.8 28.2 %collective-permute-start.5 = (bf16[256,768]{1,0:T(8,128)(2,1)S(1)}, bf16[256,768]{1,0:T(8,128)(2,1)S(1)}, u32[]{:S(2)}, u32[]{:S(2)}) collective-permute-start(bf16[256,768]{1,0:T(8,128)(2,1)S(1)} %collective-permute-done.4), channel_id=1, source_target_pairs={{0,256},{16,272},{32,288},{48,304},{64,320},{80,336},{96,352},{112... | collective-permute-start | bytes 1179656 | tf_op jit(solution)/shard_map/ppermute | solution.py:17
Sparse Core Ops, SparseCore 0:
  11.6 81.7 all-gather.4
  96.3 138.4 all-gather.8
  251.5 204.5 all-reduce.2
  460.0 102.9 all-gather.6
where the time goes:
time: 828 us; the launch traced here: 827 us
  waiting for transfers between devices  627 us (76%)
  blocking collectives  76.9 us (9%)
  starting transfers between devices  42.2 us (5%)
  matrix products  36 us (4%)
  local copies, waits for them, and re-layouts  19.1 us (2%)
  between operations  13.9 us (2%)
  other arithmetic  12.5 us (2%)
    psum x1, waiting for transfers between devices, per_device(): lax.psum(value_part.astype(jnp.bfloat16), 'seq').astype(jnp.float32)  195 us
    all_gather x1, waiting for transfers between devices, per_device(): lax.all_gather(up_output_weight[0], 'seq', axis=1, tiled=True)  137 us
    all_gather x1, waiting for transfers between devices, per_device(): query_all = lax.all_gather(query_grad, 'seq', axis=0, tiled=True)  103 us
    all_gather x1, waiting for transfers between devices, per_device(): key_value = lax.all_gather(saved[:, width:], 'seq', axis=0, tiled=True)  82.6 us
    all_to_all x1, blocking collectives, per_device(): lax.all_to_all(hidden, 'seq', split_axis=1, concat_axis=0, tiled=True)  76.9 us
    all_to_all x1, waiting for transfers between devices, per_device(): lax.all_to_all(block, 'seq', split_axis=0, concat_axis=1, tiled=True)  73.2 us
    ppermute x5, waiting for transfers between devices, from_partner(): lax.ppermute(x, axis, [(i, i ^ 1 << stride) for i in range(lax.axis_size(...  35.7 us
    ppermute x5, starting transfers between devices, from_partner(): lax.ppermute(x, axis, [(i, i ^ 1 << stride) for i in range(lax.axis_size(...  30 us
  transfers between devices with their start and end apart: 11, of which 10 were waited for; matrix products, arithmetic and copies ran while one was open for 4% of the time, Pallas kernels for 0%

commit v1 on v0

--- a/solution.py
+++ b/solution.py
@@ -5,6 +5,7 @@
 
 HEAD = 128
 GROUP = 4
+INNER = 4
 
 
 def shifted(value, axis, steps):
@@ -13,8 +14,65 @@
     return lax.ppermute(value, axis, [(source, source + steps) for source in range(initial, last)])
 
 
-def from_partner(x, axis, stride):
-    return lax.ppermute(x, axis, [(i, i ^ 1 << stride) for i in range(lax.axis_size(axis))])
+def mirrored(value, axis):
+    count = lax.axis_size(axis)
+    return lax.ppermute(value, axis, [(source, count - 1 - source) for source in range(count)])
+
+
+def seq_pairs(shift, level):
+    size = lax.axis_size("seq")
+    outer = size // INNER
+    if level == 0:
+        return [(o * INNER + i, o * INNER + (i + shift) % INNER) for o in range(outer) for i in range(INNER)]
+    return [(o * INNER + i, ((o + shift) % outer) * INNER + i) for o in range(outer) for i in range(INNER)]
+
+
+def gather_blocks(x):
+    outer = lax.axis_size("seq") // INNER
+    first = jnp.stack([x] + [lax.ppermute(x, "seq", seq_pairs(k, 0)) for k in range(1, INNER)])
+    return jnp.stack([first] + [lax.ppermute(first, "seq", seq_pairs(k, 1)) for k in range(1, outer)])
+
+
+def reduce_blocks(y):
+    outer = lax.axis_size("seq") // INNER
+    acc = y[0]
+    for k in range(1, outer):
+        acc = acc + lax.ppermute(y[k], "seq", seq_pairs(outer - k, 1))
+    total = acc[0]
+    for k in range(1, INNER):
+        total = total + lax.ppermute(acc[k], "seq", seq_pairs(INNER - k, 0))
+    return total
+
+
+def scatter_columns(x, o, i):
+    outer = lax.axis_size("seq") // INNER
+    n = x.shape[0]
+    parts = x.reshape(n, outer, INNER, -1).transpose(2, 1, 0, 3)
+    first = [parts[i]]
+    for k in range(1, INNER):
+        piece = lax.dynamic_index_in_dim(parts, (i + k) % INNER, 0, keepdims=False)
+        first.append(lax.ppermute(piece, "seq", seq_pairs(k, 0)))
+    first = jnp.stack(first, axis=1)
+    second = [first[o]]
+    for k in range(1, outer):
+        piece = lax.dynamic_index_in_dim(first, (o + k) % outer, 0, keepdims=False)
+        second.append(lax.ppermute(piece, "seq", seq_pairs(k, 1)))
+    return jnp.stack(second)
+
+
+def gather_columns(y, o, i):
+    outer = lax.axis_size("seq") // INNER
+    n, w = y.shape[2], y.shape[3]
+    first = [y[0]]
+    for k in range(1, outer):
+        first.append(lax.ppermute(y[k], "seq", seq_pairs(outer - k, 1)))
+    first = jnp.stack(first, axis=1)
+    second = [first[0]]
+    for k in range(1, INNER):
+        second.append(lax.ppermute(first[k], "seq", seq_pairs(INNER - k, 0)))
+    second = jnp.stack(second, axis=1)
+    second = jnp.roll(jnp.roll(second, o, axis=0), i, axis=1)
+    return second.transpose(2, 0, 1, 3).reshape(n, outer * INNER * w)
 
 
 def contract_last(left, right):
@@ -49,22 +107,28 @@
     factor = HEAD ** (-0.5)
     width = GROUP * HEAD
     count = up_activation.shape[1]
-    first = lax.axis_index("seq") * count
+    size = lax.axis_size("seq")
+    outer = size // INNER
+    me = lax.axis_index("seq")
+    o, i = me // INNER, me % INNER
+    first = me * count
     saved = saved_projections[0]
     cotangent = up_cotangent[0]
     unit_up, inverse_up, normed_up = normalize(up_activation[0], upward_gain[0])
     hidden = normed_up.astype(jnp.bfloat16)
-    key_value = lax.all_gather(saved[:, width:], "seq", axis=0, tiled=True)
+    output_weight = lax.all_gather(up_output_weight[0], "seq", axis=1, tiled=True)
+    key_value = gather_blocks(saved[:, width:]).reshape(size * count, 2 * HEAD)
     keys = key_value[:, :HEAD]
     values = key_value[:, HEAD:]
+    sources = (
+        ((o - jnp.arange(outer, dtype=jnp.int32)) % outer)[:, None] * INNER
+        + ((i - jnp.arange(INNER, dtype=jnp.int32)) % INNER)[None, :]
+    ).reshape(size)
+    key_positions = (sources[:, None] * count + jnp.arange(count, dtype=jnp.int32)[None, :]).reshape(-1)
+    hidden_cols = scatter_columns(hidden, o, i).reshape(size * count, -1)
     query = saved[:, :width].reshape(count, GROUP, HEAD)
-    hidden_cols = lax.all_to_all(hidden, "seq", split_axis=1, concat_axis=0, tiled=True)
-    block = cotangent
-    attn_grad = contract_last(
-        block, lax.all_gather(up_output_weight[0], "seq", axis=1, tiled=True)
-    ).astype(jnp.bfloat16)
+    attn_grad = contract_last(cotangent, output_weight).astype(jnp.bfloat16)
     positions = first + jnp.arange(count, dtype=jnp.int32)
-    key_positions = jnp.arange(keys.shape[0], dtype=jnp.int32)
     starts = doc_starts[0]
     visible = (key_positions[None, :] <= positions[:, None]) & (
         key_positions[None, :] >= starts[:, None]
@@ -86,27 +150,19 @@
     )
     key_part = jnp.einsum("tgj,tgh->jh", score_grad, query, preferred_element_type=jnp.float32)
     value_part = jnp.einsum("tgj,tgh->jh", weights, grad_heads, preferred_element_type=jnp.float32)
-    key_total, value_total = (
-        lax.psum(key_part.astype(jnp.bfloat16), "seq").astype(jnp.float32),
-        lax.psum(value_part.astype(jnp.bfloat16), "seq").astype(jnp.float32),
-    )
-    kv_grad = jnp.concatenate(
-        [key_total.astype(jnp.bfloat16), value_total.astype(jnp.bfloat16)], axis=1
-    )
-    query_all = lax.all_gather(query_grad, "seq", axis=0, tiled=True)
-    grad_all = jnp.concatenate([query_all, kv_grad], axis=1)
+    kv_part = jnp.concatenate([key_part, value_part], axis=1).reshape(outer, INNER, count, 2 * HEAD)
+    kv_grad = reduce_blocks(kv_part).astype(jnp.bfloat16)
+    own_grad = jnp.concatenate([query_grad, kv_grad], axis=1)
+    grad_all = gather_blocks(own_grad).reshape(size * count, -1)
     input_term = contract_first(hidden_cols, grad_all).astype(jnp.bfloat16)
     block = contract_last(grad_all, up_input_weight[0])
-    hidden_grad = lax.all_to_all(block, "seq", split_axis=0, concat_axis=1, tiled=True)
+    hidden_grad = gather_columns(block.reshape(outer, INNER, count, -1), o, i)
     scaled = hidden_grad * upward_gain[0]
     input_grad = cotangent.astype(jnp.float32) + inverse_up * (
         scaled - unit_up * jnp.mean(scaled * unit_up, axis=-1, keepdims=True)
     )
     moved_grad = shifted(input_grad.astype(jnp.bfloat16), "section", 1)
-    sections = lax.axis_size("section")
-    mirror_input = input_term
-    for bit in range(sections.bit_length() - 1):
-        mirror_input = from_partner(mirror_input, "section", bit)
+    mirror_input = mirrored(input_term, "section")
     project_grads = (accum_input[0].astype(jnp.float32) + mirror_input.astype(jnp.float32)).astype(
         jnp.bfloat16
     )

time: 828 us -> 558 us (0.67); the launches traced: 827 us -> 548 us
  waiting for transfers between devices: 627 us -> 312 us
  starting transfers between devices: 42.2 us -> 144 us
  blocking collectives: 76.9 us -> 0 us
  local copies, waits for them, and re-layouts: 19.1 us -> 29.7 us
    psum x1 -> x0, waiting for transfers between devices: 195 us -> none  [per_device(): lax.psum(value_part.astype(jnp.bfloat16), 'seq').astype(jnp.float32)]
    ppermute x5 -> x31, waiting for transfers between devices: 35.7 us -> 226 us  [the longest x3 66.3 us: gather_columns(): second.append(lax.ppermute(first[k], 'seq', seq_pairs(INNER - k, 0)))]
    all_gather x2 -> x0, waiting for transfers between devices: 185 us -> none  [the longest x1 103 us: per_device(): query_all = lax.all_gather(query_grad, 'seq', axis=0, tiled=True)]
    ppermute x5 -> x31, starting transfers between devices: 30 us -> 142 us  [the longest x6 40.1 us: gather_blocks(): lax.ppermute(x, 'seq', seq_pairs(k, 0))]
    all_to_all x1 -> x0, blocking collectives: 76.9 us -> none  [per_device(): lax.all_to_all(hidden, 'seq', split_axis=1, concat_axis=0, tiled=True)]
    all_to_all x1 -> x0, waiting for transfers between devices: 73.2 us -> none  [per_device(): lax.all_to_all(block, 'seq', split_axis=0, concat_axis=1, tiled=True)]
    all_gather x1, waiting for transfers between devices: 137 us -> 85.2 us  [per_device(): lax.all_gather(up_output_weight[0], 'seq', axis=1, tiled=True)]
    squeeze x0 -> x9, local copies, waits for them, and re-layouts: none -> 10.7 us  [the longest x3 6.13 us: gather_columns(): first.append(lax.ppermute(y[k], 'seq', seq_pairs(outer - k, 1)))]
  transfers between devices with their start and end apart: 11 -> 33, of which waited for: 10 -> 24; matrix products, arithmetic and copies ran while one was open for 4% -> 7% of each run, Pallas kernels for 0% -> 0%
where the time goes in v1:
time: 558 us; the launch traced here: 548 us
  waiting for transfers between devices  312 us (56%)
  starting transfers between devices  144 us (26%)
  local copies, waits for them, and re-layouts  29.7 us (5%)
  matrix products  29.5 us (5%)
  other arithmetic  17.1 us (3%)
  between operations  14.8 us (3%)
    all_gather x1, waiting for transfers between devices, per_device(): lax.all_gather(up_output_weight[0], 'seq', axis=1, tiled=True)  85.2 us
    ppermute x3, waiting for transfers between devices, gather_columns(): second.append(lax.ppermute(first[k], 'seq', seq_pairs(INNER - k, 0)))  66.3 us
    ppermute x6, starting transfers between devices, gather_blocks(): lax.ppermute(x, 'seq', seq_pairs(k, 0))  40.1 us
    ppermute x6, waiting for transfers between devices, gather_blocks(): lax.ppermute(first, 'seq', seq_pairs(k, 1))  38.9 us
    ppermute x6, waiting for transfers between devices, gather_blocks(): lax.ppermute(x, 'seq', seq_pairs(k, 0))  36.6 us
    ppermute x3, waiting for transfers between devices, reduce_blocks(): acc = acc + lax.ppermute(y[k], 'seq', seq_pairs(outer - k, 1))  23.2 us
    ppermute x3, waiting for transfers between devices, scatter_columns(): first.append(lax.ppermute(piece, 'seq', seq_pairs(k, 0)))  21.1 us
    ppermute x3, waiting for transfers between devices, gather_columns(): first.append(lax.ppermute(y[k], 'seq', seq_pairs(outer - k, 1)))  20.3 us
  transfers between devices with their start and end apart: 33, of which 24 were waited for; matrix products, arithmetic and copies ran while one was open for 7% of the time, Pallas kernels for 0%

profile of v1, /device:TPU:25, one launch (start us, length us, event | category | flops | bytes accessed | tf_op | source)
XLA Modules:
  0.0 547.5 jit_solution(16283603981363298841)
XLA Ops:
  9.0 8.8 %collective-permute-start = (bf16[128,256]{0,1:T(8,128)(2,1)S(1)}, bf16[128,256]{0,1:T(8,128)(2,1)S(1)}, u32[]{:S(2)}, u32[]{:S(2)}) collective-permute-start(bf16[128,256]{0,1:T(8,128)(2,1)S(1)} %get-tuple-element.37), channel_id=1, source_target_pairs={{0,1},{1,2},{2,3},{3,0},{4,5},{5,6},{6,7},{7,4},{8,9},{9,10},{10,1... | collective-permute-start | bytes 196616 | tf_op jit(solution)/shard_map/ppermute | solution.py:32
  17.8 10.6 %collective-permute-start.1 = (bf16[128,256]{0,1:T(8,128)(2,1)S(1)}, bf16[128,256]{0,1:T(8,128)(2,1)S(1)}, u32[]{:S(2)}, u32[]{:S(2)}) collective-permute-start(bf16[128,256]{0,1:T(8,128)(2,1)S(1)} %get-tuple-element.37), channel_id=1, source_target_pairs={{0,2},{1,3},{2,0},{3,1},{4,6},{5,7},{6,4},{7,5},{8,10},{9,11},{10,... | collective-permute-start | bytes 196616 | tf_op jit(solution)/shard_map/ppermute | solution.py:32
  28.5 5.2 collective-permute-start.2
  35.7 12.5 %collective-permute-done.2 = bf16[128,256]{0,1:T(8,128)(2,1)S(1)} collective-permute-done((bf16[128,256]{0,1:T(8,128)(2,1)S(1)}, bf16[128,256]{0,1:T(8,128)(2,1)S(1)}, u32[]{:S(2)}, u32[]{:S(2)}) %collective-permute-start.2) | collective-permute-done | bytes 65568 | tf_op jit(solution)/shard_map/ppermute | solution.py:32
  48.2 3.1 collective-permute-start.3
  51.3 4.4 collective-permute-start.4
  55.7 3.1 collective-permute-start.5
  59.7 5.4 collective-permute-done.4
  67.1 3.7 fusion.77
  70.8 85.2 %all-gather.3.cloned.1.call-done = bf16[1,512,4096]{2,1,0:T(8,128)(2,1)} async-done(((bf16[1,512,256]{2,1,0:T(8,128)(2,1)}), bf16[1,512,4096]{2,1,0:T(8,128)(2,1)}) %all-gather.3.cloned.1.call-update) | async-done | bytes 4194320 | tf_op jit(solution)/shard_map/all_gather | solution.py:119
  155.9 3.7 fusion.33
  159.8 2.8 fusion.53
  165.2 8.2 %convolution_bitcast_fusion.1 = f32[2048,128]{0,1:T(8,128)} fusion(bf16[128,4,128]{0,2,1:T(8,128)(2,1)S(1)} %bitcast.209, f32[128,4,2048]{0,2,1:T(8,128)} %fusion.53, f32[128,4,2048]{0,2,1:T(8,128)} %get-tuple-element.39, f32[128,4]{0,1:T(4,128)S(1)} %get-tuple-element.38), kind=kOutput, calls=%fused_computation.28 | convolution fusion | flops 275778048 | bytes 9570304 | tf_op jit(solution)/shard_map/tgj,tgh->jh/dot_general | solution.py:151
  176.1 4.3 collective-permute-start.6
  184.3 2.5 collective-permute-start.8
  187.0 3.0 collective-permute-done.6
  190.0 5.6 %collective-permute-done.7 = f32[4,128,256]{2,1,0:T(8,128)S(1)} collective-permute-done((f32[4,128,256]{2,1,0:T(8,128)}, f32[4,128,256]{2,1,0:T(8,128)S(1)}, u32[]{:S(2)}, u32[]{:S(2)}) %collective-permute-start.7) | collective-permute-done | bytes 524320 | tf_op jit(solution)/shard_map/ppermute | solution.py:40
  195.6 14.6 %collective-permute-done.8 = f32[4,128,256]{2,1,0:T(8,128)} collective-permute-done((f32[4,128,256]{2,1,0:T(8,128)}, f32[4,128,256]{2,1,0:T(8,128)}, u32[]{:S(2)}, u32[]{:S(2)}) %collective-permute-start.8) | collective-permute-done | bytes 524320 | tf_op jit(solution)/shard_map/ppermute | solution.py:40
  211.4 6.4 %collective-permute-start.10 = (f32[128,256]{1,0:T(8,128)S(1)}, f32[128,256]{1,0:T(8,128)S(1)}, u32[]{:S(2)}, u32[]{:S(2)}) collective-permute-start(f32[128,256]{1,0:T(8,128)S(1)} %get-tuple-element.31), channel_id=1, source_target_pairs={{0,2},{1,3},{2,0},{3,1},{4,6},{5,7},{6,4},{7,5},{8,10},{9,11},{10,... | collective-permute-start | bytes 393224 | tf_op jit(solution)/shard_map/ppermute | solution.py:43
  217.8 8.7 %collective-permute-start.11 = (f32[128,256]{1,0:T(8,128)S(1)}, f32[128,256]{1,0:T(8,128)S(1)}, u32[]{:S(2)}, u32[]{:S(2)}) collective-permute-start(f32[128,256]{1,0:T(8,128)S(1)} %get-tuple-element.30), channel_id=1, source_target_pairs={{0,1},{1,2},{2,3},{3,0},{4,5},{5,6},{6,7},{7,4},{8,9},{9,10},{10,1... | collective-permute-start | bytes 393224 | tf_op jit(solution)/shard_map/ppermute | solution.py:43
  226.6 1.9 collective-permute-start.9
  228.5 7.2 %fusion.36 = bf16[128,4,128]{0,2,1:T(8,128)(2,1)S(1)} fusion(f32[128,4,2048]{0,2,1:T(8,128)} %fusion.53, bf16[2048,256]{1,0:T(8,128)(2,1)S(1)} %bitcast.186, f32[128,4,2048]{0,2,1:T(8,128)} %get-tuple-element.39, f32[128,4]{0,1:T(4,128)S(1)} %get-tuple-element.38), kind=kOutput, calls=%fused_computation.60 | convolution fusion | flops 275843584 | bytes 17436672 | tf_op jit(solution)/shard_map/tgj,jh->tgh/dot_general | solution.py:147
  235.8 3.9 collective-permute-done.10
  239.8 4.8 collective-permute-start.12
  244.6 8.4 %collective-permute-start.13 = (bf16[128,768]{1,0:T(8,128)(2,1)S(1)}, bf16[128,768]{1,0:T(8,128)(2,1)S(1)}, u32[]{:S(2)}, u32[]{:S(2)}) collective-permute-start(bf16[128,768]{1,0:T(8,128)(2,1)S(1)} %get-tuple-element.35), channel_id=1, source_target_pairs={{0,2},{1,3},{2,0},{3,1},{4,6},{5,7},{6,4},{7,5},{8,10},{9,11},{10,... | collective-permute-start | bytes 589832 | tf_op jit(solution)/shard_map/ppermute | solution.py:32
  253.0 2.3 collective-permute-start.14
  255.4 13.2 %collective-permute-done.12 = bf16[128,768]{1,0:T(8,128)(2,1)S(1)} collective-permute-done((bf16[128,768]{1,0:T(8,128)(2,1)S(1)}, bf16[128,768]{1,0:T(8,128)(2,1)S(1)}, u32[]{:S(2)}, u32[]{:S(2)}) %collective-permute-start.12) | collective-permute-done | bytes 196640 | tf_op jit(solution)/shard_map/ppermute | solution.py:32
  268.6 7.0 %collective-permute-done.13 = bf16[128,768]{1,0:T(8,128)(2,1)S(1)} collective-permute-done((bf16[128,768]{1,0:T(8,128)(2,1)S(1)}, bf16[128,768]{1,0:T(8,128)(2,1)S(1)}, u32[]{:S(2)}, u32[]{:S(2)}) %collective-permute-start.13) | collective-permute-done | bytes 196640 | tf_op jit(solution)/shard_map/ppermute | solution.py:32
  275.5 2.3 collective-permute-done.14
  278.0 1.9 collective-permute-start.15
  279.9 2.9 collective-permute-start.16
  282.8 3.8 collective-permute-start.17
  286.6 30.0 %collective-permute-done.15 = bf16[4,128,768]{2,1,0:T(8,128)(2,1)S(1)} collective-permute-done((bf16[4,128,768]{2,1,0:T(8,128)(2,1)S(1)}, bf16[4,128,768]{2,1,0:T(8,128)(2,1)S(1)}, u32[]{:S(2)}, u32[]{:S(2)}) %collective-permute-start.15) | collective-permute-done | bytes 786464 | tf_op jit(solution)/shard_map/ppermute | solution.py:33
  316.5 2.3 collective-permute-done.17
  321.7 2.0 copy.50
  323.7 5.3 collective-permute-start.18
  329.1 2.0 copy.51
  333.0 2.0 copy.52
  335.1 2.5 collective-permute-start.20
  337.5 2.0 copy.53
  339.6 11.7 %collective-permute-done.18 = f32[4,128,256]{1,2,0:T(8,128)} collective-permute-done((f32[4,128,256]{1,2,0:T(8,128)}, f32[4,128,256]{1,2,0:T(8,128)}, u32[]{:S(2)}, u32[]{:S(2)}) %collective-permute-start.18) | collective-permute-done | bytes 524320 | tf_op jit(solution)/shard_map/ppermute | solution.py:68
  351.3 8.6 %collective-permute-done.20 = f32[4,128,256]{1,2,0:T(8,128)} collective-permute-done((f32[4,128,256]{1,2,0:T(8,128)}, f32[4,128,256]{1,2,0:T(8,128)}, u32[]{:S(2)}, u32[]{:S(2)}) %collective-permute-start.20) | collective-permute-done | bytes 524320 | tf_op jit(solution)/shard_map/ppermute | solution.py:68
  363.0 5.1 collective-permute-start.21
  368.0 8.1 %collective-permute-start.22 = (f32[4,128,256]{1,2,0:T(8,128)}, f32[4,128,256]{1,2,0:T(8,128)}, u32[]{:S(2)}, u32[]{:S(2)}) collective-permute-start(f32[4,128,256]{1,2,0:T(8,128)} %get-tuple-element.8), channel_id=1, source_target_pairs={{0,2},{1,3},{2,0},{3,1},{4,6},{5,7},{6,4},{7,5},{8,10},{9,11},{10,... | collective-permute-start | bytes 1572872 | tf_op jit(solution)/shard_map/ppermute | solution.py:72
  376.1 2.6 collective-permute-start.23
  378.8 2.3 copy.33
  387.4 3.2 collective-permute-done.21
  390.6 54.2 %collective-permute-done.22 = f32[4,128,256]{1,2,0:T(8,128)} collective-permute-done((f32[4,128,256]{1,2,0:T(8,128)}, f32[4,128,256]{1,2,0:T(8,128)}, u32[]{:S(2)}, u32[]{:S(2)}) %collective-permute-start.22) | collective-permute-done | bytes 524320 | tf_op jit(solution)/shard_map/ppermute | solution.py:72
  444.8 8.9 %collective-permute-done.23 = f32[4,128,256]{1,2,0:T(8,128)} collective-permute-done((f32[4,128,256]{1,2,0:T(8,128)}, f32[4,128,256]{1,2,0:T(8,128)}, u32[]{:S(2)}, u32[]{:S(2)}) %collective-permute-start.23) | collective-permute-done | bytes 524320 | tf_op jit(solution)/shard_map/ppermute | solution.py:72
  453.7 2.1 fusion.13
  455.8 2.3 multiply_reduce_fusion.1
  459.1 4.9 collective-permute-start.25
  464.0 6.6 %collective-permute-start.26 = (bf16[4,128,256]{1,2,0:T(8,128)(2,1)}, bf16[4,128,256]{1,2,0:T(8,128)(2,1)}, u32[]{:S(2)}, u32[]{:S(2)}) collective-permute-start(bf16[4,128,256]{1,2,0:T(8,128)(2,1)} %get-tuple-element.25), channel_id=1, source_target_pairs={{0,2},{1,3},{2,0},{3,1},{4,6},{5,7},{6,4},{7,5},{8,10},{9,11},{10,... | collective-permute-start | bytes 786440 | tf_op jit(solution)/shard_map/ppermute | solution.py:54
  470.6 4.3 collective-permute-start.27
  475.0 2.3 copy.32
  479.1 17.4 %collective-permute-done.26 = bf16[4,128,256]{1,2,0:T(8,128)(2,1)} collective-permute-done((bf16[4,128,256]{1,2,0:T(8,128)(2,1)}, bf16[4,128,256]{1,2,0:T(8,128)(2,1)}, u32[]{:S(2)}, u32[]{:S(2)}) %collective-permute-start.26) | collective-permute-done | bytes 262176 | tf_op jit(solution)/shard_map/ppermute | solution.py:54
  496.5 3.6 collective-permute-done.27
  505.3 4.6 collective-permute-start.30
  511.0 1.9 collective-permute-start.24
  512.9 3.5 collective-permute-done.28
  516.5 3.2 collective-permute-done.30
  520.7 7.8 %collective-permute-start.31 = (bf16[256,768]{1,0:T(8,128)(2,1)S(1)}, bf16[256,768]{1,0:T(8,128)(2,1)S(1)}, u32[]{:S(2)}, u32[]{:S(2)}) collective-permute-start(bf16[256,768]{1,0:T(8,128)(2,1)S(1)} %fusion.32), channel_id=1, source_target_pairs={{0,496},{16,480},{32,464},{48,448},{64,432},{80,416},{96,400},{112... | collective-permute-start | bytes 1179656 | tf_op jit(solution)/shard_map/ppermute | solution.py:19
  528.4 9.2 %collective-permute-done.31 = bf16[256,768]{1,0:T(8,128)(2,1)S(1)} collective-permute-done((bf16[256,768]{1,0:T(8,128)(2,1)S(1)}, bf16[256,768]{1,0:T(8,128)(2,1)S(1)}, u32[]{:S(2)}, u32[]{:S(2)}) %collective-permute-start.31) | collective-permute-done | bytes 393248 | tf_op jit(solution)/shard_map/ppermute | solution.py:19
  538.4 2.3 copy.60
  (87 shorter events, 42.6 us)
Async XLA Ops:
  7.2 312.1 %copy-start = (bf16[1,256,768]{2,1,0:T(8,128)(2,1)S(1)}, bf16[1,256,768]{2,1,0:T(8,128)(2,1)}, u32[]{:S(2)}) copy-start(bf16[1,256,768]{2,1,0:T(8,128)(2,1)} %param.11) | copy-start | bytes 1179652
  7.2 148.8 %all-gather.3.cloned.1.call-start = ((), (), s32[]{:S(2)}) async-start(), calls=%async_computation | async-start | bytes 4456448 | tf_op jit(solution)/shard_map/all_gather | solution.py:119
  9.0 25.0 %collective-permute-start = (bf16[128,256]{0,1:T(8,128)(2,1)S(1)}, bf16[128,256]{0,1:T(8,128)(2,1)S(1)}, u32[]{:S(2)}, u32[]{:S(2)}) collective-permute-start(bf16[128,256]{0,1:T(8,128)(2,1)S(1)} %get-tuple-element.37), channel_id=1, source_target_pairs={{0,1},{1,2},{2,3},{3,0},{4,5},{5,6},{6,7},{7,4},{8,9},{9,10},{10,1... | collective-permute-start | bytes 196616 | tf_op jit(solution)/shard_map/ppermute | solution.py:32
  17.8 17.8 %collective-permute-start.1 = (bf16[128,256]{0,1:T(8,128)(2,1)S(1)}, bf16[128,256]{0,1:T(8,128)(2,1)S(1)}, u32[]{:S(2)}, u32[]{:S(2)}) collective-permute-start(bf16[128,256]{0,1:T(8,128)(2,1)S(1)} %get-tuple-element.37), channel_id=1, source_target_pairs={{0,2},{1,3},{2,0},{3,1},{4,6},{5,7},{6,4},{7,5},{8,10},{9,11},{10,... | collective-permute-start | bytes 196616 | tf_op jit(solution)/shard_map/ppermute | solution.py:32
  28.5 19.6 %collective-permute-start.2 = (bf16[128,256]{0,1:T(8,128)(2,1)S(1)}, bf16[128,256]{0,1:T(8,128)(2,1)S(1)}, u32[]{:S(2)}, u32[]{:S(2)}) collective-permute-start(bf16[128,256]{0,1:T(8,128)(2,1)S(1)} %get-tuple-element.37), channel_id=1, source_target_pairs={{0,3},{1,0},{2,1},{3,2},{4,7},{5,4},{6,5},{7,6},{8,11},{9,8},{10,9... | collective-permute-start | bytes 196616 | tf_op jit(solution)/shard_map/ppermute | solution.py:32
  48.2 11.6 %collective-permute-start.3 = (bf16[4,128,256]{1,2,0:T(8,128)(2,1)S(1)}, bf16[4,128,256]{1,2,0:T(8,128)(2,1)S(1)}, u32[]{:S(2)}, u32[]{:S(2)}) collective-permute-start(bf16[4,128,256]{1,2,0:T(8,128)(2,1)S(1)} %get-tuple-element.33), channel_id=1, source_target_pairs={{0,4},{1,5},{2,6},{3,7},{4,8},{5,9},{6,10},{7,11},{8,12},{9,13},{1... | collective-permute-start | bytes 786440 | tf_op jit(solution)/shard_map/ppermute | solution.py:33
  51.3 13.9 %collective-permute-start.4 = (bf16[4,128,256]{1,2,0:T(8,128)(2,1)S(1)}, bf16[4,128,256]{1,2,0:T(8,128)(2,1)S(1)}, u32[]{:S(2)}, u32[]{:S(2)}) collective-permute-start(bf16[4,128,256]{1,2,0:T(8,128)(2,1)S(1)} %get-tuple-element.33), channel_id=1, source_target_pairs={{0,8},{1,9},{2,10},{3,11},{4,12},{5,13},{6,14},{7,15},{8,0},{9,1},... | collective-permute-start | bytes 786440 | tf_op jit(solution)/shard_map/ppermute | solution.py:33
  55.7 10.7 %collective-permute-start.5 = (bf16[4,128,256]{1,2,0:T(8,128)(2,1)S(1)}, bf16[4,128,256]{1,2,0:T(8,128)(2,1)S(1)}, u32[]{:S(2)}, u32[]{:S(2)}) collective-permute-start(bf16[4,128,256]{1,2,0:T(8,128)(2,1)S(1)} %get-tuple-element.33), channel_id=1, source_target_pairs={{0,12},{1,13},{2,14},{3,15},{4,0},{5,1},{6,2},{7,3},{8,4},{9,5},{1... | collective-permute-start | bytes 786440 | tf_op jit(solution)/shard_map/ppermute | solution.py:33
  67.1 88.9 %copy-start.3 = (bf16[1,128,4096]{2,1,0:T(8,128)(2,1)S(1)}, bf16[1,128,4096]{2,1,0:T(8,128)(2,1)}, u32[]{:S(2)}) copy-start(bf16[1,128,4096]{2,1,0:T(8,128)(2,1)} %param.10) | copy-start | bytes 3145732
  159.8 3.6 copy-start.12
  176.1 13.9 %collective-permute-start.6 = (f32[4,128,256]{2,1,0:T(8,128)}, f32[4,128,256]{2,1,0:T(8,128)S(1)}, u32[]{:S(2)}, u32[]{:S(2)}) collective-permute-start(f32[4,128,256]{2,1,0:T(8,128)} %bitcast.199), channel_id=1, source_target_pairs={{0,12},{1,13},{2,14},{3,15},{4,0},{5,1},{6,2},{7,3},{8,4},{9,5},{1... | collective-permute-start | bytes 1572872 | tf_op jit(solution)/shard_map/ppermute | solution.py:40
  181.4 14.2 %collective-permute-start.7 = (f32[4,128,256]{2,1,0:T(8,128)}, f32[4,128,256]{2,1,0:T(8,128)S(1)}, u32[]{:S(2)}, u32[]{:S(2)}) collective-permute-start(f32[4,128,256]{2,1,0:T(8,128)} %bitcast.200), channel_id=1, source_target_pairs={{0,8},{1,9},{2,10},{3,11},{4,12},{5,13},{6,14},{7,15},{8,0},{9,1},... | collective-permute-start | bytes 1572872 | tf_op jit(solution)/shard_map/ppermute | solution.py:40
  184.3 25.9 %collective-permute-start.8 = (f32[4,128,256]{2,1,0:T(8,128)}, f32[4,128,256]{2,1,0:T(8,128)}, u32[]{:S(2)}, u32[]{:S(2)}) collective-permute-start(f32[4,128,256]{2,1,0:T(8,128)} %bitcast.201), channel_id=1, source_target_pairs={{0,4},{1,5},{2,6},{3,7},{4,8},{5,9},{6,10},{7,11},{8,12},{9,13},{1... | collective-permute-start | bytes 1572872 | tf_op jit(solution)/shard_map/ppermute | solution.py:40
  211.4 28.3 %collective-permute-start.10 = (f32[128,256]{1,0:T(8,128)S(1)}, f32[128,256]{1,0:T(8,128)S(1)}, u32[]{:S(2)}, u32[]{:S(2)}) collective-permute-start(f32[128,256]{1,0:T(8,128)S(1)} %get-tuple-element.31), channel_id=1, source_target_pairs={{0,2},{1,3},{2,0},{3,1},{4,6},{5,7},{6,4},{7,5},{8,10},{9,11},{10,... | collective-permute-start | bytes 393224 | tf_op jit(solution)/shard_map/ppermute | solution.py:43
  217.8 21.9 %collective-permute-start.11 = (f32[128,256]{1,0:T(8,128)S(1)}, f32[128,256]{1,0:T(8,128)S(1)}, u32[]{:S(2)}, u32[]{:S(2)}) collective-permute-start(f32[128,256]{1,0:T(8,128)S(1)} %get-tuple-element.30), channel_id=1, source_target_pairs={{0,1},{1,2},{2,3},{3,0},{4,5},{5,6},{6,7},{7,4},{8,9},{9,10},{10,1... | collective-permute-start | bytes 393224 | tf_op jit(solution)/shard_map/ppermute | solution.py:43
  226.6 13.2 %collective-permute-start.9 = (f32[128,256]{1,0:T(8,128)S(1)}, f32[128,256]{1,0:T(8,128)S(1)}, u32[]{:S(2)}, u32[]{:S(2)}) collective-permute-start(f32[128,256]{1,0:T(8,128)S(1)} %get-tuple-element.29), channel_id=1, source_target_pairs={{0,3},{1,0},{2,1},{3,2},{4,7},{5,4},{6,5},{7,6},{8,11},{9,8},{10,9... | collective-permute-start | bytes 393224 | tf_op jit(solution)/shard_map/ppermute | solution.py:43
  239.8 28.7 %collective-permute-start.12 = (bf16[128,768]{1,0:T(8,128)(2,1)S(1)}, bf16[128,768]{1,0:T(8,128)(2,1)S(1)}, u32[]{:S(2)}, u32[]{:S(2)}) collective-permute-start(bf16[128,768]{1,0:T(8,128)(2,1)S(1)} %get-tuple-element.35), channel_id=1, source_target_pairs={{0,1},{1,2},{2,3},{3,0},{4,5},{5,6},{6,7},{7,4},{8,9},{9,10},{10,1... | collective-permute-start | bytes 589832 | tf_op jit(solution)/shard_map/ppermute | solution.py:32
  244.6 30.9 %collective-permute-start.13 = (bf16[128,768]{1,0:T(8,128)(2,1)S(1)}, bf16[128,768]{1,0:T(8,128)(2,1)S(1)}, u32[]{:S(2)}, u32[]{:S(2)}) collective-permute-start(bf16[128,768]{1,0:T(8,128)(2,1)S(1)} %get-tuple-element.35), channel_id=1, source_target_pairs={{0,2},{1,3},{2,0},{3,1},{4,6},{5,7},{6,4},{7,5},{8,10},{9,11},{10,... | collective-permute-start | bytes 589832 | tf_op jit(solution)/shard_map/ppermute | solution.py:32
  253.0 24.8 %collective-permute-start.14 = (bf16[128,768]{1,0:T(8,128)(2,1)S(1)}, bf16[128,768]{1,0:T(8,128)(2,1)S(1)}, u32[]{:S(2)}, u32[]{:S(2)}) collective-permute-start(bf16[128,768]{1,0:T(8,128)(2,1)S(1)} %get-tuple-element.35), channel_id=1, source_target_pairs={{0,3},{1,0},{2,1},{3,2},{4,7},{5,4},{6,5},{7,6},{8,11},{9,8},{10,9... | collective-permute-start | bytes 589832 | tf_op jit(solution)/shard_map/ppermute | solution.py:32
  278.0 38.6 %collective-permute-start.15 = (bf16[4,128,768]{2,1,0:T(8,128)(2,1)S(1)}, bf16[4,128,768]{2,1,0:T(8,128)(2,1)S(1)}, u32[]{:S(2)}, u32[]{:S(2)}) collective-permute-start(bf16[4,128,768]{2,1,0:T(8,128)(2,1)S(1)} %get-tuple-element.28), channel_id=1, source_target_pairs={{0,4},{1,5},{2,6},{3,7},{4,8},{5,9},{6,10},{7,11},{8,12},{9,13},{1... | collective-permute-start | bytes 2359304 | tf_op jit(solution)/shard_map/ppermute | solution.py:33
  279.9 36.6 %collective-permute-start.16 = (bf16[4,128,768]{2,1,0:T(8,128)(2,1)S(1)}, bf16[4,128,768]{2,1,0:T(8,128)(2,1)S(1)}, u32[]{:S(2)}, u32[]{:S(2)}) collective-permute-start(bf16[4,128,768]{2,1,0:T(8,128)(2,1)S(1)} %get-tuple-element.28), channel_id=1, source_target_pairs={{0,8},{1,9},{2,10},{3,11},{4,12},{5,13},{6,14},{7,15},{8,0},{9,1},... | collective-permute-start | bytes 2359304 | tf_op jit(solution)/shard_map/ppermute | solution.py:33
  282.8 36.1 %collective-permute-start.17 = (bf16[4,128,768]{2,1,0:T(8,128)(2,1)S(1)}, bf16[4,128,768]{2,1,0:T(8,128)(2,1)S(1)}, u32[]{:S(2)}, u32[]{:S(2)}) collective-permute-start(bf16[4,128,768]{2,1,0:T(8,128)(2,1)S(1)} %get-tuple-element.28), channel_id=1, source_target_pairs={{0,12},{1,13},{2,14},{3,15},{4,0},{5,1},{6,2},{7,3},{8,4},{9,5},{1... | collective-permute-start | bytes 2359304 | tf_op jit(solution)/shard_map/ppermute | solution.py:33
  323.7 27.5 %collective-permute-start.18 = (f32[4,128,256]{1,2,0:T(8,128)}, f32[4,128,256]{1,2,0:T(8,128)}, u32[]{:S(2)}, u32[]{:S(2)}) collective-permute-start(f32[4,128,256]{1,2,0:T(8,128)} %copy.50), channel_id=1, source_target_pairs={{0,12},{1,13},{2,14},{3,15},{4,0},{5,1},{6,2},{7,3},{8,4},{9,5},{1... | collective-permute-start | bytes 1572872 | tf_op jit(solution)/shard_map/ppermute | solution.py:68
  331.1 20.1 %collective-permute-start.19 = (f32[4,128,256]{1,2,0:T(8,128)}, f32[4,128,256]{1,2,0:T(8,128)}, u32[]{:S(2)}, u32[]{:S(2)}) collective-permute-start(f32[4,128,256]{1,2,0:T(8,128)} %copy.51), channel_id=1, source_target_pairs={{0,8},{1,9},{2,10},{3,11},{4,12},{5,13},{6,14},{7,15},{8,0},{9,1},... | collective-permute-start | bytes 1572872 | tf_op jit(solution)/shard_map/ppermute | solution.py:68
  335.1 24.8 %collective-permute-start.20 = (f32[4,128,256]{1,2,0:T(8,128)}, f32[4,128,256]{1,2,0:T(8,128)}, u32[]{:S(2)}, u32[]{:S(2)}) collective-permute-start(f32[4,128,256]{1,2,0:T(8,128)} %copy.52), channel_id=1, source_target_pairs={{0,4},{1,5},{2,6},{3,7},{4,8},{5,9},{6,10},{7,11},{8,12},{9,13},{1... | collective-permute-start | bytes 1572872 | tf_op jit(solution)/shard_map/ppermute | solution.py:68
  361.6 20.1 %copy-start.7 = (f32[1,4096]{1,0:T(1,128)S(1)}, f32[1,4096]{1,0:T(1,128)}, u32[]{:S(2)}) copy-start(f32[1,4096]{1,0:T(1,128)} %param.13) | copy-start | bytes 49156
  363.0 27.6 %collective-permute-start.21 = (f32[4,128,256]{1,2,0:T(8,128)}, f32[4,128,256]{1,2,0:T(8,128)}, u32[]{:S(2)}, u32[]{:S(2)}) collective-permute-start(f32[4,128,256]{1,2,0:T(8,128)} %get-tuple-element.9), channel_id=1, source_target_pairs={{0,3},{1,0},{2,1},{3,2},{4,7},{5,4},{6,5},{7,6},{8,11},{9,8},{10,9... | collective-permute-start | bytes 1572872 | tf_op jit(solution)/shard_map/ppermute | solution.py:72
  368.0 76.8 %collective-permute-start.22 = (f32[4,128,256]{1,2,0:T(8,128)}, f32[4,128,256]{1,2,0:T(8,128)}, u32[]{:S(2)}, u32[]{:S(2)}) collective-permute-start(f32[4,128,256]{1,2,0:T(8,128)} %get-tuple-element.8), channel_id=1, source_target_pairs={{0,2},{1,3},{2,0},{3,1},{4,6},{5,7},{6,4},{7,5},{8,10},{9,11},{10,... | collective-permute-start | bytes 1572872 | tf_op jit(solution)/shard_map/ppermute | solution.py:72
  376.1 77.6 %collective-permute-start.23 = (f32[4,128,256]{1,2,0:T(8,128)}, f32[4,128,256]{1,2,0:T(8,128)}, u32[]{:S(2)}, u32[]{:S(2)}) collective-permute-start(f32[4,128,256]{1,2,0:T(8,128)} %get-tuple-element.7), channel_id=1, source_target_pairs={{0,1},{1,2},{2,3},{3,0},{4,5},{5,6},{6,7},{7,4},{8,9},{9,10},{10,1... | collective-permute-start | bytes 1572872 | tf_op jit(solution)/shard_map/ppermute | solution.py:72
  385.5 70.3 %copy-start.1 = (bf16[1,128,4096]{1,2,0:T(8,128)(2,1)S(1)}, bf16[1,128,4096]{1,2,0:T(8,128)(2,1)}, u32[]{:S(2)}) copy-start(bf16[1,128,4096]{1,2,0:T(8,128)(2,1)} %copy.33) | copy-start | bytes 3145732
  385.5 70.3 %copy-start.8 = (f32[4,4,256]{2,0,1:T(4,128)S(1)}, f32[4,4,256]{2,0,1:T(4,128)}, u32[]{:S(2)}) copy-start(f32[4,4,256]{2,0,1:T(4,128)} %copy.55) | copy-start | bytes 49156
  387.4 70.7 %copy-start.9 = (f32[128]{0:T(128)}, f32[128]{0:T(128)S(1)}, u32[]{:S(2)}) copy-start(f32[128]{0:T(128)S(1)} %add_rsqrt_fusion) | copy-start | bytes 1540
  459.1 20.0 %collective-permute-start.25 = (bf16[4,128,256]{1,2,0:T(8,128)(2,1)}, bf16[4,128,256]{1,2,0:T(8,128)(2,1)}, u32[]{:S(2)}, u32[]{:S(2)}) collective-permute-start(bf16[4,128,256]{1,2,0:T(8,128)(2,1)} %get-tuple-element.26), channel_id=1, source_target_pairs={{0,1},{1,2},{2,3},{3,0},{4,5},{5,6},{6,7},{7,4},{8,9},{9,10},{10,1... | collective-permute-start | bytes 786440 | tf_op jit(solution)/shard_map/ppermute | solution.py:54
  464.0 32.5 %collective-permute-start.26 = (bf16[4,128,256]{1,2,0:T(8,128)(2,1)}, bf16[4,128,256]{1,2,0:T(8,128)(2,1)}, u32[]{:S(2)}, u32[]{:S(2)}) collective-permute-start(bf16[4,128,256]{1,2,0:T(8,128)(2,1)} %get-tuple-element.25), channel_id=1, source_target_pairs={{0,2},{1,3},{2,0},{3,1},{4,6},{5,7},{6,4},{7,5},{8,10},{9,11},{10,... | collective-permute-start | bytes 786440 | tf_op jit(solution)/shard_map/ppermute | solution.py:54
  470.6 29.5 %collective-permute-start.27 = (bf16[4,128,256]{1,2,0:T(8,128)(2,1)}, bf16[4,128,256]{1,2,0:T(8,128)(2,1)}, u32[]{:S(2)}, u32[]{:S(2)}) collective-permute-start(bf16[4,128,256]{1,2,0:T(8,128)(2,1)} %get-tuple-element.24), channel_id=1, source_target_pairs={{0,3},{1,0},{2,1},{3,2},{4,7},{5,4},{6,5},{7,6},{8,11},{9,8},{10,9... | collective-permute-start | bytes 786440 | tf_op jit(solution)/shard_map/ppermute | solution.py:54
  477.2 1.8 copy-start.11
  477.2 22.9 %copy-start.5 = (bf16[4,1,128,256]{2,3,1,0:T(8,128)(2,1)S(1)}, bf16[4,1,128,256]{2,3,1,0:T(8,128)(2,1)}, u32[]{:S(2)}) copy-start(bf16[4,1,128,256]{2,3,1,0:T(8,128)(2,1)} %get-tuple-element.23) | copy-start | bytes 786436
  479.0 30.9 %copy-start.2 = (bf16[1,128,4096]{1,2,0:T(8,128)(2,1)S(1)}, bf16[1,128,4096]{1,2,0:T(8,128)(2,1)}, u32[]{:S(2)}) copy-start(bf16[1,128,4096]{1,2,0:T(8,128)(2,1)} %copy.33) | copy-start | bytes 3145732
  479.0 30.9 %copy-start.4 = (bf16[1,128,4096]{1,2,0:T(8,128)(2,1)S(1)}, bf16[1,128,4096]{1,2,0:T(8,128)(2,1)}, u32[]{:S(2)}) copy-start(bf16[1,128,4096]{1,2,0:T(8,128)(2,1)} %copy.32) | copy-start | bytes 3145732
  479.1 30.9 %copy-start.10 = (f32[128]{0:T(128)S(1)}, f32[128]{0:T(128)}, u32[]{:S(2)}) copy-start(f32[128]{0:T(128)} %copy-done.9) | copy-start | bytes 1540
  501.5 15.0 %collective-permute-start.28 = (bf16[4,128,256]{1,2,0:T(8,128)(2,1)S(1)}, bf16[4,128,256]{1,2,0:T(8,128)(2,1)S(1)}, u32[]{:S(2)}, u32[]{:S(2)}) collective-permute-start(bf16[4,128,256]{1,2,0:T(8,128)(2,1)S(1)} %get-tuple-element.22), channel_id=1, source_target_pairs={{0,4},{1,5},{2,6},{3,7},{4,8},{5,9},{6,10},{7,11},{8,12},{9,13},{1... | collective-permute-start | bytes 786440 | tf_op jit(solution)/shard_map/ppermute | solution.py:59
  503.4 13.0 %collective-permute-start.29 = (bf16[4,128,256]{1,2,0:T(8,128)(2,1)S(1)}, bf16[4,128,256]{1,2,0:T(8,128)(2,1)S(1)}, u32[]{:S(2)}, u32[]{:S(2)}) collective-permute-start(bf16[4,128,256]{1,2,0:T(8,128)(2,1)S(1)} %get-tuple-element.21), channel_id=1, source_target_pairs={{0,8},{1,9},{2,10},{3,11},{4,12},{5,13},{6,14},{7,15},{8,0},{9,1},... | collective-permute-start | bytes 786440 | tf_op jit(solution)/shard_map/ppermute | solution.py:59
  505.3 14.3 %collective-permute-start.30 = (bf16[4,128,256]{1,2,0:T(8,128)(2,1)S(1)}, bf16[4,128,256]{1,2,0:T(8,128)(2,1)S(1)}, u32[]{:S(2)}, u32[]{:S(2)}) collective-permute-start(bf16[4,128,256]{1,2,0:T(8,128)(2,1)S(1)} %get-tuple-element.20), channel_id=1, source_target_pairs={{0,12},{1,13},{2,14},{3,15},{4,0},{5,1},{6,2},{7,3},{8,4},{9,5},{1... | collective-permute-start | bytes 786440 | tf_op jit(solution)/shard_map/ppermute | solution.py:59
  511.0 27.4 %collective-permute-start.24 = (bf16[128,4096]{0,1:T(8,128)(2,1)S(1)}, bf16[128,4096]{0,1:T(8,128)(2,1)}, u32[]{:S(2)}, u32[]{:S(2)}) collective-permute-start(bf16[128,4096]{0,1:T(8,128)(2,1)S(1)} %fusion.20), channel_id=1, source_target_pairs={{0,16},{16,32},{32,48},{48,64},{64,80},{80,96},{96,112},{112,128},... | collective-permute-start | bytes 3145736 | tf_op jit(solution)/shard_map/ppermute | solution.py:14
  519.7 17.9 %copy-start.6 = (bf16[1,256,768]{2,1,0:T(8,128)(2,1)S(1)}, bf16[1,256,768]{2,1,0:T(8,128)(2,1)}, u32[]{:S(2)}) copy-start(bf16[1,256,768]{2,1,0:T(8,128)(2,1)} %param.14) | copy-start | bytes 1179652
  520.7 16.9 %collective-permute-start.31 = (bf16[256,768]{1,0:T(8,128)(2,1)S(1)}, bf16[256,768]{1,0:T(8,128)(2,1)S(1)}, u32[]{:S(2)}, u32[]{:S(2)}) collective-permute-start(bf16[256,768]{1,0:T(8,128)(2,1)S(1)} %fusion.32), channel_id=1, source_target_pairs={{0,496},{16,480},{32,464},{48,448},{64,432},{80,416},{96,400},{112... | collective-permute-start | bytes 1179656 | tf_op jit(solution)/shard_map/ppermute | solution.py:19
Sparse Core Ops, SparseCore 0:
  11.0 144.8 all-gather.2

commit v2 on v1

--- a/solution.py
+++ b/solution.py
@@ -44,20 +44,40 @@
     return total
 
 
-def scatter_columns(x, o, i):
+def gather_and_scatter(x, cols, o, i):
     outer = lax.axis_size("seq") // INNER
     n = x.shape[0]
-    parts = x.reshape(n, outer, INNER, -1).transpose(2, 1, 0, 3)
-    first = [parts[i]]
+    parts = cols.reshape(n, outer, INNER, -1).transpose(2, 1, 0, 3)
+    first = [jnp.concatenate([x[None], parts[i]])]
     for k in range(1, INNER):
         piece = lax.dynamic_index_in_dim(parts, (i + k) % INNER, 0, keepdims=False)
-        first.append(lax.ppermute(piece, "seq", seq_pairs(k, 0)))
+        first.append(lax.ppermute(jnp.concatenate([x[None], piece]), "seq", seq_pairs(k, 0)))
     first = jnp.stack(first, axis=1)
-    second = [first[o]]
-    for k in range(1, outer):
-        piece = lax.dynamic_index_in_dim(first, (o + k) % outer, 0, keepdims=False)
-        second.append(lax.ppermute(piece, "seq", seq_pairs(k, 1)))
-    return jnp.stack(second)
+    second = [first]
+    for k in range(1, outer):
+        piece = lax.dynamic_index_in_dim(first[1:], (o + k) % outer, 0, keepdims=False)
+        second.append(lax.ppermute(jnp.concatenate([first[0], piece]), "seq", seq_pairs(k, 1)))
+    gathered = jnp.stack([second[0][0]] + [s[:INNER] for s in second[1:]])
+    scattered = jnp.stack([second[0][1 + o]] + [s[INNER:] for s in second[1:]])
+    return gathered, scattered
+
+
+def reduce_and_gather(partial, own):
+    outer = lax.axis_size("seq") // INNER
+    n, w = partial.shape[2], partial.shape[3]
+    acc = partial[0]
+    for k in range(1, outer):
+        acc = acc + lax.ppermute(partial[k], "seq", seq_pairs(outer - k, 1))
+    mine = jnp.concatenate([acc.transpose(1, 0, 2).reshape(n, INNER * w), own.astype(jnp.float32)], axis=1)
+    total = acc
+    rows = [own.astype(jnp.float32)]
+    for k in range(1, INNER):
+        got = lax.ppermute(mine, "seq", seq_pairs(k, 0))
+        sums = got[:, : INNER * w].reshape(n, INNER, w).transpose(1, 0, 2)
+        total = total + jnp.roll(sums, k, axis=0)
+        rows.append(got[:, INNER * w :])
+    group = jnp.concatenate([jnp.stack(rows), total], axis=2).astype(own.dtype)
+    return jnp.stack([group] + [lax.ppermute(group, "seq", seq_pairs(k, 1)) for k in range(1, outer)])
 
 
 def gather_columns(y, o, i):
@@ -117,7 +137,9 @@
     unit_up, inverse_up, normed_up = normalize(up_activation[0], upward_gain[0])
     hidden = normed_up.astype(jnp.bfloat16)
     output_weight = lax.all_gather(up_output_weight[0], "seq", axis=1, tiled=True)
-    key_value = gather_blocks(saved[:, width:]).reshape(size * count, 2 * HEAD)
+    key_value, hidden_cols = gather_and_scatter(saved[:, width:], hidden, o, i)
+    key_value = key_value.reshape(size * count, 2 * HEAD)
+    hidden_cols = hidden_cols.reshape(size * count, -1)
     keys = key_value[:, :HEAD]
     values = key_value[:, HEAD:]
     sources = (
@@ -125,7 +147,6 @@
         + ((i - jnp.arange(INNER, dtype=jnp.int32)) % INNER)[None, :]
     ).reshape(size)
     key_positions = (sources[:, None] * count + jnp.arange(count, dtype=jnp.int32)[None, :]).reshape(-1)
-    hidden_cols = scatter_columns(hidden, o, i).reshape(size * count, -1)
     query = saved[:, :width].reshape(count, GROUP, HEAD)
     attn_grad = contract_last(cotangent, output_weight).astype(jnp.bfloat16)
     positions = first + jnp.arange(count, dtype=jnp.int32)
@@ -151,12 +172,11 @@
     key_part = jnp.einsum("tgj,tgh->jh", score_grad, query, preferred_element_type=jnp.float32)
     value_part = jnp.einsum("tgj,tgh->jh", weights, grad_heads, preferred_element_type=jnp.float32)
     kv_part = jnp.concatenate([key_part, value_part], axis=1).reshape(outer, INNER, count, 2 * HEAD)
-    kv_grad = reduce_blocks(kv_part).astype(jnp.bfloat16)
-    own_grad = jnp.concatenate([query_grad, kv_grad], axis=1)
-    grad_all = gather_blocks(own_grad).reshape(size * count, -1)
+    grad_all = reduce_and_gather(kv_part, query_grad).reshape(size * count, -1)
     input_term = contract_first(hidden_cols, grad_all).astype(jnp.bfloat16)
     block = contract_last(grad_all, up_input_weight[0])
-    hidden_grad = gather_columns(block.reshape(outer, INNER, count, -1), o, i)
+    hidden_grad = gather_columns(block.astype(jnp.bfloat16).reshape(outer, INNER, count, -1), o, i)
+    hidden_grad = hidden_grad.astype(jnp.float32)
     scaled = hidden_grad * upward_gain[0]
     input_grad = cotangent.astype(jnp.float32) + inverse_up * (
         scaled - unit_up * jnp.mean(scaled * unit_up, axis=-1, keepdims=True)

time: 558 us -> 577 us (1.034)
  starting transfers between devices: 144 us -> 124 us
  waiting for transfers between devices: 312 us -> 332 us
  local copies, waits for them, and re-layouts: 29.7 us -> 44.5 us
    ppermute x24 -> x15, waiting for transfers between devices: 130 us -> 218 us  [the longest x3 91.4 us: reduce_and_gather(): got = lax.ppermute(mine, 'seq', seq_pairs(k, 0))]
    ppermute x24 -> x15, starting transfers between devices: 109 us -> 73.3 us  [the longest x3 24.6 us: gather_and_scatter(): lax.ppermute(jnp.concatenate([x[None], piece]), 'seq', seq_pairs(k, 0))]
    ppermute x3, waiting for transfers between devices: 66.3 us -> 31.4 us  [gather_columns(): second.append(lax.ppermute(first[k], 'seq', seq_pairs(INNER - k, 0)))]
    all_gather x1, waiting for transfers between devices: 85.2 us -> 54.2 us  [per_device(): lax.all_gather(up_output_weight[0], 'seq', axis=1, tiled=True)]
    ppermute x3, starting transfers between devices: 15.7 us -> 37.4 us  [gather_columns(): second.append(lax.ppermute(first[k], 'seq', seq_pairs(INNER - k, 0)))]
    ppermute x3, waiting for transfers between devices: 20.3 us -> 8.91 us  [gather_columns(): first.append(lax.ppermute(y[k], 'seq', seq_pairs(outer - k, 1)))]
    ppermute x1, waiting for transfers between devices: 9.15 us -> 18.7 us  [mirrored(): lax.ppermute(value, axis, [(source, count - 1 - source) for source in ran...]
    slice x0 -> x12, local copies, waits for them, and re-layouts: none -> 9.18 us  [the longest x6 6.2 us: reduce_and_gather(): sums = got[:, :INNER * w].reshape(n, INNER, w).transpose(1, 0, 2)]
  transfers between devices with their start and end apart: 33 -> 24, of which waited for: 24 -> 18; matrix products, arithmetic and copies ran while one was open for 7% -> 8% of each run, Pallas kernels for 0% -> 0%
where the time goes in v2:
time: 577 us; the launch traced here: 569 us
  waiting for transfers between devices  332 us (58%)
  starting transfers between devices  124 us (21%)
  local copies, waits for them, and re-layouts  44.5 us (8%)
  matrix products  33.7 us (6%)
  other arithmetic  20.3 us (4%)
  between operations  14.9 us (3%)
    ppermute x3, waiting for transfers between devices, reduce_and_gather(): got = lax.ppermute(mine, 'seq', seq_pairs(k, 0))  91.4 us
    ppermute x3, waiting for transfers between devices, gather_and_scatter(): lax.ppermute(jnp.concatenate([x[None], piece]), 'seq', seq_pairs(k, 0))  64.9 us
    all_gather x1, waiting for transfers between devices, per_device(): lax.all_gather(up_output_weight[0], 'seq', axis=1, tiled=True)  54.2 us
    ppermute x3, starting transfers between devices, gather_columns(): second.append(lax.ppermute(first[k], 'seq', seq_pairs(INNER - k, 0)))  37.4 us
    ppermute x3, waiting for transfers between devices, reduce_and_gather(): lax.ppermute(group, 'seq', seq_pairs(k, 1))  32 us
    ppermute x3, waiting for transfers between devices, gather_columns(): second.append(lax.ppermute(first[k], 'seq', seq_pairs(INNER - k, 0)))  31.4 us
    ppermute x3, starting transfers between devices, gather_and_scatter(): lax.ppermute(jnp.concatenate([x[None], piece]), 'seq', seq_pairs(k, 0))  24.6 us
    ppermute x3, waiting for transfers between devices, gather_and_scatter(): lax.ppermute(jnp.concatenate([first[0], piece]), 'seq', seq_pairs(k, 1))  22.3 us
  transfers between devices with their start and end apart: 24, of which 18 were waited for; matrix products, arithmetic and copies ran while one was open for 8% of the time, Pallas kernels for 0%

profile of v2, /device:TPU:25, one launch (start us, length us, event | category | flops | bytes accessed | tf_op | source)
XLA Modules:
  0.0 569.3 jit_solution(2678401720963428614)
XLA Ops:
  8.5 1.4 reduce.4
  11.0 1.6 copy.37
  14.2 8.8 %collective-permute-start = (bf16[5,128,256]{1,2,0:T(8,128)(2,1)S(1)}, bf16[5,128,256]{1,2,0:T(8,128)(2,1)S(1)}, u32[]{:S(2)}, u32[]{:S(2)}) collective-permute-start(bf16[5,128,256]{1,2,0:T(8,128)(2,1)S(1)} %get-tuple-element.38), channel_id=1, source_target_pairs={{0,1},{1,2},{2,3},{3,0},{4,5},{5,6},{6,7},{7,4},{8,9},{9,10},{10,1... | collective-permute-start | bytes 983048 | tf_op jit(solution)/shard_map/ppermute | solution.py:54
  23.0 10.6 %collective-permute-start.1 = (bf16[5,128,256]{1,2,0:T(8,128)(2,1)S(1)}, bf16[5,128,256]{1,2,0:T(8,128)(2,1)}, u32[]{:S(2)}, u32[]{:S(2)}) collective-permute-start(bf16[5,128,256]{1,2,0:T(8,128)(2,1)S(1)} %get-tuple-element.39), channel_id=1, source_target_pairs={{0,2},{1,3},{2,0},{3,1},{4,6},{5,7},{6,4},{7,5},{8,10},{9,11},{10,... | collective-permute-start | bytes 983048 | tf_op jit(solution)/shard_map/ppermute | solution.py:54
  33.7 5.2 collective-permute-start.2
  39.1 26.7 %collective-permute-done.1 = bf16[5,128,256]{1,2,0:T(8,128)(2,1)} collective-permute-done((bf16[5,128,256]{1,2,0:T(8,128)(2,1)S(1)}, bf16[5,128,256]{1,2,0:T(8,128)(2,1)}, u32[]{:S(2)}, u32[]{:S(2)}) %collective-permute-start.1) | collective-permute-done | bytes 327712 | tf_op jit(solution)/shard_map/ppermute | solution.py:54
  65.8 38.2 %collective-permute-done.2 = bf16[5,128,256]{1,2,0:T(8,128)(2,1)} collective-permute-done((bf16[5,128,256]{1,2,0:T(8,128)(2,1)S(1)}, bf16[5,128,256]{1,2,0:T(8,128)(2,1)}, u32[]{:S(2)}, u32[]{:S(2)}) %collective-permute-start.2) | collective-permute-done | bytes 327712 | tf_op jit(solution)/shard_map/ppermute | solution.py:54
  106.3 2.9 collective-permute-start.3
  109.3 3.8 collective-permute-start.4
  113.1 3.0 collective-permute-start.5
  117.8 2.3 collective-permute-done.3
  120.9 18.9 %collective-permute-done.4 = bf16[8,128,256]{1,2,0:T(8,128)(2,1)S(1)} collective-permute-done((bf16[8,128,256]{1,2,0:T(8,128)(2,1)S(1)}, bf16[8,128,256]{1,2,0:T(8,128)(2,1)S(1)}, u32[]{:S(2)}, u32[]{:S(2)}) %collective-permute-start.4) | collective-permute-done | bytes 524320 | tf_op jit(solution)/shard_map/ppermute | solution.py:59
  143.1 5.5 fusion.78
  148.5 54.2 %all-gather.3.cloned.1.call-done = bf16[1,512,4096]{2,1,0:T(8,128)(2,1)} async-done(((bf16[1,512,256]{2,1,0:T(8,128)(2,1)}), bf16[1,512,4096]{2,1,0:T(8,128)(2,1)}) %all-gather.3.cloned.1.call-update) | async-done | bytes 4194320 | tf_op jit(solution)/shard_map/all_gather | solution.py:139
  202.7 4.4 fusion.27
  207.1 1.7 copy.87
  208.8 3.8 fusion.58
  212.5 1.8 convolution_bitcast_fusion
  214.4 8.3 %convolution_bitcast_fusion.1 = f32[2048,128]{0,1:T(8,128)} fusion(bf16[128,4,128]{0,2,1:T(8,128)(2,1)} %bitcast.227, f32[128,4,2048]{0,2,1:T(8,128)} %fusion.58, f32[128,4,2048]{0,2,1:T(8,128)} %get-tuple-element.42, f32[128,4]{0,1:T(4,128)} %get-tuple-element.41), kind=kOutput, calls=%fused_computation.21 | convolution fusion | flops 275778048 | bytes 9570304 | tf_op jit(solution)/shard_map/tgj,tgh->jh/dot_general | solution.py:172
  222.6 2.9 fusion.57
  225.5 2.1 copy.84
  227.5 2.0 copy.86
  229.6 2.1 copy.85
  231.6 3.8 collective-permute-start.7
  235.5 3.0 collective-permute-start.8
  238.5 3.7 collective-permute-start.6
  242.2 7.9 %fusion.33 = f32[128,4,128]{0,2,1:T(8,128)} fusion(f32[128,4,2048]{0,2,1:T(8,128)} %fusion.58, bf16[2048,256]{1,0:T(8,128)(2,1)S(1)} %bitcast.193, f32[128,4,2048]{0,2,1:T(8,128)} %get-tuple-element.42, f32[128,4]{0,1:T(4,128)} %get-tuple-element.41), kind=kOutput, calls=%fused_computation.57 | convolution fusion | flops 275909120 | bytes 17567744 | tf_op jit(solution)/shard_map/tgj,jh->tgh/dot_general | solution.py:168
  250.1 1.8 copy.60
  251.9 1.2 copy.83
  253.1 7.3 %collective-permute-done.8 = f32[4,128,256]{2,1,0:T(8,128)} collective-permute-done((f32[4,128,256]{2,1,0:T(8,128)}, f32[4,128,256]{2,1,0:T(8,128)}, u32[]{:S(2)}, u32[]{:S(2)}) %collective-permute-start.8) | collective-permute-done | bytes 524320 | tf_op jit(solution)/shard_map/ppermute | solution.py:70
  260.4 1.5 add_add_fusion
  264.2 1.9 pad_maximum_fusion.4
  266.1 8.1 %collective-permute-start.11 = (f32[128,1536]{1,0:T(8,128)}, f32[128,1536]{1,0:T(8,128)}, u32[]{:S(2)}, u32[]{:S(2)}) collective-permute-start(f32[128,1536]{1,0:T(8,128)} %pad_maximum_fusion.4), channel_id=1, source_target_pairs={{0,3},{1,0},{2,1},{3,2},{4,7},{5,4},{6,5},{7,6},{8,11},{9,8},{10,9... | collective-permute-start | bytes 2359304 | tf_op jit(solution)/shard_map/ppermute | solution.py:75
  274.2 1.9 collective-permute-start.9
  276.1 7.0 %collective-permute-start.10 = (f32[128,1536]{1,0:T(8,128)}, f32[128,1536]{1,0:T(8,128)}, u32[]{:S(2)}, u32[]{:S(2)}) collective-permute-start(f32[128,1536]{1,0:T(8,128)} %pad_maximum_fusion.4), channel_id=1, source_target_pairs={{0,2},{1,3},{2,0},{3,1},{4,6},{5,7},{6,4},{7,5},{8,10},{9,11},{10,... | collective-permute-start | bytes 2359304 | tf_op jit(solution)/shard_map/ppermute | solution.py:75
  283.1 1.7 copy.61
  284.8 46.1 %collective-permute-done.11 = f32[128,1536]{1,0:T(8,128)} collective-permute-done((f32[128,1536]{1,0:T(8,128)}, f32[128,1536]{1,0:T(8,128)}, u32[]{:S(2)}, u32[]{:S(2)}) %collective-permute-start.11) | collective-permute-done | bytes 786464 | tf_op jit(solution)/shard_map/ppermute | solution.py:75
  333.0 1.2 copy.67
  335.7 29.3 %collective-permute-done.9 = f32[128,1536]{1,0:T(8,128)} collective-permute-done((f32[128,1536]{1,0:T(8,128)}, f32[128,1536]{1,0:T(8,128)}, u32[]{:S(2)}, u32[]{:S(2)}) %collective-permute-start.9) | collective-permute-done | bytes 786464 | tf_op jit(solution)/shard_map/ppermute | solution.py:75
  367.1 1.2 copy.63
  369.8 15.9 %collective-permute-done.10 = f32[128,1536]{1,0:T(8,128)} collective-permute-done((f32[128,1536]{1,0:T(8,128)}, f32[128,1536]{1,0:T(8,128)}, u32[]{:S(2)}, u32[]{:S(2)}) %collective-permute-start.10) | collective-permute-done | bytes 786464 | tf_op jit(solution)/shard_map/ppermute | solution.py:75
  394.2 1.9 collective-permute-start.14
  396.1 6.6 %collective-permute-start.13 = (bf16[4,128,768]{2,1,0:T(8,128)(2,1)S(1)}, bf16[4,128,768]{2,1,0:T(8,128)(2,1)S(1)}, u32[]{:S(2)}, u32[]{:S(2)}) collective-permute-start(bf16[4,128,768]{2,1,0:T(8,128)(2,1)S(1)} %pad_maximum_fusion.5), channel_id=1, source_target_pairs={{0,8},{1,9},{2,10},{3,11},{4,12},{5,13},{6,14},{7,15},{8,0},{9,1},... | collective-permute-start | bytes 2359304 | tf_op jit(solution)/shard_map/ppermute | solution.py:80
  402.8 2.8 collective-permute-start.12
  405.6 9.8 %collective-permute-done.14 = bf16[4,128,768]{2,1,0:T(8,128)(2,1)S(1)} collective-permute-done((bf16[4,128,768]{2,1,0:T(8,128)(2,1)S(1)}, bf16[4,128,768]{2,1,0:T(8,128)(2,1)S(1)}, u32[]{:S(2)}, u32[]{:S(2)}) %collective-permute-start.14) | collective-permute-done | bytes 786464 | tf_op jit(solution)/shard_map/ppermute | solution.py:80
  415.5 4.6 collective-permute-done.13
  420.1 17.6 %collective-permute-done.12 = bf16[4,128,768]{2,1,0:T(8,128)(2,1)S(1)} collective-permute-done((bf16[4,128,768]{2,1,0:T(8,128)(2,1)S(1)}, bf16[4,128,768]{2,1,0:T(8,128)(2,1)S(1)}, u32[]{:S(2)}, u32[]{:S(2)}) %collective-permute-start.12) | collective-permute-done | bytes 786464 | tf_op jit(solution)/shard_map/ppermute | solution.py:80
  440.8 1.9 collective-permute-start.15
  442.7 4.9 collective-permute-start.16
  447.6 2.8 collective-permute-start.17
  450.5 2.4 collective-permute-done.16
  452.9 6.5 %collective-permute-done.17 = bf16[4,128,256]{1,2,0:T(8,128)(2,1)} collective-permute-done((bf16[4,128,256]{1,2,0:T(8,128)(2,1)}, bf16[4,128,256]{1,2,0:T(8,128)(2,1)}, u32[]{:S(2)}, u32[]{:S(2)}) %collective-permute-start.17) | collective-permute-done | bytes 262176 | tf_op jit(solution)/shard_map/ppermute | solution.py:88
  459.4 1.2 pad_maximum_fusion.3
  461.6 28.5 %collective-permute-start.20 = (bf16[4,128,256]{1,2,0:T(8,128)(2,1)}, bf16[4,128,256]{1,2,0:T(8,128)(2,1)S(1)}, u32[]{:S(2)}, u32[]{:S(2)}) collective-permute-start(bf16[4,128,256]{1,2,0:T(8,128)(2,1)} %get-tuple-element.11), channel_id=1, source_target_pairs={{0,1},{1,2},{2,3},{3,0},{4,5},{5,6},{6,7},{7,4},{8,9},{9,10},{10,1... | collective-permute-start | bytes 786440 | tf_op jit(solution)/shard_map/ppermute | solution.py:92
  490.1 6.8 %collective-permute-start.19 = (bf16[4,128,256]{1,2,0:T(8,128)(2,1)}, bf16[4,128,256]{1,2,0:T(8,128)(2,1)S(1)}, u32[]{:S(2)}, u32[]{:S(2)}) collective-permute-start(bf16[4,128,256]{1,2,0:T(8,128)(2,1)} %get-tuple-element.12), channel_id=1, source_target_pairs={{0,2},{1,3},{2,0},{3,1},{4,6},{5,7},{6,4},{7,5},{8,10},{9,11},{10,... | collective-permute-start | bytes 786440 | tf_op jit(solution)/shard_map/ppermute | solution.py:92
  496.9 2.1 collective-permute-start.18
  499.1 1.3 copy.36
  500.4 2.2 collective-permute-done.20
  502.5 29.2 %collective-permute-done.19 = bf16[4,128,256]{1,2,0:T(8,128)(2,1)S(1)} collective-permute-done((bf16[4,128,256]{1,2,0:T(8,128)(2,1)}, bf16[4,128,256]{1,2,0:T(8,128)(2,1)S(1)}, u32[]{:S(2)}, u32[]{:S(2)}) %collective-permute-start.19) | collective-permute-done | bytes 262176 | tf_op jit(solution)/shard_map/ppermute | solution.py:92
  532.9 1.6 fusion.10
  536.7 1.9 collective-permute-start.21
  539.7 1.9 collective-permute-start.22
  541.6 18.7 %collective-permute-done.22 = bf16[256,768]{1,0:T(8,128)(2,1)S(1)} collective-permute-done((bf16[256,768]{1,0:T(8,128)(2,1)S(1)}, bf16[256,768]{1,0:T(8,128)(2,1)S(1)}, u32[]{:S(2)}, u32[]{:S(2)}) %collective-permute-start.22) | collective-permute-done | bytes 393248 | tf_op jit(solution)/shard_map/ppermute | solution.py:19
  561.1 1.3 copy.74
  (112 shorter events, 39.1 us)
Async XLA Ops:
  7.2 430.7 %copy-start = (bf16[1,256,768]{2,1,0:T(8,128)(2,1)S(1)}, bf16[1,256,768]{2,1,0:T(8,128)(2,1)}, u32[]{:S(2)}) copy-start(bf16[1,256,768]{2,1,0:T(8,128)(2,1)} %param.11) | copy-start | bytes 1179652
  7.2 195.5 %all-gather.3.cloned.1.call-start = ((), (), s32[]{:S(2)}) async-start(), calls=%async_computation | async-start | bytes 4456448 | tf_op jit(solution)/shard_map/all_gather | solution.py:139
  13.2 0.8 copy-start.15
  14.2 24.9 %collective-permute-start = (bf16[5,128,256]{1,2,0:T(8,128)(2,1)S(1)}, bf16[5,128,256]{1,2,0:T(8,128)(2,1)S(1)}, u32[]{:S(2)}, u32[]{:S(2)}) collective-permute-start(bf16[5,128,256]{1,2,0:T(8,128)(2,1)S(1)} %get-tuple-element.38), channel_id=1, source_target_pairs={{0,1},{1,2},{2,3},{3,0},{4,5},{5,6},{6,7},{7,4},{8,9},{9,10},{10,1... | collective-permute-start | bytes 983048 | tf_op jit(solution)/shard_map/ppermute | solution.py:54
  23.0 42.8 %collective-permute-start.1 = (bf16[5,128,256]{1,2,0:T(8,128)(2,1)S(1)}, bf16[5,128,256]{1,2,0:T(8,128)(2,1)}, u32[]{:S(2)}, u32[]{:S(2)}) collective-permute-start(bf16[5,128,256]{1,2,0:T(8,128)(2,1)S(1)} %get-tuple-element.39), channel_id=1, source_target_pairs={{0,2},{1,3},{2,0},{3,1},{4,6},{5,7},{6,4},{7,5},{8,10},{9,11},{10,... | collective-permute-start | bytes 983048 | tf_op jit(solution)/shard_map/ppermute | solution.py:54
  33.7 70.4 %collective-permute-start.2 = (bf16[5,128,256]{1,2,0:T(8,128)(2,1)S(1)}, bf16[5,128,256]{1,2,0:T(8,128)(2,1)}, u32[]{:S(2)}, u32[]{:S(2)}) collective-permute-start(bf16[5,128,256]{1,2,0:T(8,128)(2,1)S(1)} %get-tuple-element.40), channel_id=1, source_target_pairs={{0,3},{1,0},{2,1},{3,2},{4,7},{5,4},{6,5},{7,6},{8,11},{9,8},{10,9... | collective-permute-start | bytes 983048 | tf_op jit(solution)/shard_map/ppermute | solution.py:54
  105.4 10.8 %copy-start.17 = (s32[1,128]{1,0:T(1,128)S(1)}, s32[1,128]{1,0:T(1,128)}, u32[]{:S(2)}) copy-start(s32[1,128]{1,0:T(1,128)} %param.15) | copy-start | bytes 1540
  106.3 13.8 %collective-permute-start.3 = (bf16[8,128,256]{1,2,0:T(8,128)(2,1)S(1)}, bf16[8,128,256]{1,2,0:T(8,128)(2,1)S(1)}, u32[]{:S(2)}, u32[]{:S(2)}) collective-permute-start(bf16[8,128,256]{1,2,0:T(8,128)(2,1)S(1)} %get-tuple-element.34), channel_id=1, source_target_pairs={{0,4},{1,5},{2,6},{3,7},{4,8},{5,9},{6,10},{7,11},{8,12},{9,13},{1... | collective-permute-start | bytes 1572872 | tf_op jit(solution)/shard_map/ppermute | solution.py:59
  109.3 30.5 %collective-permute-start.4 = (bf16[8,128,256]{1,2,0:T(8,128)(2,1)S(1)}, bf16[8,128,256]{1,2,0:T(8,128)(2,1)S(1)}, u32[]{:S(2)}, u32[]{:S(2)}) collective-permute-start(bf16[8,128,256]{1,2,0:T(8,128)(2,1)S(1)} %get-tuple-element.35), channel_id=1, source_target_pairs={{0,8},{1,9},{2,10},{3,11},{4,12},{5,13},{6,14},{7,15},{8,0},{9,1},... | collective-permute-start | bytes 1572872 | tf_op jit(solution)/shard_map/ppermute | solution.py:59
  113.1 28.5 %collective-permute-start.5 = (bf16[8,128,256]{1,2,0:T(8,128)(2,1)S(1)}, bf16[8,128,256]{1,2,0:T(8,128)(2,1)S(1)}, u32[]{:S(2)}, u32[]{:S(2)}) collective-permute-start(bf16[8,128,256]{1,2,0:T(8,128)(2,1)S(1)} %get-tuple-element.36), channel_id=1, source_target_pairs={{0,12},{1,13},{2,14},{3,15},{4,0},{5,1},{6,2},{7,3},{8,4},{9,5},{1... | collective-permute-start | bytes 1572872 | tf_op jit(solution)/shard_map/ppermute | solution.py:59
  143.0 59.7 %copy-start.1 = (bf16[1,128,4096]{2,1,0:T(8,128)(2,1)S(1)}, bf16[1,128,4096]{2,1,0:T(8,128)(2,1)}, u32[]{:S(2)}) copy-start(bf16[1,128,4096]{2,1,0:T(8,128)(2,1)} %param.10) | copy-start | bytes 3145732
  208.7 3.8 copy-start.8
  208.8 3.8 copy-start.18
  208.8 3.8 copy-start.19
  231.6 21.5 %collective-permute-start.7 = (f32[4,128,256]{2,1,0:T(8,128)}, f32[4,128,256]{2,1,0:T(8,128)}, u32[]{:S(2)}, u32[]{:S(2)}) collective-permute-start(f32[4,128,256]{2,1,0:T(8,128)} %bitcast.221), channel_id=1, source_target_pairs={{0,8},{1,9},{2,10},{3,11},{4,12},{5,13},{6,14},{7,15},{8,0},{9,1},... | collective-permute-start | bytes 1572872 | tf_op jit(solution)/shard_map/ppermute | solution.py:70
  235.5 24.9 %collective-permute-start.8 = (f32[4,128,256]{2,1,0:T(8,128)}, f32[4,128,256]{2,1,0:T(8,128)}, u32[]{:S(2)}, u32[]{:S(2)}) collective-permute-start(f32[4,128,256]{2,1,0:T(8,128)} %bitcast.220), channel_id=1, source_target_pairs={{0,4},{1,5},{2,6},{3,7},{4,8},{5,9},{6,10},{7,11},{8,12},{9,13},{1... | collective-permute-start | bytes 1572872 | tf_op jit(solution)/shard_map/ppermute | solution.py:70
  238.5 22.0 %collective-permute-start.6 = (f32[4,128,256]{2,1,0:T(8,128)}, f32[4,128,256]{2,1,0:T(8,128)}, u32[]{:S(2)}, u32[]{:S(2)}) collective-permute-start(f32[4,128,256]{2,1,0:T(8,128)} %bitcast.219), channel_id=1, source_target_pairs={{0,12},{1,13},{2,14},{3,15},{4,0},{5,1},{6,2},{7,3},{8,4},{9,5},{1... | collective-permute-start | bytes 1572872 | tf_op jit(solution)/shard_map/ppermute | solution.py:70
  266.1 64.9 %collective-permute-start.11 = (f32[128,1536]{1,0:T(8,128)}, f32[128,1536]{1,0:T(8,128)}, u32[]{:S(2)}, u32[]{:S(2)}) collective-permute-start(f32[128,1536]{1,0:T(8,128)} %pad_maximum_fusion.4), channel_id=1, source_target_pairs={{0,3},{1,0},{2,1},{3,2},{4,7},{5,4},{6,5},{7,6},{8,11},{9,8},{10,9... | collective-permute-start | bytes 2359304 | tf_op jit(solution)/shard_map/ppermute | solution.py:75
  274.2 90.9 %collective-permute-start.9 = (f32[128,1536]{1,0:T(8,128)}, f32[128,1536]{1,0:T(8,128)}, u32[]{:S(2)}, u32[]{:S(2)}) collective-permute-start(f32[128,1536]{1,0:T(8,128)} %pad_maximum_fusion.4), channel_id=1, source_target_pairs={{0,1},{1,2},{2,3},{3,0},{4,5},{5,6},{6,7},{7,4},{8,9},{9,10},{10,1... | collective-permute-start | bytes 2359304 | tf_op jit(solution)/shard_map/ppermute | solution.py:75
  276.1 109.6 %collective-permute-start.10 = (f32[128,1536]{1,0:T(8,128)}, f32[128,1536]{1,0:T(8,128)}, u32[]{:S(2)}, u32[]{:S(2)}) collective-permute-start(f32[128,1536]{1,0:T(8,128)} %pad_maximum_fusion.4), channel_id=1, source_target_pairs={{0,2},{1,3},{2,0},{3,1},{4,6},{5,7},{6,4},{7,5},{8,10},{9,11},{10,... | collective-permute-start | bytes 2359304 | tf_op jit(solution)/shard_map/ppermute | solution.py:75
  389.0 4.0 copy-start.5
  389.0 4.0 copy-start.6
  389.1 16.5 %copy-start.7 = (bf16[1,128,512]{2,1,0:T(8,128)(2,1)S(1)}, bf16[1,128,512]{2,1,0:T(8,128)(2,1)}, u32[]{:S(2)}) copy-start(bf16[1,128,512]{2,1,0:T(8,128)(2,1)} %copy.61) | copy-start | bytes 393220
  394.2 21.3 %collective-permute-start.14 = (bf16[4,128,768]{2,1,0:T(8,128)(2,1)S(1)}, bf16[4,128,768]{2,1,0:T(8,128)(2,1)S(1)}, u32[]{:S(2)}, u32[]{:S(2)}) collective-permute-start(bf16[4,128,768]{2,1,0:T(8,128)(2,1)S(1)} %pad_maximum_fusion.5), channel_id=1, source_target_pairs={{0,12},{1,13},{2,14},{3,15},{4,0},{5,1},{6,2},{7,3},{8,4},{9,5},{1... | collective-permute-start | bytes 2359304 | tf_op jit(solution)/shard_map/ppermute | solution.py:80
  396.1 23.9 %collective-permute-start.13 = (bf16[4,128,768]{2,1,0:T(8,128)(2,1)S(1)}, bf16[4,128,768]{2,1,0:T(8,128)(2,1)S(1)}, u32[]{:S(2)}, u32[]{:S(2)}) collective-permute-start(bf16[4,128,768]{2,1,0:T(8,128)(2,1)S(1)} %pad_maximum_fusion.5), channel_id=1, source_target_pairs={{0,8},{1,9},{2,10},{3,11},{4,12},{5,13},{6,14},{7,15},{8,0},{9,1},... | collective-permute-start | bytes 2359304 | tf_op jit(solution)/shard_map/ppermute | solution.py:80
  402.8 34.8 %collective-permute-start.12 = (bf16[4,128,768]{2,1,0:T(8,128)(2,1)S(1)}, bf16[4,128,768]{2,1,0:T(8,128)(2,1)S(1)}, u32[]{:S(2)}, u32[]{:S(2)}) collective-permute-start(bf16[4,128,768]{2,1,0:T(8,128)(2,1)S(1)} %pad_maximum_fusion.5), channel_id=1, source_target_pairs={{0,4},{1,5},{2,6},{3,7},{4,8},{5,9},{6,10},{7,11},{8,12},{9,13},{1... | collective-permute-start | bytes 2359304 | tf_op jit(solution)/shard_map/ppermute | solution.py:80
  437.9 1.6 copy-start.3
  440.8 9.7 %collective-permute-start.15 = (bf16[4,128,256]{1,2,0:T(8,128)(2,1)S(1)}, bf16[4,128,256]{1,2,0:T(8,128)(2,1)}, u32[]{:S(2)}, u32[]{:S(2)}) collective-permute-start(bf16[4,128,256]{1,2,0:T(8,128)(2,1)S(1)} %copy.68), channel_id=1, source_target_pairs={{0,12},{1,13},{2,14},{3,15},{4,0},{5,1},{6,2},{7,3},{8,4},{9,5},{1... | collective-permute-start | bytes 786440 | tf_op jit(solution)/shard_map/ppermute | solution.py:88
  442.7 10.2 %collective-permute-start.16 = (bf16[4,128,256]{1,2,0:T(8,128)(2,1)S(1)}, bf16[4,128,256]{1,2,0:T(8,128)(2,1)}, u32[]{:S(2)}, u32[]{:S(2)}) collective-permute-start(bf16[4,128,256]{1,2,0:T(8,128)(2,1)S(1)} %copy.69), channel_id=1, source_target_pairs={{0,8},{1,9},{2,10},{3,11},{4,12},{5,13},{6,14},{7,15},{8,0},{9,1},... | collective-permute-start | bytes 786440 | tf_op jit(solution)/shard_map/ppermute | solution.py:88
  447.6 11.9 %collective-permute-start.17 = (bf16[4,128,256]{1,2,0:T(8,128)(2,1)}, bf16[4,128,256]{1,2,0:T(8,128)(2,1)}, u32[]{:S(2)}, u32[]{:S(2)}) collective-permute-start(bf16[4,128,256]{1,2,0:T(8,128)(2,1)} %copy.70), channel_id=1, source_target_pairs={{0,4},{1,5},{2,6},{3,7},{4,8},{5,9},{6,10},{7,11},{8,12},{9,13},{1... | collective-permute-start | bytes 786440 | tf_op jit(solution)/shard_map/ppermute | solution.py:88
  461.6 41.0 %collective-permute-start.20 = (bf16[4,128,256]{1,2,0:T(8,128)(2,1)}, bf16[4,128,256]{1,2,0:T(8,128)(2,1)S(1)}, u32[]{:S(2)}, u32[]{:S(2)}) collective-permute-start(bf16[4,128,256]{1,2,0:T(8,128)(2,1)} %get-tuple-element.11), channel_id=1, source_target_pairs={{0,1},{1,2},{2,3},{3,0},{4,5},{5,6},{6,7},{7,4},{8,9},{9,10},{10,1... | collective-permute-start | bytes 786440 | tf_op jit(solution)/shard_map/ppermute | solution.py:92
  490.1 41.7 %collective-permute-start.19 = (bf16[4,128,256]{1,2,0:T(8,128)(2,1)}, bf16[4,128,256]{1,2,0:T(8,128)(2,1)S(1)}, u32[]{:S(2)}, u32[]{:S(2)}) collective-permute-start(bf16[4,128,256]{1,2,0:T(8,128)(2,1)} %get-tuple-element.12), channel_id=1, source_target_pairs={{0,2},{1,3},{2,0},{3,1},{4,6},{5,7},{6,4},{7,5},{8,10},{9,11},{10,... | collective-permute-start | bytes 786440 | tf_op jit(solution)/shard_map/ppermute | solution.py:92
  496.9 34.9 %collective-permute-start.18 = (bf16[4,128,256]{1,2,0:T(8,128)(2,1)}, bf16[4,128,256]{1,2,0:T(8,128)(2,1)S(1)}, u32[]{:S(2)}, u32[]{:S(2)}) collective-permute-start(bf16[4,128,256]{1,2,0:T(8,128)(2,1)} %get-tuple-element.13), channel_id=1, source_target_pairs={{0,3},{1,0},{2,1},{3,2},{4,7},{5,4},{6,5},{7,6},{8,11},{9,8},{10,9... | collective-permute-start | bytes 786440 | tf_op jit(solution)/shard_map/ppermute | solution.py:92
  534.4 1.2 copy-start.2
  534.4 1.2 copy-start.14
  534.4 1.2 copy-start.16
  535.1 3.5 copy-start.4
  535.1 3.5 copy-start.10
  535.1 3.5 copy-start.11
  535.2 3.5 copy-start.12
  535.2 3.5 copy-start.13
  536.7 24.4 %collective-permute-start.21 = (bf16[128,4096]{0,1:T(8,128)(2,1)S(1)}, bf16[128,4096]{0,1:T(8,128)(2,1)S(1)}, u32[]{:S(2)}, u32[]{:S(2)}) collective-permute-start(bf16[128,4096]{0,1:T(8,128)(2,1)S(1)} %fusion.14), channel_id=1, source_target_pairs={{0,16},{16,32},{32,48},{48,64},{64,80},{80,96},{96,112},{112,128},... | collective-permute-start | bytes 3145736 | tf_op jit(solution)/shard_map/ppermute | solution.py:14
  538.7 21.6 %copy-start.9 = (bf16[1,256,768]{2,1,0:T(8,128)(2,1)S(1)}, bf16[1,256,768]{2,1,0:T(8,128)(2,1)}, u32[]{:S(2)}) copy-start(bf16[1,256,768]{2,1,0:T(8,128)(2,1)} %param.14) | copy-start | bytes 1179652
  539.7 20.6 %collective-permute-start.22 = (bf16[256,768]{1,0:T(8,128)(2,1)S(1)}, bf16[256,768]{1,0:T(8,128)(2,1)S(1)}, u32[]{:S(2)}, u32[]{:S(2)}) collective-permute-start(bf16[256,768]{1,0:T(8,128)(2,1)S(1)} %fusion.26), channel_id=1, source_target_pairs={{0,496},{16,480},{32,464},{48,448},{64,432},{80,416},{96,400},{112... | collective-permute-start | bytes 1179656 | tf_op jit(solution)/shard_map/ppermute | solution.py:19
Sparse Core Ops, SparseCore 0:
  11.0 191.6 all-gather.2

commit v3 on v2

--- a/solution.py
+++ b/solution.py
@@ -60,24 +60,6 @@
     gathered = jnp.stack([second[0][0]] + [s[:INNER] for s in second[1:]])
     scattered = jnp.stack([second[0][1 + o]] + [s[INNER:] for s in second[1:]])
     return gathered, scattered
-
-
-def reduce_and_gather(partial, own):
-    outer = lax.axis_size("seq") // INNER
-    n, w = partial.shape[2], partial.shape[3]
-    acc = partial[0]
-    for k in range(1, outer):
-        acc = acc + lax.ppermute(partial[k], "seq", seq_pairs(outer - k, 1))
-    mine = jnp.concatenate([acc.transpose(1, 0, 2).reshape(n, INNER * w), own.astype(jnp.float32)], axis=1)
-    total = acc
-    rows = [own.astype(jnp.float32)]
-    for k in range(1, INNER):
-        got = lax.ppermute(mine, "seq", seq_pairs(k, 0))
-        sums = got[:, : INNER * w].reshape(n, INNER, w).transpose(1, 0, 2)
-        total = total + jnp.roll(sums, k, axis=0)
-        rows.append(got[:, INNER * w :])
-    group = jnp.concatenate([jnp.stack(rows), total], axis=2).astype(own.dtype)
-    return jnp.stack([group] + [lax.ppermute(group, "seq", seq_pairs(k, 1)) for k in range(1, outer)])
 
 
 def gather_columns(y, o, i):
@@ -172,7 +154,9 @@
     key_part = jnp.einsum("tgj,tgh->jh", score_grad, query, preferred_element_type=jnp.float32)
     value_part = jnp.einsum("tgj,tgh->jh", weights, grad_heads, preferred_element_type=jnp.float32)
     kv_part = jnp.concatenate([key_part, value_part], axis=1).reshape(outer, INNER, count, 2 * HEAD)
-    grad_all = reduce_and_gather(kv_part, query_grad).reshape(size * count, -1)
+    kv_grad = reduce_blocks(kv_part).astype(jnp.bfloat16)
+    own_grad = jnp.concatenate([query_grad, kv_grad], axis=1)
+    grad_all = gather_blocks(own_grad).reshape(size * count, -1)
     input_term = contract_first(hidden_cols, grad_all).astype(jnp.bfloat16)
     block = contract_last(grad_all, up_input_weight[0])
     hidden_grad = gather_columns(block.astype(jnp.bfloat16).reshape(outer, INNER, count, -1), o, i)

time: 577 us -> 499 us (0.86)
  waiting for transfers between devices: 332 us -> 287 us
  local copies, waits for them, and re-layouts: 44.5 us -> 25.4 us
  starting transfers between devices: 124 us -> 115 us
    ppermute x9 -> x12, waiting for transfers between devices: 131 us -> 77.8 us  [the longest x3 32.5 us: gather_blocks(): lax.ppermute(first, 'seq', seq_pairs(k, 1))]
    ppermute x3, starting transfers between devices: 37.4 us -> 16.5 us  [gather_columns(): second.append(lax.ppermute(first[k], 'seq', seq_pairs(INNER - k, 0)))]
    ppermute x9 -> x12, starting transfers between devices: 38.9 us -> 49.8 us  [the longest x3 17.2 us: reduce_blocks(): total = total + lax.ppermute(acc[k], 'seq', seq_pairs(INNER - k, 0))]
    slice x11 -> x0, local copies, waits for them, and re-layouts: 9.11 us -> none  [the longest x6 6.2 us: reduce_and_gather(): sums = got[:, :INNER * w].reshape(n, INNER, w).transpose(1, 0, 2)]
  transfers between devices with their start and end apart: 24 -> 27, of which waited for: 18 -> 20; matrix products, arithmetic and copies ran while one was open for 8% -> 7% of each run, Pallas kernels for 0% -> 0%
where the time goes in v3:
time: 499 us; the launch traced here: 494 us
  waiting for transfers between devices  287 us (58%)
  starting transfers between devices  115 us (23%)
  matrix products  33.6 us (7%)
  local copies, waits for them, and re-layouts  25.4 us (5%)
  other arithmetic  18.2 us (4%)
  between operations  14.8 us (3%)
    ppermute x3, waiting for transfers between devices, gather_and_scatter(): lax.ppermute(jnp.concatenate([x[None], piece]), 'seq', seq_pairs(k, 0))  64.6 us
    all_gather x1, waiting for transfers between devices, per_device(): lax.all_gather(up_output_weight[0], 'seq', axis=1, tiled=True)  54.4 us
    ppermute x3, waiting for transfers between devices, gather_columns(): second.append(lax.ppermute(first[k], 'seq', seq_pairs(INNER - k, 0)))  34.1 us
    ppermute x3, waiting for transfers between devices, gather_blocks(): lax.ppermute(first, 'seq', seq_pairs(k, 1))  32.5 us
    ppermute x3, starting transfers between devices, gather_and_scatter(): lax.ppermute(jnp.concatenate([x[None], piece]), 'seq', seq_pairs(k, 0))  24.6 us
    ppermute x3, waiting for transfers between devices, gather_blocks(): lax.ppermute(x, 'seq', seq_pairs(k, 0))  22.6 us
    ppermute x3, waiting for transfers between devices, gather_and_scatter(): lax.ppermute(jnp.concatenate([first[0], piece]), 'seq', seq_pairs(k, 1))  22 us
    ppermute x1, waiting for transfers between devices, mirrored(): lax.ppermute(value, axis, [(source, count - 1 - source) for source in ran...  20.5 us
  transfers between devices with their start and end apart: 27, of which 20 were waited for; matrix products, arithmetic and copies ran while one was open for 7% of the time, Pallas kernels for 0%

profile of v3, /device:TPU:25, one launch (start us, length us, event | category | flops | bytes accessed | tf_op | source)
XLA Modules:
  0.0 493.5 jit_solution(13432784750086883338)
XLA Ops:
  8.0 1.6 copy.36
  10.1 1.4 reduce.4
  14.2 8.8 %collective-permute-start = (bf16[5,128,256]{1,2,0:T(8,128)(2,1)S(1)}, bf16[5,128,256]{1,2,0:T(8,128)(2,1)S(1)}, u32[]{:S(2)}, u32[]{:S(2)}) collective-permute-start(bf16[5,128,256]{1,2,0:T(8,128)(2,1)S(1)} %get-tuple-element.43), channel_id=1, source_target_pairs={{0,1},{1,2},{2,3},{3,0},{4,5},{5,6},{6,7},{7,4},{8,9},{9,10},{10,1... | collective-permute-start | bytes 983048 | tf_op jit(solution)/shard_map/ppermute | solution.py:54
  23.0 10.6 %collective-permute-start.1 = (bf16[5,128,256]{1,2,0:T(8,128)(2,1)S(1)}, bf16[5,128,256]{1,2,0:T(8,128)(2,1)}, u32[]{:S(2)}, u32[]{:S(2)}) collective-permute-start(bf16[5,128,256]{1,2,0:T(8,128)(2,1)S(1)} %get-tuple-element.44), channel_id=1, source_target_pairs={{0,2},{1,3},{2,0},{3,1},{4,6},{5,7},{6,4},{7,5},{8,10},{9,11},{10,... | collective-permute-start | bytes 983048 | tf_op jit(solution)/shard_map/ppermute | solution.py:54
  33.6 5.2 %collective-permute-start.2 = (bf16[5,128,256]{1,2,0:T(8,128)(2,1)S(1)}, bf16[5,128,256]{1,2,0:T(8,128)(2,1)}, u32[]{:S(2)}, u32[]{:S(2)}) collective-permute-start(bf16[5,128,256]{1,2,0:T(8,128)(2,1)S(1)} %get-tuple-element.45), channel_id=1, source_target_pairs={{0,3},{1,0},{2,1},{3,2},{4,7},{5,4},{6,5},{7,6},{8,11},{9,8},{10,9... | collective-permute-start | bytes 983048 | tf_op jit(solution)/shard_map/ppermute | solution.py:54
  39.1 26.7 %collective-permute-done.1 = bf16[5,128,256]{1,2,0:T(8,128)(2,1)} collective-permute-done((bf16[5,128,256]{1,2,0:T(8,128)(2,1)S(1)}, bf16[5,128,256]{1,2,0:T(8,128)(2,1)}, u32[]{:S(2)}, u32[]{:S(2)}) %collective-permute-start.1) | collective-permute-done | bytes 327712 | tf_op jit(solution)/shard_map/ppermute | solution.py:54
  65.8 37.9 %collective-permute-done.2 = bf16[5,128,256]{1,2,0:T(8,128)(2,1)} collective-permute-done((bf16[5,128,256]{1,2,0:T(8,128)(2,1)S(1)}, bf16[5,128,256]{1,2,0:T(8,128)(2,1)}, u32[]{:S(2)}, u32[]{:S(2)}) %collective-permute-start.2) | collective-permute-done | bytes 327712 | tf_op jit(solution)/shard_map/ppermute | solution.py:54
  103.7 1.2 pad_maximum_fusion.1
  106.0 3.0 collective-permute-start.3
  109.0 3.9 collective-permute-start.4
  113.0 3.2 collective-permute-start.5
  117.9 4.3 collective-permute-done.3
  123.0 16.6 %collective-permute-done.4 = bf16[8,128,256]{1,2,0:T(8,128)(2,1)S(1)} collective-permute-done((bf16[8,128,256]{1,2,0:T(8,128)(2,1)S(1)}, bf16[8,128,256]{1,2,0:T(8,128)(2,1)S(1)}, u32[]{:S(2)}, u32[]{:S(2)}) %collective-permute-start.4) | collective-permute-done | bytes 524320 | tf_op jit(solution)/shard_map/ppermute | solution.py:59
  142.8 5.5 %fusion.77 = (f32[128,4]{0,1:T(4,128)}, f32[128,4,2048]{0,2,1:T(8,128)}) fusion(pred[128,2048]{0,1:T(8,128)(4,1)} %compare_and_fusion, bf16[128,4,128]{0,2,1:T(8,128)(2,1)} %bitcast.218, bf16[2048,256]{1,0:T(8,128)(2,1)S(1)} %bitcast.195), kind=kOutput, calls=%fused_computation.152 | convolution fusion | flops 273680384 | bytes 5376000 | tf_op jit(solution)/shard_map/sub | solution.py:142
  148.3 54.4 %all-gather.3.cloned.1.call-done = bf16[1,512,4096]{2,1,0:T(8,128)(2,1)} async-done(((bf16[1,512,256]{2,1,0:T(8,128)(2,1)}), bf16[1,512,4096]{2,1,0:T(8,128)(2,1)}) %all-gather.3.cloned.1.call-update) | async-done | bytes 4194320 | tf_op jit(solution)/shard_map/all_gather | solution.py:121
  202.7 4.4 fusion.27
  207.0 1.7 copy.77
  208.7 3.8 fusion.55
  212.5 1.8 convolution_bitcast_fusion
  214.3 8.3 %convolution_bitcast_fusion.1 = f32[2048,128]{0,1:T(8,128)} fusion(bf16[128,4,128]{0,2,1:T(8,128)(2,1)} %bitcast.219, f32[128,4,2048]{0,2,1:T(8,128)} %fusion.55, f32[128,4,2048]{0,2,1:T(8,128)} %get-tuple-element.47, f32[128,4]{0,1:T(4,128)} %get-tuple-element.46), kind=kOutput, calls=%fused_computation.21 | convolution fusion | flops 275778048 | bytes 9570304 | tf_op jit(solution)/shard_map/tgj,tgh->jh/dot_general | solution.py:154
  222.6 2.8 fusion.54
  225.4 2.1 copy.74
  227.5 4.3 collective-permute-start.6
  231.8 2.0 copy.75
  233.8 1.9 collective-permute-start.7
  235.8 2.0 copy.76
  237.8 2.5 collective-permute-start.8
  240.3 2.0 copy.73
  242.3 5.8 %collective-permute-done.7 = f32[4,128,256]{2,1,0:T(8,128)} collective-permute-done((f32[4,128,256]{2,1,0:T(8,128)}, f32[4,128,256]{2,1,0:T(8,128)}, u32[]{:S(2)}, u32[]{:S(2)}) %collective-permute-start.7) | collective-permute-done | bytes 524320 | tf_op jit(solution)/shard_map/ppermute | solution.py:40
  248.1 14.5 %collective-permute-done.8 = f32[4,128,256]{2,1,0:T(8,128)} collective-permute-done((f32[4,128,256]{2,1,0:T(8,128)}, f32[4,128,256]{2,1,0:T(8,128)}, u32[]{:S(2)}, u32[]{:S(2)}) %collective-permute-start.8) | collective-permute-done | bytes 524320 | tf_op jit(solution)/shard_map/ppermute | solution.py:40
  262.6 1.7 add_add_fusion
  265.9 6.4 %collective-permute-start.10 = (f32[128,256]{1,0:T(8,128)}, f32[128,256]{1,0:T(8,128)}, u32[]{:S(2)}, u32[]{:S(2)}) collective-permute-start(f32[128,256]{1,0:T(8,128)} %get-tuple-element.36), channel_id=1, source_target_pairs={{0,2},{1,3},{2,0},{3,1},{4,6},{5,7},{6,4},{7,5},{8,10},{9,11},{10,... | collective-permute-start | bytes 393224 | tf_op jit(solution)/shard_map/ppermute | solution.py:43
  272.3 8.7 %collective-permute-start.11 = (f32[128,256]{1,0:T(8,128)}, f32[128,256]{1,0:T(8,128)}, u32[]{:S(2)}, u32[]{:S(2)}) collective-permute-start(f32[128,256]{1,0:T(8,128)} %get-tuple-element.35), channel_id=1, source_target_pairs={{0,1},{1,2},{2,3},{3,0},{4,5},{5,6},{6,7},{7,4},{8,9},{9,10},{10,1... | collective-permute-start | bytes 393224 | tf_op jit(solution)/shard_map/ppermute | solution.py:43
  281.0 2.1 collective-permute-start.9
  283.1 7.9 %fusion.30 = bf16[128,4,128]{0,2,1:T(8,128)(2,1)} fusion(f32[128,4,2048]{0,2,1:T(8,128)} %fusion.55, bf16[2048,256]{1,0:T(8,128)(2,1)S(1)} %bitcast.197, f32[128,4,2048]{0,2,1:T(8,128)} %get-tuple-element.47, f32[128,4]{0,1:T(4,128)} %get-tuple-element.46), kind=kOutput, calls=%fused_computation.56 | convolution fusion | flops 275843584 | bytes 17436672 | tf_op jit(solution)/shard_map/tgj,jh->tgh/dot_general | solution.py:150
  292.0 2.4 collective-permute-done.10
  295.6 4.8 collective-permute-start.12
  300.5 8.1 %collective-permute-start.13 = (bf16[128,768]{1,0:T(8,128)(2,1)S(1)}, bf16[128,768]{1,0:T(8,128)(2,1)S(1)}, u32[]{:S(2)}, u32[]{:S(2)}) collective-permute-start(bf16[128,768]{1,0:T(8,128)(2,1)S(1)} %get-tuple-element.41), channel_id=1, source_target_pairs={{0,2},{1,3},{2,0},{3,1},{4,6},{5,7},{6,4},{7,5},{8,10},{9,11},{10,... | collective-permute-start | bytes 589832 | tf_op jit(solution)/shard_map/ppermute | solution.py:32
  308.6 2.6 collective-permute-start.14
  311.1 8.3 %collective-permute-done.12 = bf16[128,768]{1,0:T(8,128)(2,1)S(1)} collective-permute-done((bf16[128,768]{1,0:T(8,128)(2,1)S(1)}, bf16[128,768]{1,0:T(8,128)(2,1)S(1)}, u32[]{:S(2)}, u32[]{:S(2)}) %collective-permute-start.12) | collective-permute-done | bytes 196640 | tf_op jit(solution)/shard_map/ppermute | solution.py:32
  319.5 6.7 %collective-permute-done.13 = bf16[128,768]{1,0:T(8,128)(2,1)S(1)} collective-permute-done((bf16[128,768]{1,0:T(8,128)(2,1)S(1)}, bf16[128,768]{1,0:T(8,128)(2,1)S(1)}, u32[]{:S(2)}, u32[]{:S(2)}) %collective-permute-start.13) | collective-permute-done | bytes 196640 | tf_op jit(solution)/shard_map/ppermute | solution.py:32
  326.1 7.6 %collective-permute-done.14 = bf16[128,768]{1,0:T(8,128)(2,1)S(1)} collective-permute-done((bf16[128,768]{1,0:T(8,128)(2,1)S(1)}, bf16[128,768]{1,0:T(8,128)(2,1)S(1)}, u32[]{:S(2)}, u32[]{:S(2)}) %collective-permute-start.14) | collective-permute-done | bytes 196640 | tf_op jit(solution)/shard_map/ppermute | solution.py:32
  333.9 1.9 collective-permute-start.15
  335.8 2.8 collective-permute-start.16
  338.6 3.7 collective-permute-start.17
  342.3 30.1 %collective-permute-done.15 = bf16[4,128,768]{2,1,0:T(8,128)(2,1)S(1)} collective-permute-done((bf16[4,128,768]{2,1,0:T(8,128)(2,1)S(1)}, bf16[4,128,768]{2,1,0:T(8,128)(2,1)S(1)}, u32[]{:S(2)}, u32[]{:S(2)}) %collective-permute-start.15) | collective-permute-done | bytes 786464 | tf_op jit(solution)/shard_map/ppermute | solution.py:33
  372.4 2.3 collective-permute-done.17
  377.7 5.3 %collective-permute-start.18 = (bf16[4,128,256]{1,2,0:T(8,128)(2,1)}, bf16[4,128,256]{1,2,0:T(8,128)(2,1)}, u32[]{:S(2)}, u32[]{:S(2)}) collective-permute-start(bf16[4,128,256]{1,2,0:T(8,128)(2,1)} %copy.58), channel_id=1, source_target_pairs={{0,12},{1,13},{2,14},{3,15},{4,0},{5,1},{6,2},{7,3},{8,4},{9,5},{1... | collective-permute-start | bytes 786440 | tf_op jit(solution)/shard_map/ppermute | solution.py:70
  383.2 1.9 collective-permute-start.19
  385.3 2.5 collective-permute-start.20
  388.0 6.0 %collective-permute-done.18 = bf16[4,128,256]{1,2,0:T(8,128)(2,1)} collective-permute-done((bf16[4,128,256]{1,2,0:T(8,128)(2,1)}, bf16[4,128,256]{1,2,0:T(8,128)(2,1)}, u32[]{:S(2)}, u32[]{:S(2)}) %collective-permute-start.18) | collective-permute-done | bytes 262176 | tf_op jit(solution)/shard_map/ppermute | solution.py:70
  394.0 6.6 %collective-permute-done.20 = bf16[4,128,256]{1,2,0:T(8,128)(2,1)} collective-permute-done((bf16[4,128,256]{1,2,0:T(8,128)(2,1)S(1)}, bf16[4,128,256]{1,2,0:T(8,128)(2,1)}, u32[]{:S(2)}, u32[]{:S(2)}) %collective-permute-start.20) | collective-permute-done | bytes 262176 | tf_op jit(solution)/shard_map/ppermute | solution.py:70
  400.6 1.2 pad_maximum_fusion.3
  402.8 5.0 %collective-permute-start.21 = (bf16[4,128,256]{1,2,0:T(8,128)(2,1)}, bf16[4,128,256]{1,2,0:T(8,128)(2,1)}, u32[]{:S(2)}, u32[]{:S(2)}) collective-permute-start(bf16[4,128,256]{1,2,0:T(8,128)(2,1)} %get-tuple-element.13), channel_id=1, source_target_pairs={{0,3},{1,0},{2,1},{3,2},{4,7},{5,4},{6,5},{7,6},{8,11},{9,8},{10,9... | collective-permute-start | bytes 786440 | tf_op jit(solution)/shard_map/ppermute | solution.py:74
  407.8 6.9 %collective-permute-start.22 = (bf16[4,128,256]{1,2,0:T(8,128)(2,1)}, bf16[4,128,256]{1,2,0:T(8,128)(2,1)}, u32[]{:S(2)}, u32[]{:S(2)}) collective-permute-start(bf16[4,128,256]{1,2,0:T(8,128)(2,1)} %get-tuple-element.12), channel_id=1, source_target_pairs={{0,2},{1,3},{2,0},{3,1},{4,6},{5,7},{6,4},{7,5},{8,10},{9,11},{10,... | collective-permute-start | bytes 786440 | tf_op jit(solution)/shard_map/ppermute | solution.py:74
  414.7 4.5 collective-permute-start.23
  420.0 16.4 %collective-permute-done.21 = bf16[4,128,256]{1,2,0:T(8,128)(2,1)} collective-permute-done((bf16[4,128,256]{1,2,0:T(8,128)(2,1)}, bf16[4,128,256]{1,2,0:T(8,128)(2,1)}, u32[]{:S(2)}, u32[]{:S(2)}) %collective-permute-start.21) | collective-permute-done | bytes 262176 | tf_op jit(solution)/shard_map/ppermute | solution.py:74
  436.4 7.6 %collective-permute-done.22 = bf16[4,128,256]{1,2,0:T(8,128)(2,1)} collective-permute-done((bf16[4,128,256]{1,2,0:T(8,128)(2,1)}, bf16[4,128,256]{1,2,0:T(8,128)(2,1)}, u32[]{:S(2)}, u32[]{:S(2)}) %collective-permute-start.22) | collective-permute-done | bytes 262176 | tf_op jit(solution)/shard_map/ppermute | solution.py:74
  444.0 10.1 %collective-permute-done.23 = bf16[4,128,256]{1,2,0:T(8,128)(2,1)} collective-permute-done((bf16[4,128,256]{1,2,0:T(8,128)(2,1)}, bf16[4,128,256]{1,2,0:T(8,128)(2,1)}, u32[]{:S(2)}, u32[]{:S(2)}) %collective-permute-start.23) | collective-permute-done | bytes 262176 | tf_op jit(solution)/shard_map/ppermute | solution.py:74
  454.1 2.1 fusion.37
  458.9 2.1 collective-permute-start.24
  462.1 1.9 collective-permute-start.25
  464.0 20.5 %collective-permute-done.25 = bf16[256,768]{1,0:T(8,128)(2,1)S(1)} collective-permute-done((bf16[256,768]{1,0:T(8,128)(2,1)S(1)}, bf16[256,768]{1,0:T(8,128)(2,1)S(1)}, u32[]{:S(2)}, u32[]{:S(2)}) %collective-permute-start.25) | collective-permute-done | bytes 393248 | tf_op jit(solution)/shard_map/ppermute | solution.py:19
  485.4 1.3 copy.64
  (91 shorter events, 24.3 us)
Async XLA Ops:
  7.2 368.0 %copy-start = (bf16[1,256,768]{2,1,0:T(8,128)(2,1)S(1)}, bf16[1,256,768]{2,1,0:T(8,128)(2,1)}, u32[]{:S(2)}) copy-start(bf16[1,256,768]{2,1,0:T(8,128)(2,1)} %param.11) | copy-start | bytes 1179652
  7.2 195.5 %all-gather.3.cloned.1.call-start = ((), (), s32[]{:S(2)}) async-start(), calls=%async_computation | async-start | bytes 4456448 | tf_op jit(solution)/shard_map/all_gather | solution.py:121
  13.2 0.8 copy-start.12
  14.2 24.9 %collective-permute-start = (bf16[5,128,256]{1,2,0:T(8,128)(2,1)S(1)}, bf16[5,128,256]{1,2,0:T(8,128)(2,1)S(1)}, u32[]{:S(2)}, u32[]{:S(2)}) collective-permute-start(bf16[5,128,256]{1,2,0:T(8,128)(2,1)S(1)} %get-tuple-element.43), channel_id=1, source_target_pairs={{0,1},{1,2},{2,3},{3,0},{4,5},{5,6},{6,7},{7,4},{8,9},{9,10},{10,1... | collective-permute-start | bytes 983048 | tf_op jit(solution)/shard_map/ppermute | solution.py:54
  23.0 42.8 %collective-permute-start.1 = (bf16[5,128,256]{1,2,0:T(8,128)(2,1)S(1)}, bf16[5,128,256]{1,2,0:T(8,128)(2,1)}, u32[]{:S(2)}, u32[]{:S(2)}) collective-permute-start(bf16[5,128,256]{1,2,0:T(8,128)(2,1)S(1)} %get-tuple-element.44), channel_id=1, source_target_pairs={{0,2},{1,3},{2,0},{3,1},{4,6},{5,7},{6,4},{7,5},{8,10},{9,11},{10,... | collective-permute-start | bytes 983048 | tf_op jit(solution)/shard_map/ppermute | solution.py:54
  33.6 70.1 %collective-permute-start.2 = (bf16[5,128,256]{1,2,0:T(8,128)(2,1)S(1)}, bf16[5,128,256]{1,2,0:T(8,128)(2,1)}, u32[]{:S(2)}, u32[]{:S(2)}) collective-permute-start(bf16[5,128,256]{1,2,0:T(8,128)(2,1)S(1)} %get-tuple-element.45), channel_id=1, source_target_pairs={{0,3},{1,0},{2,1},{3,2},{4,7},{5,4},{6,5},{7,6},{8,11},{9,8},{10,9... | collective-permute-start | bytes 983048 | tf_op jit(solution)/shard_map/ppermute | solution.py:54
  105.0 11.2 %copy-start.14 = (s32[1,128]{1,0:T(1,128)S(1)}, s32[1,128]{1,0:T(1,128)}, u32[]{:S(2)}) copy-start(s32[1,128]{1,0:T(1,128)} %param.15) | copy-start | bytes 1540
  106.0 16.2 %collective-permute-start.3 = (bf16[8,128,256]{1,2,0:T(8,128)(2,1)S(1)}, bf16[8,128,256]{1,2,0:T(8,128)(2,1)S(1)}, u32[]{:S(2)}, u32[]{:S(2)}) collective-permute-start(bf16[8,128,256]{1,2,0:T(8,128)(2,1)S(1)} %get-tuple-element.37), channel_id=1, source_target_pairs={{0,4},{1,5},{2,6},{3,7},{4,8},{5,9},{6,10},{7,11},{8,12},{9,13},{1... | collective-permute-start | bytes 1572872 | tf_op jit(solution)/shard_map/ppermute | solution.py:59
  109.0 30.6 %collective-permute-start.4 = (bf16[8,128,256]{1,2,0:T(8,128)(2,1)S(1)}, bf16[8,128,256]{1,2,0:T(8,128)(2,1)S(1)}, u32[]{:S(2)}, u32[]{:S(2)}) collective-permute-start(bf16[8,128,256]{1,2,0:T(8,128)(2,1)S(1)} %get-tuple-element.38), channel_id=1, source_target_pairs={{0,8},{1,9},{2,10},{3,11},{4,12},{5,13},{6,14},{7,15},{8,0},{9,1},... | collective-permute-start | bytes 1572872 | tf_op jit(solution)/shard_map/ppermute | solution.py:59
  113.0 28.5 %collective-permute-start.5 = (bf16[8,128,256]{1,2,0:T(8,128)(2,1)S(1)}, bf16[8,128,256]{1,2,0:T(8,128)(2,1)S(1)}, u32[]{:S(2)}, u32[]{:S(2)}) collective-permute-start(bf16[8,128,256]{1,2,0:T(8,128)(2,1)S(1)} %get-tuple-element.39), channel_id=1, source_target_pairs={{0,12},{1,13},{2,14},{3,15},{4,0},{5,1},{6,2},{7,3},{8,4},{9,5},{1... | collective-permute-start | bytes 1572872 | tf_op jit(solution)/shard_map/ppermute | solution.py:59
  142.8 59.8 %copy-start.1 = (bf16[1,128,4096]{2,1,0:T(8,128)(2,1)S(1)}, bf16[1,128,4096]{2,1,0:T(8,128)(2,1)}, u32[]{:S(2)}) copy-start(bf16[1,128,4096]{2,1,0:T(8,128)(2,1)} %param.10) | copy-start | bytes 3145732
  208.7 3.8 copy-start.5
  208.7 3.8 copy-start.15
  208.7 3.8 copy-start.16
  227.5 14.8 %collective-permute-start.6 = (f32[4,128,256]{2,1,0:T(8,128)}, f32[4,128,256]{2,1,0:T(8,128)}, u32[]{:S(2)}, u32[]{:S(2)}) collective-permute-start(f32[4,128,256]{2,1,0:T(8,128)} %bitcast.211), channel_id=1, source_target_pairs={{0,12},{1,13},{2,14},{3,15},{4,0},{5,1},{6,2},{7,3},{8,4},{9,5},{1... | collective-permute-start | bytes 1572872 | tf_op jit(solution)/shard_map/ppermute | solution.py:40
  233.8 14.3 %collective-permute-start.7 = (f32[4,128,256]{2,1,0:T(8,128)}, f32[4,128,256]{2,1,0:T(8,128)}, u32[]{:S(2)}, u32[]{:S(2)}) collective-permute-start(f32[4,128,256]{2,1,0:T(8,128)} %bitcast.212), channel_id=1, source_target_pairs={{0,8},{1,9},{2,10},{3,11},{4,12},{5,13},{6,14},{7,15},{8,0},{9,1},... | collective-permute-start | bytes 1572872 | tf_op jit(solution)/shard_map/ppermute | solution.py:40
  237.8 24.8 %collective-permute-start.8 = (f32[4,128,256]{2,1,0:T(8,128)}, f32[4,128,256]{2,1,0:T(8,128)}, u32[]{:S(2)}, u32[]{:S(2)}) collective-permute-start(f32[4,128,256]{2,1,0:T(8,128)} %bitcast.213), channel_id=1, source_target_pairs={{0,4},{1,5},{2,6},{3,7},{4,8},{5,9},{6,10},{7,11},{8,12},{9,13},{1... | collective-permute-start | bytes 1572872 | tf_op jit(solution)/shard_map/ppermute | solution.py:40
  264.3 0.8 copy-start.4
  265.9 28.6 %collective-permute-start.10 = (f32[128,256]{1,0:T(8,128)}, f32[128,256]{1,0:T(8,128)}, u32[]{:S(2)}, u32[]{:S(2)}) collective-permute-start(f32[128,256]{1,0:T(8,128)} %get-tuple-element.36), channel_id=1, source_target_pairs={{0,2},{1,3},{2,0},{3,1},{4,6},{5,7},{6,4},{7,5},{8,10},{9,11},{10,... | collective-permute-start | bytes 393224 | tf_op jit(solution)/shard_map/ppermute | solution.py:43
  272.3 22.2 %collective-permute-start.11 = (f32[128,256]{1,0:T(8,128)}, f32[128,256]{1,0:T(8,128)}, u32[]{:S(2)}, u32[]{:S(2)}) collective-permute-start(f32[128,256]{1,0:T(8,128)} %get-tuple-element.35), channel_id=1, source_target_pairs={{0,1},{1,2},{2,3},{3,0},{4,5},{5,6},{6,7},{7,4},{8,9},{9,10},{10,1... | collective-permute-start | bytes 393224 | tf_op jit(solution)/shard_map/ppermute | solution.py:43
  281.0 13.5 %collective-permute-start.9 = (f32[128,256]{1,0:T(8,128)}, f32[128,256]{1,0:T(8,128)}, u32[]{:S(2)}, u32[]{:S(2)}) collective-permute-start(f32[128,256]{1,0:T(8,128)} %get-tuple-element.34), channel_id=1, source_target_pairs={{0,3},{1,0},{2,1},{3,2},{4,7},{5,4},{6,5},{7,6},{8,11},{9,8},{10,9... | collective-permute-start | bytes 393224 | tf_op jit(solution)/shard_map/ppermute | solution.py:43
  295.6 23.8 %collective-permute-start.12 = (bf16[128,768]{1,0:T(8,128)(2,1)S(1)}, bf16[128,768]{1,0:T(8,128)(2,1)S(1)}, u32[]{:S(2)}, u32[]{:S(2)}) collective-permute-start(bf16[128,768]{1,0:T(8,128)(2,1)S(1)} %get-tuple-element.41), channel_id=1, source_target_pairs={{0,1},{1,2},{2,3},{3,0},{4,5},{5,6},{6,7},{7,4},{8,9},{9,10},{10,1... | collective-permute-start | bytes 589832 | tf_op jit(solution)/shard_map/ppermute | solution.py:32
  300.5 25.7 %collective-permute-start.13 = (bf16[128,768]{1,0:T(8,128)(2,1)S(1)}, bf16[128,768]{1,0:T(8,128)(2,1)S(1)}, u32[]{:S(2)}, u32[]{:S(2)}) collective-permute-start(bf16[128,768]{1,0:T(8,128)(2,1)S(1)} %get-tuple-element.41), channel_id=1, source_target_pairs={{0,2},{1,3},{2,0},{3,1},{4,6},{5,7},{6,4},{7,5},{8,10},{9,11},{10,... | collective-permute-start | bytes 589832 | tf_op jit(solution)/shard_map/ppermute | solution.py:32
  308.6 25.2 %collective-permute-start.14 = (bf16[128,768]{1,0:T(8,128)(2,1)S(1)}, bf16[128,768]{1,0:T(8,128)(2,1)S(1)}, u32[]{:S(2)}, u32[]{:S(2)}) collective-permute-start(bf16[128,768]{1,0:T(8,128)(2,1)S(1)} %get-tuple-element.41), channel_id=1, source_target_pairs={{0,3},{1,0},{2,1},{3,2},{4,7},{5,4},{6,5},{7,6},{8,11},{9,8},{10,9... | collective-permute-start | bytes 589832 | tf_op jit(solution)/shard_map/ppermute | solution.py:32
  333.9 38.6 %collective-permute-start.15 = (bf16[4,128,768]{2,1,0:T(8,128)(2,1)S(1)}, bf16[4,128,768]{2,1,0:T(8,128)(2,1)S(1)}, u32[]{:S(2)}, u32[]{:S(2)}) collective-permute-start(bf16[4,128,768]{2,1,0:T(8,128)(2,1)S(1)} %get-tuple-element.27), channel_id=1, source_target_pairs={{0,4},{1,5},{2,6},{3,7},{4,8},{5,9},{6,10},{7,11},{8,12},{9,13},{1... | collective-permute-start | bytes 2359304 | tf_op jit(solution)/shard_map/ppermute | solution.py:33
  335.8 36.6 %collective-permute-start.16 = (bf16[4,128,768]{2,1,0:T(8,128)(2,1)S(1)}, bf16[4,128,768]{2,1,0:T(8,128)(2,1)S(1)}, u32[]{:S(2)}, u32[]{:S(2)}) collective-permute-start(bf16[4,128,768]{2,1,0:T(8,128)(2,1)S(1)} %get-tuple-element.27), channel_id=1, source_target_pairs={{0,8},{1,9},{2,10},{3,11},{4,12},{5,13},{6,14},{7,15},{8,0},{9,1},... | collective-permute-start | bytes 2359304 | tf_op jit(solution)/shard_map/ppermute | solution.py:33
  338.6 36.2 %collective-permute-start.17 = (bf16[4,128,768]{2,1,0:T(8,128)(2,1)S(1)}, bf16[4,128,768]{2,1,0:T(8,128)(2,1)S(1)}, u32[]{:S(2)}, u32[]{:S(2)}) collective-permute-start(bf16[4,128,768]{2,1,0:T(8,128)(2,1)S(1)} %get-tuple-element.27), channel_id=1, source_target_pairs={{0,12},{1,13},{2,14},{3,15},{4,0},{5,1},{6,2},{7,3},{8,4},{9,5},{1... | collective-permute-start | bytes 2359304 | tf_op jit(solution)/shard_map/ppermute | solution.py:33
  375.2 1.6 copy-start.2
  377.7 16.3 %collective-permute-start.18 = (bf16[4,128,256]{1,2,0:T(8,128)(2,1)}, bf16[4,128,256]{1,2,0:T(8,128)(2,1)}, u32[]{:S(2)}, u32[]{:S(2)}) collective-permute-start(bf16[4,128,256]{1,2,0:T(8,128)(2,1)} %copy.58), channel_id=1, source_target_pairs={{0,12},{1,13},{2,14},{3,15},{4,0},{5,1},{6,2},{7,3},{8,4},{9,5},{1... | collective-permute-start | bytes 786440 | tf_op jit(solution)/shard_map/ppermute | solution.py:70
  383.2 10.8 %collective-permute-start.19 = (bf16[4,128,256]{1,2,0:T(8,128)(2,1)S(1)}, bf16[4,128,256]{1,2,0:T(8,128)(2,1)}, u32[]{:S(2)}, u32[]{:S(2)}) collective-permute-start(bf16[4,128,256]{1,2,0:T(8,128)(2,1)S(1)} %copy.59), channel_id=1, source_target_pairs={{0,8},{1,9},{2,10},{3,11},{4,12},{5,13},{6,14},{7,15},{8,0},{9,1},... | collective-permute-start | bytes 786440 | tf_op jit(solution)/shard_map/ppermute | solution.py:70
  385.3 15.2 %collective-permute-start.20 = (bf16[4,128,256]{1,2,0:T(8,128)(2,1)S(1)}, bf16[4,128,256]{1,2,0:T(8,128)(2,1)}, u32[]{:S(2)}, u32[]{:S(2)}) collective-permute-start(bf16[4,128,256]{1,2,0:T(8,128)(2,1)S(1)} %copy.60), channel_id=1, source_target_pairs={{0,4},{1,5},{2,6},{3,7},{4,8},{5,9},{6,10},{7,11},{8,12},{9,13},{1... | collective-permute-start | bytes 786440 | tf_op jit(solution)/shard_map/ppermute | solution.py:70
  402.8 33.6 %collective-permute-start.21 = (bf16[4,128,256]{1,2,0:T(8,128)(2,1)}, bf16[4,128,256]{1,2,0:T(8,128)(2,1)}, u32[]{:S(2)}, u32[]{:S(2)}) collective-permute-start(bf16[4,128,256]{1,2,0:T(8,128)(2,1)} %get-tuple-element.13), channel_id=1, source_target_pairs={{0,3},{1,0},{2,1},{3,2},{4,7},{5,4},{6,5},{7,6},{8,11},{9,8},{10,9... | collective-permute-start | bytes 786440 | tf_op jit(solution)/shard_map/ppermute | solution.py:74
  407.8 36.1 %collective-permute-start.22 = (bf16[4,128,256]{1,2,0:T(8,128)(2,1)}, bf16[4,128,256]{1,2,0:T(8,128)(2,1)}, u32[]{:S(2)}, u32[]{:S(2)}) collective-permute-start(bf16[4,128,256]{1,2,0:T(8,128)(2,1)} %get-tuple-element.12), channel_id=1, source_target_pairs={{0,2},{1,3},{2,0},{3,1},{4,6},{5,7},{6,4},{7,5},{8,10},{9,11},{10,... | collective-permute-start | bytes 786440 | tf_op jit(solution)/shard_map/ppermute | solution.py:74
  414.7 39.4 %collective-permute-start.23 = (bf16[4,128,256]{1,2,0:T(8,128)(2,1)}, bf16[4,128,256]{1,2,0:T(8,128)(2,1)}, u32[]{:S(2)}, u32[]{:S(2)}) collective-permute-start(bf16[4,128,256]{1,2,0:T(8,128)(2,1)} %get-tuple-element.11), channel_id=1, source_target_pairs={{0,1},{1,2},{2,3},{3,0},{4,5},{5,6},{6,7},{7,4},{8,9},{9,10},{10,1... | collective-permute-start | bytes 786440 | tf_op jit(solution)/shard_map/ppermute | solution.py:74
  420.0 36.7 %copy-start.13 = (f32[128]{0:T(128)S(1)}, f32[128]{0:T(128)}, u32[]{:S(2)}) copy-start(f32[128]{0:T(128)} %copy-done.12) | copy-start | bytes 1540
  456.7 1.2 copy-start.11
  457.8 3.2 copy-start.3
  457.8 3.2 copy-start.7
  457.8 3.2 copy-start.8
  457.9 3.2 copy-start.9
  457.9 3.2 copy-start.10
  458.9 26.4 %collective-permute-start.24 = (bf16[128,4096]{0,1:T(8,128)(2,1)S(1)}, bf16[128,4096]{0,1:T(8,128)(2,1)S(1)}, u32[]{:S(2)}, u32[]{:S(2)}) collective-permute-start(bf16[128,4096]{0,1:T(8,128)(2,1)S(1)} %fusion.14), channel_id=1, source_target_pairs={{0,16},{16,32},{32,48},{48,64},{64,80},{80,96},{96,112},{112,128},... | collective-permute-start | bytes 3145736 | tf_op jit(solution)/shard_map/ppermute | solution.py:14
  461.0 23.5 %copy-start.6 = (bf16[1,256,768]{2,1,0:T(8,128)(2,1)S(1)}, bf16[1,256,768]{2,1,0:T(8,128)(2,1)}, u32[]{:S(2)}) copy-start(bf16[1,256,768]{2,1,0:T(8,128)(2,1)} %param.14) | copy-start | bytes 1179652
  462.1 22.5 %collective-permute-start.25 = (bf16[256,768]{1,0:T(8,128)(2,1)S(1)}, bf16[256,768]{1,0:T(8,128)(2,1)S(1)}, u32[]{:S(2)}, u32[]{:S(2)}) collective-permute-start(bf16[256,768]{1,0:T(8,128)(2,1)S(1)} %fusion.26), channel_id=1, source_target_pairs={{0,496},{16,480},{32,464},{48,448},{64,432},{80,416},{96,400},{112... | collective-permute-start | bytes 1179656 | tf_op jit(solution)/shard_map/ppermute | solution.py:19
Sparse Core Ops, SparseCore 0:
  11.0 191.6 all-gather.2

commit v4 on v3

--- a/solution.py
+++ b/solution.py
@@ -154,9 +154,9 @@
     key_part = jnp.einsum("tgj,tgh->jh", score_grad, query, preferred_element_type=jnp.float32)
     value_part = jnp.einsum("tgj,tgh->jh", weights, grad_heads, preferred_element_type=jnp.float32)
     kv_part = jnp.concatenate([key_part, value_part], axis=1).reshape(outer, INNER, count, 2 * HEAD)
+    query_all = gather_blocks(query_grad)
     kv_grad = reduce_blocks(kv_part).astype(jnp.bfloat16)
-    own_grad = jnp.concatenate([query_grad, kv_grad], axis=1)
-    grad_all = gather_blocks(own_grad).reshape(size * count, -1)
+    grad_all = jnp.concatenate([query_all, gather_blocks(kv_grad)], axis=-1).reshape(size * count, -1)
     input_term = contract_first(hidden_cols, grad_all).astype(jnp.bfloat16)
     block = contract_last(grad_all, up_input_weight[0])
     hidden_grad = gather_columns(block.astype(jnp.bfloat16).reshape(outer, INNER, count, -1), o, i)

time: 499 us -> 469 us (0.940)
  the two profiles are of different devices: /device:TPU:25 before, /device:TPU:64 now
where the time goes in v4:
time: 469 us; the launch traced here: 467 us
  waiting for transfers between devices  231 us (49%)
  starting transfers between devices  144 us (31%)
  matrix products  33.6 us (7%)
  local copies, waits for them, and re-layouts  24.7 us (5%)
  other arithmetic  19.3 us (4%)
  between operations  15 us (3%)
    ppermute x3, waiting for transfers between devices, gather_and_scatter(): lax.ppermute(jnp.concatenate([x[None], piece]), 'seq', seq_pairs(k, 0))  64.2 us
    all_gather x1, waiting for transfers between devices, per_device(): lax.all_gather(up_output_weight[0], 'seq', axis=1, tiled=True)  47.6 us
    ppermute x3, waiting for transfers between devices, gather_columns(): second.append(lax.ppermute(first[k], 'seq', seq_pairs(INNER - k, 0)))  31.8 us
    ppermute x6, starting transfers between devices, gather_blocks(): lax.ppermute(x, 'seq', seq_pairs(k, 0))  29.8 us
    ppermute x3, waiting for transfers between devices, gather_and_scatter(): lax.ppermute(jnp.concatenate([first[0], piece]), 'seq', seq_pairs(k, 1))  24.1 us
    ppermute x1, waiting for transfers between devices, mirrored(): lax.ppermute(value, axis, [(source, count - 1 - source) for source in ran...  23.8 us
    ppermute x3, starting transfers between devices, gather_and_scatter(): lax.ppermute(jnp.concatenate([x[None], piece]), 'seq', seq_pairs(k, 0))  23.7 us
    ppermute x3, starting transfers between devices, reduce_blocks(): total = total + lax.ppermute(acc[k], 'seq', seq_pairs(INNER - k, 0))  18.6 us
  transfers between devices with their start and end apart: 33, of which 20 were waited for; matrix products, arithmetic and copies ran while one was open for 7% of the time, Pallas kernels for 0%

profile of v4, /device:TPU:64, one launch (start us, length us, event | category | flops | bytes accessed | tf_op | source)
XLA Modules:
  0.0 467.1 jit_solution(16384463248650034287)
XLA Ops:
  14.2 9.1 %collective-permute-start = (bf16[5,128,256]{1,2,0:T(8,128)(2,1)S(1)}, bf16[5,128,256]{1,2,0:T(8,128)(2,1)S(1)}, u32[]{:S(2)}, u32[]{:S(2)}) collective-permute-start(bf16[5,128,256]{1,2,0:T(8,128)(2,1)S(1)} %get-tuple-element.43), channel_id=1, source_target_pairs={{0,1},{1,2},{2,3},{3,0},{4,5},{5,6},{6,7},{7,4},{8,9},{9,10},{10,1... | collective-permute-start | bytes 983048 | tf_op jit(solution)/shard_map/ppermute | solution.py:54
  23.3 9.1 %collective-permute-start.1 = (bf16[5,128,256]{1,2,0:T(8,128)(2,1)S(1)}, bf16[5,128,256]{1,2,0:T(8,128)(2,1)}, u32[]{:S(2)}, u32[]{:S(2)}) collective-permute-start(bf16[5,128,256]{1,2,0:T(8,128)(2,1)S(1)} %get-tuple-element.44), channel_id=1, source_target_pairs={{0,2},{1,3},{2,0},{3,1},{4,6},{5,7},{6,4},{7,5},{8,10},{9,11},{10,... | collective-permute-start | bytes 983048 | tf_op jit(solution)/shard_map/ppermute | solution.py:54
  32.4 5.5 %collective-permute-start.2 = (bf16[5,128,256]{1,2,0:T(8,128)(2,1)S(1)}, bf16[5,128,256]{1,2,0:T(8,128)(2,1)}, u32[]{:S(2)}, u32[]{:S(2)}) collective-permute-start(bf16[5,128,256]{1,2,0:T(8,128)(2,1)S(1)} %get-tuple-element.45), channel_id=1, source_target_pairs={{0,3},{1,0},{2,1},{3,2},{4,7},{5,4},{6,5},{7,6},{8,11},{9,8},{10,9... | collective-permute-start | bytes 983048 | tf_op jit(solution)/shard_map/ppermute | solution.py:54
  38.1 40.3 %collective-permute-done = bf16[5,128,256]{1,2,0:T(8,128)(2,1)S(1)} collective-permute-done((bf16[5,128,256]{1,2,0:T(8,128)(2,1)S(1)}, bf16[5,128,256]{1,2,0:T(8,128)(2,1)S(1)}, u32[]{:S(2)}, u32[]{:S(2)}) %collective-permute-start) | collective-permute-done | bytes 327712 | tf_op jit(solution)/shard_map/ppermute | solution.py:54
  78.5 16.8 %collective-permute-done.1 = bf16[5,128,256]{1,2,0:T(8,128)(2,1)} collective-permute-done((bf16[5,128,256]{1,2,0:T(8,128)(2,1)S(1)}, bf16[5,128,256]{1,2,0:T(8,128)(2,1)}, u32[]{:S(2)}, u32[]{:S(2)}) %collective-permute-start.1) | collective-permute-done | bytes 327712 | tf_op jit(solution)/shard_map/ppermute | solution.py:54
  95.3 7.0 %collective-permute-done.2 = bf16[5,128,256]{1,2,0:T(8,128)(2,1)} collective-permute-done((bf16[5,128,256]{1,2,0:T(8,128)(2,1)S(1)}, bf16[5,128,256]{1,2,0:T(8,128)(2,1)}, u32[]{:S(2)}, u32[]{:S(2)}) %collective-permute-start.2) | collective-permute-done | bytes 327712 | tf_op jit(solution)/shard_map/ppermute | solution.py:54
  104.7 1.9 collective-permute-start.3
  106.6 3.4 collective-permute-start.4
  110.0 3.6 collective-permute-start.5
  115.4 18.7 %collective-permute-done.3 = bf16[8,128,256]{1,2,0:T(8,128)(2,1)S(1)} collective-permute-done((bf16[8,128,256]{1,2,0:T(8,128)(2,1)S(1)}, bf16[8,128,256]{1,2,0:T(8,128)(2,1)S(1)}, u32[]{:S(2)}, u32[]{:S(2)}) %collective-permute-start.3) | collective-permute-done | bytes 524320 | tf_op jit(solution)/shard_map/ppermute | solution.py:59
  134.8 2.0 collective-permute-done.4
  137.6 3.4 collective-permute-done.5
  142.4 5.5 %fusion.77 = (f32[128,4]{0,1:T(4,128)}, f32[128,4,2048]{0,2,1:T(8,128)}) fusion(pred[128,2048]{0,1:T(8,128)(4,1)} %compare_and_fusion, bf16[128,4,128]{0,2,1:T(8,128)(2,1)} %bitcast.232, bf16[2048,256]{1,0:T(8,128)(2,1)S(1)} %bitcast.203), kind=kOutput, calls=%fused_computation.152 | convolution fusion | flops 273680384 | bytes 5376000 | tf_op jit(solution)/shard_map/sub | solution.py:142
  147.9 47.6 %all-gather.3.cloned.1.call-done = bf16[1,512,4096]{2,1,0:T(8,128)(2,1)} async-done(((bf16[1,512,256]{2,1,0:T(8,128)(2,1)}), bf16[1,512,4096]{2,1,0:T(8,128)(2,1)}) %all-gather.3.cloned.1.call-update) | async-done | bytes 4194320 | tf_op jit(solution)/shard_map/all_gather | solution.py:121
  195.5 4.4 fusion.27
  199.9 1.7 copy.83
  201.6 3.8 fusion.55
  205.4 1.8 convolution_bitcast_fusion
  207.2 8.3 %convolution_bitcast_fusion.1 = f32[2048,128]{0,1:T(8,128)} fusion(bf16[128,4,128]{0,2,1:T(8,128)(2,1)} %bitcast.233, f32[128,4,2048]{0,2,1:T(8,128)} %fusion.55, f32[128,4,2048]{0,2,1:T(8,128)} %get-tuple-element.47, f32[128,4]{0,1:T(4,128)} %get-tuple-element.46), kind=kOutput, calls=%fused_computation.21 | convolution fusion | flops 275778048 | bytes 9570304 | tf_op jit(solution)/shard_map/tgj,tgh->jh/dot_general | solution.py:154
  215.4 2.9 fusion.54
  218.3 2.1 copy.80
  220.3 2.0 copy.82
  222.4 2.0 copy.81
  224.4 4.7 %collective-permute-start.13 = (f32[4,128,256]{2,1,0:T(8,128)}, f32[4,128,256]{2,1,0:T(8,128)}, u32[]{:S(2)}, u32[]{:S(2)}) collective-permute-start(f32[4,128,256]{2,1,0:T(8,128)} %bitcast.221), channel_id=1, source_target_pairs={{0,8},{1,9},{2,10},{3,11},{4,12},{5,13},{6,14},{7,15},{8,0},{9,1},... | collective-permute-start | bytes 1572872 | tf_op jit(solution)/shard_map/ppermute | solution.py:40
  229.1 2.5 collective-permute-start.14
  231.6 4.6 collective-permute-start.12
  236.2 7.9 %fusion.30 = bf16[128,4,128]{0,2,1:T(8,128)(2,1)} fusion(f32[128,4,2048]{0,2,1:T(8,128)} %fusion.55, bf16[2048,256]{1,0:T(8,128)(2,1)S(1)} %bitcast.205, f32[128,4,2048]{0,2,1:T(8,128)} %get-tuple-element.47, f32[128,4]{0,1:T(4,128)} %get-tuple-element.46), kind=kOutput, calls=%fused_computation.56 | convolution fusion | flops 275843584 | bytes 17436672 | tf_op jit(solution)/shard_map/tgj,jh->tgh/dot_general | solution.py:150
  244.0 1.7 copy.53
  245.7 4.8 %collective-permute-start.8 = (bf16[128,512]{1,0:T(8,128)(2,1)}, bf16[128,512]{1,0:T(8,128)(2,1)S(1)}, u32[]{:S(2)}, u32[]{:S(2)}) collective-permute-start(bf16[128,512]{1,0:T(8,128)(2,1)} %copy.53), channel_id=1, source_target_pairs={{0,3},{1,0},{2,1},{3,2},{4,7},{5,4},{6,5},{7,6},{8,11},{9,8},{10,9... | collective-permute-start | bytes 393224 | tf_op jit(solution)/shard_map/ppermute | solution.py:32
  250.5 3.4 collective-permute-start.7
  256.2 7.4 %collective-permute-start.6 = (bf16[128,512]{1,0:T(8,128)(2,1)}, bf16[128,512]{1,0:T(8,128)(2,1)S(1)}, u32[]{:S(2)}, u32[]{:S(2)}) collective-permute-start(bf16[128,512]{1,0:T(8,128)(2,1)} %copy.53), channel_id=1, source_target_pairs={{0,1},{1,2},{2,3},{3,0},{4,5},{5,6},{6,7},{7,4},{8,9},{9,10},{10,1... | collective-permute-start | bytes 393224 | tf_op jit(solution)/shard_map/ppermute | solution.py:32
  265.2 3.5 collective-permute-start.15
  268.7 6.2 %collective-permute-start.17 = (f32[128,256]{1,0:T(8,128)S(1)}, f32[128,256]{1,0:T(8,128)S(1)}, u32[]{:S(2)}, u32[]{:S(2)}) collective-permute-start(f32[128,256]{1,0:T(8,128)S(1)} %get-tuple-element.35), channel_id=1, source_target_pairs={{0,1},{1,2},{2,3},{3,0},{4,5},{5,6},{6,7},{7,4},{8,9},{9,10},{10,1... | collective-permute-start | bytes 393224 | tf_op jit(solution)/shard_map/ppermute | solution.py:43
  274.9 8.9 %collective-permute-start.16 = (f32[128,256]{1,0:T(8,128)S(1)}, f32[128,256]{1,0:T(8,128)S(1)}, u32[]{:S(2)}, u32[]{:S(2)}) collective-permute-start(f32[128,256]{1,0:T(8,128)S(1)} %get-tuple-element.36), channel_id=1, source_target_pairs={{0,2},{1,3},{2,0},{3,1},{4,6},{5,7},{6,4},{7,5},{8,10},{9,11},{10,... | collective-permute-start | bytes 393224 | tf_op jit(solution)/shard_map/ppermute | solution.py:43
  283.9 1.9 collective-permute-start.10
  285.9 2.8 collective-permute-start.9
  288.6 4.3 collective-permute-start.11
  294.6 11.6 %collective-permute-done.16 = f32[128,256]{1,0:T(8,128)S(1)} collective-permute-done((f32[128,256]{1,0:T(8,128)S(1)}, f32[128,256]{1,0:T(8,128)S(1)}, u32[]{:S(2)}, u32[]{:S(2)}) %collective-permute-start.16) | collective-permute-done | bytes 131104 | tf_op jit(solution)/shard_map/ppermute | solution.py:43
  306.3 1.9 collective-permute-start.20
  308.2 6.7 %collective-permute-start.19 = (bf16[128,256]{1,0:T(8,128)(2,1)S(1)}, bf16[128,256]{1,0:T(8,128)(2,1)S(1)}, u32[]{:S(2)}, u32[]{:S(2)}) collective-permute-start(bf16[128,256]{1,0:T(8,128)(2,1)S(1)} %fusion.63), channel_id=1, source_target_pairs={{0,2},{1,3},{2,0},{3,1},{4,6},{5,7},{6,4},{7,5},{8,10},{9,11},{10,... | collective-permute-start | bytes 196616 | tf_op jit(solution)/shard_map/ppermute | solution.py:32
  314.9 2.2 collective-permute-done.20
  317.1 5.6 %collective-permute-start.18 = (bf16[128,256]{1,0:T(8,128)(2,1)S(1)}, bf16[128,256]{1,0:T(8,128)(2,1)S(1)}, u32[]{:S(2)}, u32[]{:S(2)}) collective-permute-start(bf16[128,256]{1,0:T(8,128)(2,1)S(1)} %fusion.63), channel_id=1, source_target_pairs={{0,1},{1,2},{2,3},{3,0},{4,5},{5,6},{6,7},{7,4},{8,9},{9,10},{10,1... | collective-permute-start | bytes 196616 | tf_op jit(solution)/shard_map/ppermute | solution.py:32
  323.1 4.6 collective-permute-done.18
  327.7 1.9 collective-permute-start.22
  329.6 1.9 collective-permute-start.21
  331.6 5.1 %collective-permute-start.23 = (bf16[4,128,256]{2,1,0:T(8,128)(2,1)S(1)}, bf16[4,128,256]{2,1,0:T(8,128)(2,1)S(1)}, u32[]{:S(2)}, u32[]{:S(2)}) collective-permute-start(bf16[4,128,256]{2,1,0:T(8,128)(2,1)S(1)} %get-tuple-element.38), channel_id=1, source_target_pairs={{0,12},{1,13},{2,14},{3,15},{4,0},{5,1},{6,2},{7,3},{8,4},{9,5},{1... | collective-permute-start | bytes 786440 | tf_op jit(solution)/shard_map/ppermute | solution.py:33
  336.7 3.6 collective-permute-done.22
  340.4 3.4 collective-permute-done.21
  343.8 2.1 maximum_maximum_fusion
  348.8 2.8 collective-permute-start.24
  351.6 2.7 collective-permute-start.25
  354.4 2.2 collective-permute-start.26
  356.8 3.2 collective-permute-done.24
  360.0 3.8 collective-permute-done.25
  363.7 4.3 collective-permute-done.26
  370.2 8.0 %collective-permute-start.29 = (bf16[4,128,256]{1,2,0:T(8,128)(2,1)}, bf16[4,128,256]{1,2,0:T(8,128)(2,1)}, u32[]{:S(2)}, u32[]{:S(2)}) collective-permute-start(bf16[4,128,256]{1,2,0:T(8,128)(2,1)} %get-tuple-element.11), channel_id=1, source_target_pairs={{0,1},{1,2},{2,3},{3,0},{4,5},{5,6},{6,7},{7,4},{8,9},{9,10},{10,1... | collective-permute-start | bytes 786440 | tf_op jit(solution)/shard_map/ppermute | solution.py:74
  378.2 4.0 collective-permute-start.28
  382.2 5.2 %collective-permute-start.27 = (bf16[4,128,256]{1,2,0:T(8,128)(2,1)}, bf16[4,128,256]{1,2,0:T(8,128)(2,1)}, u32[]{:S(2)}, u32[]{:S(2)}) collective-permute-start(bf16[4,128,256]{1,2,0:T(8,128)(2,1)} %get-tuple-element.13), channel_id=1, source_target_pairs={{0,3},{1,0},{2,1},{3,2},{4,7},{5,4},{6,5},{7,6},{8,11},{9,8},{10,9... | collective-permute-start | bytes 786440 | tf_op jit(solution)/shard_map/ppermute | solution.py:74
  388.1 4.1 collective-permute-done.29
  392.3 27.7 %collective-permute-done.28 = bf16[4,128,256]{1,2,0:T(8,128)(2,1)} collective-permute-done((bf16[4,128,256]{1,2,0:T(8,128)(2,1)}, bf16[4,128,256]{1,2,0:T(8,128)(2,1)}, u32[]{:S(2)}, u32[]{:S(2)}) %collective-permute-start.28) | collective-permute-done | bytes 262176 | tf_op jit(solution)/shard_map/ppermute | solution.py:74
  420.0 2.1 fusion.37
  425.4 2.1 collective-permute-start.30
  428.5 5.8 %collective-permute-start.31 = (bf16[256,768]{1,0:T(8,128)(2,1)S(1)}, bf16[256,768]{1,0:T(8,128)(2,1)S(1)}, u32[]{:S(2)}, u32[]{:S(2)}) collective-permute-start(bf16[256,768]{1,0:T(8,128)(2,1)S(1)} %fusion.26), channel_id=1, source_target_pairs={{0,496},{16,480},{32,464},{48,448},{64,432},{80,416},{96,400},{112... | collective-permute-start | bytes 1179656 | tf_op jit(solution)/shard_map/ppermute | solution.py:19
  434.2 23.8 %collective-permute-done.31 = bf16[256,768]{1,0:T(8,128)(2,1)S(1)} collective-permute-done((bf16[256,768]{1,0:T(8,128)(2,1)S(1)}, bf16[256,768]{1,0:T(8,128)(2,1)S(1)}, u32[]{:S(2)}, u32[]{:S(2)}) %collective-permute-start.31) | collective-permute-done | bytes 393248 | tf_op jit(solution)/shard_map/ppermute | solution.py:19
  (102 shorter events, 32.3 us)
Async XLA Ops:
  7.2 338.7 %copy-start = (bf16[1,256,768]{2,1,0:T(8,128)(2,1)S(1)}, bf16[1,256,768]{2,1,0:T(8,128)(2,1)}, u32[]{:S(2)}) copy-start(bf16[1,256,768]{2,1,0:T(8,128)(2,1)} %param.11) | copy-start | bytes 1179652
  7.2 188.4 %all-gather.3.cloned.1.call-start = ((), (), s32[]{:S(2)}) async-start(), calls=%async_computation | async-start | bytes 4456448 | tf_op jit(solution)/shard_map/all_gather | solution.py:121
  13.2 0.9 copy-start.11
  14.2 64.3 %collective-permute-start = (bf16[5,128,256]{1,2,0:T(8,128)(2,1)S(1)}, bf16[5,128,256]{1,2,0:T(8,128)(2,1)S(1)}, u32[]{:S(2)}, u32[]{:S(2)}) collective-permute-start(bf16[5,128,256]{1,2,0:T(8,128)(2,1)S(1)} %get-tuple-element.43), channel_id=1, source_target_pairs={{0,1},{1,2},{2,3},{3,0},{4,5},{5,6},{6,7},{7,4},{8,9},{9,10},{10,1... | collective-permute-start | bytes 983048 | tf_op jit(solution)/shard_map/ppermute | solution.py:54
  23.3 72.0 %collective-permute-start.1 = (bf16[5,128,256]{1,2,0:T(8,128)(2,1)S(1)}, bf16[5,128,256]{1,2,0:T(8,128)(2,1)}, u32[]{:S(2)}, u32[]{:S(2)}) collective-permute-start(bf16[5,128,256]{1,2,0:T(8,128)(2,1)S(1)} %get-tuple-element.44), channel_id=1, source_target_pairs={{0,2},{1,3},{2,0},{3,1},{4,6},{5,7},{6,4},{7,5},{8,10},{9,11},{10,... | collective-permute-start | bytes 983048 | tf_op jit(solution)/shard_map/ppermute | solution.py:54
  32.4 69.9 %collective-permute-start.2 = (bf16[5,128,256]{1,2,0:T(8,128)(2,1)S(1)}, bf16[5,128,256]{1,2,0:T(8,128)(2,1)}, u32[]{:S(2)}, u32[]{:S(2)}) collective-permute-start(bf16[5,128,256]{1,2,0:T(8,128)(2,1)S(1)} %get-tuple-element.45), channel_id=1, source_target_pairs={{0,3},{1,0},{2,1},{3,2},{4,7},{5,4},{6,5},{7,6},{8,11},{9,8},{10,9... | collective-permute-start | bytes 983048 | tf_op jit(solution)/shard_map/ppermute | solution.py:54
  103.7 10.0 %copy-start.13 = (s32[1,128]{1,0:T(1,128)S(1)}, s32[1,128]{1,0:T(1,128)}, u32[]{:S(2)}) copy-start(s32[1,128]{1,0:T(1,128)} %param.15) | copy-start | bytes 1540
  104.7 29.4 %collective-permute-start.3 = (bf16[8,128,256]{1,2,0:T(8,128)(2,1)S(1)}, bf16[8,128,256]{1,2,0:T(8,128)(2,1)S(1)}, u32[]{:S(2)}, u32[]{:S(2)}) collective-permute-start(bf16[8,128,256]{1,2,0:T(8,128)(2,1)S(1)} %get-tuple-element.39), channel_id=1, source_target_pairs={{0,4},{1,5},{2,6},{3,7},{4,8},{5,9},{6,10},{7,11},{8,12},{9,13},{1... | collective-permute-start | bytes 1572872 | tf_op jit(solution)/shard_map/ppermute | solution.py:59
  106.6 30.3 %collective-permute-start.4 = (bf16[8,128,256]{1,2,0:T(8,128)(2,1)S(1)}, bf16[8,128,256]{1,2,0:T(8,128)(2,1)S(1)}, u32[]{:S(2)}, u32[]{:S(2)}) collective-permute-start(bf16[8,128,256]{1,2,0:T(8,128)(2,1)S(1)} %get-tuple-element.40), channel_id=1, source_target_pairs={{0,8},{1,9},{2,10},{3,11},{4,12},{5,13},{6,14},{7,15},{8,0},{9,1},... | collective-permute-start | bytes 1572872 | tf_op jit(solution)/shard_map/ppermute | solution.py:59
  110.0 31.0 %collective-permute-start.5 = (bf16[8,128,256]{1,2,0:T(8,128)(2,1)S(1)}, bf16[8,128,256]{1,2,0:T(8,128)(2,1)S(1)}, u32[]{:S(2)}, u32[]{:S(2)}) collective-permute-start(bf16[8,128,256]{1,2,0:T(8,128)(2,1)S(1)} %get-tuple-element.41), channel_id=1, source_target_pairs={{0,12},{1,13},{2,14},{3,15},{4,0},{5,1},{6,2},{7,3},{8,4},{9,5},{1... | collective-permute-start | bytes 1572872 | tf_op jit(solution)/shard_map/ppermute | solution.py:59
  142.4 53.1 %copy-start.1 = (bf16[1,128,4096]{2,1,0:T(8,128)(2,1)S(1)}, bf16[1,128,4096]{2,1,0:T(8,128)(2,1)}, u32[]{:S(2)}) copy-start(bf16[1,128,4096]{2,1,0:T(8,128)(2,1)} %param.10) | copy-start | bytes 3145732
  201.6 3.8 copy-start.4
  201.6 3.8 copy-start.14
  201.6 3.8 copy-start.15
  224.4 31.8 %collective-permute-start.13 = (f32[4,128,256]{2,1,0:T(8,128)}, f32[4,128,256]{2,1,0:T(8,128)}, u32[]{:S(2)}, u32[]{:S(2)}) collective-permute-start(f32[4,128,256]{2,1,0:T(8,128)} %bitcast.221), channel_id=1, source_target_pairs={{0,8},{1,9},{2,10},{3,11},{4,12},{5,13},{6,14},{7,15},{8,0},{9,1},... | collective-permute-start | bytes 1572872 | tf_op jit(solution)/shard_map/ppermute | solution.py:40
  229.1 34.5 %collective-permute-start.14 = (f32[4,128,256]{2,1,0:T(8,128)}, f32[4,128,256]{2,1,0:T(8,128)}, u32[]{:S(2)}, u32[]{:S(2)}) collective-permute-start(f32[4,128,256]{2,1,0:T(8,128)} %bitcast.220), channel_id=1, source_target_pairs={{0,4},{1,5},{2,6},{3,7},{4,8},{5,9},{6,10},{7,11},{8,12},{9,13},{1... | collective-permute-start | bytes 1572872 | tf_op jit(solution)/shard_map/ppermute | solution.py:40
  231.6 32.0 %collective-permute-start.12 = (f32[4,128,256]{2,1,0:T(8,128)}, f32[4,128,256]{2,1,0:T(8,128)}, u32[]{:S(2)}, u32[]{:S(2)}) collective-permute-start(f32[4,128,256]{2,1,0:T(8,128)} %bitcast.219), channel_id=1, source_target_pairs={{0,12},{1,13},{2,14},{3,15},{4,0},{5,1},{6,2},{7,3},{8,4},{9,5},{1... | collective-permute-start | bytes 1572872 | tf_op jit(solution)/shard_map/ppermute | solution.py:40
  245.7 29.2 %collective-permute-start.8 = (bf16[128,512]{1,0:T(8,128)(2,1)}, bf16[128,512]{1,0:T(8,128)(2,1)S(1)}, u32[]{:S(2)}, u32[]{:S(2)}) collective-permute-start(bf16[128,512]{1,0:T(8,128)(2,1)} %copy.53), channel_id=1, source_target_pairs={{0,3},{1,0},{2,1},{3,2},{4,7},{5,4},{6,5},{7,6},{8,11},{9,8},{10,9... | collective-permute-start | bytes 393224 | tf_op jit(solution)/shard_map/ppermute | solution.py:32
  250.5 33.3 %collective-permute-start.7 = (bf16[128,512]{1,0:T(8,128)(2,1)}, bf16[128,512]{1,0:T(8,128)(2,1)S(1)}, u32[]{:S(2)}, u32[]{:S(2)}) collective-permute-start(bf16[128,512]{1,0:T(8,128)(2,1)} %copy.53), channel_id=1, source_target_pairs={{0,2},{1,3},{2,0},{3,1},{4,6},{5,7},{6,4},{7,5},{8,10},{9,11},{10,... | collective-permute-start | bytes 393224 | tf_op jit(solution)/shard_map/ppermute | solution.py:32
  256.2 27.6 %collective-permute-start.6 = (bf16[128,512]{1,0:T(8,128)(2,1)}, bf16[128,512]{1,0:T(8,128)(2,1)S(1)}, u32[]{:S(2)}, u32[]{:S(2)}) collective-permute-start(bf16[128,512]{1,0:T(8,128)(2,1)} %copy.53), channel_id=1, source_target_pairs={{0,1},{1,2},{2,3},{3,0},{4,5},{5,6},{6,7},{7,4},{8,9},{9,10},{10,1... | collective-permute-start | bytes 393224 | tf_op jit(solution)/shard_map/ppermute | solution.py:32
  265.2 23.5 %collective-permute-start.15 = (f32[128,256]{1,0:T(8,128)S(1)}, f32[128,256]{1,0:T(8,128)S(1)}, u32[]{:S(2)}, u32[]{:S(2)}) collective-permute-start(f32[128,256]{1,0:T(8,128)S(1)} %get-tuple-element.34), channel_id=1, source_target_pairs={{0,3},{1,0},{2,1},{3,2},{4,7},{5,4},{6,5},{7,6},{8,11},{9,8},{10,9... | collective-permute-start | bytes 393224 | tf_op jit(solution)/shard_map/ppermute | solution.py:43
  268.7 25.9 %collective-permute-start.17 = (f32[128,256]{1,0:T(8,128)S(1)}, f32[128,256]{1,0:T(8,128)S(1)}, u32[]{:S(2)}, u32[]{:S(2)}) collective-permute-start(f32[128,256]{1,0:T(8,128)S(1)} %get-tuple-element.35), channel_id=1, source_target_pairs={{0,1},{1,2},{2,3},{3,0},{4,5},{5,6},{6,7},{7,4},{8,9},{9,10},{10,1... | collective-permute-start | bytes 393224 | tf_op jit(solution)/shard_map/ppermute | solution.py:43
  274.9 31.3 %collective-permute-start.16 = (f32[128,256]{1,0:T(8,128)S(1)}, f32[128,256]{1,0:T(8,128)S(1)}, u32[]{:S(2)}, u32[]{:S(2)}) collective-permute-start(f32[128,256]{1,0:T(8,128)S(1)} %get-tuple-element.36), channel_id=1, source_target_pairs={{0,2},{1,3},{2,0},{3,1},{4,6},{5,7},{6,4},{7,5},{8,10},{9,11},{10,... | collective-permute-start | bytes 393224 | tf_op jit(solution)/shard_map/ppermute | solution.py:43
  283.9 47.6 %collective-permute-start.10 = (bf16[4,128,512]{2,1,0:T(8,128)(2,1)S(1)}, bf16[4,128,512]{2,1,0:T(8,128)(2,1)S(1)}, u32[]{:S(2)}, u32[]{:S(2)}) collective-permute-start(bf16[4,128,512]{2,1,0:T(8,128)(2,1)S(1)} %get-tuple-element.33), channel_id=1, source_target_pairs={{0,8},{1,9},{2,10},{3,11},{4,12},{5,13},{6,14},{7,15},{8,0},{9,1},... | collective-permute-start | bytes 1572872 | tf_op jit(solution)/shard_map/ppermute | solution.py:33
  285.9 50.9 %collective-permute-start.9 = (bf16[4,128,512]{2,1,0:T(8,128)(2,1)S(1)}, bf16[4,128,512]{2,1,0:T(8,128)(2,1)S(1)}, u32[]{:S(2)}, u32[]{:S(2)}) collective-permute-start(bf16[4,128,512]{2,1,0:T(8,128)(2,1)S(1)} %get-tuple-element.33), channel_id=1, source_target_pairs={{0,4},{1,5},{2,6},{3,7},{4,8},{5,9},{6,10},{7,11},{8,12},{9,13},{1... | collective-permute-start | bytes 1572872 | tf_op jit(solution)/shard_map/ppermute | solution.py:33
  288.6 48.1 %collective-permute-start.11 = (bf16[4,128,512]{2,1,0:T(8,128)(2,1)S(1)}, bf16[4,128,512]{2,1,0:T(8,128)(2,1)S(1)}, u32[]{:S(2)}, u32[]{:S(2)}) collective-permute-start(bf16[4,128,512]{2,1,0:T(8,128)(2,1)S(1)} %get-tuple-element.33), channel_id=1, source_target_pairs={{0,12},{1,13},{2,14},{3,15},{4,0},{5,1},{6,2},{7,3},{8,4},{9,5},{1... | collective-permute-start | bytes 1572872 | tf_op jit(solution)/shard_map/ppermute | solution.py:33
  306.3 10.9 %collective-permute-start.20 = (bf16[128,256]{1,0:T(8,128)(2,1)S(1)}, bf16[128,256]{1,0:T(8,128)(2,1)S(1)}, u32[]{:S(2)}, u32[]{:S(2)}) collective-permute-start(bf16[128,256]{1,0:T(8,128)(2,1)S(1)} %fusion.63), channel_id=1, source_target_pairs={{0,3},{1,0},{2,1},{3,2},{4,7},{5,4},{6,5},{7,6},{8,11},{9,8},{10,9... | collective-permute-start | bytes 196616 | tf_op jit(solution)/shard_map/ppermute | solution.py:32
  308.2 14.9 %collective-permute-start.19 = (bf16[128,256]{1,0:T(8,128)(2,1)S(1)}, bf16[128,256]{1,0:T(8,128)(2,1)S(1)}, u32[]{:S(2)}, u32[]{:S(2)}) collective-permute-start(bf16[128,256]{1,0:T(8,128)(2,1)S(1)} %fusion.63), channel_id=1, source_target_pairs={{0,2},{1,3},{2,0},{3,1},{4,6},{5,7},{6,4},{7,5},{8,10},{9,11},{10,... | collective-permute-start | bytes 196616 | tf_op jit(solution)/shard_map/ppermute | solution.py:32
  317.1 10.5 %collective-permute-start.18 = (bf16[128,256]{1,0:T(8,128)(2,1)S(1)}, bf16[128,256]{1,0:T(8,128)(2,1)S(1)}, u32[]{:S(2)}, u32[]{:S(2)}) collective-permute-start(bf16[128,256]{1,0:T(8,128)(2,1)S(1)} %fusion.63), channel_id=1, source_target_pairs={{0,1},{1,2},{2,3},{3,0},{4,5},{5,6},{6,7},{7,4},{8,9},{9,10},{10,1... | collective-permute-start | bytes 196616 | tf_op jit(solution)/shard_map/ppermute | solution.py:32
  327.7 12.7 %collective-permute-start.22 = (bf16[4,128,256]{2,1,0:T(8,128)(2,1)S(1)}, bf16[4,128,256]{2,1,0:T(8,128)(2,1)S(1)}, u32[]{:S(2)}, u32[]{:S(2)}) collective-permute-start(bf16[4,128,256]{2,1,0:T(8,128)(2,1)S(1)} %get-tuple-element.38), channel_id=1, source_target_pairs={{0,8},{1,9},{2,10},{3,11},{4,12},{5,13},{6,14},{7,15},{8,0},{9,1},... | collective-permute-start | bytes 786440 | tf_op jit(solution)/shard_map/ppermute | solution.py:33
  329.6 14.1 %collective-permute-start.21 = (bf16[4,128,256]{2,1,0:T(8,128)(2,1)S(1)}, bf16[4,128,256]{2,1,0:T(8,128)(2,1)S(1)}, u32[]{:S(2)}, u32[]{:S(2)}) collective-permute-start(bf16[4,128,256]{2,1,0:T(8,128)(2,1)S(1)} %get-tuple-element.38), channel_id=1, source_target_pairs={{0,4},{1,5},{2,6},{3,7},{4,8},{5,9},{6,10},{7,11},{8,12},{9,13},{1... | collective-permute-start | bytes 786440 | tf_op jit(solution)/shard_map/ppermute | solution.py:33
  331.6 12.2 %collective-permute-start.23 = (bf16[4,128,256]{2,1,0:T(8,128)(2,1)S(1)}, bf16[4,128,256]{2,1,0:T(8,128)(2,1)S(1)}, u32[]{:S(2)}, u32[]{:S(2)}) collective-permute-start(bf16[4,128,256]{2,1,0:T(8,128)(2,1)S(1)} %get-tuple-element.38), channel_id=1, source_target_pairs={{0,12},{1,13},{2,14},{3,15},{4,0},{5,1},{6,2},{7,3},{8,4},{9,5},{1... | collective-permute-start | bytes 786440 | tf_op jit(solution)/shard_map/ppermute | solution.py:33
  345.9 1.6 copy-start.2
  348.8 11.2 %collective-permute-start.24 = (bf16[4,128,256]{1,2,0:T(8,128)(2,1)S(1)}, bf16[4,128,256]{1,2,0:T(8,128)(2,1)}, u32[]{:S(2)}, u32[]{:S(2)}) collective-permute-start(bf16[4,128,256]{1,2,0:T(8,128)(2,1)S(1)} %copy.64), channel_id=1, source_target_pairs={{0,12},{1,13},{2,14},{3,15},{4,0},{5,1},{6,2},{7,3},{8,4},{9,5},{1... | collective-permute-start | bytes 786440 | tf_op jit(solution)/shard_map/ppermute | solution.py:70
  351.6 12.1 %collective-permute-start.25 = (bf16[4,128,256]{1,2,0:T(8,128)(2,1)S(1)}, bf16[4,128,256]{1,2,0:T(8,128)(2,1)}, u32[]{:S(2)}, u32[]{:S(2)}) collective-permute-start(bf16[4,128,256]{1,2,0:T(8,128)(2,1)S(1)} %copy.65), channel_id=1, source_target_pairs={{0,8},{1,9},{2,10},{3,11},{4,12},{5,13},{6,14},{7,15},{8,0},{9,1},... | collective-permute-start | bytes 786440 | tf_op jit(solution)/shard_map/ppermute | solution.py:70
  354.4 13.6 %collective-permute-start.26 = (bf16[4,128,256]{1,2,0:T(8,128)(2,1)}, bf16[4,128,256]{1,2,0:T(8,128)(2,1)}, u32[]{:S(2)}, u32[]{:S(2)}) collective-permute-start(bf16[4,128,256]{1,2,0:T(8,128)(2,1)} %copy.66), channel_id=1, source_target_pairs={{0,4},{1,5},{2,6},{3,7},{4,8},{5,9},{6,10},{7,11},{8,12},{9,13},{1... | collective-permute-start | bytes 786440 | tf_op jit(solution)/shard_map/ppermute | solution.py:70
  370.2 22.0 %collective-permute-start.29 = (bf16[4,128,256]{1,2,0:T(8,128)(2,1)}, bf16[4,128,256]{1,2,0:T(8,128)(2,1)}, u32[]{:S(2)}, u32[]{:S(2)}) collective-permute-start(bf16[4,128,256]{1,2,0:T(8,128)(2,1)} %get-tuple-element.11), channel_id=1, source_target_pairs={{0,1},{1,2},{2,3},{3,0},{4,5},{5,6},{6,7},{7,4},{8,9},{9,10},{10,1... | collective-permute-start | bytes 786440 | tf_op jit(solution)/shard_map/ppermute | solution.py:74
  378.2 41.8 %collective-permute-start.28 = (bf16[4,128,256]{1,2,0:T(8,128)(2,1)}, bf16[4,128,256]{1,2,0:T(8,128)(2,1)}, u32[]{:S(2)}, u32[]{:S(2)}) collective-permute-start(bf16[4,128,256]{1,2,0:T(8,128)(2,1)} %get-tuple-element.12), channel_id=1, source_target_pairs={{0,2},{1,3},{2,0},{3,1},{4,6},{5,7},{6,4},{7,5},{8,10},{9,11},{10,... | collective-permute-start | bytes 786440 | tf_op jit(solution)/shard_map/ppermute | solution.py:74
  382.2 37.8 %collective-permute-start.27 = (bf16[4,128,256]{1,2,0:T(8,128)(2,1)}, bf16[4,128,256]{1,2,0:T(8,128)(2,1)}, u32[]{:S(2)}, u32[]{:S(2)}) collective-permute-start(bf16[4,128,256]{1,2,0:T(8,128)(2,1)} %get-tuple-element.13), channel_id=1, source_target_pairs={{0,3},{1,0},{2,1},{3,2},{4,7},{5,4},{6,5},{7,6},{8,11},{9,8},{10,9... | collective-permute-start | bytes 786440 | tf_op jit(solution)/shard_map/ppermute | solution.py:74
  423.6 0.7 copy-start.10
  423.6 0.7 copy-start.12
  424.3 3.2 copy-start.3
  424.3 3.2 copy-start.6
  424.3 3.2 copy-start.7
  424.3 3.2 copy-start.8
  424.3 3.2 copy-start.9
  425.4 33.6 %collective-permute-start.30 = (bf16[128,4096]{0,1:T(8,128)(2,1)S(1)}, bf16[128,4096]{0,1:T(8,128)(2,1)S(1)}, u32[]{:S(2)}, u32[]{:S(2)}) collective-permute-start(bf16[128,4096]{0,1:T(8,128)(2,1)S(1)} %fusion.14), channel_id=1, source_target_pairs={{0,16},{16,32},{32,48},{48,64},{64,80},{80,96},{96,112},{112,128},... | collective-permute-start | bytes 3145736 | tf_op jit(solution)/shard_map/ppermute | solution.py:14
  427.5 30.6 %copy-start.5 = (bf16[1,256,768]{2,1,0:T(8,128)(2,1)S(1)}, bf16[1,256,768]{2,1,0:T(8,128)(2,1)}, u32[]{:S(2)}) copy-start(bf16[1,256,768]{2,1,0:T(8,128)(2,1)} %param.14) | copy-start | bytes 1179652
  428.5 29.6 %collective-permute-start.31 = (bf16[256,768]{1,0:T(8,128)(2,1)S(1)}, bf16[256,768]{1,0:T(8,128)(2,1)S(1)}, u32[]{:S(2)}, u32[]{:S(2)}) collective-permute-start(bf16[256,768]{1,0:T(8,128)(2,1)S(1)} %fusion.26), channel_id=1, source_target_pairs={{0,496},{16,480},{32,464},{48,448},{64,432},{80,416},{96,400},{112... | collective-permute-start | bytes 1179656 | tf_op jit(solution)/shard_map/ppermute | solution.py:19
Sparse Core Ops, SparseCore 0:
  11.0 184.4 all-gather.2

commit v5 on v4

--- a/solution.py
+++ b/solution.py
@@ -46,19 +46,21 @@
 
 def gather_and_scatter(x, cols, o, i):
     outer = lax.axis_size("seq") // INNER
-    n = x.shape[0]
-    parts = cols.reshape(n, outer, INNER, -1).transpose(2, 1, 0, 3)
-    first = [jnp.concatenate([x[None], parts[i]])]
+    m, n, w = x.shape
+    parts = cols.reshape(n, outer, INNER, w).transpose(2, 1, 0, 3)
+    first = [jnp.concatenate([x, parts[i]])]
     for k in range(1, INNER):
         piece = lax.dynamic_index_in_dim(parts, (i + k) % INNER, 0, keepdims=False)
-        first.append(lax.ppermute(jnp.concatenate([x[None], piece]), "seq", seq_pairs(k, 0)))
+        first.append(lax.ppermute(jnp.concatenate([x, piece]), "seq", seq_pairs(k, 0)))
     first = jnp.stack(first, axis=1)
-    second = [first]
+    own, rest = first[:m], first[m:]
+    second = []
     for k in range(1, outer):
-        piece = lax.dynamic_index_in_dim(first[1:], (o + k) % outer, 0, keepdims=False)
-        second.append(lax.ppermute(jnp.concatenate([first[0], piece]), "seq", seq_pairs(k, 1)))
-    gathered = jnp.stack([second[0][0]] + [s[:INNER] for s in second[1:]])
-    scattered = jnp.stack([second[0][1 + o]] + [s[INNER:] for s in second[1:]])
+        piece = lax.dynamic_index_in_dim(rest, (o + k) % outer, 0, keepdims=False)
+        payload = jnp.concatenate([own.reshape(m * INNER, n, w), piece])
+        second.append(lax.ppermute(payload, "seq", seq_pairs(k, 1)))
+    gathered = jnp.stack([own] + [s[: m * INNER].reshape(m, INNER, n, w) for s in second])
+    scattered = jnp.stack([lax.dynamic_index_in_dim(rest, o, 0, keepdims=False)] + [s[m * INNER :] for s in second])
     return gathered, scattered
 
 
@@ -119,9 +121,7 @@
     unit_up, inverse_up, normed_up = normalize(up_activation[0], upward_gain[0])
     hidden = normed_up.astype(jnp.bfloat16)
     output_weight = lax.all_gather(up_output_weight[0], "seq", axis=1, tiled=True)
-    key_value, hidden_cols = gather_and_scatter(saved[:, width:], hidden, o, i)
-    key_value = key_value.reshape(size * count, 2 * HEAD)
-    hidden_cols = hidden_cols.reshape(size * count, -1)
+    key_value = gather_blocks(saved[:, width:]).reshape(size * count, 2 * HEAD)
     keys = key_value[:, :HEAD]
     values = key_value[:, HEAD:]
     sources = (
@@ -154,7 +154,12 @@
     key_part = jnp.einsum("tgj,tgh->jh", score_grad, query, preferred_element_type=jnp.float32)
     value_part = jnp.einsum("tgj,tgh->jh", weights, grad_heads, preferred_element_type=jnp.float32)
     kv_part = jnp.concatenate([key_part, value_part], axis=1).reshape(outer, INNER, count, 2 * HEAD)
-    query_all = gather_blocks(query_grad)
+    pieces = hidden.shape[1] // size
+    query_all, hidden_cols = gather_and_scatter(
+        query_grad.reshape(count, width // pieces, pieces).transpose(1, 0, 2), hidden, o, i
+    )
+    query_all = query_all.transpose(0, 2, 3, 1, 4).reshape(outer, INNER, count, width)
+    hidden_cols = hidden_cols.reshape(size * count, -1)
     kv_grad = reduce_blocks(kv_part).astype(jnp.bfloat16)
     grad_all = jnp.concatenate([query_all, gather_blocks(kv_grad)], axis=-1).reshape(size * count, -1)
     input_term = contract_first(hidden_cols, grad_all).astype(jnp.bfloat16)

time: 469 us -> 500 us (1.066)
  the two profiles are of different devices: /device:TPU:64 before, /device:TPU:25 now
where the time goes in v5:
time: 500 us; the launch traced here: 491 us
  waiting for transfers between devices  238 us (48%)
  starting transfers between devices  141 us (28%)
  local copies, waits for them, and re-layouts  42.3 us (8%)
  matrix products  34.8 us (7%)
  other arithmetic  20.6 us (4%)
  between operations  15 us (3%)
    all_gather x1, waiting for transfers between devices, per_device(): lax.all_gather(up_output_weight[0], 'seq', axis=1, tiled=True)  88.2 us
    ppermute x6, waiting for transfers between devices, gather_blocks(): lax.ppermute(first, 'seq', seq_pairs(k, 1))  43.8 us
    ppermute x6, starting transfers between devices, gather_blocks(): lax.ppermute(x, 'seq', seq_pairs(k, 0))  40.2 us
    ppermute x3, waiting for transfers between devices, gather_columns(): second.append(lax.ppermute(first[k], 'seq', seq_pairs(INNER - k, 0)))  37.3 us
    ppermute x3, waiting for transfers between devices, gather_and_scatter(): lax.ppermute(jnp.concatenate([x, piece]), 'seq', seq_pairs(k, 0))  33 us
    ppermute x1, waiting for transfers between devices, mirrored(): lax.ppermute(value, axis, [(source, count - 1 - source) for source in ran...  21.8 us
    ppermute x6, starting transfers between devices, gather_blocks(): lax.ppermute(first, 'seq', seq_pairs(k, 1))  17.7 us
    ppermute x3, starting transfers between devices, gather_and_scatter(): lax.ppermute(jnp.concatenate([x, piece]), 'seq', seq_pairs(k, 0))  17.2 us
  transfers between devices with their start and end apart: 33, of which 18 were waited for; matrix products, arithmetic and copies ran while one was open for 11% of the time, Pallas kernels for 0%

profile of v5, /device:TPU:25, one launch (start us, length us, event | category | flops | bytes accessed | tf_op | source)
XLA Modules:
  0.0 491.2 jit_solution(11051789005843410937)
XLA Ops:
  9.0 12.5 %collective-permute-start.2 = (bf16[128,256]{0,1:T(8,128)(2,1)S(1)}, bf16[128,256]{0,1:T(8,128)(2,1)S(1)}, u32[]{:S(2)}, u32[]{:S(2)}) collective-permute-start(bf16[128,256]{0,1:T(8,128)(2,1)S(1)} %get-tuple-element.35), channel_id=1, source_target_pairs={{0,3},{1,0},{2,1},{3,2},{4,7},{5,4},{6,5},{7,6},{8,11},{9,8},{10,9... | collective-permute-start | bytes 196616 | tf_op jit(solution)/shard_map/ppermute | solution.py:32
  21.5 4.9 collective-permute-start.1
  26.4 7.3 %collective-permute-start = (bf16[128,256]{0,1:T(8,128)(2,1)S(1)}, bf16[128,256]{0,1:T(8,128)(2,1)S(1)}, u32[]{:S(2)}, u32[]{:S(2)}) collective-permute-start(bf16[128,256]{0,1:T(8,128)(2,1)S(1)} %get-tuple-element.35), channel_id=1, source_target_pairs={{0,1},{1,2},{2,3},{3,0},{4,5},{5,6},{6,7},{7,4},{8,9},{9,10},{10,1... | collective-permute-start | bytes 196616 | tf_op jit(solution)/shard_map/ppermute | solution.py:32
  40.1 4.4 collective-permute-start.5
  44.5 2.4 collective-permute-start.4
  46.9 2.5 collective-permute-start.3
  51.8 5.1 %collective-permute-done.4 = bf16[4,128,256]{1,2,0:T(8,128)(2,1)} collective-permute-done((bf16[4,128,256]{1,2,0:T(8,128)(2,1)S(1)}, bf16[4,128,256]{1,2,0:T(8,128)(2,1)}, u32[]{:S(2)}, u32[]{:S(2)}) %collective-permute-start.4) | collective-permute-done | bytes 262176 | tf_op jit(solution)/shard_map/ppermute | solution.py:33
  56.9 6.1 %collective-permute-done.3 = bf16[4,128,256]{1,2,0:T(8,128)(2,1)} collective-permute-done((bf16[4,128,256]{1,2,0:T(8,128)(2,1)S(1)}, bf16[4,128,256]{1,2,0:T(8,128)(2,1)}, u32[]{:S(2)}, u32[]{:S(2)}) %collective-permute-start.3) | collective-permute-done | bytes 262176 | tf_op jit(solution)/shard_map/ppermute | solution.py:33
  64.7 5.4 %fusion.100 = (f32[128,4]{0,1:T(4,128)}, f32[128,4,2048]{0,2,1:T(8,128)}) fusion(pred[128,2048]{0,1:T(8,128)(4,1)} %compare_and_fusion, bf16[128,4,128]{0,2,1:T(8,128)(2,1)} %bitcast.244, bf16[2048,256]{1,0:T(8,128)(2,1)S(1)} %bitcast.214), kind=kOutput, calls=%fused_computation.167 | convolution fusion | flops 273680384 | bytes 5376000 | tf_op jit(solution)/shard_map/sub | solution.py:142
  70.2 88.2 %all-gather.3.cloned.1.call-done = bf16[1,512,4096]{2,1,0:T(8,128)(2,1)} async-done(((bf16[1,512,256]{2,1,0:T(8,128)(2,1)}), bf16[1,512,4096]{2,1,0:T(8,128)(2,1)}) %all-gather.3.cloned.1.call-update) | async-done | bytes 4194320 | tf_op jit(solution)/shard_map/all_gather | solution.py:123
  158.4 4.4 fusion.49
  163.8 2.7 fusion.77
  166.5 7.9 %fusion.52 = bf16[128,4,128]{0,2,1:T(8,128)(2,1)} fusion(f32[128,4,2048]{0,2,1:T(8,128)} %fusion.77, bf16[2048,256]{1,0:T(8,128)(2,1)S(1)} %bitcast.216, f32[128,4,2048]{0,2,1:T(8,128)} %get-tuple-element.41, f32[128,4]{0,1:T(4,128)S(1)} %copy-done.28), kind=kOutput, calls=%fused_computation.69 | convolution fusion | flops 275843584 | bytes 17436672 | tf_op jit(solution)/shard_map/tgj,jh->tgh/dot_general | solution.py:150
  174.4 2.2 fusion.78
  176.6 8.3 %collective-permute-start.8 = (bf16[6,128,256]{1,2,0:T(8,128)(2,1)}, bf16[6,128,256]{1,2,0:T(8,128)(2,1)S(1)}, u32[]{:S(2)}, u32[]{:S(2)}) collective-permute-start(bf16[6,128,256]{1,2,0:T(8,128)(2,1)} %get-tuple-element.39), channel_id=1, source_target_pairs={{0,3},{1,0},{2,1},{3,2},{4,7},{5,4},{6,5},{7,6},{8,11},{9,8},{10,9... | collective-permute-start | bytes 1179656 | tf_op jit(solution)/shard_map/ppermute | solution.py:54
  184.8 4.0 convolution_bitcast_fusion
  188.8 5.6 %collective-permute-start.7 = (bf16[6,128,256]{1,2,0:T(8,128)(2,1)}, bf16[6,128,256]{1,2,0:T(8,128)(2,1)S(1)}, u32[]{:S(2)}, u32[]{:S(2)}) collective-permute-start(bf16[6,128,256]{1,2,0:T(8,128)(2,1)} %get-tuple-element.38), channel_id=1, source_target_pairs={{0,2},{1,3},{2,0},{3,1},{4,6},{5,7},{6,4},{7,5},{8,10},{9,11},{10,... | collective-permute-start | bytes 1179656 | tf_op jit(solution)/shard_map/ppermute | solution.py:54
  194.4 3.3 collective-permute-start.6
  197.7 8.3 %convolution_bitcast_fusion.1 = f32[2048,128]{0,1:T(8,128)} fusion(bf16[128,4,128]{0,2,1:T(8,128)(2,1)S(1)} %bitcast.245, f32[128,4,2048]{0,2,1:T(8,128)} %fusion.77, f32[128,4,2048]{0,2,1:T(8,128)} %get-tuple-element.41, f32[128,4]{0,1:T(4,128)S(1)} %copy-done.29), kind=kOutput, calls=%fused_computation.34 | convolution fusion | flops 275778048 | bytes 9570304 | tf_op jit(solution)/shard_map/tgj,tgh->jh/dot_general | solution.py:154
  206.1 2.7 fusion.76
  208.8 2.0 copy.75
  210.8 1.9 collective-permute-start.14
  212.7 2.0 copy.74
  214.8 5.5 %collective-permute-start.13 = (f32[4,128,256]{2,1,0:T(8,128)}, f32[4,128,256]{2,1,0:T(8,128)}, u32[]{:S(2)}, u32[]{:S(2)}) collective-permute-start(f32[4,128,256]{2,1,0:T(8,128)} %bitcast.234), channel_id=1, source_target_pairs={{0,8},{1,9},{2,10},{3,11},{4,12},{5,13},{6,14},{7,15},{8,0},{9,1},... | collective-permute-start | bytes 1572872 | tf_op jit(solution)/shard_map/ppermute | solution.py:40
  222.7 4.2 collective-permute-start.12
  228.2 23.7 %collective-permute-done.7 = bf16[6,128,256]{1,2,0:T(8,128)(2,1)S(1)} collective-permute-done((bf16[6,128,256]{1,2,0:T(8,128)(2,1)}, bf16[6,128,256]{1,2,0:T(8,128)(2,1)S(1)}, u32[]{:S(2)}, u32[]{:S(2)}) %collective-permute-start.7) | collective-permute-done | bytes 393248 | tf_op jit(solution)/shard_map/ppermute | solution.py:54
  251.9 7.8 %collective-permute-done.6 = bf16[6,128,256]{1,2,0:T(8,128)(2,1)S(1)} collective-permute-done((bf16[6,128,256]{1,2,0:T(8,128)(2,1)}, bf16[6,128,256]{1,2,0:T(8,128)(2,1)S(1)}, u32[]{:S(2)}, u32[]{:S(2)}) %collective-permute-start.6) | collective-permute-done | bytes 393248 | tf_op jit(solution)/shard_map/ppermute | solution.py:54
  261.4 3.8 collective-permute-start.17
  265.2 6.3 %collective-permute-start.16 = (f32[128,256]{1,0:T(8,128)S(1)}, f32[128,256]{1,0:T(8,128)S(1)}, u32[]{:S(2)}, u32[]{:S(2)}) collective-permute-start(f32[128,256]{1,0:T(8,128)S(1)} %get-tuple-element.29), channel_id=1, source_target_pairs={{0,2},{1,3},{2,0},{3,1},{4,6},{5,7},{6,4},{7,5},{8,10},{9,11},{10,... | collective-permute-start | bytes 393224 | tf_op jit(solution)/shard_map/ppermute | solution.py:43
  271.5 2.6 collective-permute-start.15
  276.3 3.6 collective-permute-done.16
  280.0 6.1 %collective-permute-done.15 = f32[128,256]{1,0:T(8,128)S(1)} collective-permute-done((f32[128,256]{1,0:T(8,128)S(1)}, f32[128,256]{1,0:T(8,128)S(1)}, u32[]{:S(2)}, u32[]{:S(2)}) %collective-permute-start.15) | collective-permute-done | bytes 131104 | tf_op jit(solution)/shard_map/ppermute | solution.py:43
  286.1 1.9 collective-permute-start.20
  288.1 9.1 %collective-permute-start.19 = (bf16[128,256]{1,0:T(8,128)(2,1)S(1)}, bf16[128,256]{1,0:T(8,128)(2,1)S(1)}, u32[]{:S(2)}, u32[]{:S(2)}) collective-permute-start(bf16[128,256]{1,0:T(8,128)(2,1)S(1)} %fusion.85), channel_id=1, source_target_pairs={{0,2},{1,3},{2,0},{3,1},{4,6},{5,7},{6,4},{7,5},{8,10},{9,11},{10,... | collective-permute-start | bytes 196616 | tf_op jit(solution)/shard_map/ppermute | solution.py:32
  297.2 4.5 collective-permute-start.18
  301.9 4.4 collective-permute-start.11
  306.2 4.3 collective-permute-start.10
  310.6 2.5 collective-permute-start.9
  313.2 4.0 collective-permute-start.23
  317.2 1.9 collective-permute-start.22
  319.1 26.1 %collective-permute-done.23 = bf16[4,128,256]{2,1,0:T(8,128)(2,1)S(1)} collective-permute-done((bf16[4,128,256]{2,1,0:T(8,128)(2,1)S(1)}, bf16[4,128,256]{2,1,0:T(8,128)(2,1)S(1)}, u32[]{:S(2)}, u32[]{:S(2)}) %collective-permute-start.23) | collective-permute-done | bytes 262176 | tf_op jit(solution)/shard_map/ppermute | solution.py:33
  345.2 2.5 collective-permute-start.21
  347.7 1.8 collective-permute-done.22
  349.6 4.7 collective-permute-done.21
  359.6 4.9 copy.48
  367.8 1.8 copy.58
  369.5 3.1 collective-permute-start.26
  372.6 1.8 copy.57
  374.4 3.4 collective-permute-start.25
  377.8 1.8 copy.56
  379.6 4.0 collective-permute-start.24
  383.6 2.3 copy.33
  385.9 1.8 copy.59
  392.4 1.9 collective-permute-start.27
  394.3 8.0 %collective-permute-start.28 = (bf16[4,128,256]{1,2,0:T(8,128)(2,1)}, bf16[4,128,256]{1,2,0:T(8,128)(2,1)}, u32[]{:S(2)}, u32[]{:S(2)}) collective-permute-start(bf16[4,128,256]{1,2,0:T(8,128)(2,1)} %get-tuple-element.13), channel_id=1, source_target_pairs={{0,2},{1,3},{2,0},{3,1},{4,6},{5,7},{6,4},{7,5},{8,10},{9,11},{10,... | collective-permute-start | bytes 786440 | tf_op jit(solution)/shard_map/ppermute | solution.py:76
  402.3 3.7 collective-permute-start.29
  407.7 2.6 reshape.212
  411.3 16.4 %collective-permute-done.27 = bf16[4,128,256]{1,2,0:T(8,128)(2,1)} collective-permute-done((bf16[4,128,256]{1,2,0:T(8,128)(2,1)}, bf16[4,128,256]{1,2,0:T(8,128)(2,1)}, u32[]{:S(2)}, u32[]{:S(2)}) %collective-permute-start.27) | collective-permute-done | bytes 262176 | tf_op jit(solution)/shard_map/ppermute | solution.py:76
  427.7 16.2 %collective-permute-done.28 = bf16[4,128,256]{1,2,0:T(8,128)(2,1)} collective-permute-done((bf16[4,128,256]{1,2,0:T(8,128)(2,1)}, bf16[4,128,256]{1,2,0:T(8,128)(2,1)}, u32[]{:S(2)}, u32[]{:S(2)}) %collective-permute-start.28) | collective-permute-done | bytes 262176 | tf_op jit(solution)/shard_map/ppermute | solution.py:76
  443.9 4.6 collective-permute-done.29
  448.6 2.1 fusion.59
  453.4 4.0 collective-permute-start.30
  458.5 1.9 collective-permute-start.31
  460.4 21.8 %collective-permute-done.31 = bf16[256,768]{1,0:T(8,128)(2,1)S(1)} collective-permute-done((bf16[256,768]{1,0:T(8,128)(2,1)S(1)}, bf16[256,768]{1,0:T(8,128)(2,1)S(1)}, u32[]{:S(2)}, u32[]{:S(2)}) %collective-permute-start.31) | collective-permute-done | bytes 393248 | tf_op jit(solution)/shard_map/ppermute | solution.py:19
  (135 shorter events, 42.7 us)
Async XLA Ops:
  7.2 357.8 %copy-start = (bf16[1,256,768]{2,1,0:T(8,128)(2,1)S(1)}, bf16[1,256,768]{2,1,0:T(8,128)(2,1)}, u32[]{:S(2)}) copy-start(bf16[1,256,768]{2,1,0:T(8,128)(2,1)} %param.11) | copy-start | bytes 1179652
  7.2 29.0 %copy-start.27 = (s32[1,128]{1,0:T(1,128)S(1)}, s32[1,128]{1,0:T(1,128)}, u32[]{:S(2)}) copy-start(s32[1,128]{1,0:T(1,128)} %param.15) | copy-start | bytes 1540
  7.2 30.6 %copy-start.23 = (f32[1,4096]{1,0:T(1,128)S(1)}, f32[1,4096]{1,0:T(1,128)}, u32[]{:S(2)}) copy-start(f32[1,4096]{1,0:T(1,128)} %param.13) | copy-start | bytes 49156
  7.2 151.2 %all-gather.3.cloned.1.call-start = ((), (), s32[]{:S(2)}) async-start(), calls=%async_computation | async-start | bytes 4456448 | tf_op jit(solution)/shard_map/all_gather | solution.py:123
  9.0 29.4 %collective-permute-start.2 = (bf16[128,256]{0,1:T(8,128)(2,1)S(1)}, bf16[128,256]{0,1:T(8,128)(2,1)S(1)}, u32[]{:S(2)}, u32[]{:S(2)}) collective-permute-start(bf16[128,256]{0,1:T(8,128)(2,1)S(1)} %get-tuple-element.35), channel_id=1, source_target_pairs={{0,3},{1,0},{2,1},{3,2},{4,7},{5,4},{6,5},{7,6},{8,11},{9,8},{10,9... | collective-permute-start | bytes 196616 | tf_op jit(solution)/shard_map/ppermute | solution.py:32
  21.5 17.0 %collective-permute-start.1 = (bf16[128,256]{0,1:T(8,128)(2,1)S(1)}, bf16[128,256]{0,1:T(8,128)(2,1)S(1)}, u32[]{:S(2)}, u32[]{:S(2)}) collective-permute-start(bf16[128,256]{0,1:T(8,128)(2,1)S(1)} %get-tuple-element.35), channel_id=1, source_target_pairs={{0,2},{1,3},{2,0},{3,1},{4,6},{5,7},{6,4},{7,5},{8,10},{9,11},{10,... | collective-permute-start | bytes 196616 | tf_op jit(solution)/shard_map/ppermute | solution.py:32
  26.4 13.6 %collective-permute-start = (bf16[128,256]{0,1:T(8,128)(2,1)S(1)}, bf16[128,256]{0,1:T(8,128)(2,1)S(1)}, u32[]{:S(2)}, u32[]{:S(2)}) collective-permute-start(bf16[128,256]{0,1:T(8,128)(2,1)S(1)} %get-tuple-element.35), channel_id=1, source_target_pairs={{0,1},{1,2},{2,3},{3,0},{4,5},{5,6},{6,7},{7,4},{8,9},{9,10},{10,1... | collective-permute-start | bytes 196616 | tf_op jit(solution)/shard_map/ppermute | solution.py:32
  37.2 25.8 %copy-start.25 = (f32[128]{0:T(128)}, f32[128]{0:T(128)S(1)}, u32[]{:S(2)}) copy-start(f32[128]{0:T(128)S(1)} %add_rsqrt_fusion) | copy-start | bytes 1540
  40.1 11.7 %collective-permute-start.5 = (bf16[4,128,256]{1,2,0:T(8,128)(2,1)S(1)}, bf16[4,128,256]{1,2,0:T(8,128)(2,1)S(1)}, u32[]{:S(2)}, u32[]{:S(2)}) collective-permute-start(bf16[4,128,256]{1,2,0:T(8,128)(2,1)S(1)} %get-tuple-element.33), channel_id=1, source_target_pairs={{0,12},{1,13},{2,14},{3,15},{4,0},{5,1},{6,2},{7,3},{8,4},{9,5},{1... | collective-permute-start | bytes 786440 | tf_op jit(solution)/shard_map/ppermute | solution.py:33
  44.5 12.4 %collective-permute-start.4 = (bf16[4,128,256]{1,2,0:T(8,128)(2,1)S(1)}, bf16[4,128,256]{1,2,0:T(8,128)(2,1)}, u32[]{:S(2)}, u32[]{:S(2)}) collective-permute-start(bf16[4,128,256]{1,2,0:T(8,128)(2,1)S(1)} %get-tuple-element.33), channel_id=1, source_target_pairs={{0,8},{1,9},{2,10},{3,11},{4,12},{5,13},{6,14},{7,15},{8,0},{9,1},... | collective-permute-start | bytes 786440 | tf_op jit(solution)/shard_map/ppermute | solution.py:33
  46.9 16.1 %collective-permute-start.3 = (bf16[4,128,256]{1,2,0:T(8,128)(2,1)S(1)}, bf16[4,128,256]{1,2,0:T(8,128)(2,1)}, u32[]{:S(2)}, u32[]{:S(2)}) collective-permute-start(bf16[4,128,256]{1,2,0:T(8,128)(2,1)S(1)} %get-tuple-element.33), channel_id=1, source_target_pairs={{0,4},{1,5},{2,6},{3,7},{4,8},{5,9},{6,10},{7,11},{8,12},{9,13},{1... | collective-permute-start | bytes 786440 | tf_op jit(solution)/shard_map/ppermute | solution.py:33
  64.7 93.6 %copy-start.1 = (bf16[1,128,4096]{2,1,0:T(8,128)(2,1)S(1)}, bf16[1,128,4096]{2,1,0:T(8,128)(2,1)}, u32[]{:S(2)}) copy-start(bf16[1,128,4096]{2,1,0:T(8,128)(2,1)} %param.10) | copy-start | bytes 3145732
  162.8 3.7 copy-start.28
  166.5 7.9 %copy-start.7 = (bf16[4,128,256]{1,2,0:T(8,128)(2,1)S(1)}, bf16[4,128,256]{1,2,0:T(8,128)(2,1)}, u32[]{:S(2)}) copy-start(bf16[4,128,256]{1,2,0:T(8,128)(2,1)} %get-tuple-element.20) | copy-start | bytes 786436
  166.5 7.9 %copy-start.8 = (bf16[4,128,256]{1,2,0:T(8,128)(2,1)S(1)}, bf16[4,128,256]{1,2,0:T(8,128)(2,1)}, u32[]{:S(2)}) copy-start(bf16[4,128,256]{1,2,0:T(8,128)(2,1)} %get-tuple-element.21) | copy-start | bytes 786436
  176.6 21.2 %copy-start.22 = (bf16[128,512]{0,1:T(8,128)(2,1)S(1)}, bf16[128,512]{0,1:T(8,128)(2,1)}, u32[]{:S(2)}) copy-start(bf16[128,512]{0,1:T(8,128)(2,1)} %slice.122) | copy-start | bytes 393220
  176.6 21.2 %copy-start.29 = (f32[128,4]{0,1:T(4,128)S(1)}, f32[128,4]{0,1:T(4,128)}, u32[]{:S(2)}) copy-start(f32[128,4]{0,1:T(4,128)} %get-tuple-element.40) | copy-start | bytes 6148
  176.6 46.1 %collective-permute-start.8 = (bf16[6,128,256]{1,2,0:T(8,128)(2,1)}, bf16[6,128,256]{1,2,0:T(8,128)(2,1)S(1)}, u32[]{:S(2)}, u32[]{:S(2)}) collective-permute-start(bf16[6,128,256]{1,2,0:T(8,128)(2,1)} %get-tuple-element.39), channel_id=1, source_target_pairs={{0,3},{1,0},{2,1},{3,2},{4,7},{5,4},{6,5},{7,6},{8,11},{9,8},{10,9... | collective-permute-start | bytes 1179656 | tf_op jit(solution)/shard_map/ppermute | solution.py:54
  188.8 63.1 %collective-permute-start.7 = (bf16[6,128,256]{1,2,0:T(8,128)(2,1)}, bf16[6,128,256]{1,2,0:T(8,128)(2,1)S(1)}, u32[]{:S(2)}, u32[]{:S(2)}) collective-permute-start(bf16[6,128,256]{1,2,0:T(8,128)(2,1)} %get-tuple-element.38), channel_id=1, source_target_pairs={{0,2},{1,3},{2,0},{3,1},{4,6},{5,7},{6,4},{7,5},{8,10},{9,11},{10,... | collective-permute-start | bytes 1179656 | tf_op jit(solution)/shard_map/ppermute | solution.py:54
  194.4 65.3 %collective-permute-start.6 = (bf16[6,128,256]{1,2,0:T(8,128)(2,1)}, bf16[6,128,256]{1,2,0:T(8,128)(2,1)S(1)}, u32[]{:S(2)}, u32[]{:S(2)}) collective-permute-start(bf16[6,128,256]{1,2,0:T(8,128)(2,1)} %get-tuple-element.37), channel_id=1, source_target_pairs={{0,1},{1,2},{2,3},{3,0},{4,5},{5,6},{6,7},{7,4},{8,9},{9,10},{10,1... | collective-permute-start | bytes 1179656 | tf_op jit(solution)/shard_map/ppermute | solution.py:54
  210.8 49.0 %collective-permute-start.14 = (f32[4,128,256]{2,1,0:T(8,128)}, f32[4,128,256]{2,1,0:T(8,128)}, u32[]{:S(2)}, u32[]{:S(2)}) collective-permute-start(f32[4,128,256]{2,1,0:T(8,128)} %bitcast.233), channel_id=1, source_target_pairs={{0,4},{1,5},{2,6},{3,7},{4,8},{5,9},{6,10},{7,11},{8,12},{9,13},{1... | collective-permute-start | bytes 1572872 | tf_op jit(solution)/shard_map/ppermute | solution.py:40
  214.8 45.1 %collective-permute-start.13 = (f32[4,128,256]{2,1,0:T(8,128)}, f32[4,128,256]{2,1,0:T(8,128)}, u32[]{:S(2)}, u32[]{:S(2)}) collective-permute-start(f32[4,128,256]{2,1,0:T(8,128)} %bitcast.234), channel_id=1, source_target_pairs={{0,8},{1,9},{2,10},{3,11},{4,12},{5,13},{6,14},{7,15},{8,0},{9,1},... | collective-permute-start | bytes 1572872 | tf_op jit(solution)/shard_map/ppermute | solution.py:40
  222.7 37.2 %collective-permute-start.12 = (f32[4,128,256]{2,1,0:T(8,128)}, f32[4,128,256]{2,1,0:T(8,128)}, u32[]{:S(2)}, u32[]{:S(2)}) collective-permute-start(f32[4,128,256]{2,1,0:T(8,128)} %bitcast.235), channel_id=1, source_target_pairs={{0,12},{1,13},{2,14},{3,15},{4,0},{5,1},{6,2},{7,3},{8,4},{9,5},{1... | collective-permute-start | bytes 1572872 | tf_op jit(solution)/shard_map/ppermute | solution.py:40
  261.4 14.9 %collective-permute-start.17 = (f32[128,256]{1,0:T(8,128)S(1)}, f32[128,256]{1,0:T(8,128)S(1)}, u32[]{:S(2)}, u32[]{:S(2)}) collective-permute-start(f32[128,256]{1,0:T(8,128)S(1)} %get-tuple-element.28), channel_id=1, source_target_pairs={{0,1},{1,2},{2,3},{3,0},{4,5},{5,6},{6,7},{7,4},{8,9},{9,10},{10,1... | collective-permute-start | bytes 393224 | tf_op jit(solution)/shard_map/ppermute | solution.py:43
  265.2 14.7 %collective-permute-start.16 = (f32[128,256]{1,0:T(8,128)S(1)}, f32[128,256]{1,0:T(8,128)S(1)}, u32[]{:S(2)}, u32[]{:S(2)}) collective-permute-start(f32[128,256]{1,0:T(8,128)S(1)} %get-tuple-element.29), channel_id=1, source_target_pairs={{0,2},{1,3},{2,0},{3,1},{4,6},{5,7},{6,4},{7,5},{8,10},{9,11},{10,... | collective-permute-start | bytes 393224 | tf_op jit(solution)/shard_map/ppermute | solution.py:43
  271.5 14.5 %collective-permute-start.15 = (f32[128,256]{1,0:T(8,128)S(1)}, f32[128,256]{1,0:T(8,128)S(1)}, u32[]{:S(2)}, u32[]{:S(2)}) collective-permute-start(f32[128,256]{1,0:T(8,128)S(1)} %get-tuple-element.27), channel_id=1, source_target_pairs={{0,3},{1,0},{2,1},{3,2},{4,7},{5,4},{6,5},{7,6},{8,11},{9,8},{10,9... | collective-permute-start | bytes 393224 | tf_op jit(solution)/shard_map/ppermute | solution.py:43
  286.1 24.5 %collective-permute-start.20 = (bf16[128,256]{1,0:T(8,128)(2,1)S(1)}, bf16[128,256]{1,0:T(8,128)(2,1)S(1)}, u32[]{:S(2)}, u32[]{:S(2)}) collective-permute-start(bf16[128,256]{1,0:T(8,128)(2,1)S(1)} %fusion.85), channel_id=1, source_target_pairs={{0,3},{1,0},{2,1},{3,2},{4,7},{5,4},{6,5},{7,6},{8,11},{9,8},{10,9... | collective-permute-start | bytes 196616 | tf_op jit(solution)/shard_map/ppermute | solution.py:32
  288.1 25.0 %collective-permute-start.19 = (bf16[128,256]{1,0:T(8,128)(2,1)S(1)}, bf16[128,256]{1,0:T(8,128)(2,1)S(1)}, u32[]{:S(2)}, u32[]{:S(2)}) collective-permute-start(bf16[128,256]{1,0:T(8,128)(2,1)S(1)} %fusion.85), channel_id=1, source_target_pairs={{0,2},{1,3},{2,0},{3,1},{4,6},{5,7},{6,4},{7,5},{8,10},{9,11},{10,... | collective-permute-start | bytes 196616 | tf_op jit(solution)/shard_map/ppermute | solution.py:32
  297.2 15.9 %collective-permute-start.18 = (bf16[128,256]{1,0:T(8,128)(2,1)S(1)}, bf16[128,256]{1,0:T(8,128)(2,1)S(1)}, u32[]{:S(2)}, u32[]{:S(2)}) collective-permute-start(bf16[128,256]{1,0:T(8,128)(2,1)S(1)} %fusion.85), channel_id=1, source_target_pairs={{0,1},{1,2},{2,3},{3,0},{4,5},{5,6},{6,7},{7,4},{8,9},{9,10},{10,1... | collective-permute-start | bytes 196616 | tf_op jit(solution)/shard_map/ppermute | solution.py:32
  301.9 53.5 %collective-permute-start.11 = (bf16[12,128,256]{1,2,0:T(8,128)(2,1)S(1)}, bf16[12,128,256]{1,2,0:T(8,128)(2,1)S(1)}, u32[]{:S(2)}, u32[]{:S(2)}) collective-permute-start(bf16[12,128,256]{1,2,0:T(8,128)(2,1)S(1)} %get-tuple-element.26), channel_id=1, source_target_pairs={{0,12},{1,13},{2,14},{3,15},{4,0},{5,1},{6,2},{7,3},{8,4},{9,5},{1... | collective-permute-start | bytes 2359304 | tf_op jit(solution)/shard_map/ppermute | solution.py:61
  306.2 50.0 %collective-permute-start.10 = (bf16[12,128,256]{1,2,0:T(8,128)(2,1)S(1)}, bf16[12,128,256]{1,2,0:T(8,128)(2,1)S(1)}, u32[]{:S(2)}, u32[]{:S(2)}) collective-permute-start(bf16[12,128,256]{1,2,0:T(8,128)(2,1)S(1)} %get-tuple-element.25), channel_id=1, source_target_pairs={{0,8},{1,9},{2,10},{3,11},{4,12},{5,13},{6,14},{7,15},{8,0},{9,1},... | collective-permute-start | bytes 2359304 | tf_op jit(solution)/shard_map/ppermute | solution.py:61
  310.6 45.7 %collective-permute-start.9 = (bf16[12,128,256]{1,2,0:T(8,128)(2,1)S(1)}, bf16[12,128,256]{1,2,0:T(8,128)(2,1)S(1)}, u32[]{:S(2)}, u32[]{:S(2)}) collective-permute-start(bf16[12,128,256]{1,2,0:T(8,128)(2,1)S(1)} %get-tuple-element.24), channel_id=1, source_target_pairs={{0,4},{1,5},{2,6},{3,7},{4,8},{5,9},{6,10},{7,11},{8,12},{9,13},{1... | collective-permute-start | bytes 2359304 | tf_op jit(solution)/shard_map/ppermute | solution.py:61
  313.2 43.1 %copy-start.5 = (bf16[1,4,128,256]{3,2,1,0:T(8,128)(2,1)}, bf16[1,4,128,256]{3,2,1,0:T(8,128)(2,1)S(1)}, u32[]{:S(2)}) copy-start(bf16[1,4,128,256]{3,2,1,0:T(8,128)(2,1)S(1)} %get-tuple-element.30) | copy-start | bytes 786436
  313.2 32.0 %collective-permute-start.23 = (bf16[4,128,256]{2,1,0:T(8,128)(2,1)S(1)}, bf16[4,128,256]{2,1,0:T(8,128)(2,1)S(1)}, u32[]{:S(2)}, u32[]{:S(2)}) collective-permute-start(bf16[4,128,256]{2,1,0:T(8,128)(2,1)S(1)} %get-tuple-element.31), channel_id=1, source_target_pairs={{0,12},{1,13},{2,14},{3,15},{4,0},{5,1},{6,2},{7,3},{8,4},{9,5},{1... | collective-permute-start | bytes 786440 | tf_op jit(solution)/shard_map/ppermute | solution.py:33
  317.2 32.4 %collective-permute-start.22 = (bf16[4,128,256]{2,1,0:T(8,128)(2,1)S(1)}, bf16[4,128,256]{2,1,0:T(8,128)(2,1)S(1)}, u32[]{:S(2)}, u32[]{:S(2)}) collective-permute-start(bf16[4,128,256]{2,1,0:T(8,128)(2,1)S(1)} %get-tuple-element.31), channel_id=1, source_target_pairs={{0,8},{1,9},{2,10},{3,11},{4,12},{5,13},{6,14},{7,15},{8,0},{9,1},... | collective-permute-start | bytes 786440 | tf_op jit(solution)/shard_map/ppermute | solution.py:33
  345.2 11.1 %copy-start.16 = (bf16[4,128,256]{2,1,0:T(8,128)(2,1)}, bf16[4,128,256]{2,1,0:T(8,128)(2,1)S(1)}, u32[]{:S(2)}) copy-start(bf16[4,128,256]{2,1,0:T(8,128)(2,1)S(1)} %collective-permute-done.23) | copy-start | bytes 786436
  345.2 9.1 %collective-permute-start.21 = (bf16[4,128,256]{2,1,0:T(8,128)(2,1)S(1)}, bf16[4,128,256]{2,1,0:T(8,128)(2,1)S(1)}, u32[]{:S(2)}, u32[]{:S(2)}) collective-permute-start(bf16[4,128,256]{2,1,0:T(8,128)(2,1)S(1)} %get-tuple-element.31), channel_id=1, source_target_pairs={{0,4},{1,5},{2,6},{3,7},{4,8},{5,9},{6,10},{7,11},{8,12},{9,13},{1... | collective-permute-start | bytes 786440 | tf_op jit(solution)/shard_map/ppermute | solution.py:33
  349.6 8.4 %copy-start.18 = (bf16[4,128,256]{2,1,0:T(8,128)(2,1)}, bf16[4,128,256]{2,1,0:T(8,128)(2,1)S(1)}, u32[]{:S(2)}) copy-start(bf16[4,128,256]{2,1,0:T(8,128)(2,1)S(1)} %collective-permute-done.22) | copy-start | bytes 786436
  354.2 3.8 copy-start.20
  355.3 0.9 copy-start.11
  356.2 0.9 copy-start.9
  357.1 0.9 copy-start.10
  364.5 1.2 copy-start.4
  369.5 19.8 %collective-permute-start.26 = (bf16[4,128,256]{1,2,0:T(8,128)(2,1)}, bf16[4,128,256]{1,2,0:T(8,128)(2,1)}, u32[]{:S(2)}, u32[]{:S(2)}) collective-permute-start(bf16[4,128,256]{1,2,0:T(8,128)(2,1)} %copy.58), channel_id=1, source_target_pairs={{0,4},{1,5},{2,6},{3,7},{4,8},{5,9},{6,10},{7,11},{8,12},{9,13},{1... | collective-permute-start | bytes 786440 | tf_op jit(solution)/shard_map/ppermute | solution.py:72
  374.4 14.9 %collective-permute-start.25 = (bf16[4,128,256]{1,2,0:T(8,128)(2,1)}, bf16[4,128,256]{1,2,0:T(8,128)(2,1)}, u32[]{:S(2)}, u32[]{:S(2)}) collective-permute-start(bf16[4,128,256]{1,2,0:T(8,128)(2,1)} %copy.57), channel_id=1, source_target_pairs={{0,8},{1,9},{2,10},{3,11},{4,12},{5,13},{6,14},{7,15},{8,0},{9,1},... | collective-permute-start | bytes 786440 | tf_op jit(solution)/shard_map/ppermute | solution.py:72
  379.6 10.4 %collective-permute-start.24 = (bf16[4,128,256]{1,2,0:T(8,128)(2,1)}, bf16[4,128,256]{1,2,0:T(8,128)(2,1)}, u32[]{:S(2)}, u32[]{:S(2)}) collective-permute-start(bf16[4,128,256]{1,2,0:T(8,128)(2,1)} %copy.56), channel_id=1, source_target_pairs={{0,12},{1,13},{2,14},{3,15},{4,0},{5,1},{6,2},{7,3},{8,4},{9,5},{1... | collective-permute-start | bytes 786440 | tf_op jit(solution)/shard_map/ppermute | solution.py:72
  392.4 35.3 %collective-permute-start.27 = (bf16[4,128,256]{1,2,0:T(8,128)(2,1)}, bf16[4,128,256]{1,2,0:T(8,128)(2,1)}, u32[]{:S(2)}, u32[]{:S(2)}) collective-permute-start(bf16[4,128,256]{1,2,0:T(8,128)(2,1)} %get-tuple-element.14), channel_id=1, source_target_pairs={{0,3},{1,0},{2,1},{3,2},{4,7},{5,4},{6,5},{7,6},{8,11},{9,8},{10,9... | collective-permute-start | bytes 786440 | tf_op jit(solution)/shard_map/ppermute | solution.py:76
  394.3 49.6 %collective-permute-start.28 = (bf16[4,128,256]{1,2,0:T(8,128)(2,1)}, bf16[4,128,256]{1,2,0:T(8,128)(2,1)}, u32[]{:S(2)}, u32[]{:S(2)}) collective-permute-start(bf16[4,128,256]{1,2,0:T(8,128)(2,1)} %get-tuple-element.13), channel_id=1, source_target_pairs={{0,2},{1,3},{2,0},{3,1},{4,6},{5,7},{6,4},{7,5},{8,10},{9,11},{10,... | collective-permute-start | bytes 786440 | tf_op jit(solution)/shard_map/ppermute | solution.py:76
  402.3 46.2 %collective-permute-start.29 = (bf16[4,128,256]{1,2,0:T(8,128)(2,1)}, bf16[4,128,256]{1,2,0:T(8,128)(2,1)}, u32[]{:S(2)}, u32[]{:S(2)}) collective-permute-start(bf16[4,128,256]{1,2,0:T(8,128)(2,1)} %get-tuple-element.12), channel_id=1, source_target_pairs={{0,1},{1,2},{2,3},{3,0},{4,5},{5,6},{6,7},{7,4},{8,9},{9,10},{10,1... | collective-permute-start | bytes 786440 | tf_op jit(solution)/shard_map/ppermute | solution.py:76
  410.3 40.8 %copy-start.26 = (f32[128]{0:T(128)S(1)}, f32[128]{0:T(128)}, u32[]{:S(2)}) copy-start(f32[128]{0:T(128)} %copy-done.25) | copy-start | bytes 1540
  451.1 1.2 copy-start.2
  451.1 1.2 copy-start.24
  452.3 5.1 %copy-start.3 = (bf16[4,4,128,512]{3,2,1,0:T(8,128)(2,1)S(1)}, bf16[4,4,128,512]{3,2,1,0:T(8,128)(2,1)}, u32[]{:S(2)}) copy-start(bf16[4,4,128,512]{3,2,1,0:T(8,128)(2,1)} %reshape.212) | copy-start | bytes 6291460
  452.3 5.1 %copy-start.6 = (bf16[1,4,128,256]{3,2,1,0:T(8,128)(2,1)S(1)}, bf16[1,4,128,256]{3,2,1,0:T(8,128)(2,1)}, u32[]{:S(2)}) copy-start(bf16[1,4,128,256]{3,2,1,0:T(8,128)(2,1)} %copy-done.5) | copy-start | bytes 786436
  452.3 5.1 %copy-start.13 = (bf16[1,4,128,256]{2,3,1,0:T(8,128)(2,1)S(1)}, bf16[1,4,128,256]{2,3,1,0:T(8,128)(2,1)}, u32[]{:S(2)}) copy-start(bf16[1,4,128,256]{2,3,1,0:T(8,128)(2,1)} %get-tuple-element.8) | copy-start | bytes 786436
  452.3 5.1 %copy-start.14 = (bf16[1,4,128,256]{2,3,1,0:T(8,128)(2,1)S(1)}, bf16[1,4,128,256]{2,3,1,0:T(8,128)(2,1)}, u32[]{:S(2)}) copy-start(bf16[1,4,128,256]{2,3,1,0:T(8,128)(2,1)} %slice_bitcast_fusion.9) | copy-start | bytes 786436
  452.3 5.1 %copy-start.15 = (bf16[1,4,128,256]{2,3,1,0:T(8,128)(2,1)S(1)}, bf16[1,4,128,256]{2,3,1,0:T(8,128)(2,1)}, u32[]{:S(2)}) copy-start(bf16[1,4,128,256]{2,3,1,0:T(8,128)(2,1)} %slice_bitcast_fusion.10) | copy-start | bytes 786436
  452.3 5.1 %copy-start.17 = (bf16[4,128,256]{2,1,0:T(8,128)(2,1)S(1)}, bf16[4,128,256]{2,1,0:T(8,128)(2,1)}, u32[]{:S(2)}) copy-start(bf16[4,128,256]{2,1,0:T(8,128)(2,1)} %copy-done.16) | copy-start | bytes 786436
  452.3 5.1 %copy-start.19 = (bf16[4,128,256]{2,1,0:T(8,128)(2,1)S(1)}, bf16[4,128,256]{2,1,0:T(8,128)(2,1)}, u32[]{:S(2)}) copy-start(bf16[4,128,256]{2,1,0:T(8,128)(2,1)} %copy-done.18) | copy-start | bytes 786436
  452.3 5.1 %copy-start.21 = (bf16[4,128,256]{2,1,0:T(8,128)(2,1)S(1)}, bf16[4,128,256]{2,1,0:T(8,128)(2,1)}, u32[]{:S(2)}) copy-start(bf16[4,128,256]{2,1,0:T(8,128)(2,1)} %copy-done.20) | copy-start | bytes 786436
  453.4 29.6 %collective-permute-start.30 = (bf16[128,4096]{0,1:T(8,128)(2,1)S(1)}, bf16[128,4096]{0,1:T(8,128)(2,1)S(1)}, u32[]{:S(2)}, u32[]{:S(2)}) collective-permute-start(bf16[128,4096]{0,1:T(8,128)(2,1)S(1)} %fusion.31), channel_id=1, source_target_pairs={{0,16},{16,32},{32,48},{48,64},{64,80},{80,96},{96,112},{112,128},... | collective-permute-start | bytes 3145736 | tf_op jit(solution)/shard_map/ppermute | solution.py:14
  457.5 24.7 %copy-start.12 = (bf16[1,256,768]{2,1,0:T(8,128)(2,1)S(1)}, bf16[1,256,768]{2,1,0:T(8,128)(2,1)}, u32[]{:S(2)}) copy-start(bf16[1,256,768]{2,1,0:T(8,128)(2,1)} %param.14) | copy-start | bytes 1179652
  458.5 23.7 %collective-permute-start.31 = (bf16[256,768]{1,0:T(8,128)(2,1)S(1)}, bf16[256,768]{1,0:T(8,128)(2,1)S(1)}, u32[]{:S(2)}, u32[]{:S(2)}) collective-permute-start(bf16[256,768]{1,0:T(8,128)(2,1)S(1)} %fusion.46), channel_id=1, source_target_pairs={{0,496},{16,480},{32,464},{48,448},{64,432},{80,416},{96,400},{112... | collective-permute-start | bytes 1179656 | tf_op jit(solution)/shard_map/ppermute | solution.py:19
Sparse Core Ops, SparseCore 0:
  11.0 147.3 all-gather.2

commit v6 on v4

--- a/solution.py
+++ b/solution.py
@@ -60,6 +60,30 @@
     gathered = jnp.stack([second[0][0]] + [s[:INNER] for s in second[1:]])
     scattered = jnp.stack([second[0][1 + o]] + [s[INNER:] for s in second[1:]])
     return gathered, scattered
+
+
+def reduce_and_gather(partial, own):
+    outer = lax.axis_size("seq") // INNER
+    n, w = partial.shape[2], partial.shape[3]
+    wire = own.dtype
+    pieces = own.reshape(n, -1, w).transpose(1, 0, 2)
+    acc = partial[0]
+    for k in range(1, outer):
+        acc = acc + lax.ppermute(partial[k].astype(wire), "seq", seq_pairs(outer - k, 1)).astype(acc.dtype)
+    total = acc[0]
+    rows = [pieces]
+    for k in range(1, INNER):
+        payload = jnp.concatenate([acc[INNER - k].astype(wire)[None], pieces])
+        got = lax.ppermute(payload, "seq", seq_pairs(k, 0))
+        total = total + got[0].astype(acc.dtype)
+        rows.append(got[1:])
+    reduced = total.astype(wire)
+    sums = jnp.stack([reduced] + [lax.ppermute(reduced, "seq", seq_pairs(k, 0)) for k in range(1, INNER)])
+    group = jnp.concatenate([jnp.stack(rows).reshape(-1, n, w), sums])
+    full = jnp.stack([group] + [lax.ppermute(group, "seq", seq_pairs(k, 1)) for k in range(1, outer)])
+    m = pieces.shape[0]
+    rows_all = full[:, : INNER * m].reshape(outer, INNER, m, n, w).transpose(0, 1, 3, 2, 4).reshape(outer, INNER, n, m * w)
+    return jnp.concatenate([rows_all, full[:, INNER * m :]], axis=-1)
 
 
 def gather_columns(y, o, i):
@@ -154,9 +178,7 @@
     key_part = jnp.einsum("tgj,tgh->jh", score_grad, query, preferred_element_type=jnp.float32)
     value_part = jnp.einsum("tgj,tgh->jh", weights, grad_heads, preferred_element_type=jnp.float32)
     kv_part = jnp.concatenate([key_part, value_part], axis=1).reshape(outer, INNER, count, 2 * HEAD)
-    query_all = gather_blocks(query_grad)
-    kv_grad = reduce_blocks(kv_part).astype(jnp.bfloat16)
-    grad_all = jnp.concatenate([query_all, gather_blocks(kv_grad)], axis=-1).reshape(size * count, -1)
+    grad_all = reduce_and_gather(kv_part, query_grad).reshape(size * count, -1)
     input_term = contract_first(hidden_cols, grad_all).astype(jnp.bfloat16)
     block = contract_last(grad_all, up_input_weight[0])
     hidden_grad = gather_columns(block.astype(jnp.bfloat16).reshape(outer, INNER, count, -1), o, i)

time: 469 us -> 481 us (1.026)
  the two profiles are of different devices: /device:TPU:64 before, /device:TPU:25 now
where the time goes in v6:
time: 481 us; the launch traced here: 476 us
  waiting for transfers between devices  256 us (53%)
  starting transfers between devices  118 us (25%)
  local copies, waits for them, and re-layouts  37.3 us (8%)
  matrix products  34.3 us (7%)
  other arithmetic  15.9 us (3%)
  between operations  14.9 us (3%)
    all_gather x1, waiting for transfers between devices, per_device(): lax.all_gather(up_output_weight[0], 'seq', axis=1, tiled=True)  72.7 us
    ppermute x3, waiting for transfers between devices, gather_and_scatter(): lax.ppermute(jnp.concatenate([x[None], piece]), 'seq', seq_pairs(k, 0))  52.6 us
    ppermute x3, waiting for transfers between devices, reduce_and_gather(): lax.ppermute(group, 'seq', seq_pairs(k, 1))  32.9 us
    ppermute x3, waiting for transfers between devices, reduce_and_gather(): got = lax.ppermute(payload, 'seq', seq_pairs(k, 0))  29.9 us
    ppermute x3, waiting for transfers between devices, gather_columns(): second.append(lax.ppermute(first[k], 'seq', seq_pairs(INNER - k, 0)))  26.4 us
    ppermute x3, starting transfers between devices, gather_and_scatter(): lax.ppermute(jnp.concatenate([x[None], piece]), 'seq', seq_pairs(k, 0))  24.6 us
    ppermute x3, waiting for transfers between devices, gather_and_scatter(): lax.ppermute(jnp.concatenate([first[0], piece]), 'seq', seq_pairs(k, 1))  17.8 us
    ppermute x3, starting transfers between devices, gather_columns(): second.append(lax.ppermute(first[k], 'seq', seq_pairs(INNER - k, 0)))  16.9 us
  transfers between devices with their start and end apart: 27, of which 18 were waited for; matrix products, arithmetic and copies ran while one was open for 10% of the time, Pallas kernels for 0%

profile of v6, /device:TPU:25, one launch (start us, length us, event | category | flops | bytes accessed | tf_op | source)
XLA Modules:
  0.0 476.2 jit_solution(698728251516120653)
XLA Ops:
  11.0 1.6 copy.37
  14.2 12.5 %collective-permute-start.2 = (bf16[5,128,256]{1,2,0:T(8,128)(2,1)S(1)}, bf16[5,128,256]{1,2,0:T(8,128)(2,1)S(1)}, u32[]{:S(2)}, u32[]{:S(2)}) collective-permute-start(bf16[5,128,256]{1,2,0:T(8,128)(2,1)S(1)} %get-tuple-element.49), channel_id=1, source_target_pairs={{0,3},{1,0},{2,1},{3,2},{4,7},{5,4},{6,5},{7,6},{8,11},{9,8},{10,9... | collective-permute-start | bytes 983048 | tf_op jit(solution)/shard_map/ppermute | solution.py:54
  26.6 4.9 %collective-permute-start.1 = (bf16[5,128,256]{1,2,0:T(8,128)(2,1)S(1)}, bf16[5,128,256]{1,2,0:T(8,128)(2,1)}, u32[]{:S(2)}, u32[]{:S(2)}) collective-permute-start(bf16[5,128,256]{1,2,0:T(8,128)(2,1)S(1)} %get-tuple-element.48), channel_id=1, source_target_pairs={{0,2},{1,3},{2,0},{3,1},{4,6},{5,7},{6,4},{7,5},{8,10},{9,11},{10,... | collective-permute-start | bytes 983048 | tf_op jit(solution)/shard_map/ppermute | solution.py:54
  31.6 7.3 %collective-permute-start = (bf16[5,128,256]{1,2,0:T(8,128)(2,1)S(1)}, bf16[5,128,256]{1,2,0:T(8,128)(2,1)}, u32[]{:S(2)}, u32[]{:S(2)}) collective-permute-start(bf16[5,128,256]{1,2,0:T(8,128)(2,1)S(1)} %get-tuple-element.47), channel_id=1, source_target_pairs={{0,1},{1,2},{2,3},{3,0},{4,5},{5,6},{6,7},{7,4},{8,9},{9,10},{10,1... | collective-permute-start | bytes 983048 | tf_op jit(solution)/shard_map/ppermute | solution.py:54
  39.1 52.6 %collective-permute-done.2 = bf16[5,128,256]{1,2,0:T(8,128)(2,1)S(1)} collective-permute-done((bf16[5,128,256]{1,2,0:T(8,128)(2,1)S(1)}, bf16[5,128,256]{1,2,0:T(8,128)(2,1)S(1)}, u32[]{:S(2)}, u32[]{:S(2)}) %collective-permute-start.2) | collective-permute-done | bytes 327712 | tf_op jit(solution)/shard_map/ppermute | solution.py:54
  94.0 4.4 collective-permute-start.5
  98.4 2.4 collective-permute-start.4
  100.8 2.5 collective-permute-start.3
  105.1 2.3 collective-permute-done.5
  108.1 1.8 collective-permute-done.4
  110.7 13.7 %collective-permute-done.3 = bf16[8,128,256]{1,2,0:T(8,128)(2,1)S(1)} collective-permute-done((bf16[8,128,256]{1,2,0:T(8,128)(2,1)S(1)}, bf16[8,128,256]{1,2,0:T(8,128)(2,1)S(1)}, u32[]{:S(2)}, u32[]{:S(2)}) %collective-permute-start.3) | collective-permute-done | bytes 524320 | tf_op jit(solution)/shard_map/ppermute | solution.py:59
  125.8 5.8 %fusion.94 = (f32[128,4]{0,1:T(4,128)}, f32[128,4,2048]{0,2,1:T(8,128)}) fusion(pred[128,2048]{0,1:T(8,128)(4,1)} %compare_and_fusion, bf16[128,4,128]{0,2,1:T(8,128)(2,1)} %bitcast.227, bf16[2048,256]{1,0:T(8,128)(2,1)S(1)} %bitcast.205), kind=kOutput, calls=%fused_computation.165 | convolution fusion | flops 273680384 | bytes 5376000 | tf_op jit(solution)/shard_map/sub | solution.py:166
  131.6 72.7 %all-gather.3.cloned.1.call-done = bf16[1,512,4096]{2,1,0:T(8,128)(2,1)} async-done(((bf16[1,512,256]{2,1,0:T(8,128)(2,1)}), bf16[1,512,4096]{2,1,0:T(8,128)(2,1)}) %all-gather.3.cloned.1.call-update) | async-done | bytes 4194320 | tf_op jit(solution)/shard_map/all_gather | solution.py:145
  204.3 4.4 fusion.44
  209.8 2.8 fusion.70
  213.4 1.7 convolution_bitcast_fusion
  215.2 7.3 %convolution_bitcast_fusion.1 = f32[2048,128]{0,1:T(8,128)S(1)} fusion(bf16[128,4,128]{0,2,1:T(8,128)(2,1)} %bitcast.228, f32[128,4,2048]{0,2,1:T(8,128)} %fusion.70, f32[128,4,2048]{0,2,1:T(8,128)} %get-tuple-element.51, f32[128,4]{0,1:T(4,128)} %get-tuple-element.50), kind=kOutput, calls=%fused_computation.26 | convolution fusion | flops 275778048 | bytes 9570304 | tf_op jit(solution)/shard_map/tgj,tgh->jh/dot_general | solution.py:178
  223.5 1.8 copy.78
  225.3 2.3 collective-permute-start.8
  227.6 1.8 copy.77
  229.4 4.1 collective-permute-start.7
  233.5 1.8 copy.76
  235.3 3.3 collective-permute-start.6
  238.6 8.0 %fusion.47 = bf16[128,4,128]{0,2,1:T(8,128)(2,1)} fusion(f32[128,4,2048]{0,2,1:T(8,128)} %fusion.70, bf16[2048,256]{1,0:T(8,128)(2,1)} %bitcast.207, f32[128,4,2048]{0,2,1:T(8,128)} %get-tuple-element.51, f32[128,4]{0,1:T(4,128)} %get-tuple-element.50), kind=kOutput, calls=%fused_computation.62 | convolution fusion | flops 275843584 | bytes 17436672 | tf_op jit(solution)/shard_map/tgj,jh->tgh/dot_general | solution.py:174
  246.6 1.6 copy.51
  251.7 7.4 %collective-permute-start.11 = (bf16[3,128,256]{2,1,0:T(8,128)(2,1)S(1)}, bf16[3,128,256]{2,1,0:T(8,128)(2,1)S(1)}, u32[]{:S(2)}, u32[]{:S(2)}) collective-permute-start(bf16[3,128,256]{2,1,0:T(8,128)(2,1)S(1)} %get-tuple-element.45), channel_id=1, source_target_pairs={{0,3},{1,0},{2,1},{3,2},{4,7},{5,4},{6,5},{7,6},{8,11},{9,8},{10,9... | collective-permute-start | bytes 589832 | tf_op jit(solution)/shard_map/ppermute | solution.py:77
  259.1 7.3 %collective-permute-start.10 = (bf16[3,128,256]{2,1,0:T(8,128)(2,1)S(1)}, bf16[3,128,256]{2,1,0:T(8,128)(2,1)S(1)}, u32[]{:S(2)}, u32[]{:S(2)}) collective-permute-start(bf16[3,128,256]{2,1,0:T(8,128)(2,1)S(1)} %get-tuple-element.44), channel_id=1, source_target_pairs={{0,2},{1,3},{2,0},{3,1},{4,6},{5,7},{6,4},{7,5},{8,10},{9,11},{10,... | collective-permute-start | bytes 589832 | tf_op jit(solution)/shard_map/ppermute | solution.py:77
  266.4 2.1 collective-permute-start.9
  268.5 5.7 %collective-permute-done.11 = bf16[3,128,256]{2,1,0:T(8,128)(2,1)S(1)} collective-permute-done((bf16[3,128,256]{2,1,0:T(8,128)(2,1)S(1)}, bf16[3,128,256]{2,1,0:T(8,128)(2,1)S(1)}, u32[]{:S(2)}, u32[]{:S(2)}) %collective-permute-start.11) | collective-permute-done | bytes 196640 | tf_op jit(solution)/shard_map/ppermute | solution.py:77
  274.2 15.8 %collective-permute-done.10 = bf16[3,128,256]{2,1,0:T(8,128)(2,1)S(1)} collective-permute-done((bf16[3,128,256]{2,1,0:T(8,128)(2,1)S(1)}, bf16[3,128,256]{2,1,0:T(8,128)(2,1)S(1)}, u32[]{:S(2)}, u32[]{:S(2)}) %collective-permute-start.10) | collective-permute-done | bytes 196640 | tf_op jit(solution)/shard_map/ppermute | solution.py:77
  290.0 8.5 %collective-permute-done.9 = bf16[3,128,256]{2,1,0:T(8,128)(2,1)S(1)} collective-permute-done((bf16[3,128,256]{2,1,0:T(8,128)(2,1)S(1)}, bf16[3,128,256]{2,1,0:T(8,128)(2,1)S(1)}, u32[]{:S(2)}, u32[]{:S(2)}) %collective-permute-start.9) | collective-permute-done | bytes 196640 | tf_op jit(solution)/shard_map/ppermute | solution.py:77
  298.6 4.9 %collective-permute-start.12 = (bf16[128,256]{1,0:T(8,128)(2,1)S(1)}, bf16[128,256]{1,0:T(8,128)(2,1)S(1)}, u32[]{:S(2)}, u32[]{:S(2)}) collective-permute-start(bf16[128,256]{1,0:T(8,128)(2,1)S(1)} %bitcast.231), channel_id=1, source_target_pairs={{0,1},{1,2},{2,3},{3,0},{4,5},{5,6},{6,7},{7,4},{8,9},{9,10},{10,1... | collective-permute-start | bytes 196616 | tf_op jit(solution)/shard_map/ppermute | solution.py:81
  303.6 4.5 collective-permute-start.13
  308.1 6.5 %collective-permute-start.14 = (bf16[128,256]{1,0:T(8,128)(2,1)S(1)}, bf16[128,256]{1,0:T(8,128)(2,1)S(1)}, u32[]{:S(2)}, u32[]{:S(2)}) collective-permute-start(bf16[128,256]{1,0:T(8,128)(2,1)S(1)} %bitcast.233), channel_id=1, source_target_pairs={{0,3},{1,0},{2,1},{3,2},{4,7},{5,4},{6,5},{7,6},{8,11},{9,8},{10,9... | collective-permute-start | bytes 196616 | tf_op jit(solution)/shard_map/ppermute | solution.py:81
  314.6 2.7 collective-permute-done.13
  317.3 2.2 collective-permute-start.17
  319.5 6.0 %collective-permute-start.16 = (bf16[12,128,256]{2,1,0:T(8,128)(2,1)S(1)}, bf16[12,128,256]{2,1,0:T(8,128)(2,1)S(1)}, u32[]{:S(2)}, u32[]{:S(2)}) collective-permute-start(bf16[12,128,256]{2,1,0:T(8,128)(2,1)S(1)} %bitcast_dynamic-update-slice_fusion), channel_id=1, source_target_pairs={{0,8},{1,9},{2,10},{3,11},{4,12},{5,13},{6,14},{7,15},{8,0},{9,1},... | collective-permute-start | bytes 2359304 | tf_op jit(solution)/shard_map/ppermute | solution.py:83
  325.5 1.9 collective-permute-start.15
  327.5 10.8 %collective-permute-done.17 = bf16[12,128,256]{2,1,0:T(8,128)(2,1)S(1)} collective-permute-done((bf16[12,128,256]{2,1,0:T(8,128)(2,1)S(1)}, bf16[12,128,256]{2,1,0:T(8,128)(2,1)S(1)}, u32[]{:S(2)}, u32[]{:S(2)}) %collective-permute-start.17) | collective-permute-done | bytes 786464 | tf_op jit(solution)/shard_map/ppermute | solution.py:83
  338.3 3.1 collective-permute-done.16
  341.4 19.0 %collective-permute-done.15 = bf16[12,128,256]{2,1,0:T(8,128)(2,1)S(1)} collective-permute-done((bf16[12,128,256]{2,1,0:T(8,128)(2,1)S(1)}, bf16[12,128,256]{2,1,0:T(8,128)(2,1)S(1)}, u32[]{:S(2)}, u32[]{:S(2)}) %collective-permute-start.15) | collective-permute-done | bytes 786464 | tf_op jit(solution)/shard_map/ppermute | solution.py:83
  361.1 2.2 copy.88
  365.8 1.8 copy.62
  367.6 2.3 collective-permute-start.20
  369.9 1.8 copy.61
  371.7 4.4 collective-permute-start.19
  376.1 1.8 copy.60
  377.9 4.0 collective-permute-start.18
  381.9 1.8 copy.63
  384.4 4.1 collective-permute-done.18
  390.8 4.5 collective-permute-start.21
  395.3 7.0 %collective-permute-start.22 = (bf16[4,128,256]{1,2,0:T(8,128)(2,1)}, bf16[4,128,256]{1,2,0:T(8,128)(2,1)}, u32[]{:S(2)}, u32[]{:S(2)}) collective-permute-start(bf16[4,128,256]{1,2,0:T(8,128)(2,1)} %get-tuple-element.14), channel_id=1, source_target_pairs={{0,2},{1,3},{2,0},{3,1},{4,6},{5,7},{6,4},{7,5},{8,10},{9,11},{10,... | collective-permute-start | bytes 786440 | tf_op jit(solution)/shard_map/ppermute | solution.py:98
  402.3 5.5 %collective-permute-start.23 = (bf16[4,128,256]{1,2,0:T(8,128)(2,1)}, bf16[4,128,256]{1,2,0:T(8,128)(2,1)}, u32[]{:S(2)}, u32[]{:S(2)}) collective-permute-start(bf16[4,128,256]{1,2,0:T(8,128)(2,1)} %get-tuple-element.13), channel_id=1, source_target_pairs={{0,1},{1,2},{2,3},{3,0},{4,5},{5,6},{6,7},{7,4},{8,9},{9,10},{10,1... | collective-permute-start | bytes 786440 | tf_op jit(solution)/shard_map/ppermute | solution.py:98
  407.8 2.3 copy.36
  410.1 3.8 collective-permute-done.21
  413.9 16.0 %collective-permute-done.22 = bf16[4,128,256]{1,2,0:T(8,128)(2,1)} collective-permute-done((bf16[4,128,256]{1,2,0:T(8,128)(2,1)}, bf16[4,128,256]{1,2,0:T(8,128)(2,1)}, u32[]{:S(2)}, u32[]{:S(2)}) %collective-permute-start.22) | collective-permute-done | bytes 262176 | tf_op jit(solution)/shard_map/ppermute | solution.py:98
  429.8 6.7 %collective-permute-done.23 = bf16[4,128,256]{1,2,0:T(8,128)(2,1)} collective-permute-done((bf16[4,128,256]{1,2,0:T(8,128)(2,1)}, bf16[4,128,256]{1,2,0:T(8,128)(2,1)}, u32[]{:S(2)}, u32[]{:S(2)}) %collective-permute-start.23) | collective-permute-done | bytes 262176 | tf_op jit(solution)/shard_map/ppermute | solution.py:98
  436.5 2.1 fusion.54
  440.3 1.8 fusion.26
  442.2 1.9 collective-permute-start.24
  444.1 2.6 reshape.224
  446.7 3.3 fusion.41
  450.0 1.9 collective-permute-start.25
  451.9 15.3 %collective-permute-done.25 = bf16[256,768]{1,0:T(8,128)(2,1)S(1)} collective-permute-done((bf16[256,768]{1,0:T(8,128)(2,1)S(1)}, bf16[256,768]{1,0:T(8,128)(2,1)S(1)}, u32[]{:S(2)}, u32[]{:S(2)}) %collective-permute-start.25) | collective-permute-done | bytes 393248 | tf_op jit(solution)/shard_map/ppermute | solution.py:19
  (99 shorter events, 28.9 us)
Async XLA Ops:
  7.2 356.6 %copy-start = (bf16[1,256,768]{2,1,0:T(8,128)(2,1)S(1)}, bf16[1,256,768]{2,1,0:T(8,128)(2,1)}, u32[]{:S(2)}) copy-start(bf16[1,256,768]{2,1,0:T(8,128)(2,1)} %param.11) | copy-start | bytes 1179652
  7.2 197.2 %all-gather.3.cloned.1.call-start = ((), (), s32[]{:S(2)}) async-start(), calls=%async_computation | async-start | bytes 4456448 | tf_op jit(solution)/shard_map/all_gather | solution.py:145
  13.2 0.8 copy-start.9
  14.2 77.5 %collective-permute-start.2 = (bf16[5,128,256]{1,2,0:T(8,128)(2,1)S(1)}, bf16[5,128,256]{1,2,0:T(8,128)(2,1)S(1)}, u32[]{:S(2)}, u32[]{:S(2)}) collective-permute-start(bf16[5,128,256]{1,2,0:T(8,128)(2,1)S(1)} %get-tuple-element.49), channel_id=1, source_target_pairs={{0,3},{1,0},{2,1},{3,2},{4,7},{5,4},{6,5},{7,6},{8,11},{9,8},{10,9... | collective-permute-start | bytes 983048 | tf_op jit(solution)/shard_map/ppermute | solution.py:54
  26.6 65.0 %collective-permute-start.1 = (bf16[5,128,256]{1,2,0:T(8,128)(2,1)S(1)}, bf16[5,128,256]{1,2,0:T(8,128)(2,1)}, u32[]{:S(2)}, u32[]{:S(2)}) collective-permute-start(bf16[5,128,256]{1,2,0:T(8,128)(2,1)S(1)} %get-tuple-element.48), channel_id=1, source_target_pairs={{0,2},{1,3},{2,0},{3,1},{4,6},{5,7},{6,4},{7,5},{8,10},{9,11},{10,... | collective-permute-start | bytes 983048 | tf_op jit(solution)/shard_map/ppermute | solution.py:54
  31.6 60.1 %collective-permute-start = (bf16[5,128,256]{1,2,0:T(8,128)(2,1)S(1)}, bf16[5,128,256]{1,2,0:T(8,128)(2,1)}, u32[]{:S(2)}, u32[]{:S(2)}) collective-permute-start(bf16[5,128,256]{1,2,0:T(8,128)(2,1)S(1)} %get-tuple-element.47), channel_id=1, source_target_pairs={{0,1},{1,2},{2,3},{3,0},{4,5},{5,6},{6,7},{7,4},{8,9},{9,10},{10,1... | collective-permute-start | bytes 983048 | tf_op jit(solution)/shard_map/ppermute | solution.py:54
  93.0 10.4 %copy-start.11 = (s32[1,128]{1,0:T(1,128)S(1)}, s32[1,128]{1,0:T(1,128)}, u32[]{:S(2)}) copy-start(s32[1,128]{1,0:T(1,128)} %param.15) | copy-start | bytes 1540
  94.0 13.4 %collective-permute-start.5 = (bf16[8,128,256]{1,2,0:T(8,128)(2,1)S(1)}, bf16[8,128,256]{1,2,0:T(8,128)(2,1)S(1)}, u32[]{:S(2)}, u32[]{:S(2)}) collective-permute-start(bf16[8,128,256]{1,2,0:T(8,128)(2,1)S(1)} %get-tuple-element.42), channel_id=1, source_target_pairs={{0,12},{1,13},{2,14},{3,15},{4,0},{5,1},{6,2},{7,3},{8,4},{9,5},{1... | collective-permute-start | bytes 1572872 | tf_op jit(solution)/shard_map/ppermute | solution.py:59
  98.4 11.5 %collective-permute-start.4 = (bf16[8,128,256]{1,2,0:T(8,128)(2,1)S(1)}, bf16[8,128,256]{1,2,0:T(8,128)(2,1)S(1)}, u32[]{:S(2)}, u32[]{:S(2)}) collective-permute-start(bf16[8,128,256]{1,2,0:T(8,128)(2,1)S(1)} %get-tuple-element.41), channel_id=1, source_target_pairs={{0,8},{1,9},{2,10},{3,11},{4,12},{5,13},{6,14},{7,15},{8,0},{9,1},... | collective-permute-start | bytes 1572872 | tf_op jit(solution)/shard_map/ppermute | solution.py:59
  100.8 23.5 %collective-permute-start.3 = (bf16[8,128,256]{1,2,0:T(8,128)(2,1)S(1)}, bf16[8,128,256]{1,2,0:T(8,128)(2,1)S(1)}, u32[]{:S(2)}, u32[]{:S(2)}) collective-permute-start(bf16[8,128,256]{1,2,0:T(8,128)(2,1)S(1)} %get-tuple-element.40), channel_id=1, source_target_pairs={{0,4},{1,5},{2,6},{3,7},{4,8},{5,9},{6,10},{7,11},{8,12},{9,13},{1... | collective-permute-start | bytes 1572872 | tf_op jit(solution)/shard_map/ppermute | solution.py:59
  125.8 84.0 %copy-start.3 = (bf16[4,4,128,256]{3,2,1,0:T(8,128)(2,1)}, bf16[4,4,128,256]{3,2,1,0:T(8,128)(2,1)S(1)}, u32[]{:S(2)}) copy-start(bf16[4,4,128,256]{3,2,1,0:T(8,128)(2,1)S(1)} %copy.44) | copy-start | bytes 3145732
  125.8 78.6 %copy-start.1 = (bf16[1,128,4096]{2,1,0:T(8,128)(2,1)S(1)}, bf16[1,128,4096]{2,1,0:T(8,128)(2,1)}, u32[]{:S(2)}) copy-start(bf16[1,128,4096]{2,1,0:T(8,128)(2,1)} %param.10) | copy-start | bytes 3145732
  209.7 2.8 copy-start.6
  209.8 3.7 copy-start.12
  209.8 3.7 copy-start.13
  225.3 25.0 %collective-permute-start.8 = (bf16[4,128,256]{2,1,0:T(8,128)(2,1)}, bf16[4,128,256]{2,1,0:T(8,128)(2,1)}, u32[]{:S(2)}, u32[]{:S(2)}) collective-permute-start(bf16[4,128,256]{2,1,0:T(8,128)(2,1)} %bitcast.224), channel_id=1, source_target_pairs={{0,4},{1,5},{2,6},{3,7},{4,8},{5,9},{6,10},{7,11},{8,12},{9,13},{1... | collective-permute-start | bytes 786440 | tf_op jit(solution)/shard_map/ppermute | solution.py:72
  229.4 20.9 %collective-permute-start.7 = (bf16[4,128,256]{2,1,0:T(8,128)(2,1)}, bf16[4,128,256]{2,1,0:T(8,128)(2,1)}, u32[]{:S(2)}, u32[]{:S(2)}) collective-permute-start(bf16[4,128,256]{2,1,0:T(8,128)(2,1)} %bitcast.225), channel_id=1, source_target_pairs={{0,8},{1,9},{2,10},{3,11},{4,12},{5,13},{6,14},{7,15},{8,0},{9,1},... | collective-permute-start | bytes 786440 | tf_op jit(solution)/shard_map/ppermute | solution.py:72
  235.3 15.0 %collective-permute-start.6 = (bf16[4,128,256]{2,1,0:T(8,128)(2,1)}, bf16[4,128,256]{2,1,0:T(8,128)(2,1)}, u32[]{:S(2)}, u32[]{:S(2)}) collective-permute-start(bf16[4,128,256]{2,1,0:T(8,128)(2,1)} %bitcast.226), channel_id=1, source_target_pairs={{0,12},{1,13},{2,14},{3,15},{4,0},{5,1},{6,2},{7,3},{8,4},{9,5},{1... | collective-permute-start | bytes 786440 | tf_op jit(solution)/shard_map/ppermute | solution.py:72
  249.1 2.6 copy-start.4
  251.7 22.5 %collective-permute-start.11 = (bf16[3,128,256]{2,1,0:T(8,128)(2,1)S(1)}, bf16[3,128,256]{2,1,0:T(8,128)(2,1)S(1)}, u32[]{:S(2)}, u32[]{:S(2)}) collective-permute-start(bf16[3,128,256]{2,1,0:T(8,128)(2,1)S(1)} %get-tuple-element.45), channel_id=1, source_target_pairs={{0,3},{1,0},{2,1},{3,2},{4,7},{5,4},{6,5},{7,6},{8,11},{9,8},{10,9... | collective-permute-start | bytes 589832 | tf_op jit(solution)/shard_map/ppermute | solution.py:77
  259.1 30.9 %collective-permute-start.10 = (bf16[3,128,256]{2,1,0:T(8,128)(2,1)S(1)}, bf16[3,128,256]{2,1,0:T(8,128)(2,1)S(1)}, u32[]{:S(2)}, u32[]{:S(2)}) collective-permute-start(bf16[3,128,256]{2,1,0:T(8,128)(2,1)S(1)} %get-tuple-element.44), channel_id=1, source_target_pairs={{0,2},{1,3},{2,0},{3,1},{4,6},{5,7},{6,4},{7,5},{8,10},{9,11},{10,... | collective-permute-start | bytes 589832 | tf_op jit(solution)/shard_map/ppermute | solution.py:77
  266.4 32.1 %collective-permute-start.9 = (bf16[3,128,256]{2,1,0:T(8,128)(2,1)S(1)}, bf16[3,128,256]{2,1,0:T(8,128)(2,1)S(1)}, u32[]{:S(2)}, u32[]{:S(2)}) collective-permute-start(bf16[3,128,256]{2,1,0:T(8,128)(2,1)S(1)} %get-tuple-element.43), channel_id=1, source_target_pairs={{0,1},{1,2},{2,3},{3,0},{4,5},{5,6},{6,7},{7,4},{8,9},{9,10},{10,1... | collective-permute-start | bytes 589832 | tf_op jit(solution)/shard_map/ppermute | solution.py:77
  298.6 16.0 %collective-permute-start.12 = (bf16[128,256]{1,0:T(8,128)(2,1)S(1)}, bf16[128,256]{1,0:T(8,128)(2,1)S(1)}, u32[]{:S(2)}, u32[]{:S(2)}) collective-permute-start(bf16[128,256]{1,0:T(8,128)(2,1)S(1)} %bitcast.231), channel_id=1, source_target_pairs={{0,1},{1,2},{2,3},{3,0},{4,5},{5,6},{6,7},{7,4},{8,9},{9,10},{10,1... | collective-permute-start | bytes 196616 | tf_op jit(solution)/shard_map/ppermute | solution.py:81
  303.6 13.7 %collective-permute-start.13 = (bf16[128,256]{1,0:T(8,128)(2,1)S(1)}, bf16[128,256]{1,0:T(8,128)(2,1)S(1)}, u32[]{:S(2)}, u32[]{:S(2)}) collective-permute-start(bf16[128,256]{1,0:T(8,128)(2,1)S(1)} %bitcast.232), channel_id=1, source_target_pairs={{0,2},{1,3},{2,0},{3,1},{4,6},{5,7},{6,4},{7,5},{8,10},{9,11},{10,... | collective-permute-start | bytes 196616 | tf_op jit(solution)/shard_map/ppermute | solution.py:81
  308.1 9.3 %collective-permute-start.14 = (bf16[128,256]{1,0:T(8,128)(2,1)S(1)}, bf16[128,256]{1,0:T(8,128)(2,1)S(1)}, u32[]{:S(2)}, u32[]{:S(2)}) collective-permute-start(bf16[128,256]{1,0:T(8,128)(2,1)S(1)} %bitcast.233), channel_id=1, source_target_pairs={{0,3},{1,0},{2,1},{3,2},{4,7},{5,4},{6,5},{7,6},{8,11},{9,8},{10,9... | collective-permute-start | bytes 196616 | tf_op jit(solution)/shard_map/ppermute | solution.py:81
  317.3 20.9 %collective-permute-start.17 = (bf16[12,128,256]{2,1,0:T(8,128)(2,1)S(1)}, bf16[12,128,256]{2,1,0:T(8,128)(2,1)S(1)}, u32[]{:S(2)}, u32[]{:S(2)}) collective-permute-start(bf16[12,128,256]{2,1,0:T(8,128)(2,1)S(1)} %bitcast_dynamic-update-slice_fusion), channel_id=1, source_target_pairs={{0,12},{1,13},{2,14},{3,15},{4,0},{5,1},{6,2},{7,3},{8,4},{9,5},{1... | collective-permute-start | bytes 2359304 | tf_op jit(solution)/shard_map/ppermute | solution.py:83
  319.5 21.9 %collective-permute-start.16 = (bf16[12,128,256]{2,1,0:T(8,128)(2,1)S(1)}, bf16[12,128,256]{2,1,0:T(8,128)(2,1)S(1)}, u32[]{:S(2)}, u32[]{:S(2)}) collective-permute-start(bf16[12,128,256]{2,1,0:T(8,128)(2,1)S(1)} %bitcast_dynamic-update-slice_fusion), channel_id=1, source_target_pairs={{0,8},{1,9},{2,10},{3,11},{4,12},{5,13},{6,14},{7,15},{8,0},{9,1},... | collective-permute-start | bytes 2359304 | tf_op jit(solution)/shard_map/ppermute | solution.py:83
  325.5 34.8 %collective-permute-start.15 = (bf16[12,128,256]{2,1,0:T(8,128)(2,1)S(1)}, bf16[12,128,256]{2,1,0:T(8,128)(2,1)S(1)}, u32[]{:S(2)}, u32[]{:S(2)}) collective-permute-start(bf16[12,128,256]{2,1,0:T(8,128)(2,1)S(1)} %bitcast_dynamic-update-slice_fusion), channel_id=1, source_target_pairs={{0,4},{1,5},{2,6},{3,7},{4,8},{5,9},{6,10},{7,11},{8,12},{9,13},{1... | collective-permute-start | bytes 2359304 | tf_op jit(solution)/shard_map/ppermute | solution.py:83
  360.5 3.2 copy-start.5
  367.6 16.1 %collective-permute-start.20 = (bf16[4,128,256]{1,2,0:T(8,128)(2,1)}, bf16[4,128,256]{1,2,0:T(8,128)(2,1)}, u32[]{:S(2)}, u32[]{:S(2)}) collective-permute-start(bf16[4,128,256]{1,2,0:T(8,128)(2,1)} %copy.62), channel_id=1, source_target_pairs={{0,4},{1,5},{2,6},{3,7},{4,8},{5,9},{6,10},{7,11},{8,12},{9,13},{1... | collective-permute-start | bytes 786440 | tf_op jit(solution)/shard_map/ppermute | solution.py:94
  371.7 12.7 %collective-permute-start.19 = (bf16[4,128,256]{1,2,0:T(8,128)(2,1)}, bf16[4,128,256]{1,2,0:T(8,128)(2,1)}, u32[]{:S(2)}, u32[]{:S(2)}) collective-permute-start(bf16[4,128,256]{1,2,0:T(8,128)(2,1)} %copy.61), channel_id=1, source_target_pairs={{0,8},{1,9},{2,10},{3,11},{4,12},{5,13},{6,14},{7,15},{8,0},{9,1},... | collective-permute-start | bytes 786440 | tf_op jit(solution)/shard_map/ppermute | solution.py:94
  377.9 10.6 %collective-permute-start.18 = (bf16[4,128,256]{1,2,0:T(8,128)(2,1)}, bf16[4,128,256]{1,2,0:T(8,128)(2,1)}, u32[]{:S(2)}, u32[]{:S(2)}) collective-permute-start(bf16[4,128,256]{1,2,0:T(8,128)(2,1)} %copy.60), channel_id=1, source_target_pairs={{0,12},{1,13},{2,14},{3,15},{4,0},{5,1},{6,2},{7,3},{8,4},{9,5},{1... | collective-permute-start | bytes 786440 | tf_op jit(solution)/shard_map/ppermute | solution.py:94
  390.8 23.0 %collective-permute-start.21 = (bf16[4,128,256]{1,2,0:T(8,128)(2,1)}, bf16[4,128,256]{1,2,0:T(8,128)(2,1)}, u32[]{:S(2)}, u32[]{:S(2)}) collective-permute-start(bf16[4,128,256]{1,2,0:T(8,128)(2,1)} %get-tuple-element.15), channel_id=1, source_target_pairs={{0,3},{1,0},{2,1},{3,2},{4,7},{5,4},{6,5},{7,6},{8,11},{9,8},{10,9... | collective-permute-start | bytes 786440 | tf_op jit(solution)/shard_map/ppermute | solution.py:98
  395.3 34.5 %collective-permute-start.22 = (bf16[4,128,256]{1,2,0:T(8,128)(2,1)}, bf16[4,128,256]{1,2,0:T(8,128)(2,1)}, u32[]{:S(2)}, u32[]{:S(2)}) collective-permute-start(bf16[4,128,256]{1,2,0:T(8,128)(2,1)} %get-tuple-element.14), channel_id=1, source_target_pairs={{0,2},{1,3},{2,0},{3,1},{4,6},{5,7},{6,4},{7,5},{8,10},{9,11},{10,... | collective-permute-start | bytes 786440 | tf_op jit(solution)/shard_map/ppermute | solution.py:98
  402.3 34.3 %collective-permute-start.23 = (bf16[4,128,256]{1,2,0:T(8,128)(2,1)}, bf16[4,128,256]{1,2,0:T(8,128)(2,1)}, u32[]{:S(2)}, u32[]{:S(2)}) collective-permute-start(bf16[4,128,256]{1,2,0:T(8,128)(2,1)} %get-tuple-element.13), channel_id=1, source_target_pairs={{0,1},{1,2},{2,3},{3,0},{4,5},{5,6},{6,7},{7,4},{8,9},{9,10},{10,1... | collective-permute-start | bytes 786440 | tf_op jit(solution)/shard_map/ppermute | solution.py:98
  410.1 29.0 %copy-start.10 = (f32[128]{0:T(128)S(1)}, f32[128]{0:T(128)}, u32[]{:S(2)}) copy-start(f32[128]{0:T(128)} %copy-done.9) | copy-start | bytes 1540
  439.1 1.2 copy-start.2
  439.1 1.2 copy-start.8
  442.2 25.9 %collective-permute-start.24 = (bf16[128,4096]{0,1:T(8,128)(2,1)}, bf16[128,4096]{0,1:T(8,128)(2,1)S(1)}, u32[]{:S(2)}, u32[]{:S(2)}) collective-permute-start(bf16[128,4096]{0,1:T(8,128)(2,1)} %fusion.26), channel_id=1, source_target_pairs={{0,16},{16,32},{32,48},{48,64},{64,80},{80,96},{96,112},{112,128},... | collective-permute-start | bytes 3145736 | tf_op jit(solution)/shard_map/ppermute | solution.py:14
  446.7 20.5 %copy-start.7 = (bf16[1,256,768]{2,1,0:T(8,128)(2,1)S(1)}, bf16[1,256,768]{2,1,0:T(8,128)(2,1)}, u32[]{:S(2)}) copy-start(bf16[1,256,768]{2,1,0:T(8,128)(2,1)} %param.14) | copy-start | bytes 1179652
  450.0 17.2 %collective-permute-start.25 = (bf16[256,768]{1,0:T(8,128)(2,1)S(1)}, bf16[256,768]{1,0:T(8,128)(2,1)S(1)}, u32[]{:S(2)}, u32[]{:S(2)}) collective-permute-start(bf16[256,768]{1,0:T(8,128)(2,1)S(1)} %fusion.41), channel_id=1, source_target_pairs={{0,496},{16,480},{32,464},{48,448},{64,432},{80,416},{96,400},{112... | collective-permute-start | bytes 1179656 | tf_op jit(solution)/shard_map/ppermute | solution.py:19
Sparse Core Ops, SparseCore 0:
  11.0 193.2 all-gather.2

commit v7 on v5

--- a/solution.py
+++ b/solution.py
@@ -33,14 +33,14 @@
     return jnp.stack([first] + [lax.ppermute(first, "seq", seq_pairs(k, 1)) for k in range(1, outer)])
 
 
-def reduce_blocks(y):
+def reduce_blocks(y, wire):
     outer = lax.axis_size("seq") // INNER
     acc = y[0]
     for k in range(1, outer):
-        acc = acc + lax.ppermute(y[k], "seq", seq_pairs(outer - k, 1))
+        acc = acc + lax.ppermute(y[k].astype(wire), "seq", seq_pairs(outer - k, 1)).astype(y.dtype)
     total = acc[0]
     for k in range(1, INNER):
-        total = total + lax.ppermute(acc[k], "seq", seq_pairs(INNER - k, 0))
+        total = total + lax.ppermute(acc[k].astype(wire), "seq", seq_pairs(INNER - k, 0)).astype(y.dtype)
     return total
 
 
@@ -121,7 +121,18 @@
     unit_up, inverse_up, normed_up = normalize(up_activation[0], upward_gain[0])
     hidden = normed_up.astype(jnp.bfloat16)
     output_weight = lax.all_gather(up_output_weight[0], "seq", axis=1, tiled=True)
-    key_value = gather_blocks(saved[:, width:]).reshape(size * count, 2 * HEAD)
+    pieces = hidden.shape[1] // size
+    kv_weight = up_input_weight[0][:, width:]
+    riders = jnp.concatenate(
+        [saved[None, :, width:], kv_weight.reshape(-1, count, pieces)]
+    )
+    gathered, hidden_cols = gather_and_scatter(riders, hidden, o, i)
+    key_value = gathered[:, 0].reshape(size * count, 2 * HEAD)
+    hidden_cols = hidden_cols.reshape(size * count, -1)
+    kv_weight_all = gathered[:, 1:].transpose(0, 2, 1, 3, 4)
+    kv_weight_all = jnp.take(kv_weight_all, (o - jnp.arange(outer)) % outer, axis=0)
+    kv_weight_all = jnp.take(kv_weight_all, (i - jnp.arange(INNER)) % INNER, axis=1)
+    kv_weight_all = kv_weight_all.reshape(-1, 2 * HEAD)
     keys = key_value[:, :HEAD]
     values = key_value[:, HEAD:]
     sources = (
@@ -154,18 +165,13 @@
     key_part = jnp.einsum("tgj,tgh->jh", score_grad, query, preferred_element_type=jnp.float32)
     value_part = jnp.einsum("tgj,tgh->jh", weights, grad_heads, preferred_element_type=jnp.float32)
     kv_part = jnp.concatenate([key_part, value_part], axis=1).reshape(outer, INNER, count, 2 * HEAD)
-    pieces = hidden.shape[1] // size
-    query_all, hidden_cols = gather_and_scatter(
-        query_grad.reshape(count, width // pieces, pieces).transpose(1, 0, 2), hidden, o, i
-    )
-    query_all = query_all.transpose(0, 2, 3, 1, 4).reshape(outer, INNER, count, width)
-    hidden_cols = hidden_cols.reshape(size * count, -1)
-    kv_grad = reduce_blocks(kv_part).astype(jnp.bfloat16)
+    query_all = gather_blocks(query_grad)
+    kv_grad = reduce_blocks(kv_part, jnp.bfloat16).astype(jnp.bfloat16)
     grad_all = jnp.concatenate([query_all, gather_blocks(kv_grad)], axis=-1).reshape(size * count, -1)
     input_term = contract_first(hidden_cols, grad_all).astype(jnp.bfloat16)
-    block = contract_last(grad_all, up_input_weight[0])
+    block = contract_last(query_all.reshape(size * count, -1), up_input_weight[0][:, :width])
     hidden_grad = gather_columns(block.astype(jnp.bfloat16).reshape(outer, INNER, count, -1), o, i)
-    hidden_grad = hidden_grad.astype(jnp.float32)
+    hidden_grad = hidden_grad.astype(jnp.float32) + contract_last(kv_grad, kv_weight_all)
     scaled = hidden_grad * upward_gain[0]
     input_grad = cotangent.astype(jnp.float32) + inverse_up * (
         scaled - unit_up * jnp.mean(scaled * unit_up, axis=-1, keepdims=True)

time: 500 us -> 466 us (0.932)
  the two profiles are of different devices: /device:TPU:25 before, /device:TPU:192 now
where the time goes in v7:
time: 466 us; the launch traced here: 464 us
  waiting for transfers between devices  201 us (43%)
  starting transfers between devices  145 us (31%)
  local copies, waits for them, and re-layouts  45.3 us (10%)
  matrix products  33 us (7%)
  other arithmetic  24.9 us (5%)
  between operations  15.2 us (3%)
    ppermute x3, waiting for transfers between devices, gather_and_scatter(): lax.ppermute(jnp.concatenate([x, piece]), 'seq', seq_pairs(k, 0))  92.1 us
    ppermute x3, waiting for transfers between devices, gather_and_scatter(): second.append(lax.ppermute(payload, 'seq', seq_pairs(k, 1)))  55.1 us
    ppermute x6, starting transfers between devices, gather_blocks(): lax.ppermute(x, 'seq', seq_pairs(k, 0))  30.4 us
    ppermute x3, waiting for transfers between devices, gather_columns(): second.append(lax.ppermute(first[k], 'seq', seq_pairs(INNER - k, 0)))  26.6 us
    ppermute x1, waiting for transfers between devices, mirrored(): lax.ppermute(value, axis, [(source, count - 1 - source) for source in ran...  24.3 us
    ppermute x6, starting transfers between devices, gather_blocks(): lax.ppermute(first, 'seq', seq_pairs(k, 1))  20.3 us
    ppermute x3, starting transfers between devices, gather_and_scatter(): lax.ppermute(jnp.concatenate([x, piece]), 'seq', seq_pairs(k, 0))  18.9 us
    ppermute x3, starting transfers between devices, gather_columns(): second.append(lax.ppermute(first[k], 'seq', seq_pairs(INNER - k, 0)))  18.1 us
  transfers between devices with their start and end apart: 33, of which 9 were waited for; matrix products, arithmetic and copies ran while one was open for 17% of the time, Pallas kernels for 0%

profile of v7, /device:TPU:192, one launch (start us, length us, event | category | flops | bytes accessed | tf_op | source)
XLA Modules:
  0.0 464.3 jit_solution(10213519995541179168)
XLA Ops:
  12.1 2.7 reshape.308
  14.8 2.0 copy.39
  19.1 7.3 %collective-permute-start = (bf16[7,128,256]{1,2,0:T(8,128)(2,1)}, bf16[7,128,256]{1,2,0:T(8,128)(2,1)S(1)}, u32[]{:S(2)}, u32[]{:S(2)}) collective-permute-start(bf16[7,128,256]{1,2,0:T(8,128)(2,1)} %get-tuple-element.34), channel_id=1, source_target_pairs={{0,1},{1,2},{2,3},{3,0},{4,5},{5,6},{6,7},{7,4},{8,9},{9,10},{10,1... | collective-permute-start | bytes 1376264 | tf_op jit(solution)/shard_map/ppermute | solution.py:54
  26.4 3.7 collective-permute-start.1
  30.2 7.8 %collective-permute-start.2 = (bf16[7,128,256]{1,2,0:T(8,128)(2,1)}, bf16[7,128,256]{1,2,0:T(8,128)(2,1)S(1)}, u32[]{:S(2)}, u32[]{:S(2)}) collective-permute-start(bf16[7,128,256]{1,2,0:T(8,128)(2,1)} %get-tuple-element.36), channel_id=1, source_target_pairs={{0,3},{1,0},{2,1},{3,2},{4,7},{5,4},{6,5},{7,6},{8,11},{9,8},{10,9... | collective-permute-start | bytes 1376264 | tf_op jit(solution)/shard_map/ppermute | solution.py:54
  38.8 54.9 %collective-permute-done = bf16[7,128,256]{1,2,0:T(8,128)(2,1)S(1)} collective-permute-done((bf16[7,128,256]{1,2,0:T(8,128)(2,1)}, bf16[7,128,256]{1,2,0:T(8,128)(2,1)S(1)}, u32[]{:S(2)}, u32[]{:S(2)}) %collective-permute-start) | collective-permute-done | bytes 458784 | tf_op jit(solution)/shard_map/ppermute | solution.py:54
  93.7 31.0 %collective-permute-done.1 = bf16[7,128,256]{1,2,0:T(8,128)(2,1)S(1)} collective-permute-done((bf16[7,128,256]{1,2,0:T(8,128)(2,1)}, bf16[7,128,256]{1,2,0:T(8,128)(2,1)S(1)}, u32[]{:S(2)}, u32[]{:S(2)}) %collective-permute-start.1) | collective-permute-done | bytes 458784 | tf_op jit(solution)/shard_map/ppermute | solution.py:54
  124.7 6.2 %collective-permute-done.2 = bf16[7,128,256]{1,2,0:T(8,128)(2,1)S(1)} collective-permute-done((bf16[7,128,256]{1,2,0:T(8,128)(2,1)}, bf16[7,128,256]{1,2,0:T(8,128)(2,1)S(1)}, u32[]{:S(2)}, u32[]{:S(2)}) %collective-permute-start.2) | collective-permute-done | bytes 458784 | tf_op jit(solution)/shard_map/ppermute | solution.py:54
  131.9 1.9 pad_maximum_fusion.7
  133.8 3.1 collective-permute-start.3
  136.9 4.7 %collective-permute-start.4 = (bf16[16,128,256]{1,2,0:T(8,128)(2,1)}, bf16[16,128,256]{1,2,0:T(8,128)(2,1)}, u32[]{:S(2)}, u32[]{:S(2)}) collective-permute-start(bf16[16,128,256]{1,2,0:T(8,128)(2,1)} %get-tuple-element.24), channel_id=1, source_target_pairs={{0,8},{1,9},{2,10},{3,11},{4,12},{5,13},{6,14},{7,15},{8,0},{9,1},... | collective-permute-start | bytes 3145736 | tf_op jit(solution)/shard_map/ppermute | solution.py:61
  141.6 3.5 collective-permute-start.5
  146.0 26.5 %collective-permute-done.3 = bf16[16,128,256]{1,2,0:T(8,128)(2,1)} collective-permute-done((bf16[16,128,256]{1,2,0:T(8,128)(2,1)}, bf16[16,128,256]{1,2,0:T(8,128)(2,1)}, u32[]{:S(2)}, u32[]{:S(2)}) %collective-permute-start.3) | collective-permute-done | bytes 1048608 | tf_op jit(solution)/shard_map/ppermute | solution.py:61
  173.7 28.6 %collective-permute-done.4 = bf16[16,128,256]{1,2,0:T(8,128)(2,1)} collective-permute-done((bf16[16,128,256]{1,2,0:T(8,128)(2,1)}, bf16[16,128,256]{1,2,0:T(8,128)(2,1)}, u32[]{:S(2)}, u32[]{:S(2)}) %collective-permute-start.4) | collective-permute-done | bytes 1048608 | tf_op jit(solution)/shard_map/ppermute | solution.py:61
  207.5 2.5 gather_fusion
  210.1 2.3 broadcast_select_fusion
  212.3 3.8 gather_fusion.1
  216.1 2.8 copy.70
  218.9 2.3 pad_maximum_fusion.8
  221.2 2.3 copy.48
  223.5 4.8 %fusion.95 = (f32[128,4]{0,1:T(4,128)S(1)}, f32[128,4,2048]{0,2,1:T(8,128)}) fusion(pred[128,2048]{0,1:T(8,128)(4,1)S(1)} %compare_and_fusion, bf16[128,4,128]{0,2,1:T(8,128)(2,1)S(1)} %bitcast.238, bf16[2048,256]{1,0:T(8,128)(2,1)} %bitcast.211), kind=kOutput, calls=%fused_computation.183 | convolution fusion | flops 273680384 | bytes 5376000 | tf_op jit(solution)/shard_map/sub | solution.py:153
  228.3 1.8 bitcast_select_fusion.2
  230.1 4.1 fusion.43
  234.4 2.8 fusion.69
  238.7 7.2 %fusion.46 = bf16[128,4,128]{0,2,1:T(8,128)(2,1)S(1)} fusion(f32[128,4,2048]{0,2,1:T(8,128)} %fusion.69, bf16[2048,256]{1,0:T(8,128)(2,1)S(1)} %bitcast.213, f32[128,4,2048]{0,2,1:T(8,128)} %get-tuple-element.38, f32[128,4]{0,1:T(4,128)S(1)} %get-tuple-element.37), kind=kOutput, calls=%fused_computation.70 | convolution fusion | flops 275843584 | bytes 17436672 | tf_op jit(solution)/shard_map/tgj,jh->tgh/dot_general | solution.py:161
  246.0 7.3 %convolution_bitcast_fusion.1 = f32[2048,128]{0,1:T(8,128)S(1)} fusion(bf16[128,4,128]{0,2,1:T(8,128)(2,1)S(1)} %bitcast.239, f32[128,4,2048]{0,2,1:T(8,128)} %fusion.69, f32[128,4,2048]{0,2,1:T(8,128)} %get-tuple-element.38, f32[128,4]{0,1:T(4,128)S(1)} %get-tuple-element.37), kind=kOutput, calls=%fused_computation.35 | convolution fusion | flops 275778048 | bytes 9570304 | tf_op jit(solution)/shard_map/tgj,tgh->jh/dot_general | solution.py:165
  254.0 3.2 collective-permute-start.8
  257.2 7.4 %collective-permute-start.7 = (bf16[128,512]{1,0:T(8,128)(2,1)}, bf16[128,512]{1,0:T(8,128)(2,1)}, u32[]{:S(2)}, u32[]{:S(2)}) collective-permute-start(bf16[128,512]{1,0:T(8,128)(2,1)} %copy.55), channel_id=1, source_target_pairs={{0,2},{1,3},{2,0},{3,1},{4,6},{5,7},{6,4},{7,5},{8,10},{9,11},{10,... | collective-permute-start | bytes 393224 | tf_op jit(solution)/shard_map/ppermute | solution.py:32
  264.6 3.9 collective-permute-start.6
  269.6 1.8 copy.80
  271.4 1.8 copy.82
  274.0 4.1 collective-permute-start.19
  278.2 1.9 collective-permute-start.20
  280.1 5.1 %collective-permute-start.18 = (bf16[4,128,256]{2,1,0:T(8,128)(2,1)}, bf16[4,128,256]{2,1,0:T(8,128)(2,1)}, u32[]{:S(2)}, u32[]{:S(2)}) collective-permute-start(bf16[4,128,256]{2,1,0:T(8,128)(2,1)} %bitcast.229), channel_id=1, source_target_pairs={{0,12},{1,13},{2,14},{3,15},{4,0},{5,1},{6,2},{7,3},{8,4},{9,5},{1... | collective-permute-start | bytes 786440 | tf_op jit(solution)/shard_map/ppermute | solution.py:40
  287.1 1.8 collective-permute-done.6
  288.9 2.1 fusion.91
  291.0 5.0 %collective-permute-start.10 = (bf16[4,128,512]{2,1,0:T(8,128)(2,1)}, bf16[4,128,512]{2,1,0:T(8,128)(2,1)}, u32[]{:S(2)}, u32[]{:S(2)}) collective-permute-start(bf16[4,128,512]{2,1,0:T(8,128)(2,1)} %get-tuple-element.27), channel_id=1, source_target_pairs={{0,8},{1,9},{2,10},{3,11},{4,12},{5,13},{6,14},{7,15},{8,0},{9,1},... | collective-permute-start | bytes 1572872 | tf_op jit(solution)/shard_map/ppermute | solution.py:33
  296.0 1.9 collective-permute-start.9
  298.0 5.1 %collective-permute-start.11 = (bf16[4,128,512]{2,1,0:T(8,128)(2,1)}, bf16[4,128,512]{2,1,0:T(8,128)(2,1)}, u32[]{:S(2)}, u32[]{:S(2)}) collective-permute-start(bf16[4,128,512]{2,1,0:T(8,128)(2,1)} %get-tuple-element.27), channel_id=1, source_target_pairs={{0,12},{1,13},{2,14},{3,15},{4,0},{5,1},{6,2},{7,3},{8,4},{9,5},{1... | collective-permute-start | bytes 1572872 | tf_op jit(solution)/shard_map/ppermute | solution.py:33
  306.6 2.5 collective-permute-start.21
  309.0 7.3 %collective-permute-start.23 = (bf16[128,256]{1,0:T(8,128)(2,1)S(1)}, bf16[128,256]{1,0:T(8,128)(2,1)S(1)}, u32[]{:S(2)}, u32[]{:S(2)}) collective-permute-start(bf16[128,256]{1,0:T(8,128)(2,1)S(1)} %get-tuple-element.31), channel_id=1, source_target_pairs={{0,1},{1,2},{2,3},{3,0},{4,5},{5,6},{6,7},{7,4},{8,9},{9,10},{10,1... | collective-permute-start | bytes 196616 | tf_op jit(solution)/shard_map/ppermute | solution.py:43
  316.3 7.8 %collective-permute-start.22 = (bf16[128,256]{1,0:T(8,128)(2,1)S(1)}, bf16[128,256]{1,0:T(8,128)(2,1)S(1)}, u32[]{:S(2)}, u32[]{:S(2)}) collective-permute-start(bf16[128,256]{1,0:T(8,128)(2,1)S(1)} %get-tuple-element.32), channel_id=1, source_target_pairs={{0,2},{1,3},{2,0},{3,1},{4,6},{5,7},{6,4},{7,5},{8,10},{9,11},{10,... | collective-permute-start | bytes 196616 | tf_op jit(solution)/shard_map/ppermute | solution.py:43
  326.7 1.9 collective-permute-start.14
  328.6 5.4 %collective-permute-start.13 = (bf16[4,128,256]{2,1,0:T(8,128)(2,1)S(1)}, bf16[4,128,256]{2,1,0:T(8,128)(2,1)S(1)}, u32[]{:S(2)}, u32[]{:S(2)}) collective-permute-start(bf16[4,128,256]{2,1,0:T(8,128)(2,1)S(1)} %bitcast.234), channel_id=1, source_target_pairs={{0,8},{1,9},{2,10},{3,11},{4,12},{5,13},{6,14},{7,15},{8,0},{9,1},... | collective-permute-start | bytes 786440 | tf_op jit(solution)/shard_map/ppermute | solution.py:72
  334.0 2.5 collective-permute-start.12
  338.2 4.4 collective-permute-start.27
  342.7 5.1 %collective-permute-start.26 = (bf16[128,256]{1,0:T(8,128)(2,1)S(1)}, bf16[128,256]{1,0:T(8,128)(2,1)S(1)}, u32[]{:S(2)}, u32[]{:S(2)}) collective-permute-start(bf16[128,256]{1,0:T(8,128)(2,1)S(1)} %fusion.76), channel_id=1, source_target_pairs={{0,2},{1,3},{2,0},{3,1},{4,6},{5,7},{6,4},{7,5},{8,10},{9,11},{10,... | collective-permute-start | bytes 196616 | tf_op jit(solution)/shard_map/ppermute | solution.py:32
  347.8 6.3 %collective-permute-start.25 = (bf16[128,256]{1,0:T(8,128)(2,1)S(1)}, bf16[128,256]{1,0:T(8,128)(2,1)S(1)}, u32[]{:S(2)}, u32[]{:S(2)}) collective-permute-start(bf16[128,256]{1,0:T(8,128)(2,1)S(1)} %fusion.76), channel_id=1, source_target_pairs={{0,1},{1,2},{2,3},{3,0},{4,5},{5,6},{6,7},{7,4},{8,9},{9,10},{10,1... | collective-permute-start | bytes 196616 | tf_op jit(solution)/shard_map/ppermute | solution.py:32
  354.4 5.5 %collective-permute-start.17 = (bf16[4,128,256]{2,1,0:T(8,128)(2,1)S(1)}, bf16[4,128,256]{2,1,0:T(8,128)(2,1)S(1)}, u32[]{:S(2)}, u32[]{:S(2)}) collective-permute-start(bf16[4,128,256]{2,1,0:T(8,128)(2,1)S(1)} %get-tuple-element.11), channel_id=1, source_target_pairs={{0,1},{1,2},{2,3},{3,0},{4,5},{5,6},{6,7},{7,4},{8,9},{9,10},{10,1... | collective-permute-start | bytes 786440 | tf_op jit(solution)/shard_map/ppermute | solution.py:76
  360.0 4.2 collective-permute-start.15
  364.2 8.4 %collective-permute-start.16 = (bf16[4,128,256]{2,1,0:T(8,128)(2,1)S(1)}, bf16[4,128,256]{2,1,0:T(8,128)(2,1)S(1)}, u32[]{:S(2)}, u32[]{:S(2)}) collective-permute-start(bf16[4,128,256]{2,1,0:T(8,128)(2,1)S(1)} %get-tuple-element.14), channel_id=1, source_target_pairs={{0,2},{1,3},{2,0},{3,1},{4,6},{5,7},{6,4},{7,5},{8,10},{9,11},{10,... | collective-permute-start | bytes 786440 | tf_op jit(solution)/shard_map/ppermute | solution.py:76
  372.6 1.7 slice_bitcast_fusion.9
  375.1 4.0 collective-permute-start.29
  379.1 1.9 collective-permute-start.28
  381.0 2.8 collective-permute-done.17
  383.8 2.3 collective-permute-start.30
  386.1 23.8 %collective-permute-done.16 = bf16[4,128,256]{2,1,0:T(8,128)(2,1)S(1)} collective-permute-done((bf16[4,128,256]{2,1,0:T(8,128)(2,1)S(1)}, bf16[4,128,256]{2,1,0:T(8,128)(2,1)S(1)}, u32[]{:S(2)}, u32[]{:S(2)}) %collective-permute-start.16) | collective-permute-done | bytes 262176 | tf_op jit(solution)/shard_map/ppermute | solution.py:76
  411.5 2.7 copy.62
  414.2 3.5 reshape.309
  417.6 2.6 multiply_reduce_fusion.1
  421.0 1.9 collective-permute-start.24
  423.0 2.6 fusion.40
  425.7 5.7 %collective-permute-start.31 = (bf16[256,768]{1,0:T(8,128)(2,1)S(1)}, bf16[256,768]{1,0:T(8,128)(2,1)S(1)}, u32[]{:S(2)}, u32[]{:S(2)}) collective-permute-start(bf16[256,768]{1,0:T(8,128)(2,1)S(1)} %fusion.40), channel_id=1, source_target_pairs={{0,496},{16,480},{32,464},{48,448},{64,432},{80,416},{96,400},{112... | collective-permute-start | bytes 1179656 | tf_op jit(solution)/shard_map/ppermute | solution.py:19
  431.4 24.3 %collective-permute-done.31 = bf16[256,768]{1,0:T(8,128)(2,1)S(1)} collective-permute-done((bf16[256,768]{1,0:T(8,128)(2,1)S(1)}, bf16[256,768]{1,0:T(8,128)(2,1)S(1)}, u32[]{:S(2)}, u32[]{:S(2)}) %collective-permute-start.31) | collective-permute-done | bytes 393248 | tf_op jit(solution)/shard_map/ppermute | solution.py:19
  (129 shorter events, 34.7 us)
Async XLA Ops:
  7.2 4.9 %copy-start = (bf16[1,128,4096]{2,1,0:T(8,128)(2,1)S(1)}, bf16[1,128,4096]{2,1,0:T(8,128)(2,1)}, u32[]{:S(2)}) copy-start(bf16[1,128,4096]{2,1,0:T(8,128)(2,1)} %param.8) | copy-start | bytes 3145732
  7.2 222.9 %all-gather.3.cloned.1.call-start = ((), (), s32[]{:S(2)}) async-start(), calls=%async_computation | async-start | bytes 4456448 | tf_op jit(solution)/shard_map/all_gather | solution.py:123
  19.1 74.6 %collective-permute-start = (bf16[7,128,256]{1,2,0:T(8,128)(2,1)}, bf16[7,128,256]{1,2,0:T(8,128)(2,1)S(1)}, u32[]{:S(2)}, u32[]{:S(2)}) collective-permute-start(bf16[7,128,256]{1,2,0:T(8,128)(2,1)} %get-tuple-element.34), channel_id=1, source_target_pairs={{0,1},{1,2},{2,3},{3,0},{4,5},{5,6},{6,7},{7,4},{8,9},{9,10},{10,1... | collective-permute-start | bytes 1376264 | tf_op jit(solution)/shard_map/ppermute | solution.py:54
  26.4 98.2 %collective-permute-start.1 = (bf16[7,128,256]{1,2,0:T(8,128)(2,1)}, bf16[7,128,256]{1,2,0:T(8,128)(2,1)S(1)}, u32[]{:S(2)}, u32[]{:S(2)}) collective-permute-start(bf16[7,128,256]{1,2,0:T(8,128)(2,1)} %get-tuple-element.35), channel_id=1, source_target_pairs={{0,2},{1,3},{2,0},{3,1},{4,6},{5,7},{6,4},{7,5},{8,10},{9,11},{10,... | collective-permute-start | bytes 1376264 | tf_op jit(solution)/shard_map/ppermute | solution.py:54
  30.2 100.7 %collective-permute-start.2 = (bf16[7,128,256]{1,2,0:T(8,128)(2,1)}, bf16[7,128,256]{1,2,0:T(8,128)(2,1)S(1)}, u32[]{:S(2)}, u32[]{:S(2)}) collective-permute-start(bf16[7,128,256]{1,2,0:T(8,128)(2,1)} %get-tuple-element.36), channel_id=1, source_target_pairs={{0,3},{1,0},{2,1},{3,2},{4,7},{5,4},{6,5},{7,6},{8,11},{9,8},{10,9... | collective-permute-start | bytes 1376264 | tf_op jit(solution)/shard_map/ppermute | solution.py:54
  131.9 13.6 %copy-start.19 = (s32[1,128]{1,0:T(1,128)S(1)}, s32[1,128]{1,0:T(1,128)}, u32[]{:S(2)}) copy-start(s32[1,128]{1,0:T(1,128)} %param.15) | copy-start | bytes 1540
  133.8 38.7 %collective-permute-start.3 = (bf16[16,128,256]{1,2,0:T(8,128)(2,1)}, bf16[16,128,256]{1,2,0:T(8,128)(2,1)}, u32[]{:S(2)}, u32[]{:S(2)}) collective-permute-start(bf16[16,128,256]{1,2,0:T(8,128)(2,1)} %get-tuple-element.23), channel_id=1, source_target_pairs={{0,4},{1,5},{2,6},{3,7},{4,8},{5,9},{6,10},{7,11},{8,12},{9,13},{1... | collective-permute-start | bytes 3145736 | tf_op jit(solution)/shard_map/ppermute | solution.py:61
  136.9 65.5 %collective-permute-start.4 = (bf16[16,128,256]{1,2,0:T(8,128)(2,1)}, bf16[16,128,256]{1,2,0:T(8,128)(2,1)}, u32[]{:S(2)}, u32[]{:S(2)}) collective-permute-start(bf16[16,128,256]{1,2,0:T(8,128)(2,1)} %get-tuple-element.24), channel_id=1, source_target_pairs={{0,8},{1,9},{2,10},{3,11},{4,12},{5,13},{6,14},{7,15},{8,0},{9,1},... | collective-permute-start | bytes 3145736 | tf_op jit(solution)/shard_map/ppermute | solution.py:61
  141.6 61.9 %collective-permute-start.5 = (bf16[16,128,256]{1,2,0:T(8,128)(2,1)}, bf16[16,128,256]{1,2,0:T(8,128)(2,1)}, u32[]{:S(2)}, u32[]{:S(2)}) collective-permute-start(bf16[16,128,256]{1,2,0:T(8,128)(2,1)} %get-tuple-element.25), channel_id=1, source_target_pairs={{0,12},{1,13},{2,14},{3,15},{4,0},{5,1},{6,2},{7,3},{8,4},{9,5},{1... | collective-permute-start | bytes 3145736 | tf_op jit(solution)/shard_map/ppermute | solution.py:61
  145.2 78.3 %copy-start.15 = (bf16[128,512]{0,1:T(8,128)(2,1)}, bf16[128,512]{0,1:T(8,128)(2,1)S(1)}, u32[]{:S(2)}) copy-start(bf16[128,512]{0,1:T(8,128)(2,1)S(1)} %slice.152) | copy-start | bytes 393220
  146.0 59.0 %copy-start.5 = (bf16[1,3,4,128,256]{3,4,2,1,0:T(8,128)(2,1)}, bf16[1,3,4,128,256]{3,4,2,1,0:T(8,128)(2,1)S(1)}, u32[]{:S(2)}) copy-start(bf16[1,3,4,128,256]{3,4,2,1,0:T(8,128)(2,1)S(1)} %fusion.103) | copy-start | bytes 2359300
  173.7 31.3 %copy-start.2 = (bf16[12,128,256]{1,2,0:T(8,128)(2,1)}, bf16[12,128,256]{1,2,0:T(8,128)(2,1)S(1)}, u32[]{:S(2)}) copy-start(bf16[12,128,256]{1,2,0:T(8,128)(2,1)S(1)} %slice.148) | copy-start | bytes 2359300
  203.5 1.5 copy-start.3
  205.0 0.9 copy-start.4
  230.1 4.3 copy-start.7
  234.3 3.5 copy-start.20
  238.7 7.2 %copy-start.16 = (bf16[128,512]{0,1:T(8,128)(2,1)S(1)}, bf16[128,512]{0,1:T(8,128)(2,1)}, u32[]{:S(2)}) copy-start(bf16[128,512]{0,1:T(8,128)(2,1)} %copy-done.15) | copy-start | bytes 393220
  254.0 26.1 %collective-permute-start.8 = (bf16[128,512]{1,0:T(8,128)(2,1)}, bf16[128,512]{1,0:T(8,128)(2,1)}, u32[]{:S(2)}, u32[]{:S(2)}) collective-permute-start(bf16[128,512]{1,0:T(8,128)(2,1)} %copy.55), channel_id=1, source_target_pairs={{0,3},{1,0},{2,1},{3,2},{4,7},{5,4},{6,5},{7,6},{8,11},{9,8},{10,9... | collective-permute-start | bytes 393224 | tf_op jit(solution)/shard_map/ppermute | solution.py:32
  257.2 29.8 %collective-permute-start.7 = (bf16[128,512]{1,0:T(8,128)(2,1)}, bf16[128,512]{1,0:T(8,128)(2,1)}, u32[]{:S(2)}, u32[]{:S(2)}) collective-permute-start(bf16[128,512]{1,0:T(8,128)(2,1)} %copy.55), channel_id=1, source_target_pairs={{0,2},{1,3},{2,0},{3,1},{4,6},{5,7},{6,4},{7,5},{8,10},{9,11},{10,... | collective-permute-start | bytes 393224 | tf_op jit(solution)/shard_map/ppermute | solution.py:32
  264.6 24.3 %collective-permute-start.6 = (bf16[128,512]{1,0:T(8,128)(2,1)}, bf16[128,512]{1,0:T(8,128)(2,1)}, u32[]{:S(2)}, u32[]{:S(2)}) collective-permute-start(bf16[128,512]{1,0:T(8,128)(2,1)} %copy.55), channel_id=1, source_target_pairs={{0,1},{1,2},{2,3},{3,0},{4,5},{5,6},{6,7},{7,4},{8,9},{9,10},{10,1... | collective-permute-start | bytes 393224 | tf_op jit(solution)/shard_map/ppermute | solution.py:32
  274.0 23.9 %collective-permute-start.19 = (bf16[4,128,256]{2,1,0:T(8,128)(2,1)}, bf16[4,128,256]{2,1,0:T(8,128)(2,1)}, u32[]{:S(2)}, u32[]{:S(2)}) collective-permute-start(bf16[4,128,256]{2,1,0:T(8,128)(2,1)} %bitcast.231), channel_id=1, source_target_pairs={{0,8},{1,9},{2,10},{3,11},{4,12},{5,13},{6,14},{7,15},{8,0},{9,1},... | collective-permute-start | bytes 786440 | tf_op jit(solution)/shard_map/ppermute | solution.py:40
  278.2 27.1 %collective-permute-start.20 = (bf16[4,128,256]{2,1,0:T(8,128)(2,1)}, bf16[4,128,256]{2,1,0:T(8,128)(2,1)}, u32[]{:S(2)}, u32[]{:S(2)}) collective-permute-start(bf16[4,128,256]{2,1,0:T(8,128)(2,1)} %bitcast.230), channel_id=1, source_target_pairs={{0,4},{1,5},{2,6},{3,7},{4,8},{5,9},{6,10},{7,11},{8,12},{9,13},{1... | collective-permute-start | bytes 786440 | tf_op jit(solution)/shard_map/ppermute | solution.py:40
  280.1 25.2 %collective-permute-start.18 = (bf16[4,128,256]{2,1,0:T(8,128)(2,1)}, bf16[4,128,256]{2,1,0:T(8,128)(2,1)}, u32[]{:S(2)}, u32[]{:S(2)}) collective-permute-start(bf16[4,128,256]{2,1,0:T(8,128)(2,1)} %bitcast.229), channel_id=1, source_target_pairs={{0,12},{1,13},{2,14},{3,15},{4,0},{5,1},{6,2},{7,3},{8,4},{9,5},{1... | collective-permute-start | bytes 786440 | tf_op jit(solution)/shard_map/ppermute | solution.py:40
  291.0 25.3 %collective-permute-start.10 = (bf16[4,128,512]{2,1,0:T(8,128)(2,1)}, bf16[4,128,512]{2,1,0:T(8,128)(2,1)}, u32[]{:S(2)}, u32[]{:S(2)}) collective-permute-start(bf16[4,128,512]{2,1,0:T(8,128)(2,1)} %get-tuple-element.27), channel_id=1, source_target_pairs={{0,8},{1,9},{2,10},{3,11},{4,12},{5,13},{6,14},{7,15},{8,0},{9,1},... | collective-permute-start | bytes 1572872 | tf_op jit(solution)/shard_map/ppermute | solution.py:33
  296.0 28.1 %collective-permute-start.9 = (bf16[4,128,512]{2,1,0:T(8,128)(2,1)}, bf16[4,128,512]{2,1,0:T(8,128)(2,1)}, u32[]{:S(2)}, u32[]{:S(2)}) collective-permute-start(bf16[4,128,512]{2,1,0:T(8,128)(2,1)} %get-tuple-element.27), channel_id=1, source_target_pairs={{0,4},{1,5},{2,6},{3,7},{4,8},{5,9},{6,10},{7,11},{8,12},{9,13},{1... | collective-permute-start | bytes 1572872 | tf_op jit(solution)/shard_map/ppermute | solution.py:33
  298.0 26.2 %collective-permute-start.11 = (bf16[4,128,512]{2,1,0:T(8,128)(2,1)}, bf16[4,128,512]{2,1,0:T(8,128)(2,1)}, u32[]{:S(2)}, u32[]{:S(2)}) collective-permute-start(bf16[4,128,512]{2,1,0:T(8,128)(2,1)} %get-tuple-element.27), channel_id=1, source_target_pairs={{0,12},{1,13},{2,14},{3,15},{4,0},{5,1},{6,2},{7,3},{8,4},{9,5},{1... | collective-permute-start | bytes 1572872 | tf_op jit(solution)/shard_map/ppermute | solution.py:33
  304.0 20.2 %copy-start.8 = (bf16[1,4,128,512]{3,2,1,0:T(8,128)(2,1)S(1)}, bf16[1,4,128,512]{3,2,1,0:T(8,128)(2,1)}, u32[]{:S(2)}) copy-start(bf16[1,4,128,512]{3,2,1,0:T(8,128)(2,1)} %get-tuple-element.26) | copy-start | bytes 1572868
  306.6 27.4 %collective-permute-start.21 = (bf16[128,256]{1,0:T(8,128)(2,1)S(1)}, bf16[128,256]{1,0:T(8,128)(2,1)S(1)}, u32[]{:S(2)}, u32[]{:S(2)}) collective-permute-start(bf16[128,256]{1,0:T(8,128)(2,1)S(1)} %get-tuple-element.30), channel_id=1, source_target_pairs={{0,3},{1,0},{2,1},{3,2},{4,7},{5,4},{6,5},{7,6},{8,11},{9,8},{10,9... | collective-permute-start | bytes 196616 | tf_op jit(solution)/shard_map/ppermute | solution.py:43
  309.0 29.2 %collective-permute-start.23 = (bf16[128,256]{1,0:T(8,128)(2,1)S(1)}, bf16[128,256]{1,0:T(8,128)(2,1)S(1)}, u32[]{:S(2)}, u32[]{:S(2)}) collective-permute-start(bf16[128,256]{1,0:T(8,128)(2,1)S(1)} %get-tuple-element.31), channel_id=1, source_target_pairs={{0,1},{1,2},{2,3},{3,0},{4,5},{5,6},{6,7},{7,4},{8,9},{9,10},{10,1... | collective-permute-start | bytes 196616 | tf_op jit(solution)/shard_map/ppermute | solution.py:43
  316.3 21.9 %collective-permute-start.22 = (bf16[128,256]{1,0:T(8,128)(2,1)S(1)}, bf16[128,256]{1,0:T(8,128)(2,1)S(1)}, u32[]{:S(2)}, u32[]{:S(2)}) collective-permute-start(bf16[128,256]{1,0:T(8,128)(2,1)S(1)} %get-tuple-element.32), channel_id=1, source_target_pairs={{0,2},{1,3},{2,0},{3,1},{4,6},{5,7},{6,4},{7,5},{8,10},{9,11},{10,... | collective-permute-start | bytes 196616 | tf_op jit(solution)/shard_map/ppermute | solution.py:43
  324.2 1.7 copy-start.18
  326.7 21.1 %collective-permute-start.14 = (bf16[4,128,256]{2,1,0:T(8,128)(2,1)S(1)}, bf16[4,128,256]{2,1,0:T(8,128)(2,1)S(1)}, u32[]{:S(2)}, u32[]{:S(2)}) collective-permute-start(bf16[4,128,256]{2,1,0:T(8,128)(2,1)S(1)} %bitcast.236), channel_id=1, source_target_pairs={{0,4},{1,5},{2,6},{3,7},{4,8},{5,9},{6,10},{7,11},{8,12},{9,13},{1... | collective-permute-start | bytes 786440 | tf_op jit(solution)/shard_map/ppermute | solution.py:72
  328.6 25.6 %collective-permute-start.13 = (bf16[4,128,256]{2,1,0:T(8,128)(2,1)S(1)}, bf16[4,128,256]{2,1,0:T(8,128)(2,1)S(1)}, u32[]{:S(2)}, u32[]{:S(2)}) collective-permute-start(bf16[4,128,256]{2,1,0:T(8,128)(2,1)S(1)} %bitcast.234), channel_id=1, source_target_pairs={{0,8},{1,9},{2,10},{3,11},{4,12},{5,13},{6,14},{7,15},{8,0},{9,1},... | collective-permute-start | bytes 786440 | tf_op jit(solution)/shard_map/ppermute | solution.py:72
  334.0 20.2 %collective-permute-start.12 = (bf16[4,128,256]{2,1,0:T(8,128)(2,1)S(1)}, bf16[4,128,256]{2,1,0:T(8,128)(2,1)S(1)}, u32[]{:S(2)}, u32[]{:S(2)}) collective-permute-start(bf16[4,128,256]{2,1,0:T(8,128)(2,1)S(1)} %bitcast.232), channel_id=1, source_target_pairs={{0,12},{1,13},{2,14},{3,15},{4,0},{5,1},{6,2},{7,3},{8,4},{9,5},{1... | collective-permute-start | bytes 786440 | tf_op jit(solution)/shard_map/ppermute | solution.py:72
  338.2 26.0 %collective-permute-start.27 = (bf16[128,256]{1,0:T(8,128)(2,1)S(1)}, bf16[128,256]{1,0:T(8,128)(2,1)S(1)}, u32[]{:S(2)}, u32[]{:S(2)}) collective-permute-start(bf16[128,256]{1,0:T(8,128)(2,1)S(1)} %fusion.76), channel_id=1, source_target_pairs={{0,3},{1,0},{2,1},{3,2},{4,7},{5,4},{6,5},{7,6},{8,11},{9,8},{10,9... | collective-permute-start | bytes 196616 | tf_op jit(solution)/shard_map/ppermute | solution.py:32
  342.7 31.6 %collective-permute-start.26 = (bf16[128,256]{1,0:T(8,128)(2,1)S(1)}, bf16[128,256]{1,0:T(8,128)(2,1)S(1)}, u32[]{:S(2)}, u32[]{:S(2)}) collective-permute-start(bf16[128,256]{1,0:T(8,128)(2,1)S(1)} %fusion.76), channel_id=1, source_target_pairs={{0,2},{1,3},{2,0},{3,1},{4,6},{5,7},{6,4},{7,5},{8,10},{9,11},{10,... | collective-permute-start | bytes 196616 | tf_op jit(solution)/shard_map/ppermute | solution.py:32
  347.8 26.5 %collective-permute-start.25 = (bf16[128,256]{1,0:T(8,128)(2,1)S(1)}, bf16[128,256]{1,0:T(8,128)(2,1)S(1)}, u32[]{:S(2)}, u32[]{:S(2)}) collective-permute-start(bf16[128,256]{1,0:T(8,128)(2,1)S(1)} %fusion.76), channel_id=1, source_target_pairs={{0,1},{1,2},{2,3},{3,0},{4,5},{5,6},{6,7},{7,4},{8,9},{9,10},{10,1... | collective-permute-start | bytes 196616 | tf_op jit(solution)/shard_map/ppermute | solution.py:32
  354.4 29.4 %collective-permute-start.17 = (bf16[4,128,256]{2,1,0:T(8,128)(2,1)S(1)}, bf16[4,128,256]{2,1,0:T(8,128)(2,1)S(1)}, u32[]{:S(2)}, u32[]{:S(2)}) collective-permute-start(bf16[4,128,256]{2,1,0:T(8,128)(2,1)S(1)} %get-tuple-element.11), channel_id=1, source_target_pairs={{0,1},{1,2},{2,3},{3,0},{4,5},{5,6},{6,7},{7,4},{8,9},{9,10},{10,1... | collective-permute-start | bytes 786440 | tf_op jit(solution)/shard_map/ppermute | solution.py:76
  360.0 26.2 %collective-permute-start.15 = (bf16[4,128,256]{2,1,0:T(8,128)(2,1)S(1)}, bf16[4,128,256]{2,1,0:T(8,128)(2,1)S(1)}, u32[]{:S(2)}, u32[]{:S(2)}) collective-permute-start(bf16[4,128,256]{2,1,0:T(8,128)(2,1)S(1)} %get-tuple-element.12), channel_id=1, source_target_pairs={{0,3},{1,0},{2,1},{3,2},{4,7},{5,4},{6,5},{7,6},{8,11},{9,8},{10,9... | collective-permute-start | bytes 786440 | tf_op jit(solution)/shard_map/ppermute | solution.py:76
  364.2 45.7 %collective-permute-start.16 = (bf16[4,128,256]{2,1,0:T(8,128)(2,1)S(1)}, bf16[4,128,256]{2,1,0:T(8,128)(2,1)S(1)}, u32[]{:S(2)}, u32[]{:S(2)}) collective-permute-start(bf16[4,128,256]{2,1,0:T(8,128)(2,1)S(1)} %get-tuple-element.14), channel_id=1, source_target_pairs={{0,2},{1,3},{2,0},{3,1},{4,6},{5,7},{6,4},{7,5},{8,10},{9,11},{10,... | collective-permute-start | bytes 786440 | tf_op jit(solution)/shard_map/ppermute | solution.py:76
  375.1 47.9 %collective-permute-start.29 = (bf16[4,128,256]{2,1,0:T(8,128)(2,1)}, bf16[4,128,256]{2,1,0:T(8,128)(2,1)}, u32[]{:S(2)}, u32[]{:S(2)}) collective-permute-start(bf16[4,128,256]{2,1,0:T(8,128)(2,1)} %get-tuple-element.29), channel_id=1, source_target_pairs={{0,8},{1,9},{2,10},{3,11},{4,12},{5,13},{6,14},{7,15},{8,0},{9,1},... | collective-permute-start | bytes 786440 | tf_op jit(solution)/shard_map/ppermute | solution.py:33
  379.1 43.9 %collective-permute-start.28 = (bf16[4,128,256]{2,1,0:T(8,128)(2,1)}, bf16[4,128,256]{2,1,0:T(8,128)(2,1)}, u32[]{:S(2)}, u32[]{:S(2)}) collective-permute-start(bf16[4,128,256]{2,1,0:T(8,128)(2,1)} %get-tuple-element.29), channel_id=1, source_target_pairs={{0,4},{1,5},{2,6},{3,7},{4,8},{5,9},{6,10},{7,11},{8,12},{9,13},{1... | collective-permute-start | bytes 786440 | tf_op jit(solution)/shard_map/ppermute | solution.py:33
  383.8 39.1 %collective-permute-start.30 = (bf16[4,128,256]{2,1,0:T(8,128)(2,1)}, bf16[4,128,256]{2,1,0:T(8,128)(2,1)}, u32[]{:S(2)}, u32[]{:S(2)}) collective-permute-start(bf16[4,128,256]{2,1,0:T(8,128)(2,1)} %get-tuple-element.29), channel_id=1, source_target_pairs={{0,12},{1,13},{2,14},{3,15},{4,0},{5,1},{6,2},{7,3},{8,4},{9,5},{1... | collective-permute-start | bytes 786440 | tf_op jit(solution)/shard_map/ppermute | solution.py:33
  414.2 3.5 copy-start.1
  414.2 3.5 copy-start.17
  417.6 2.6 copy-start.6
  420.3 2.7 copy-start.9
  420.3 2.7 copy-start.11
  420.3 2.7 copy-start.12
  420.3 2.7 copy-start.13
  420.3 2.7 copy-start.14
  421.0 35.5 %collective-permute-start.24 = (bf16[128,4096]{1,0:T(8,128)(2,1)S(1)}, bf16[128,4096]{1,0:T(8,128)(2,1)S(1)}, u32[]{:S(2)}, u32[]{:S(2)}) collective-permute-start(bf16[128,4096]{1,0:T(8,128)(2,1)S(1)} %add_convert_fusion), channel_id=1, source_target_pairs={{0,16},{16,32},{32,48},{48,64},{64,80},{80,96},{96,112},{112,128},... | collective-permute-start | bytes 3145736 | tf_op jit(solution)/shard_map/ppermute | solution.py:14
  423.0 32.7 %copy-start.10 = (bf16[1,256,768]{2,1,0:T(8,128)(2,1)S(1)}, bf16[1,256,768]{2,1,0:T(8,128)(2,1)}, u32[]{:S(2)}) copy-start(bf16[1,256,768]{2,1,0:T(8,128)(2,1)} %param.14) | copy-start | bytes 1179652
  425.7 30.0 %collective-permute-start.31 = (bf16[256,768]{1,0:T(8,128)(2,1)S(1)}, bf16[256,768]{1,0:T(8,128)(2,1)S(1)}, u32[]{:S(2)}, u32[]{:S(2)}) collective-permute-start(bf16[256,768]{1,0:T(8,128)(2,1)S(1)} %fusion.40), channel_id=1, source_target_pairs={{0,496},{16,480},{32,464},{48,448},{64,432},{80,416},{96,400},{112... | collective-permute-start | bytes 1179656 | tf_op jit(solution)/shard_map/ppermute | solution.py:19
Sparse Core Ops, SparseCore 0:
  11.0 192.6 all-gather.2

commit v8 on v7

--- a/solution.py
+++ b/solution.py
@@ -126,10 +126,9 @@
     riders = jnp.concatenate(
         [saved[None, :, width:], kv_weight.reshape(-1, count, pieces)]
     )
-    gathered, hidden_cols = gather_and_scatter(riders, hidden, o, i)
-    key_value = gathered[:, 0].reshape(size * count, 2 * HEAD)
-    hidden_cols = hidden_cols.reshape(size * count, -1)
-    kv_weight_all = gathered[:, 1:].transpose(0, 2, 1, 3, 4)
+    gathered = gather_blocks(riders)
+    key_value = gathered[:, :, 0].reshape(size * count, 2 * HEAD)
+    kv_weight_all = gathered[:, :, 1:]
     kv_weight_all = jnp.take(kv_weight_all, (o - jnp.arange(outer)) % outer, axis=0)
     kv_weight_all = jnp.take(kv_weight_all, (i - jnp.arange(INNER)) % INNER, axis=1)
     kv_weight_all = kv_weight_all.reshape(-1, 2 * HEAD)
@@ -167,7 +166,9 @@
     kv_part = jnp.concatenate([key_part, value_part], axis=1).reshape(outer, INNER, count, 2 * HEAD)
     query_all = gather_blocks(query_grad)
     kv_grad = reduce_blocks(kv_part, jnp.bfloat16).astype(jnp.bfloat16)
-    grad_all = jnp.concatenate([query_all, gather_blocks(kv_grad)], axis=-1).reshape(size * count, -1)
+    kv_all, hidden_cols = gather_and_scatter(kv_grad[None], hidden, o, i)
+    hidden_cols = hidden_cols.reshape(size * count, -1)
+    grad_all = jnp.concatenate([query_all, kv_all[:, 0]], axis=-1).reshape(size * count, -1)
     input_term = contract_first(hidden_cols, grad_all).astype(jnp.bfloat16)
     block = contract_last(query_all.reshape(size * count, -1), up_input_weight[0][:, :width])
     hidden_grad = gather_columns(block.astype(jnp.bfloat16).reshape(outer, INNER, count, -1), o, i)

time: 466 us -> 450 us (0.966)
  the two profiles are of different devices: /device:TPU:192 before, /device:TPU:25 now
where the time goes in v8:
time: 450 us; the launch traced here: 445 us
  starting transfers between devices  175 us (39%)
  waiting for transfers between devices  154 us (34%)
  local copies, waits for them, and re-layouts  39.9 us (9%)
  matrix products  35.6 us (8%)
  other arithmetic  24.7 us (5%)
  between operations  15.2 us (3%)
    ppermute x3, starting transfers between devices, gather_and_scatter(): lax.ppermute(jnp.concatenate([x, piece]), 'seq', seq_pairs(k, 0))  46.8 us
    ppermute x6, starting transfers between devices, gather_blocks(): lax.ppermute(x, 'seq', seq_pairs(k, 0))  41.3 us
    all_gather x1, waiting for transfers between devices, per_device(): lax.all_gather(up_output_weight[0], 'seq', axis=1, tiled=True)  34.8 us
    ppermute x6, waiting for transfers between devices, gather_blocks(): lax.ppermute(x, 'seq', seq_pairs(k, 0))  34.5 us
    ppermute x6, waiting for transfers between devices, gather_blocks(): lax.ppermute(first, 'seq', seq_pairs(k, 1))  33 us
    ppermute x3, waiting for transfers between devices, gather_and_scatter(): lax.ppermute(jnp.concatenate([x, piece]), 'seq', seq_pairs(k, 0))  20.5 us
    ppermute x6, starting transfers between devices, gather_blocks(): lax.ppermute(first, 'seq', seq_pairs(k, 1))  19.7 us
    ppermute x3, starting transfers between devices, reduce_blocks(): lax.ppermute(acc[k].astype(wire), 'seq', seq_pairs(INNER - k, 0))  17.7 us
  transfers between devices with their start and end apart: 33, of which 11 were waited for; matrix products, arithmetic and copies ran while one was open for 15% of the time, Pallas kernels for 0%

profile of v8, /device:TPU:25, one launch (start us, length us, event | category | flops | bytes accessed | tf_op | source)
XLA Modules:
  0.0 445.2 jit_solution(9826607759195529240)
XLA Ops:
  10.4 15.4 %collective-permute-start.1 = (bf16[3,128,256]{2,1,0:T(8,128)(2,1)}, bf16[3,128,256]{2,1,0:T(8,128)(2,1)}, u32[]{:S(2)}, u32[]{:S(2)}) collective-permute-start(bf16[3,128,256]{2,1,0:T(8,128)(2,1)} %get-tuple-element.40), channel_id=1, source_target_pairs={{0,2},{1,3},{2,0},{3,1},{4,6},{5,7},{6,4},{7,5},{8,10},{9,11},{10,... | collective-permute-start | bytes 589832 | tf_op jit(solution)/shard_map/ppermute | solution.py:32
  25.9 4.0 collective-permute-start
  29.9 5.2 %collective-permute-start.2 = (bf16[3,128,256]{2,1,0:T(8,128)(2,1)}, bf16[3,128,256]{2,1,0:T(8,128)(2,1)}, u32[]{:S(2)}, u32[]{:S(2)}) collective-permute-start(bf16[3,128,256]{2,1,0:T(8,128)(2,1)} %get-tuple-element.40), channel_id=1, source_target_pairs={{0,3},{1,0},{2,1},{3,2},{4,7},{5,4},{6,5},{7,6},{8,11},{9,8},{10,9... | collective-permute-start | bytes 589832 | tf_op jit(solution)/shard_map/ppermute | solution.py:32
  39.7 1.7 reshape.310
  44.0 2.1 collective-permute-done
  46.2 27.4 %collective-permute-done.2 = bf16[3,128,256]{2,1,0:T(8,128)(2,1)} collective-permute-done((bf16[3,128,256]{2,1,0:T(8,128)(2,1)}, bf16[3,128,256]{2,1,0:T(8,128)(2,1)}, u32[]{:S(2)}, u32[]{:S(2)}) %collective-permute-start.2) | collective-permute-done | bytes 196640 | tf_op jit(solution)/shard_map/ppermute | solution.py:32
  74.8 4.8 %collective-permute-start.4 = (bf16[4,3,128,256]{3,2,1,0:T(8,128)(2,1)S(1)}, bf16[4,3,128,256]{3,2,1,0:T(8,128)(2,1)S(1)}, u32[]{:S(2)}, u32[]{:S(2)}) collective-permute-start(bf16[4,3,128,256]{3,2,1,0:T(8,128)(2,1)S(1)} %get-tuple-element.24), channel_id=1, source_target_pairs={{0,8},{1,9},{2,10},{3,11},{4,12},{5,13},{6,14},{7,15},{8,0},{9,1},... | collective-permute-start | bytes 2359304 | tf_op jit(solution)/shard_map/ppermute | solution.py:33
  79.6 2.2 collective-permute-start.3
  81.9 4.3 collective-permute-start.5
  87.3 9.5 %collective-permute-done.4 = bf16[4,3,128,256]{3,2,1,0:T(8,128)(2,1)S(1)} collective-permute-done((bf16[4,3,128,256]{3,2,1,0:T(8,128)(2,1)S(1)}, bf16[4,3,128,256]{3,2,1,0:T(8,128)(2,1)S(1)}, u32[]{:S(2)}, u32[]{:S(2)}) %collective-permute-start.4) | collective-permute-done | bytes 786464 | tf_op jit(solution)/shard_map/ppermute | solution.py:33
  96.8 23.5 %collective-permute-done.3 = bf16[4,3,128,256]{3,2,1,0:T(8,128)(2,1)S(1)} collective-permute-done((bf16[4,3,128,256]{3,2,1,0:T(8,128)(2,1)S(1)}, bf16[4,3,128,256]{3,2,1,0:T(8,128)(2,1)S(1)}, u32[]{:S(2)}, u32[]{:S(2)}) %collective-permute-start.3) | collective-permute-done | bytes 786464 | tf_op jit(solution)/shard_map/ppermute | solution.py:33
  123.1 2.3 gather_fusion
  125.3 2.3 broadcast_select_fusion
  127.6 3.6 gather_fusion.1
  131.3 1.9 copy.145
  134.8 4.9 %fusion.92 = (f32[128,4]{0,1:T(4,128)S(1)}, f32[128,4,2048]{0,2,1:T(8,128)}) fusion(pred[128,2048]{0,1:T(8,128)(4,1)} %compare_and_fusion, bf16[128,4,128]{0,2,1:T(8,128)(2,1)S(1)} %bitcast.253, bf16[2048,256]{1,0:T(8,128)(2,1)} %bitcast.211), kind=kOutput, calls=%fused_computation.182 | convolution fusion | flops 273680384 | bytes 5376000 | tf_op jit(solution)/shard_map/sub | solution.py:152
  139.8 34.8 %all-gather.3.cloned.1.call-done = bf16[1,512,4096]{2,1,0:T(8,128)(2,1)} async-done(((bf16[1,512,256]{2,1,0:T(8,128)(2,1)}), bf16[1,512,4096]{2,1,0:T(8,128)(2,1)}) %all-gather.3.cloned.1.call-update) | async-done | bytes 4194320 | tf_op jit(solution)/shard_map/all_gather | solution.py:123
  174.5 4.7 %fusion.38 = bf16[128,512]{1,0:T(8,128)(2,1)} fusion(bf16[1,512,4096]{2,1,0:T(8,128)(2,1)} %all-gather.3.cloned.1.call-done, bf16[1,128,4096]{2,1,0:T(8,128)(2,1)} %param.10), kind=kOutput, calls=%fused_computation.65 | convolution fusion | flops 536936448 | bytes 5373952 | tf_op jit(solution)/shard_map/dot_general | solution.py:83
  180.3 3.9 fusion.64
  184.1 1.8 convolution_bitcast_fusion
  185.9 8.4 %convolution_bitcast_fusion.1 = f32[2048,128]{0,1:T(8,128)} fusion(bf16[128,4,128]{0,2,1:T(8,128)(2,1)} %bitcast.254, f32[128,4,2048]{0,2,1:T(8,128)} %fusion.64, f32[128,4,2048]{0,2,1:T(8,128)} %get-tuple-element.46, f32[128,4]{0,1:T(4,128)S(1)} %get-tuple-element.45), kind=kOutput, calls=%fused_computation.29 | convolution fusion | flops 275778048 | bytes 9570304 | tf_op jit(solution)/shard_map/tgj,tgh->jh/dot_general | solution.py:164
  194.4 1.7 fusion.19
  197.0 1.8 copy.165
  198.7 1.8 copy.167
  200.5 1.8 copy.166
  202.3 3.7 collective-permute-start.19
  206.0 3.1 collective-permute-start.20
  209.1 3.5 collective-permute-start.18
  212.7 7.5 %fusion.41 = bf16[128,4,128]{0,2,1:T(8,128)(2,1)S(1)} fusion(f32[128,4,2048]{0,2,1:T(8,128)} %fusion.64, bf16[2048,256]{1,0:T(8,128)(2,1)} %bitcast.213, f32[128,4,2048]{0,2,1:T(8,128)} %get-tuple-element.46, f32[128,4]{0,1:T(4,128)S(1)} %get-tuple-element.45), kind=kOutput, calls=%fused_computation.66 | convolution fusion | flops 275843584 | bytes 17436672 | tf_op jit(solution)/shard_map/tgj,jh->tgh/dot_general | solution.py:160
  221.0 7.6 %collective-permute-start.8 = (bf16[128,512]{1,0:T(8,128)(2,1)}, bf16[128,512]{1,0:T(8,128)(2,1)}, u32[]{:S(2)}, u32[]{:S(2)}) collective-permute-start(bf16[128,512]{1,0:T(8,128)(2,1)} %copy.130), channel_id=1, source_target_pairs={{0,3},{1,0},{2,1},{3,2},{4,7},{5,4},{6,5},{7,6},{8,11},{9,8},{10,9... | collective-permute-start | bytes 393224 | tf_op jit(solution)/shard_map/ppermute | solution.py:32
  228.6 7.2 %collective-permute-start.7 = (bf16[128,512]{1,0:T(8,128)(2,1)}, bf16[128,512]{1,0:T(8,128)(2,1)}, u32[]{:S(2)}, u32[]{:S(2)}) collective-permute-start(bf16[128,512]{1,0:T(8,128)(2,1)} %copy.130), channel_id=1, source_target_pairs={{0,2},{1,3},{2,0},{3,1},{4,6},{5,7},{6,4},{7,5},{8,10},{9,11},{10,... | collective-permute-start | bytes 393224 | tf_op jit(solution)/shard_map/ppermute | solution.py:32
  236.8 1.9 fusion.63
  238.7 2.0 copy.164
  240.7 1.9 collective-permute-start.6
  244.1 7.3 %collective-permute-start.21 = (bf16[128,256]{1,0:T(8,128)(2,1)S(1)}, bf16[128,256]{1,0:T(8,128)(2,1)S(1)}, u32[]{:S(2)}, u32[]{:S(2)}) collective-permute-start(bf16[128,256]{1,0:T(8,128)(2,1)S(1)} %get-tuple-element.36), channel_id=1, source_target_pairs={{0,3},{1,0},{2,1},{3,2},{4,7},{5,4},{6,5},{7,6},{8,11},{9,8},{10,9... | collective-permute-start | bytes 196616 | tf_op jit(solution)/shard_map/ppermute | solution.py:43
  251.4 1.7 collective-permute-done.7
  253.1 3.3 collective-permute-done.6
  257.5 1.9 collective-permute-start.10
  259.4 2.6 collective-permute-start.9
  262.0 3.9 collective-permute-start.11
  265.9 4.9 %collective-permute-start.23 = (bf16[128,256]{1,0:T(8,128)(2,1)S(1)}, bf16[128,256]{1,0:T(8,128)(2,1)S(1)}, u32[]{:S(2)}, u32[]{:S(2)}) collective-permute-start(bf16[128,256]{1,0:T(8,128)(2,1)S(1)} %get-tuple-element.37), channel_id=1, source_target_pairs={{0,1},{1,2},{2,3},{3,0},{4,5},{5,6},{6,7},{7,4},{8,9},{9,10},{10,1... | collective-permute-start | bytes 196616 | tf_op jit(solution)/shard_map/ppermute | solution.py:43
  270.8 5.6 %collective-permute-start.22 = (bf16[128,256]{1,0:T(8,128)(2,1)S(1)}, bf16[128,256]{1,0:T(8,128)(2,1)S(1)}, u32[]{:S(2)}, u32[]{:S(2)}) collective-permute-start(bf16[128,256]{1,0:T(8,128)(2,1)S(1)} %get-tuple-element.38), channel_id=1, source_target_pairs={{0,2},{1,3},{2,0},{3,1},{4,6},{5,7},{6,4},{7,5},{8,10},{9,11},{10,... | collective-permute-start | bytes 196616 | tf_op jit(solution)/shard_map/ppermute | solution.py:43
  276.4 1.9 bitcast_select_fusion.2
  278.3 10.3 %collective-permute-done.22 = bf16[128,256]{1,0:T(8,128)(2,1)S(1)} collective-permute-done((bf16[128,256]{1,0:T(8,128)(2,1)S(1)}, bf16[128,256]{1,0:T(8,128)(2,1)S(1)}, u32[]{:S(2)}, u32[]{:S(2)}) %collective-permute-start.22) | collective-permute-done | bytes 65568 | tf_op jit(solution)/shard_map/ppermute | solution.py:43
  288.7 37.4 %collective-permute-start.25 = (bf16[5,128,256]{2,1,0:T(8,128)(2,1)S(1)}, bf16[5,128,256]{2,1,0:T(8,128)(2,1)S(1)}, u32[]{:S(2)}, u32[]{:S(2)}) collective-permute-start(bf16[5,128,256]{2,1,0:T(8,128)(2,1)S(1)} %get-tuple-element.42), channel_id=1, source_target_pairs={{0,1},{1,2},{2,3},{3,0},{4,5},{5,6},{6,7},{7,4},{8,9},{9,10},{10,1... | collective-permute-start | bytes 983048 | tf_op jit(solution)/shard_map/ppermute | solution.py:54
  326.2 7.5 %collective-permute-start.26 = (bf16[5,128,256]{2,1,0:T(8,128)(2,1)S(1)}, bf16[5,128,256]{2,1,0:T(8,128)(2,1)S(1)}, u32[]{:S(2)}, u32[]{:S(2)}) collective-permute-start(bf16[5,128,256]{2,1,0:T(8,128)(2,1)S(1)} %get-tuple-element.43), channel_id=1, source_target_pairs={{0,2},{1,3},{2,0},{3,1},{4,6},{5,7},{6,4},{7,5},{8,10},{9,11},{10,... | collective-permute-start | bytes 983048 | tf_op jit(solution)/shard_map/ppermute | solution.py:54
  333.7 1.9 collective-permute-start.27
  337.8 1.9 collective-permute-start.14
  339.7 3.6 collective-permute-start.13
  343.3 3.8 collective-permute-start.12
  347.1 20.5 %collective-permute-done.26 = bf16[5,128,256]{2,1,0:T(8,128)(2,1)S(1)} collective-permute-done((bf16[5,128,256]{2,1,0:T(8,128)(2,1)S(1)}, bf16[5,128,256]{2,1,0:T(8,128)(2,1)S(1)}, u32[]{:S(2)}, u32[]{:S(2)}) %collective-permute-start.26) | collective-permute-done | bytes 327712 | tf_op jit(solution)/shard_map/ppermute | solution.py:54
  368.2 1.9 collective-permute-start.17
  370.1 7.3 %collective-permute-start.15 = (bf16[4,128,256]{2,1,0:T(8,128)(2,1)S(1)}, bf16[4,128,256]{2,1,0:T(8,128)(2,1)S(1)}, u32[]{:S(2)}, u32[]{:S(2)}) collective-permute-start(bf16[4,128,256]{2,1,0:T(8,128)(2,1)S(1)} %get-tuple-element.16), channel_id=1, source_target_pairs={{0,3},{1,0},{2,1},{3,2},{4,7},{5,4},{6,5},{7,6},{8,11},{9,8},{10,9... | collective-permute-start | bytes 786440 | tf_op jit(solution)/shard_map/ppermute | solution.py:76
  377.4 4.8 %collective-permute-start.16 = (bf16[4,128,256]{2,1,0:T(8,128)(2,1)S(1)}, bf16[4,128,256]{2,1,0:T(8,128)(2,1)S(1)}, u32[]{:S(2)}, u32[]{:S(2)}) collective-permute-start(bf16[4,128,256]{2,1,0:T(8,128)(2,1)S(1)} %get-tuple-element.18), channel_id=1, source_target_pairs={{0,2},{1,3},{2,0},{3,1},{4,6},{5,7},{6,4},{7,5},{8,10},{9,11},{10,... | collective-permute-start | bytes 786440 | tf_op jit(solution)/shard_map/ppermute | solution.py:76
  384.2 4.6 %collective-permute-start.28 = (bf16[8,128,256]{2,1,0:T(8,128)(2,1)}, bf16[8,128,256]{2,1,0:T(8,128)(2,1)}, u32[]{:S(2)}, u32[]{:S(2)}) collective-permute-start(bf16[8,128,256]{2,1,0:T(8,128)(2,1)} %get-tuple-element.33), channel_id=1, source_target_pairs={{0,4},{1,5},{2,6},{3,7},{4,8},{5,9},{6,10},{7,11},{8,12},{9,13},{1... | collective-permute-start | bytes 1572872 | tf_op jit(solution)/shard_map/ppermute | solution.py:61
  388.8 3.7 collective-permute-start.29
  392.5 4.0 collective-permute-start.30
  396.5 5.0 %collective-permute-done.16 = bf16[4,128,256]{2,1,0:T(8,128)(2,1)S(1)} collective-permute-done((bf16[4,128,256]{2,1,0:T(8,128)(2,1)S(1)}, bf16[4,128,256]{2,1,0:T(8,128)(2,1)S(1)}, u32[]{:S(2)}, u32[]{:S(2)}) %collective-permute-start.16) | collective-permute-done | bytes 262176 | tf_op jit(solution)/shard_map/ppermute | solution.py:76
  403.1 2.7 copy.137
  405.8 3.4 reshape.308
  409.3 2.6 multiply_reduce_fusion.1
  412.6 1.9 collective-permute-start.24
  419.2 1.9 collective-permute-start.31
  421.1 15.4 %collective-permute-done.31 = bf16[256,768]{1,0:T(8,128)(2,1)S(1)} collective-permute-done((bf16[256,768]{1,0:T(8,128)(2,1)S(1)}, bf16[256,768]{1,0:T(8,128)(2,1)S(1)}, u32[]{:S(2)}, u32[]{:S(2)}) %collective-permute-start.31) | collective-permute-done | bytes 393248 | tf_op jit(solution)/shard_map/ppermute | solution.py:19
  (147 shorter events, 36.4 us)
Async XLA Ops:
  7.2 32.5 %copy-start = (bf16[1,128,4096]{2,1,0:T(8,128)(2,1)S(1)}, bf16[1,128,4096]{2,1,0:T(8,128)(2,1)}, u32[]{:S(2)}) copy-start(bf16[1,128,4096]{2,1,0:T(8,128)(2,1)} %param.8) | copy-start | bytes 3145732
  7.2 167.3 %all-gather.3.cloned.1.call-start = ((), (), s32[]{:S(2)}) async-start(), calls=%async_computation | async-start | bytes 4456448 | tf_op jit(solution)/shard_map/all_gather | solution.py:123
  10.4 33.6 %collective-permute-start.1 = (bf16[3,128,256]{2,1,0:T(8,128)(2,1)}, bf16[3,128,256]{2,1,0:T(8,128)(2,1)}, u32[]{:S(2)}, u32[]{:S(2)}) collective-permute-start(bf16[3,128,256]{2,1,0:T(8,128)(2,1)} %get-tuple-element.40), channel_id=1, source_target_pairs={{0,2},{1,3},{2,0},{3,1},{4,6},{5,7},{6,4},{7,5},{8,10},{9,11},{10,... | collective-permute-start | bytes 589832 | tf_op jit(solution)/shard_map/ppermute | solution.py:32
  25.9 20.3 %collective-permute-start = (bf16[3,128,256]{2,1,0:T(8,128)(2,1)}, bf16[3,128,256]{2,1,0:T(8,128)(2,1)}, u32[]{:S(2)}, u32[]{:S(2)}) collective-permute-start(bf16[3,128,256]{2,1,0:T(8,128)(2,1)} %get-tuple-element.40), channel_id=1, source_target_pairs={{0,1},{1,2},{2,3},{3,0},{4,5},{5,6},{6,7},{7,4},{8,9},{9,10},{10,1... | collective-permute-start | bytes 589832 | tf_op jit(solution)/shard_map/ppermute | solution.py:32
  29.9 43.7 %collective-permute-start.2 = (bf16[3,128,256]{2,1,0:T(8,128)(2,1)}, bf16[3,128,256]{2,1,0:T(8,128)(2,1)}, u32[]{:S(2)}, u32[]{:S(2)}) collective-permute-start(bf16[3,128,256]{2,1,0:T(8,128)(2,1)} %get-tuple-element.40), channel_id=1, source_target_pairs={{0,3},{1,0},{2,1},{3,2},{4,7},{5,4},{6,5},{7,6},{8,11},{9,8},{10,9... | collective-permute-start | bytes 589832 | tf_op jit(solution)/shard_map/ppermute | solution.py:32
  39.6 95.2 %copy-start.26 = (bf16[128,512]{0,1:T(8,128)(2,1)}, bf16[128,512]{0,1:T(8,128)(2,1)S(1)}, u32[]{:S(2)}) copy-start(bf16[128,512]{0,1:T(8,128)(2,1)S(1)} %copy.123) | copy-start | bytes 393220
  41.8 31.8 %copy-start.16 = (bf16[1,3,128,256]{3,2,1,0:T(8,128)(2,1)S(1)}, bf16[1,3,128,256]{3,2,1,0:T(8,128)(2,1)}, u32[]{:S(2)}) copy-start(bf16[1,3,128,256]{3,2,1,0:T(8,128)(2,1)} %get-tuple-element.39) | copy-start | bytes 589828
  43.1 43.1 %copy-start.29 = (s32[16]{0:T(128)S(1)}, s32[16]{0:T(128)}, u32[]{:S(2)}) copy-start(s32[16]{0:T(128)} %mul.95) | copy-start | bytes 196
  43.1 43.2 %copy-start.30 = (s32[1,128]{1,0:T(1,128)S(1)}, s32[1,128]{1,0:T(1,128)}, u32[]{:S(2)}) copy-start(s32[1,128]{1,0:T(1,128)} %param.15) | copy-start | bytes 1540
  74.8 45.5 %copy-start.2 = (bf16[1,4,3,128,256]{4,3,2,1,0:T(8,128)(2,1)}, bf16[1,4,3,128,256]{4,3,2,1,0:T(8,128)(2,1)S(1)}, u32[]{:S(2)}) copy-start(bf16[1,4,3,128,256]{4,3,2,1,0:T(8,128)(2,1)S(1)} %get-tuple-element.23) | copy-start | bytes 2359300
  74.8 21.9 %collective-permute-start.4 = (bf16[4,3,128,256]{3,2,1,0:T(8,128)(2,1)S(1)}, bf16[4,3,128,256]{3,2,1,0:T(8,128)(2,1)S(1)}, u32[]{:S(2)}, u32[]{:S(2)}) collective-permute-start(bf16[4,3,128,256]{3,2,1,0:T(8,128)(2,1)S(1)} %get-tuple-element.24), channel_id=1, source_target_pairs={{0,8},{1,9},{2,10},{3,11},{4,12},{5,13},{6,14},{7,15},{8,0},{9,1},... | collective-permute-start | bytes 2359304 | tf_op jit(solution)/shard_map/ppermute | solution.py:33
  79.6 40.6 %collective-permute-start.3 = (bf16[4,3,128,256]{3,2,1,0:T(8,128)(2,1)S(1)}, bf16[4,3,128,256]{3,2,1,0:T(8,128)(2,1)S(1)}, u32[]{:S(2)}, u32[]{:S(2)}) collective-permute-start(bf16[4,3,128,256]{3,2,1,0:T(8,128)(2,1)S(1)} %get-tuple-element.24), channel_id=1, source_target_pairs={{0,4},{1,5},{2,6},{3,7},{4,8},{5,9},{6,10},{7,11},{8,12},{9,13},{1... | collective-permute-start | bytes 2359304 | tf_op jit(solution)/shard_map/ppermute | solution.py:33
  81.9 38.4 %collective-permute-start.5 = (bf16[4,3,128,256]{3,2,1,0:T(8,128)(2,1)S(1)}, bf16[4,3,128,256]{3,2,1,0:T(8,128)(2,1)S(1)}, u32[]{:S(2)}, u32[]{:S(2)}) collective-permute-start(bf16[4,3,128,256]{3,2,1,0:T(8,128)(2,1)S(1)} %get-tuple-element.24), channel_id=1, source_target_pairs={{0,12},{1,13},{2,14},{3,15},{4,0},{5,1},{6,2},{7,3},{8,4},{9,5},{1... | collective-permute-start | bytes 2359304 | tf_op jit(solution)/shard_map/ppermute | solution.py:33
  96.8 23.5 %copy-start.5 = (bf16[4,3,128,256]{3,2,1,0:T(8,128)(2,1)}, bf16[4,3,128,256]{3,2,1,0:T(8,128)(2,1)S(1)}, u32[]{:S(2)}) copy-start(bf16[4,3,128,256]{3,2,1,0:T(8,128)(2,1)S(1)} %collective-permute-done.4) | copy-start | bytes 2359300
  120.3 0.9 copy-start.7
  120.3 1.1 copy-start.9
  131.2 1.9 copy-start.3
  131.2 2.0 copy-start.6
  131.2 2.2 copy-start.8
  131.2 2.5 copy-start.10
  180.2 3.9 copy-start.31
  202.3 38.4 %collective-permute-start.19 = (bf16[4,128,256]{2,1,0:T(8,128)(2,1)}, bf16[4,128,256]{2,1,0:T(8,128)(2,1)}, u32[]{:S(2)}, u32[]{:S(2)}) collective-permute-start(bf16[4,128,256]{2,1,0:T(8,128)(2,1)} %bitcast.243), channel_id=1, source_target_pairs={{0,8},{1,9},{2,10},{3,11},{4,12},{5,13},{6,14},{7,15},{8,0},{9,1},... | collective-permute-start | bytes 786440 | tf_op jit(solution)/shard_map/ppermute | solution.py:40
  206.0 36.7 %collective-permute-start.20 = (bf16[4,128,256]{2,1,0:T(8,128)(2,1)}, bf16[4,128,256]{2,1,0:T(8,128)(2,1)}, u32[]{:S(2)}, u32[]{:S(2)}) collective-permute-start(bf16[4,128,256]{2,1,0:T(8,128)(2,1)} %bitcast.242), channel_id=1, source_target_pairs={{0,4},{1,5},{2,6},{3,7},{4,8},{5,9},{6,10},{7,11},{8,12},{9,13},{1... | collective-permute-start | bytes 786440 | tf_op jit(solution)/shard_map/ppermute | solution.py:40
  209.1 33.5 %collective-permute-start.18 = (bf16[4,128,256]{2,1,0:T(8,128)(2,1)}, bf16[4,128,256]{2,1,0:T(8,128)(2,1)}, u32[]{:S(2)}, u32[]{:S(2)}) collective-permute-start(bf16[4,128,256]{2,1,0:T(8,128)(2,1)} %bitcast.241), channel_id=1, source_target_pairs={{0,12},{1,13},{2,14},{3,15},{4,0},{5,1},{6,2},{7,3},{8,4},{9,5},{1... | collective-permute-start | bytes 786440 | tf_op jit(solution)/shard_map/ppermute | solution.py:40
  220.2 15.6 %copy-start.17 = (bf16[128,4,128]{0,2,1:T(8,128)(2,1)}, bf16[128,4,128]{0,2,1:T(8,128)(2,1)S(1)}, u32[]{:S(2)}) copy-start(bf16[128,4,128]{0,2,1:T(8,128)(2,1)S(1)} %fusion.41) | copy-start | bytes 393220
  221.0 30.4 %collective-permute-start.8 = (bf16[128,512]{1,0:T(8,128)(2,1)}, bf16[128,512]{1,0:T(8,128)(2,1)}, u32[]{:S(2)}, u32[]{:S(2)}) collective-permute-start(bf16[128,512]{1,0:T(8,128)(2,1)} %copy.130), channel_id=1, source_target_pairs={{0,3},{1,0},{2,1},{3,2},{4,7},{5,4},{6,5},{7,6},{8,11},{9,8},{10,9... | collective-permute-start | bytes 393224 | tf_op jit(solution)/shard_map/ppermute | solution.py:32
  228.6 24.6 %collective-permute-start.7 = (bf16[128,512]{1,0:T(8,128)(2,1)}, bf16[128,512]{1,0:T(8,128)(2,1)}, u32[]{:S(2)}, u32[]{:S(2)}) collective-permute-start(bf16[128,512]{1,0:T(8,128)(2,1)} %copy.130), channel_id=1, source_target_pairs={{0,2},{1,3},{2,0},{3,1},{4,6},{5,7},{6,4},{7,5},{8,10},{9,11},{10,... | collective-permute-start | bytes 393224 | tf_op jit(solution)/shard_map/ppermute | solution.py:32
  240.7 15.6 %collective-permute-start.6 = (bf16[128,512]{1,0:T(8,128)(2,1)}, bf16[128,512]{1,0:T(8,128)(2,1)S(1)}, u32[]{:S(2)}, u32[]{:S(2)}) collective-permute-start(bf16[128,512]{1,0:T(8,128)(2,1)} %copy.130), channel_id=1, source_target_pairs={{0,1},{1,2},{2,3},{3,0},{4,5},{5,6},{6,7},{7,4},{8,9},{9,10},{10,1... | collective-permute-start | bytes 393224 | tf_op jit(solution)/shard_map/ppermute | solution.py:32
  244.1 26.7 %collective-permute-start.21 = (bf16[128,256]{1,0:T(8,128)(2,1)S(1)}, bf16[128,256]{1,0:T(8,128)(2,1)S(1)}, u32[]{:S(2)}, u32[]{:S(2)}) collective-permute-start(bf16[128,256]{1,0:T(8,128)(2,1)S(1)} %get-tuple-element.36), channel_id=1, source_target_pairs={{0,3},{1,0},{2,1},{3,2},{4,7},{5,4},{6,5},{7,6},{8,11},{9,8},{10,9... | collective-permute-start | bytes 196616 | tf_op jit(solution)/shard_map/ppermute | solution.py:43
  257.4 78.2 %copy-start.11 = (bf16[1,4,128,512]{3,2,1,0:T(8,128)(2,1)}, bf16[1,4,128,512]{3,2,1,0:T(8,128)(2,1)S(1)}, u32[]{:S(2)}) copy-start(bf16[1,4,128,512]{3,2,1,0:T(8,128)(2,1)S(1)} %get-tuple-element.31) | copy-start | bytes 1572868
  257.5 76.2 %collective-permute-start.10 = (bf16[4,128,512]{2,1,0:T(8,128)(2,1)S(1)}, bf16[4,128,512]{2,1,0:T(8,128)(2,1)S(1)}, u32[]{:S(2)}, u32[]{:S(2)}) collective-permute-start(bf16[4,128,512]{2,1,0:T(8,128)(2,1)S(1)} %get-tuple-element.32), channel_id=1, source_target_pairs={{0,8},{1,9},{2,10},{3,11},{4,12},{5,13},{6,14},{7,15},{8,0},{9,1},... | collective-permute-start | bytes 1572872 | tf_op jit(solution)/shard_map/ppermute | solution.py:33
  259.4 76.2 %collective-permute-start.9 = (bf16[4,128,512]{2,1,0:T(8,128)(2,1)S(1)}, bf16[4,128,512]{2,1,0:T(8,128)(2,1)S(1)}, u32[]{:S(2)}, u32[]{:S(2)}) collective-permute-start(bf16[4,128,512]{2,1,0:T(8,128)(2,1)S(1)} %get-tuple-element.32), channel_id=1, source_target_pairs={{0,4},{1,5},{2,6},{3,7},{4,8},{5,9},{6,10},{7,11},{8,12},{9,13},{1... | collective-permute-start | bytes 1572872 | tf_op jit(solution)/shard_map/ppermute | solution.py:33
  262.0 73.6 %collective-permute-start.11 = (bf16[4,128,512]{2,1,0:T(8,128)(2,1)S(1)}, bf16[4,128,512]{2,1,0:T(8,128)(2,1)S(1)}, u32[]{:S(2)}, u32[]{:S(2)}) collective-permute-start(bf16[4,128,512]{2,1,0:T(8,128)(2,1)S(1)} %get-tuple-element.32), channel_id=1, source_target_pairs={{0,12},{1,13},{2,14},{3,15},{4,0},{5,1},{6,2},{7,3},{8,4},{9,5},{1... | collective-permute-start | bytes 1572872 | tf_op jit(solution)/shard_map/ppermute | solution.py:33
  265.9 12.4 %collective-permute-start.23 = (bf16[128,256]{1,0:T(8,128)(2,1)S(1)}, bf16[128,256]{1,0:T(8,128)(2,1)S(1)}, u32[]{:S(2)}, u32[]{:S(2)}) collective-permute-start(bf16[128,256]{1,0:T(8,128)(2,1)S(1)} %get-tuple-element.37), channel_id=1, source_target_pairs={{0,1},{1,2},{2,3},{3,0},{4,5},{5,6},{6,7},{7,4},{8,9},{9,10},{10,1... | collective-permute-start | bytes 196616 | tf_op jit(solution)/shard_map/ppermute | solution.py:43
  270.8 17.8 %copy-start.13 = (bf16[4,128,256]{2,1,0:T(8,128)(2,1)S(1)}, bf16[4,128,256]{2,1,0:T(8,128)(2,1)}, u32[]{:S(2)}) copy-start(bf16[4,128,256]{2,1,0:T(8,128)(2,1)} %get-tuple-element.9) | copy-start | bytes 786436
  270.8 17.8 %copy-start.14 = (bf16[4,128,256]{2,1,0:T(8,128)(2,1)S(1)}, bf16[4,128,256]{2,1,0:T(8,128)(2,1)}, u32[]{:S(2)}) copy-start(bf16[4,128,256]{2,1,0:T(8,128)(2,1)} %get-tuple-element.10) | copy-start | bytes 786436
  270.8 17.8 %copy-start.15 = (bf16[4,128,256]{2,1,0:T(8,128)(2,1)S(1)}, bf16[4,128,256]{2,1,0:T(8,128)(2,1)}, u32[]{:S(2)}) copy-start(bf16[4,128,256]{2,1,0:T(8,128)(2,1)} %get-tuple-element.11) | copy-start | bytes 786436
  270.8 17.8 %collective-permute-start.22 = (bf16[128,256]{1,0:T(8,128)(2,1)S(1)}, bf16[128,256]{1,0:T(8,128)(2,1)S(1)}, u32[]{:S(2)}, u32[]{:S(2)}) collective-permute-start(bf16[128,256]{1,0:T(8,128)(2,1)S(1)} %get-tuple-element.38), channel_id=1, source_target_pairs={{0,2},{1,3},{2,0},{3,1},{4,6},{5,7},{6,4},{7,5},{8,10},{9,11},{10,... | collective-permute-start | bytes 196616 | tf_op jit(solution)/shard_map/ppermute | solution.py:43
  288.7 54.5 %collective-permute-start.25 = (bf16[5,128,256]{2,1,0:T(8,128)(2,1)S(1)}, bf16[5,128,256]{2,1,0:T(8,128)(2,1)S(1)}, u32[]{:S(2)}, u32[]{:S(2)}) collective-permute-start(bf16[5,128,256]{2,1,0:T(8,128)(2,1)S(1)} %get-tuple-element.42), channel_id=1, source_target_pairs={{0,1},{1,2},{2,3},{3,0},{4,5},{5,6},{6,7},{7,4},{8,9},{9,10},{10,1... | collective-permute-start | bytes 983048 | tf_op jit(solution)/shard_map/ppermute | solution.py:54
  326.2 41.4 %collective-permute-start.26 = (bf16[5,128,256]{2,1,0:T(8,128)(2,1)S(1)}, bf16[5,128,256]{2,1,0:T(8,128)(2,1)S(1)}, u32[]{:S(2)}, u32[]{:S(2)}) collective-permute-start(bf16[5,128,256]{2,1,0:T(8,128)(2,1)S(1)} %get-tuple-element.43), channel_id=1, source_target_pairs={{0,2},{1,3},{2,0},{3,1},{4,6},{5,7},{6,4},{7,5},{8,10},{9,11},{10,... | collective-permute-start | bytes 983048 | tf_op jit(solution)/shard_map/ppermute | solution.py:54
  333.7 2.3 copy-start.18
  333.7 34.0 %collective-permute-start.27 = (bf16[5,128,256]{2,1,0:T(8,128)(2,1)S(1)}, bf16[5,128,256]{2,1,0:T(8,128)(2,1)S(1)}, u32[]{:S(2)}, u32[]{:S(2)}) collective-permute-start(bf16[5,128,256]{2,1,0:T(8,128)(2,1)S(1)} %get-tuple-element.44), channel_id=1, source_target_pairs={{0,3},{1,0},{2,1},{3,2},{4,7},{5,4},{6,5},{7,6},{8,11},{9,8},{10,9... | collective-permute-start | bytes 983048 | tf_op jit(solution)/shard_map/ppermute | solution.py:54
  335.6 1.0 copy-start.22
  335.6 1.3 copy-start.28
  337.8 30.2 %collective-permute-start.14 = (bf16[4,128,256]{2,1,0:T(8,128)(2,1)S(1)}, bf16[4,128,256]{2,1,0:T(8,128)(2,1)S(1)}, u32[]{:S(2)}, u32[]{:S(2)}) collective-permute-start(bf16[4,128,256]{2,1,0:T(8,128)(2,1)S(1)} %bitcast.248), channel_id=1, source_target_pairs={{0,4},{1,5},{2,6},{3,7},{4,8},{5,9},{6,10},{7,11},{8,12},{9,13},{1... | collective-permute-start | bytes 786440 | tf_op jit(solution)/shard_map/ppermute | solution.py:72
  339.7 28.2 %collective-permute-start.13 = (bf16[4,128,256]{2,1,0:T(8,128)(2,1)S(1)}, bf16[4,128,256]{2,1,0:T(8,128)(2,1)S(1)}, u32[]{:S(2)}, u32[]{:S(2)}) collective-permute-start(bf16[4,128,256]{2,1,0:T(8,128)(2,1)S(1)} %bitcast.246), channel_id=1, source_target_pairs={{0,8},{1,9},{2,10},{3,11},{4,12},{5,13},{6,14},{7,15},{8,0},{9,1},... | collective-permute-start | bytes 786440 | tf_op jit(solution)/shard_map/ppermute | solution.py:72
  343.3 24.6 %collective-permute-start.12 = (bf16[4,128,256]{2,1,0:T(8,128)(2,1)S(1)}, bf16[4,128,256]{2,1,0:T(8,128)(2,1)S(1)}, u32[]{:S(2)}, u32[]{:S(2)}) collective-permute-start(bf16[4,128,256]{2,1,0:T(8,128)(2,1)S(1)} %bitcast.244), channel_id=1, source_target_pairs={{0,12},{1,13},{2,14},{3,15},{4,0},{5,1},{6,2},{7,3},{8,4},{9,5},{1... | collective-permute-start | bytes 786440 | tf_op jit(solution)/shard_map/ppermute | solution.py:72
  368.2 24.4 %collective-permute-start.17 = (bf16[4,128,256]{2,1,0:T(8,128)(2,1)S(1)}, bf16[4,128,256]{2,1,0:T(8,128)(2,1)S(1)}, u32[]{:S(2)}, u32[]{:S(2)}) collective-permute-start(bf16[4,128,256]{2,1,0:T(8,128)(2,1)S(1)} %get-tuple-element.15), channel_id=1, source_target_pairs={{0,1},{1,2},{2,3},{3,0},{4,5},{5,6},{6,7},{7,4},{8,9},{9,10},{10,1... | collective-permute-start | bytes 786440 | tf_op jit(solution)/shard_map/ppermute | solution.py:76
  370.1 26.4 %collective-permute-start.15 = (bf16[4,128,256]{2,1,0:T(8,128)(2,1)S(1)}, bf16[4,128,256]{2,1,0:T(8,128)(2,1)S(1)}, u32[]{:S(2)}, u32[]{:S(2)}) collective-permute-start(bf16[4,128,256]{2,1,0:T(8,128)(2,1)S(1)} %get-tuple-element.16), channel_id=1, source_target_pairs={{0,3},{1,0},{2,1},{3,2},{4,7},{5,4},{6,5},{7,6},{8,11},{9,8},{10,9... | collective-permute-start | bytes 786440 | tf_op jit(solution)/shard_map/ppermute | solution.py:76
  377.4 24.2 %collective-permute-start.16 = (bf16[4,128,256]{2,1,0:T(8,128)(2,1)S(1)}, bf16[4,128,256]{2,1,0:T(8,128)(2,1)S(1)}, u32[]{:S(2)}, u32[]{:S(2)}) collective-permute-start(bf16[4,128,256]{2,1,0:T(8,128)(2,1)S(1)} %get-tuple-element.18), channel_id=1, source_target_pairs={{0,2},{1,3},{2,0},{3,1},{4,6},{5,7},{6,4},{7,5},{8,10},{9,11},{10,... | collective-permute-start | bytes 786440 | tf_op jit(solution)/shard_map/ppermute | solution.py:76
  384.2 30.3 %collective-permute-start.28 = (bf16[8,128,256]{2,1,0:T(8,128)(2,1)}, bf16[8,128,256]{2,1,0:T(8,128)(2,1)}, u32[]{:S(2)}, u32[]{:S(2)}) collective-permute-start(bf16[8,128,256]{2,1,0:T(8,128)(2,1)} %get-tuple-element.33), channel_id=1, source_target_pairs={{0,4},{1,5},{2,6},{3,7},{4,8},{5,9},{6,10},{7,11},{8,12},{9,13},{1... | collective-permute-start | bytes 1572872 | tf_op jit(solution)/shard_map/ppermute | solution.py:61
  388.8 26.8 %collective-permute-start.29 = (bf16[8,128,256]{2,1,0:T(8,128)(2,1)}, bf16[8,128,256]{2,1,0:T(8,128)(2,1)}, u32[]{:S(2)}, u32[]{:S(2)}) collective-permute-start(bf16[8,128,256]{2,1,0:T(8,128)(2,1)} %get-tuple-element.34), channel_id=1, source_target_pairs={{0,8},{1,9},{2,10},{3,11},{4,12},{5,13},{6,14},{7,15},{8,0},{9,1},... | collective-permute-start | bytes 1572872 | tf_op jit(solution)/shard_map/ppermute | solution.py:61
  392.5 24.3 %collective-permute-start.30 = (bf16[8,128,256]{2,1,0:T(8,128)(2,1)}, bf16[8,128,256]{2,1,0:T(8,128)(2,1)}, u32[]{:S(2)}, u32[]{:S(2)}) collective-permute-start(bf16[8,128,256]{2,1,0:T(8,128)(2,1)} %get-tuple-element.35), channel_id=1, source_target_pairs={{0,12},{1,13},{2,14},{3,15},{4,0},{5,1},{6,2},{7,3},{8,4},{9,5},{1... | collective-permute-start | bytes 1572872 | tf_op jit(solution)/shard_map/ppermute | solution.py:61
  405.8 3.4 copy-start.1
  405.8 3.4 copy-start.27
  409.2 2.6 copy-start.4
  412.6 24.8 %collective-permute-start.24 = (bf16[128,4096]{1,0:T(8,128)(2,1)S(1)}, bf16[128,4096]{1,0:T(8,128)(2,1)S(1)}, u32[]{:S(2)}, u32[]{:S(2)}) collective-permute-start(bf16[128,4096]{1,0:T(8,128)(2,1)S(1)} %add_convert_fusion), channel_id=1, source_target_pairs={{0,16},{16,32},{32,48},{48,64},{64,80},{80,96},{96,112},{112,128},... | collective-permute-start | bytes 3145736 | tf_op jit(solution)/shard_map/ppermute | solution.py:14
  415.6 2.5 copy-start.12
  415.6 2.5 copy-start.19
  415.6 2.5 copy-start.21
  415.6 2.5 copy-start.23
  415.6 2.5 copy-start.25
  418.1 18.4 %copy-start.24 = (bf16[1,256,768]{2,1,0:T(8,128)(2,1)S(1)}, bf16[1,256,768]{2,1,0:T(8,128)(2,1)}, u32[]{:S(2)}) copy-start(bf16[1,256,768]{2,1,0:T(8,128)(2,1)} %param.14) | copy-start | bytes 1179652
  419.2 17.3 %collective-permute-start.31 = (bf16[256,768]{1,0:T(8,128)(2,1)S(1)}, bf16[256,768]{1,0:T(8,128)(2,1)S(1)}, u32[]{:S(2)}, u32[]{:S(2)}) collective-permute-start(bf16[256,768]{1,0:T(8,128)(2,1)S(1)} %fusion.35), channel_id=1, source_target_pairs={{0,496},{16,480},{32,464},{48,448},{64,432},{80,416},{96,400},{112... | collective-permute-start | bytes 1179656 | tf_op jit(solution)/shard_map/ppermute | solution.py:19
  (1 other events, 0.8 us)
Sparse Core Ops, SparseCore 0:
  11.0 163.4 all-gather.2

commit v9 on v8

--- a/solution.py
+++ b/solution.py
@@ -121,17 +121,8 @@
     unit_up, inverse_up, normed_up = normalize(up_activation[0], upward_gain[0])
     hidden = normed_up.astype(jnp.bfloat16)
     output_weight = lax.all_gather(up_output_weight[0], "seq", axis=1, tiled=True)
-    pieces = hidden.shape[1] // size
-    kv_weight = up_input_weight[0][:, width:]
-    riders = jnp.concatenate(
-        [saved[None, :, width:], kv_weight.reshape(-1, count, pieces)]
-    )
-    gathered = gather_blocks(riders)
-    key_value = gathered[:, :, 0].reshape(size * count, 2 * HEAD)
-    kv_weight_all = gathered[:, :, 1:]
-    kv_weight_all = jnp.take(kv_weight_all, (o - jnp.arange(outer)) % outer, axis=0)
-    kv_weight_all = jnp.take(kv_weight_all, (i - jnp.arange(INNER)) % INNER, axis=1)
-    kv_weight_all = kv_weight_all.reshape(-1, 2 * HEAD)
+    key_value = gather_blocks(saved[:, width:]).reshape(size * count, 2 * HEAD)
+    kv_weight_all = lax.all_gather(up_input_weight[0][:, width:], "seq", axis=0, tiled=True)
     keys = key_value[:, :HEAD]
     values = key_value[:, HEAD:]
     sources = (

time: 450 us -> 439 us (0.976)
  waiting for transfers between devices: 154 us -> 186 us
  local copies, waits for them, and re-layouts: 39.9 us -> 22.6 us
  starting transfers between devices: 175 us -> 159 us
  other arithmetic: 24.7 us -> 18.5 us
    all_gather x1, waiting for transfers between devices: 34.8 us -> 84.6 us  [per_device(): lax.all_gather(up_output_weight[0], 'seq', axis=1, tiled=True)]
    ppermute x3, starting transfers between devices: 46.8 us -> 14.1 us  [gather_and_scatter(): lax.ppermute(jnp.concatenate([x, piece]), 'seq', seq_pairs(k, 0))]
    ppermute x6, waiting for transfers between devices: 33 us -> 6.46 us  [gather_blocks(): lax.ppermute(first, 'seq', seq_pairs(k, 1))]
    ppermute x6, waiting for transfers between devices: 34.5 us -> 12.6 us  [gather_blocks(): lax.ppermute(x, 'seq', seq_pairs(k, 0))]
    ppermute x3, waiting for transfers between devices: 10.3 us -> 22.4 us  [reduce_blocks(): lax.ppermute(acc[k].astype(wire), 'seq', seq_pairs(INNER - k, 0))]
    ppermute x3, waiting for transfers between devices: 20.5 us -> 31 us  [gather_and_scatter(): lax.ppermute(jnp.concatenate([x, piece]), 'seq', seq_pairs(k, 0))]
    gather x3 -> x0, local copies, waits for them, and re-layouts: 7.79 us -> none  [the longest x2 5.52 us: per_device(): jnp.take(kv_weight_all, (i - jnp.arange(INNER)) % INNER, axis=1)]
    ppermute x3, waiting for transfers between devices: 5.03 us -> 12.8 us  [gather_columns(): second.append(lax.ppermute(first[k], 'seq', seq_pairs(INNER - k, 0)))]
  transfers between devices with their start and end apart: 33 -> 34, of which waited for: 11 -> 12; matrix products, arithmetic and copies ran while one was open for 15% -> 17% of each run, Pallas kernels for 0% -> 0%
where the time goes in v9:
time: 439 us; the launch traced here: 434 us
  waiting for transfers between devices  186 us (42%)
  starting transfers between devices  159 us (36%)
  matrix products  32.8 us (7%)
  local copies, waits for them, and re-layouts  22.6 us (5%)
  other arithmetic  18.5 us (4%)
  between operations  15.1 us (3%)
    all_gather x1, waiting for transfers between devices, per_device(): lax.all_gather(up_output_weight[0], 'seq', axis=1, tiled=True)  84.6 us
    ppermute x6, starting transfers between devices, gather_blocks(): lax.ppermute(x, 'seq', seq_pairs(k, 0))  40.8 us
    ppermute x3, waiting for transfers between devices, gather_and_scatter(): lax.ppermute(jnp.concatenate([x, piece]), 'seq', seq_pairs(k, 0))  31 us
    ppermute x3, waiting for transfers between devices, reduce_blocks(): lax.ppermute(acc[k].astype(wire), 'seq', seq_pairs(INNER - k, 0))  22.4 us
    ppermute x3, starting transfers between devices, reduce_blocks(): lax.ppermute(acc[k].astype(wire), 'seq', seq_pairs(INNER - k, 0))  21.4 us
    ppermute x6, starting transfers between devices, gather_blocks(): lax.ppermute(first, 'seq', seq_pairs(k, 1))  20.2 us
    ppermute x3, starting transfers between devices, gather_and_scatter(): second.append(lax.ppermute(payload, 'seq', seq_pairs(k, 1)))  18.4 us
    ppermute x3, starting transfers between devices, gather_columns(): second.append(lax.ppermute(first[k], 'seq', seq_pairs(INNER - k, 0)))  15.6 us
  transfers between devices with their start and end apart: 34, of which 12 were waited for; matrix products, arithmetic and copies ran while one was open for 17% of the time, Pallas kernels for 0%

profile of v9, /device:TPU:25, one launch (start us, length us, event | category | flops | bytes accessed | tf_op | source)
XLA Modules:
  0.0 433.8 jit_solution(3843633651568549297)
XLA Ops:
  8.0 1.1 copy.40
  9.1 8.8 %collective-permute-start = (bf16[128,256]{0,1:T(8,128)(2,1)S(1)}, bf16[128,256]{0,1:T(8,128)(2,1)S(1)}, u32[]{:S(2)}, u32[]{:S(2)}) collective-permute-start(bf16[128,256]{0,1:T(8,128)(2,1)S(1)} %get-tuple-element.40), channel_id=1, source_target_pairs={{0,1},{1,2},{2,3},{3,0},{4,5},{5,6},{6,7},{7,4},{8,9},{9,10},{10,1... | collective-permute-start | bytes 196616 | tf_op jit(solution)/shard_map/ppermute | solution.py:32
  17.9 10.6 %collective-permute-start.1 = (bf16[128,256]{0,1:T(8,128)(2,1)S(1)}, bf16[128,256]{0,1:T(8,128)(2,1)S(1)}, u32[]{:S(2)}, u32[]{:S(2)}) collective-permute-start(bf16[128,256]{0,1:T(8,128)(2,1)S(1)} %get-tuple-element.40), channel_id=1, source_target_pairs={{0,2},{1,3},{2,0},{3,1},{4,6},{5,7},{6,4},{7,5},{8,10},{9,11},{10,... | collective-permute-start | bytes 196616 | tf_op jit(solution)/shard_map/ppermute | solution.py:32
  28.5 5.2 %collective-permute-start.2 = (bf16[128,256]{0,1:T(8,128)(2,1)S(1)}, bf16[128,256]{0,1:T(8,128)(2,1)S(1)}, u32[]{:S(2)}, u32[]{:S(2)}) collective-permute-start(bf16[128,256]{0,1:T(8,128)(2,1)S(1)} %get-tuple-element.40), channel_id=1, source_target_pairs={{0,3},{1,0},{2,1},{3,2},{4,7},{5,4},{6,5},{7,6},{8,11},{9,8},{10,9... | collective-permute-start | bytes 196616 | tf_op jit(solution)/shard_map/ppermute | solution.py:32
  33.7 1.6 slice.156
  35.7 12.5 %collective-permute-done.2 = bf16[128,256]{0,1:T(8,128)(2,1)S(1)} collective-permute-done((bf16[128,256]{0,1:T(8,128)(2,1)S(1)}, bf16[128,256]{0,1:T(8,128)(2,1)S(1)}, u32[]{:S(2)}, u32[]{:S(2)}) %collective-permute-start.2) | collective-permute-done | bytes 65568 | tf_op jit(solution)/shard_map/ppermute | solution.py:32
  48.2 3.1 collective-permute-start.3
  51.4 4.4 %collective-permute-start.4 = (bf16[4,128,256]{1,2,0:T(8,128)(2,1)S(1)}, bf16[4,128,256]{1,2,0:T(8,128)(2,1)S(1)}, u32[]{:S(2)}, u32[]{:S(2)}) collective-permute-start(bf16[4,128,256]{1,2,0:T(8,128)(2,1)S(1)} %get-tuple-element.38), channel_id=1, source_target_pairs={{0,8},{1,9},{2,10},{3,11},{4,12},{5,13},{6,14},{7,15},{8,0},{9,1},... | collective-permute-start | bytes 786440 | tf_op jit(solution)/shard_map/ppermute | solution.py:33
  55.7 3.1 collective-permute-start.5
  60.0 5.3 %collective-permute-done.4 = bf16[4,128,256]{1,2,0:T(8,128)(2,1)S(1)} collective-permute-done((bf16[4,128,256]{1,2,0:T(8,128)(2,1)S(1)}, bf16[4,128,256]{1,2,0:T(8,128)(2,1)S(1)}, u32[]{:S(2)}, u32[]{:S(2)}) %collective-permute-start.4) | collective-permute-done | bytes 262176 | tf_op jit(solution)/shard_map/ppermute | solution.py:33
  65.2 1.2 collective-permute-done.5
  67.1 3.8 fusion.88
  70.9 84.6 %all-gather.6.cloned.1.call-done = bf16[1,512,4096]{2,1,0:T(8,128)(2,1)} async-done(((bf16[1,512,256]{2,1,0:T(8,128)(2,1)}), bf16[1,512,4096]{2,1,0:T(8,128)(2,1)}) %all-gather.6.cloned.1.call-update) | async-done | bytes 4194320 | tf_op jit(solution)/shard_map/all_gather | solution.py:123
  155.5 3.7 fusion.38
  159.4 2.8 fusion.64
  163.8 7.6 %convolution_bitcast_fusion.1 = f32[2048,128]{0,1:T(8,128)S(1)} fusion(bf16[128,4,128]{0,2,1:T(8,128)(2,1)S(1)} %bitcast.230, f32[128,4,2048]{0,2,1:T(8,128)} %fusion.64, f32[128,4,2048]{0,2,1:T(8,128)} %get-tuple-element.46, f32[128,4]{0,1:T(4,128)S(1)} %get-tuple-element.45), kind=kOutput, calls=%fused_computation.27 | convolution fusion | flops 275778048 | bytes 9570304 | tf_op jit(solution)/shard_map/tgj,tgh->jh/dot_general | solution.py:155
  171.4 7.8 %fusion.41 = bf16[128,4,128]{0,2,1:T(8,128)(2,1)S(1)} fusion(f32[128,4,2048]{0,2,1:T(8,128)} %fusion.64, bf16[2048,256]{1,0:T(8,128)(2,1)} %bitcast.196, f32[128,4,2048]{0,2,1:T(8,128)} %get-tuple-element.46, f32[128,4]{0,1:T(4,128)S(1)} %get-tuple-element.45), kind=kOutput, calls=%fused_computation.59 | convolution fusion | flops 275843584 | bytes 17436672 | tf_op jit(solution)/shard_map/tgj,jh->tgh/dot_general | solution.py:151
  179.9 7.2 %collective-permute-start.6 = (bf16[128,512]{1,0:T(8,128)(2,1)}, bf16[128,512]{1,0:T(8,128)(2,1)S(1)}, u32[]{:S(2)}, u32[]{:S(2)}) collective-permute-start(bf16[128,512]{1,0:T(8,128)(2,1)} %copy.48), channel_id=1, source_target_pairs={{0,1},{1,2},{2,3},{3,0},{4,5},{5,6},{6,7},{7,4},{8,9},{9,10},{10,1... | collective-permute-start | bytes 393224 | tf_op jit(solution)/shard_map/ppermute | solution.py:32
  187.2 6.8 %collective-permute-start.7 = (bf16[128,512]{1,0:T(8,128)(2,1)}, bf16[128,512]{1,0:T(8,128)(2,1)}, u32[]{:S(2)}, u32[]{:S(2)}) collective-permute-start(bf16[128,512]{1,0:T(8,128)(2,1)} %copy.48), channel_id=1, source_target_pairs={{0,2},{1,3},{2,0},{3,1},{4,6},{5,7},{6,4},{7,5},{8,10},{9,11},{10,... | collective-permute-start | bytes 393224 | tf_op jit(solution)/shard_map/ppermute | solution.py:32
  193.9 2.2 collective-permute-start.8
  197.2 5.5 %collective-permute-start.18 = (bf16[4,128,256]{2,1,0:T(8,128)(2,1)}, bf16[4,128,256]{2,1,0:T(8,128)(2,1)}, u32[]{:S(2)}, u32[]{:S(2)}) collective-permute-start(bf16[4,128,256]{2,1,0:T(8,128)(2,1)} %bitcast.49), channel_id=1, source_target_pairs={{0,12},{1,13},{2,14},{3,15},{4,0},{5,1},{6,2},{7,3},{8,4},{9,5},{1... | collective-permute-start | bytes 786440 | tf_op jit(solution)/shard_map/ppermute | solution.py:40
  203.6 2.5 collective-permute-start.19
  206.9 2.5 collective-permute-start.20
  209.9 1.7 reshape.212
  213.5 1.9 fusion.63
  215.3 2.0 copy.81
  217.5 2.0 fusion.84
  219.5 3.4 collective-permute-start.9
  222.9 3.7 collective-permute-start.10
  226.6 2.5 collective-permute-start.11
  229.2 2.2 fusion.85
  231.4 6.1 %collective-permute-start.21 = (bf16[128,256]{1,0:T(8,128)(2,1)S(1)}, bf16[128,256]{1,0:T(8,128)(2,1)S(1)}, u32[]{:S(2)}, u32[]{:S(2)}) collective-permute-start(bf16[128,256]{1,0:T(8,128)(2,1)S(1)} %get-tuple-element.34), channel_id=1, source_target_pairs={{0,3},{1,0},{2,1},{3,2},{4,7},{5,4},{6,5},{7,6},{8,11},{9,8},{10,9... | collective-permute-start | bytes 196616 | tf_op jit(solution)/shard_map/ppermute | solution.py:43
  237.5 2.2 fusion.22
  239.7 8.4 %collective-permute-start.22 = (bf16[128,256]{1,0:T(8,128)(2,1)S(1)}, bf16[128,256]{1,0:T(8,128)(2,1)S(1)}, u32[]{:S(2)}, u32[]{:S(2)}) collective-permute-start(bf16[128,256]{1,0:T(8,128)(2,1)S(1)} %get-tuple-element.36), channel_id=1, source_target_pairs={{0,2},{1,3},{2,0},{3,1},{4,6},{5,7},{6,4},{7,5},{8,10},{9,11},{10,... | collective-permute-start | bytes 196616 | tf_op jit(solution)/shard_map/ppermute | solution.py:43
  248.1 15.6 %collective-permute-done.21 = bf16[128,256]{1,0:T(8,128)(2,1)S(1)} collective-permute-done((bf16[128,256]{1,0:T(8,128)(2,1)S(1)}, bf16[128,256]{1,0:T(8,128)(2,1)S(1)}, u32[]{:S(2)}, u32[]{:S(2)}) %collective-permute-start.21) | collective-permute-done | bytes 65568 | tf_op jit(solution)/shard_map/ppermute | solution.py:43
  263.7 7.0 %collective-permute-start.23 = (bf16[128,256]{1,0:T(8,128)(2,1)S(1)}, bf16[128,256]{1,0:T(8,128)(2,1)S(1)}, u32[]{:S(2)}, u32[]{:S(2)}) collective-permute-start(bf16[128,256]{1,0:T(8,128)(2,1)S(1)} %get-tuple-element.35), channel_id=1, source_target_pairs={{0,1},{1,2},{2,3},{3,0},{4,5},{5,6},{6,7},{7,4},{8,9},{9,10},{10,1... | collective-permute-start | bytes 196616 | tf_op jit(solution)/shard_map/ppermute | solution.py:43
  270.6 1.3 dynamic-slice_bitcast_fusion.6
  272.0 5.6 %collective-permute-done.22 = bf16[128,256]{1,0:T(8,128)(2,1)S(1)} collective-permute-done((bf16[128,256]{1,0:T(8,128)(2,1)S(1)}, bf16[128,256]{1,0:T(8,128)(2,1)S(1)}, u32[]{:S(2)}, u32[]{:S(2)}) %collective-permute-start.22) | collective-permute-done | bytes 65568 | tf_op jit(solution)/shard_map/ppermute | solution.py:43
  277.6 1.2 collective-permute-done.23
  279.9 4.7 %collective-permute-start.25 = (bf16[5,128,256]{2,1,0:T(8,128)(2,1)S(1)}, bf16[5,128,256]{2,1,0:T(8,128)(2,1)S(1)}, u32[]{:S(2)}, u32[]{:S(2)}) collective-permute-start(bf16[5,128,256]{2,1,0:T(8,128)(2,1)S(1)} %get-tuple-element.42), channel_id=1, source_target_pairs={{0,1},{1,2},{2,3},{3,0},{4,5},{5,6},{6,7},{7,4},{8,9},{9,10},{10,1... | collective-permute-start | bytes 983048 | tf_op jit(solution)/shard_map/ppermute | solution.py:54
  284.6 7.4 %collective-permute-start.26 = (bf16[5,128,256]{2,1,0:T(8,128)(2,1)S(1)}, bf16[5,128,256]{2,1,0:T(8,128)(2,1)S(1)}, u32[]{:S(2)}, u32[]{:S(2)}) collective-permute-start(bf16[5,128,256]{2,1,0:T(8,128)(2,1)S(1)} %get-tuple-element.43), channel_id=1, source_target_pairs={{0,2},{1,3},{2,0},{3,1},{4,6},{5,7},{6,4},{7,5},{8,10},{9,11},{10,... | collective-permute-start | bytes 983048 | tf_op jit(solution)/shard_map/ppermute | solution.py:54
  292.0 2.0 collective-permute-start.27
  294.0 1.7 pad_maximum_fusion.1
  296.6 9.5 %collective-permute-start.12 = (bf16[4,128,256]{2,1,0:T(8,128)(2,1)S(1)}, bf16[4,128,256]{2,1,0:T(8,128)(2,1)S(1)}, u32[]{:S(2)}, u32[]{:S(2)}) collective-permute-start(bf16[4,128,256]{2,1,0:T(8,128)(2,1)S(1)} %bitcast.223), channel_id=1, source_target_pairs={{0,12},{1,13},{2,14},{3,15},{4,0},{5,1},{6,2},{7,3},{8,4},{9,5},{1... | collective-permute-start | bytes 786440 | tf_op jit(solution)/shard_map/ppermute | solution.py:72
  306.1 2.8 collective-permute-start.13
  308.9 14.2 %collective-permute-done.25 = bf16[5,128,256]{2,1,0:T(8,128)(2,1)S(1)} collective-permute-done((bf16[5,128,256]{2,1,0:T(8,128)(2,1)S(1)}, bf16[5,128,256]{2,1,0:T(8,128)(2,1)S(1)}, u32[]{:S(2)}, u32[]{:S(2)}) %collective-permute-start.25) | collective-permute-done | bytes 327712 | tf_op jit(solution)/shard_map/ppermute | solution.py:54
  323.1 1.9 collective-permute-start.14
  325.0 16.8 %collective-permute-done.26 = bf16[5,128,256]{2,1,0:T(8,128)(2,1)S(1)} collective-permute-done((bf16[5,128,256]{2,1,0:T(8,128)(2,1)S(1)}, bf16[5,128,256]{2,1,0:T(8,128)(2,1)S(1)}, u32[]{:S(2)}, u32[]{:S(2)}) %collective-permute-start.26) | collective-permute-done | bytes 327712 | tf_op jit(solution)/shard_map/ppermute | solution.py:54
  342.4 1.9 collective-permute-start.15
  344.3 6.4 %collective-permute-start.16 = (bf16[4,128,256]{2,1,0:T(8,128)(2,1)S(1)}, bf16[4,128,256]{2,1,0:T(8,128)(2,1)S(1)}, u32[]{:S(2)}, u32[]{:S(2)}) collective-permute-start(bf16[4,128,256]{2,1,0:T(8,128)(2,1)S(1)} %get-tuple-element.18), channel_id=1, source_target_pairs={{0,2},{1,3},{2,0},{3,1},{4,6},{5,7},{6,4},{7,5},{8,10},{9,11},{10,... | collective-permute-start | bytes 786440 | tf_op jit(solution)/shard_map/ppermute | solution.py:76
  350.7 7.3 %collective-permute-start.17 = (bf16[4,128,256]{2,1,0:T(8,128)(2,1)S(1)}, bf16[4,128,256]{2,1,0:T(8,128)(2,1)S(1)}, u32[]{:S(2)}, u32[]{:S(2)}) collective-permute-start(bf16[4,128,256]{2,1,0:T(8,128)(2,1)S(1)} %get-tuple-element.15), channel_id=1, source_target_pairs={{0,1},{1,2},{2,3},{3,0},{4,5},{5,6},{6,7},{7,4},{8,9},{9,10},{10,1... | collective-permute-start | bytes 786440 | tf_op jit(solution)/shard_map/ppermute | solution.py:76
  358.7 1.2 pad_maximum_fusion.7
  359.9 11.7 %collective-permute-start.28 = (bf16[8,128,256]{2,1,0:T(8,128)(2,1)}, bf16[8,128,256]{2,1,0:T(8,128)(2,1)}, u32[]{:S(2)}, u32[]{:S(2)}) collective-permute-start(bf16[8,128,256]{2,1,0:T(8,128)(2,1)} %get-tuple-element.31), channel_id=1, source_target_pairs={{0,4},{1,5},{2,6},{3,7},{4,8},{5,9},{6,10},{7,11},{8,12},{9,13},{1... | collective-permute-start | bytes 1572872 | tf_op jit(solution)/shard_map/ppermute | solution.py:61
  371.6 1.9 collective-permute-start.29
  373.6 4.8 %collective-permute-start.30 = (bf16[8,128,256]{2,1,0:T(8,128)(2,1)}, bf16[8,128,256]{2,1,0:T(8,128)(2,1)}, u32[]{:S(2)}, u32[]{:S(2)}) collective-permute-start(bf16[8,128,256]{2,1,0:T(8,128)(2,1)} %get-tuple-element.33), channel_id=1, source_target_pairs={{0,12},{1,13},{2,14},{3,15},{4,0},{5,1},{6,2},{7,3},{8,4},{9,5},{1... | collective-permute-start | bytes 1572872 | tf_op jit(solution)/shard_map/ppermute | solution.py:61
  378.4 12.8 %collective-permute-done.17 = bf16[4,128,256]{2,1,0:T(8,128)(2,1)S(1)} collective-permute-done((bf16[4,128,256]{2,1,0:T(8,128)(2,1)S(1)}, bf16[4,128,256]{2,1,0:T(8,128)(2,1)S(1)}, u32[]{:S(2)}, u32[]{:S(2)}) %collective-permute-start.17) | collective-permute-done | bytes 262176 | tf_op jit(solution)/shard_map/ppermute | solution.py:76
  392.7 1.4 copy.55
  394.1 2.1 reshape.210
  396.2 3.2 multiply_reduce_fusion.1
  400.1 1.9 collective-permute-start.24
  403.2 1.1 slice_bitcast_fusion.13
  405.6 2.4 fusion.35
  408.0 1.9 collective-permute-start.31
  409.9 15.3 %collective-permute-done.31 = bf16[256,768]{1,0:T(8,128)(2,1)S(1)} collective-permute-done((bf16[256,768]{1,0:T(8,128)(2,1)S(1)}, bf16[256,768]{1,0:T(8,128)(2,1)S(1)}, u32[]{:S(2)}, u32[]{:S(2)}) %collective-permute-start.31) | collective-permute-done | bytes 393248 | tf_op jit(solution)/shard_map/ppermute | solution.py:19
  (109 shorter events, 20.2 us)
Async XLA Ops:
  7.2 51.6 %copy-start.15 = (s32[1,128]{1,0:T(1,128)S(1)}, s32[1,128]{1,0:T(1,128)}, u32[]{:S(2)}) copy-start(s32[1,128]{1,0:T(1,128)} %param.15) | copy-start | bytes 1540
  7.2 52.0 %copy-start = (bf16[1,128,4096]{2,1,0:T(8,128)(2,1)S(1)}, bf16[1,128,4096]{2,1,0:T(8,128)(2,1)}, u32[]{:S(2)}) copy-start(bf16[1,128,4096]{2,1,0:T(8,128)(2,1)} %param.8) | copy-start | bytes 3145732
  7.2 148.3 %all-gather.6.cloned.1.call-start = ((), (), s32[]{:S(2)}) async-start(), calls=%async_computation.1 | async-start | bytes 4456448 | tf_op jit(solution)/shard_map/all_gather | solution.py:123
  7.9 388.3 %all-gather.4.cloned.1.call-start = ((), (), s32[]{:S(2)}) async-start(), calls=%async_computation | async-start | bytes 2228224 | tf_op jit(solution)/shard_map/all_gather | solution.py:125
  9.1 26.5 %collective-permute-start = (bf16[128,256]{0,1:T(8,128)(2,1)S(1)}, bf16[128,256]{0,1:T(8,128)(2,1)S(1)}, u32[]{:S(2)}, u32[]{:S(2)}) collective-permute-start(bf16[128,256]{0,1:T(8,128)(2,1)S(1)} %get-tuple-element.40), channel_id=1, source_target_pairs={{0,1},{1,2},{2,3},{3,0},{4,5},{5,6},{6,7},{7,4},{8,9},{9,10},{10,1... | collective-permute-start | bytes 196616 | tf_op jit(solution)/shard_map/ppermute | solution.py:32
  17.9 17.8 %collective-permute-start.1 = (bf16[128,256]{0,1:T(8,128)(2,1)S(1)}, bf16[128,256]{0,1:T(8,128)(2,1)S(1)}, u32[]{:S(2)}, u32[]{:S(2)}) collective-permute-start(bf16[128,256]{0,1:T(8,128)(2,1)S(1)} %get-tuple-element.40), channel_id=1, source_target_pairs={{0,2},{1,3},{2,0},{3,1},{4,6},{5,7},{6,4},{7,5},{8,10},{9,11},{10,... | collective-permute-start | bytes 196616 | tf_op jit(solution)/shard_map/ppermute | solution.py:32
  28.5 19.6 %collective-permute-start.2 = (bf16[128,256]{0,1:T(8,128)(2,1)S(1)}, bf16[128,256]{0,1:T(8,128)(2,1)S(1)}, u32[]{:S(2)}, u32[]{:S(2)}) collective-permute-start(bf16[128,256]{0,1:T(8,128)(2,1)S(1)} %get-tuple-element.40), channel_id=1, source_target_pairs={{0,3},{1,0},{2,1},{3,2},{4,7},{5,4},{6,5},{7,6},{8,11},{9,8},{10,9... | collective-permute-start | bytes 196616 | tf_op jit(solution)/shard_map/ppermute | solution.py:32
  48.2 11.8 %collective-permute-start.3 = (bf16[4,128,256]{1,2,0:T(8,128)(2,1)S(1)}, bf16[4,128,256]{1,2,0:T(8,128)(2,1)S(1)}, u32[]{:S(2)}, u32[]{:S(2)}) collective-permute-start(bf16[4,128,256]{1,2,0:T(8,128)(2,1)S(1)} %get-tuple-element.38), channel_id=1, source_target_pairs={{0,4},{1,5},{2,6},{3,7},{4,8},{5,9},{6,10},{7,11},{8,12},{9,13},{1... | collective-permute-start | bytes 786440 | tf_op jit(solution)/shard_map/ppermute | solution.py:33
  51.4 13.9 %collective-permute-start.4 = (bf16[4,128,256]{1,2,0:T(8,128)(2,1)S(1)}, bf16[4,128,256]{1,2,0:T(8,128)(2,1)S(1)}, u32[]{:S(2)}, u32[]{:S(2)}) collective-permute-start(bf16[4,128,256]{1,2,0:T(8,128)(2,1)S(1)} %get-tuple-element.38), channel_id=1, source_target_pairs={{0,8},{1,9},{2,10},{3,11},{4,12},{5,13},{6,14},{7,15},{8,0},{9,1},... | collective-permute-start | bytes 786440 | tf_op jit(solution)/shard_map/ppermute | solution.py:33
  55.7 10.7 %collective-permute-start.5 = (bf16[4,128,256]{1,2,0:T(8,128)(2,1)S(1)}, bf16[4,128,256]{1,2,0:T(8,128)(2,1)S(1)}, u32[]{:S(2)}, u32[]{:S(2)}) collective-permute-start(bf16[4,128,256]{1,2,0:T(8,128)(2,1)S(1)} %get-tuple-element.38), channel_id=1, source_target_pairs={{0,12},{1,13},{2,14},{3,15},{4,0},{5,1},{6,2},{7,3},{8,4},{9,5},{1... | collective-permute-start | bytes 786440 | tf_op jit(solution)/shard_map/ppermute | solution.py:33
  67.1 92.3 %copy-start.5 = (bf16[4,4,128,256]{3,2,1,0:T(8,128)(2,1)}, bf16[4,4,128,256]{3,2,1,0:T(8,128)(2,1)S(1)}, u32[]{:S(2)}) copy-start(bf16[4,4,128,256]{3,2,1,0:T(8,128)(2,1)S(1)} %copy.41) | copy-start | bytes 3145732
  67.1 88.4 %copy-start.3 = (bf16[1,128,4096]{2,1,0:T(8,128)(2,1)S(1)}, bf16[1,128,4096]{2,1,0:T(8,128)(2,1)}, u32[]{:S(2)}) copy-start(bf16[1,128,4096]{2,1,0:T(8,128)(2,1)} %param.10) | copy-start | bytes 3145732
  159.4 3.5 copy-start.17
  163.7 32.4 %copy-start.1 = (f32[2048,128]{0,1:T(8,128)}, f32[2048,128]{0,1:T(8,128)S(1)}, u32[]{:S(2)}) copy-start(f32[2048,128]{0,1:T(8,128)S(1)} %convolution_bitcast_fusion) | copy-start | bytes 3145732
  171.4 24.7 %copy-start.2 = (f32[2048,128]{0,1:T(8,128)}, f32[2048,128]{0,1:T(8,128)S(1)}, u32[]{:S(2)}) copy-start(f32[2048,128]{0,1:T(8,128)S(1)} %convolution_bitcast_fusion.1) | copy-start | bytes 3145732
  179.9 27.0 %collective-permute-start.6 = (bf16[128,512]{1,0:T(8,128)(2,1)}, bf16[128,512]{1,0:T(8,128)(2,1)S(1)}, u32[]{:S(2)}, u32[]{:S(2)}) collective-permute-start(bf16[128,512]{1,0:T(8,128)(2,1)} %copy.48), channel_id=1, source_target_pairs={{0,1},{1,2},{2,3},{3,0},{4,5},{5,6},{6,7},{7,4},{8,9},{9,10},{10,1... | collective-permute-start | bytes 393224 | tf_op jit(solution)/shard_map/ppermute | solution.py:32
  187.2 30.3 %collective-permute-start.7 = (bf16[128,512]{1,0:T(8,128)(2,1)}, bf16[128,512]{1,0:T(8,128)(2,1)}, u32[]{:S(2)}, u32[]{:S(2)}) collective-permute-start(bf16[128,512]{1,0:T(8,128)(2,1)} %copy.48), channel_id=1, source_target_pairs={{0,2},{1,3},{2,0},{3,1},{4,6},{5,7},{6,4},{7,5},{8,10},{9,11},{10,... | collective-permute-start | bytes 393224 | tf_op jit(solution)/shard_map/ppermute | solution.py:32
  193.9 23.6 %collective-permute-start.8 = (bf16[128,512]{1,0:T(8,128)(2,1)}, bf16[128,512]{1,0:T(8,128)(2,1)}, u32[]{:S(2)}, u32[]{:S(2)}) collective-permute-start(bf16[128,512]{1,0:T(8,128)(2,1)} %copy.48), channel_id=1, source_target_pairs={{0,3},{1,0},{2,1},{3,2},{4,7},{5,4},{6,5},{7,6},{8,11},{9,8},{10,9... | collective-permute-start | bytes 393224 | tf_op jit(solution)/shard_map/ppermute | solution.py:32
  196.3 13.1 %copy-start.16 = (f32[128]{0:T(128)S(1)}, f32[128]{0:T(128)}, u32[]{:S(2)}) copy-start(f32[128]{0:T(128)} %fusion.20) | copy-start | bytes 1540
  197.2 29.4 %collective-permute-start.18 = (bf16[4,128,256]{2,1,0:T(8,128)(2,1)}, bf16[4,128,256]{2,1,0:T(8,128)(2,1)}, u32[]{:S(2)}, u32[]{:S(2)}) collective-permute-start(bf16[4,128,256]{2,1,0:T(8,128)(2,1)} %bitcast.49), channel_id=1, source_target_pairs={{0,12},{1,13},{2,14},{3,15},{4,0},{5,1},{6,2},{7,3},{8,4},{9,5},{1... | collective-permute-start | bytes 786440 | tf_op jit(solution)/shard_map/ppermute | solution.py:40
  202.7 9.4 %copy-start.10 = (f32[1,4096]{1,0:T(1,128)S(1)}, f32[1,4096]{1,0:T(1,128)}, u32[]{:S(2)}) copy-start(f32[1,4096]{1,0:T(1,128)} %param.13) | copy-start | bytes 49156
  203.6 25.6 %collective-permute-start.19 = (bf16[4,128,256]{2,1,0:T(8,128)(2,1)}, bf16[4,128,256]{2,1,0:T(8,128)(2,1)}, u32[]{:S(2)}, u32[]{:S(2)}) collective-permute-start(bf16[4,128,256]{2,1,0:T(8,128)(2,1)} %bitcast.50), channel_id=1, source_target_pairs={{0,8},{1,9},{2,10},{3,11},{4,12},{5,13},{6,14},{7,15},{8,0},{9,1},... | collective-permute-start | bytes 786440 | tf_op jit(solution)/shard_map/ppermute | solution.py:40
  206.9 22.3 %collective-permute-start.20 = (bf16[4,128,256]{2,1,0:T(8,128)(2,1)}, bf16[4,128,256]{2,1,0:T(8,128)(2,1)}, u32[]{:S(2)}, u32[]{:S(2)}) collective-permute-start(bf16[4,128,256]{2,1,0:T(8,128)(2,1)} %bitcast.51), channel_id=1, source_target_pairs={{0,4},{1,5},{2,6},{3,7},{4,8},{5,9},{6,10},{7,11},{8,12},{9,13},{1... | collective-permute-start | bytes 786440 | tf_op jit(solution)/shard_map/ppermute | solution.py:40
  217.5 20.0 %copy-start.11 = (f32[4,4,256]{2,0,1:T(4,128)S(1)}, f32[4,4,256]{2,0,1:T(4,128)}, u32[]{:S(2)}) copy-start(f32[4,4,256]{2,0,1:T(4,128)} %copy.64) | copy-start | bytes 49156
  217.5 20.0 %copy-start.13 = (f32[128]{0:T(128)S(1)}, f32[128]{0:T(128)}, u32[]{:S(2)}) copy-start(f32[128]{0:T(128)} %add_rsqrt_fusion) | copy-start | bytes 1540
  219.5 72.4 %collective-permute-start.9 = (bf16[4,128,512]{2,1,0:T(8,128)(2,1)}, bf16[4,128,512]{2,1,0:T(8,128)(2,1)}, u32[]{:S(2)}, u32[]{:S(2)}) collective-permute-start(bf16[4,128,512]{2,1,0:T(8,128)(2,1)} %get-tuple-element.30), channel_id=1, source_target_pairs={{0,4},{1,5},{2,6},{3,7},{4,8},{5,9},{6,10},{7,11},{8,12},{9,13},{1... | collective-permute-start | bytes 1572872 | tf_op jit(solution)/shard_map/ppermute | solution.py:33
  222.9 71.1 %collective-permute-start.10 = (bf16[4,128,512]{2,1,0:T(8,128)(2,1)}, bf16[4,128,512]{2,1,0:T(8,128)(2,1)}, u32[]{:S(2)}, u32[]{:S(2)}) collective-permute-start(bf16[4,128,512]{2,1,0:T(8,128)(2,1)} %get-tuple-element.30), channel_id=1, source_target_pairs={{0,8},{1,9},{2,10},{3,11},{4,12},{5,13},{6,14},{7,15},{8,0},{9,1},... | collective-permute-start | bytes 1572872 | tf_op jit(solution)/shard_map/ppermute | solution.py:33
  226.6 67.4 %collective-permute-start.11 = (bf16[4,128,512]{2,1,0:T(8,128)(2,1)}, bf16[4,128,512]{2,1,0:T(8,128)(2,1)}, u32[]{:S(2)}, u32[]{:S(2)}) collective-permute-start(bf16[4,128,512]{2,1,0:T(8,128)(2,1)} %get-tuple-element.30), channel_id=1, source_target_pairs={{0,12},{1,13},{2,14},{3,15},{4,0},{5,1},{6,2},{7,3},{8,4},{9,5},{1... | collective-permute-start | bytes 1572872 | tf_op jit(solution)/shard_map/ppermute | solution.py:33
  231.4 32.3 %collective-permute-start.21 = (bf16[128,256]{1,0:T(8,128)(2,1)S(1)}, bf16[128,256]{1,0:T(8,128)(2,1)S(1)}, u32[]{:S(2)}, u32[]{:S(2)}) collective-permute-start(bf16[128,256]{1,0:T(8,128)(2,1)S(1)} %get-tuple-element.34), channel_id=1, source_target_pairs={{0,3},{1,0},{2,1},{3,2},{4,7},{5,4},{6,5},{7,6},{8,11},{9,8},{10,9... | collective-permute-start | bytes 196616 | tf_op jit(solution)/shard_map/ppermute | solution.py:43
  239.7 37.9 %collective-permute-start.22 = (bf16[128,256]{1,0:T(8,128)(2,1)S(1)}, bf16[128,256]{1,0:T(8,128)(2,1)S(1)}, u32[]{:S(2)}, u32[]{:S(2)}) collective-permute-start(bf16[128,256]{1,0:T(8,128)(2,1)S(1)} %get-tuple-element.36), channel_id=1, source_target_pairs={{0,2},{1,3},{2,0},{3,1},{4,6},{5,7},{6,4},{7,5},{8,10},{9,11},{10,... | collective-permute-start | bytes 196616 | tf_op jit(solution)/shard_map/ppermute | solution.py:43
  263.7 30.3 %copy-start.6 = (bf16[1,4,128,512]{3,2,1,0:T(8,128)(2,1)S(1)}, bf16[1,4,128,512]{3,2,1,0:T(8,128)(2,1)}, u32[]{:S(2)}) copy-start(bf16[1,4,128,512]{3,2,1,0:T(8,128)(2,1)} %get-tuple-element.29) | copy-start | bytes 1572868
  263.7 15.1 %collective-permute-start.23 = (bf16[128,256]{1,0:T(8,128)(2,1)S(1)}, bf16[128,256]{1,0:T(8,128)(2,1)S(1)}, u32[]{:S(2)}, u32[]{:S(2)}) collective-permute-start(bf16[128,256]{1,0:T(8,128)(2,1)S(1)} %get-tuple-element.35), channel_id=1, source_target_pairs={{0,1},{1,2},{2,3},{3,0},{4,5},{5,6},{6,7},{7,4},{8,9},{9,10},{10,1... | collective-permute-start | bytes 196616 | tf_op jit(solution)/shard_map/ppermute | solution.py:43
  279.9 43.2 %collective-permute-start.25 = (bf16[5,128,256]{2,1,0:T(8,128)(2,1)S(1)}, bf16[5,128,256]{2,1,0:T(8,128)(2,1)S(1)}, u32[]{:S(2)}, u32[]{:S(2)}) collective-permute-start(bf16[5,128,256]{2,1,0:T(8,128)(2,1)S(1)} %get-tuple-element.42), channel_id=1, source_target_pairs={{0,1},{1,2},{2,3},{3,0},{4,5},{5,6},{6,7},{7,4},{8,9},{9,10},{10,1... | collective-permute-start | bytes 983048 | tf_op jit(solution)/shard_map/ppermute | solution.py:54
  284.6 57.2 %collective-permute-start.26 = (bf16[5,128,256]{2,1,0:T(8,128)(2,1)S(1)}, bf16[5,128,256]{2,1,0:T(8,128)(2,1)S(1)}, u32[]{:S(2)}, u32[]{:S(2)}) collective-permute-start(bf16[5,128,256]{2,1,0:T(8,128)(2,1)S(1)} %get-tuple-element.43), channel_id=1, source_target_pairs={{0,2},{1,3},{2,0},{3,1},{4,6},{5,7},{6,4},{7,5},{8,10},{9,11},{10,... | collective-permute-start | bytes 983048 | tf_op jit(solution)/shard_map/ppermute | solution.py:54
  292.0 49.9 %collective-permute-start.27 = (bf16[5,128,256]{2,1,0:T(8,128)(2,1)S(1)}, bf16[5,128,256]{2,1,0:T(8,128)(2,1)S(1)}, u32[]{:S(2)}, u32[]{:S(2)}) collective-permute-start(bf16[5,128,256]{2,1,0:T(8,128)(2,1)S(1)} %get-tuple-element.44), channel_id=1, source_target_pairs={{0,3},{1,0},{2,1},{3,2},{4,7},{5,4},{6,5},{7,6},{8,11},{9,8},{10,9... | collective-permute-start | bytes 983048 | tf_op jit(solution)/shard_map/ppermute | solution.py:54
  294.0 1.7 copy-start.12
  296.6 45.6 %collective-permute-start.12 = (bf16[4,128,256]{2,1,0:T(8,128)(2,1)S(1)}, bf16[4,128,256]{2,1,0:T(8,128)(2,1)S(1)}, u32[]{:S(2)}, u32[]{:S(2)}) collective-permute-start(bf16[4,128,256]{2,1,0:T(8,128)(2,1)S(1)} %bitcast.223), channel_id=1, source_target_pairs={{0,12},{1,13},{2,14},{3,15},{4,0},{5,1},{6,2},{7,3},{8,4},{9,5},{1... | collective-permute-start | bytes 786440 | tf_op jit(solution)/shard_map/ppermute | solution.py:72
  306.1 36.0 %collective-permute-start.13 = (bf16[4,128,256]{2,1,0:T(8,128)(2,1)S(1)}, bf16[4,128,256]{2,1,0:T(8,128)(2,1)S(1)}, u32[]{:S(2)}, u32[]{:S(2)}) collective-permute-start(bf16[4,128,256]{2,1,0:T(8,128)(2,1)S(1)} %bitcast.221), channel_id=1, source_target_pairs={{0,8},{1,9},{2,10},{3,11},{4,12},{5,13},{6,14},{7,15},{8,0},{9,1},... | collective-permute-start | bytes 786440 | tf_op jit(solution)/shard_map/ppermute | solution.py:72
  323.1 19.0 %collective-permute-start.14 = (bf16[4,128,256]{2,1,0:T(8,128)(2,1)S(1)}, bf16[4,128,256]{2,1,0:T(8,128)(2,1)S(1)}, u32[]{:S(2)}, u32[]{:S(2)}) collective-permute-start(bf16[4,128,256]{2,1,0:T(8,128)(2,1)S(1)} %bitcast.219), channel_id=1, source_target_pairs={{0,4},{1,5},{2,6},{3,7},{4,8},{5,9},{6,10},{7,11},{8,12},{9,13},{1... | collective-permute-start | bytes 786440 | tf_op jit(solution)/shard_map/ppermute | solution.py:72
  342.4 31.2 %collective-permute-start.15 = (bf16[4,128,256]{2,1,0:T(8,128)(2,1)S(1)}, bf16[4,128,256]{2,1,0:T(8,128)(2,1)S(1)}, u32[]{:S(2)}, u32[]{:S(2)}) collective-permute-start(bf16[4,128,256]{2,1,0:T(8,128)(2,1)S(1)} %get-tuple-element.16), channel_id=1, source_target_pairs={{0,3},{1,0},{2,1},{3,2},{4,7},{5,4},{6,5},{7,6},{8,11},{9,8},{10,9... | collective-permute-start | bytes 786440 | tf_op jit(solution)/shard_map/ppermute | solution.py:76
  344.3 34.1 %collective-permute-start.16 = (bf16[4,128,256]{2,1,0:T(8,128)(2,1)S(1)}, bf16[4,128,256]{2,1,0:T(8,128)(2,1)S(1)}, u32[]{:S(2)}, u32[]{:S(2)}) collective-permute-start(bf16[4,128,256]{2,1,0:T(8,128)(2,1)S(1)} %get-tuple-element.18), channel_id=1, source_target_pairs={{0,2},{1,3},{2,0},{3,1},{4,6},{5,7},{6,4},{7,5},{8,10},{9,11},{10,... | collective-permute-start | bytes 786440 | tf_op jit(solution)/shard_map/ppermute | solution.py:76
  350.7 40.5 %collective-permute-start.17 = (bf16[4,128,256]{2,1,0:T(8,128)(2,1)S(1)}, bf16[4,128,256]{2,1,0:T(8,128)(2,1)S(1)}, u32[]{:S(2)}, u32[]{:S(2)}) collective-permute-start(bf16[4,128,256]{2,1,0:T(8,128)(2,1)S(1)} %get-tuple-element.15), channel_id=1, source_target_pairs={{0,1},{1,2},{2,3},{3,0},{4,5},{5,6},{6,7},{7,4},{8,9},{9,10},{10,1... | collective-permute-start | bytes 786440 | tf_op jit(solution)/shard_map/ppermute | solution.py:76
  359.9 42.1 %collective-permute-start.28 = (bf16[8,128,256]{2,1,0:T(8,128)(2,1)}, bf16[8,128,256]{2,1,0:T(8,128)(2,1)}, u32[]{:S(2)}, u32[]{:S(2)}) collective-permute-start(bf16[8,128,256]{2,1,0:T(8,128)(2,1)} %get-tuple-element.31), channel_id=1, source_target_pairs={{0,4},{1,5},{2,6},{3,7},{4,8},{5,9},{6,10},{7,11},{8,12},{9,13},{1... | collective-permute-start | bytes 1572872 | tf_op jit(solution)/shard_map/ppermute | solution.py:61
  371.6 31.5 %collective-permute-start.29 = (bf16[8,128,256]{2,1,0:T(8,128)(2,1)}, bf16[8,128,256]{2,1,0:T(8,128)(2,1)}, u32[]{:S(2)}, u32[]{:S(2)}) collective-permute-start(bf16[8,128,256]{2,1,0:T(8,128)(2,1)} %get-tuple-element.32), channel_id=1, source_target_pairs={{0,8},{1,9},{2,10},{3,11},{4,12},{5,13},{6,14},{7,15},{8,0},{9,1},... | collective-permute-start | bytes 1572872 | tf_op jit(solution)/shard_map/ppermute | solution.py:61
  373.6 30.7 %collective-permute-start.30 = (bf16[8,128,256]{2,1,0:T(8,128)(2,1)}, bf16[8,128,256]{2,1,0:T(8,128)(2,1)}, u32[]{:S(2)}, u32[]{:S(2)}) collective-permute-start(bf16[8,128,256]{2,1,0:T(8,128)(2,1)} %get-tuple-element.33), channel_id=1, source_target_pairs={{0,12},{1,13},{2,14},{3,15},{4,0},{5,1},{6,2},{7,3},{8,4},{9,5},{1... | collective-permute-start | bytes 1572872 | tf_op jit(solution)/shard_map/ppermute | solution.py:61
  394.1 2.1 copy-start.14
  396.2 3.3 copy-start.4
  400.1 25.9 %collective-permute-start.24 = (bf16[128,4096]{1,0:T(8,128)(2,1)S(1)}, bf16[128,4096]{1,0:T(8,128)(2,1)S(1)}, u32[]{:S(2)}, u32[]{:S(2)}) collective-permute-start(bf16[128,4096]{1,0:T(8,128)(2,1)S(1)} %add_convert_fusion), channel_id=1, source_target_pairs={{0,16},{16,32},{32,48},{48,64},{64,80},{80,96},{96,112},{112,128},... | collective-permute-start | bytes 3145736 | tf_op jit(solution)/shard_map/ppermute | solution.py:14
  403.1 2.4 copy-start.7
  403.1 2.4 copy-start.9
  405.5 19.7 %copy-start.8 = (bf16[1,256,768]{2,1,0:T(8,128)(2,1)S(1)}, bf16[1,256,768]{2,1,0:T(8,128)(2,1)}, u32[]{:S(2)}) copy-start(bf16[1,256,768]{2,1,0:T(8,128)(2,1)} %param.14) | copy-start | bytes 1179652
  408.0 17.2 %collective-permute-start.31 = (bf16[256,768]{1,0:T(8,128)(2,1)S(1)}, bf16[256,768]{1,0:T(8,128)(2,1)S(1)}, u32[]{:S(2)}, u32[]{:S(2)}) collective-permute-start(bf16[256,768]{1,0:T(8,128)(2,1)S(1)} %fusion.35), channel_id=1, source_target_pairs={{0,496},{16,480},{32,464},{48,448},{64,432},{80,416},{96,400},{112... | collective-permute-start | bytes 1179656 | tf_op jit(solution)/shard_map/ppermute | solution.py:19
Sparse Core Ops, SparseCore 0:
  11.0 144.4 all-gather.5
  158.5 135.6 all-gather.3

commit v10 on v9

--- a/solution.py
+++ b/solution.py
@@ -120,8 +120,13 @@
     cotangent = up_cotangent[0]
     unit_up, inverse_up, normed_up = normalize(up_activation[0], upward_gain[0])
     hidden = normed_up.astype(jnp.bfloat16)
-    output_weight = lax.all_gather(up_output_weight[0], "seq", axis=1, tiled=True)
-    key_value = gather_blocks(saved[:, width:]).reshape(size * count, 2 * HEAD)
+    split = width - HEAD
+    output_main = lax.all_gather(up_output_weight[0][:split], "seq", axis=1, tiled=True)
+    riders = gather_blocks(jnp.stack([saved[:, width:], up_output_weight[0][split:]]))
+    key_value = riders[:, :, 0].reshape(size * count, 2 * HEAD)
+    output_tail = jnp.take(riders[:, :, 1], (o - jnp.arange(outer)) % outer, axis=0)
+    output_tail = jnp.take(output_tail, (i - jnp.arange(INNER)) % INNER, axis=1)
+    output_tail = output_tail.transpose(2, 0, 1, 3).reshape(HEAD, -1)
     kv_weight_all = lax.all_gather(up_input_weight[0][:, width:], "seq", axis=0, tiled=True)
     keys = key_value[:, :HEAD]
     values = key_value[:, HEAD:]
@@ -131,7 +136,9 @@
     ).reshape(size)
     key_positions = (sources[:, None] * count + jnp.arange(count, dtype=jnp.int32)[None, :]).reshape(-1)
     query = saved[:, :width].reshape(count, GROUP, HEAD)
-    attn_grad = contract_last(cotangent, output_weight).astype(jnp.bfloat16)
+    attn_grad = jnp.concatenate(
+        [contract_last(cotangent, output_main), contract_last(cotangent, output_tail)], axis=1
+    ).astype(jnp.bfloat16)
     positions = first + jnp.arange(count, dtype=jnp.int32)
     starts = doc_starts[0]
     visible = (key_positions[None, :] <= positions[:, None]) & (

time: 439 us -> 441 us (level)
  the two profiles are of different devices: /device:TPU:25 before, /device:TPU:34 now
where the time goes in v10:
time: 441 us; the launch traced here: 439 us
  starting transfers between devices  213 us (48%)
  waiting for transfers between devices  118 us (27%)
  local copies, waits for them, and re-layouts  38.2 us (9%)
  matrix products  33.6 us (8%)
  other arithmetic  21.5 us (5%)
  between operations  15 us (3%)
    all_gather x1, waiting for transfers between devices, per_device(): lax.all_gather(up_output_weight[0][:split], 'seq', axis=1, tiled=True)  47.5 us
    ppermute x1, starting transfers between devices, mirrored(): lax.ppermute(value, axis, [(source, count - 1 - source) for source in ran...  43.4 us
    ppermute x6, starting transfers between devices, gather_blocks(): lax.ppermute(x, 'seq', seq_pairs(k, 0))  40.9 us
    ppermute x3, starting transfers between devices, gather_and_scatter(): second.append(lax.ppermute(payload, 'seq', seq_pairs(k, 1)))  28.9 us
    ppermute x6, starting transfers between devices, gather_blocks(): lax.ppermute(first, 'seq', seq_pairs(k, 1))  20.2 us
    ppermute x6, waiting for transfers between devices, gather_blocks(): lax.ppermute(first, 'seq', seq_pairs(k, 1))  20.2 us
    ppermute x3, starting transfers between devices, gather_columns(): second.append(lax.ppermute(first[k], 'seq', seq_pairs(INNER - k, 0)))  17.8 us
    ppermute x3, waiting for transfers between devices, reduce_blocks(): lax.ppermute(acc[k].astype(wire), 'seq', seq_pairs(INNER - k, 0))  17 us
  transfers between devices with their start and end apart: 34, of which 13 were waited for; matrix products, arithmetic and copies ran while one was open for 20% of the time, Pallas kernels for 0%

profile of v10, /device:TPU:34, one launch (start us, length us, event | category | flops | bytes accessed | tf_op | source)
XLA Modules:
  0.0 439.4 jit_solution(16619821561942653378)
XLA Ops:
  7.2 1.7 slice.125
  11.1 9.1 %collective-permute-start = (bf16[2,128,256]{1,2,0:T(8,128)(2,1)S(1)}, bf16[2,128,256]{1,2,0:T(8,128)(2,1)S(1)}, u32[]{:S(2)}, u32[]{:S(2)}) collective-permute-start(bf16[2,128,256]{1,2,0:T(8,128)(2,1)S(1)} %get-tuple-element.42), channel_id=1, source_target_pairs={{0,1},{1,2},{2,3},{3,0},{4,5},{5,6},{6,7},{7,4},{8,9},{9,10},{10,1... | collective-permute-start | bytes 393224 | tf_op jit(solution)/shard_map/ppermute | solution.py:32
  20.2 10.0 %collective-permute-start.1 = (bf16[2,128,256]{1,2,0:T(8,128)(2,1)S(1)}, bf16[2,128,256]{1,2,0:T(8,128)(2,1)S(1)}, u32[]{:S(2)}, u32[]{:S(2)}) collective-permute-start(bf16[2,128,256]{1,2,0:T(8,128)(2,1)S(1)} %get-tuple-element.42), channel_id=1, source_target_pairs={{0,2},{1,3},{2,0},{3,1},{4,6},{5,7},{6,4},{7,5},{8,10},{9,11},{10,... | collective-permute-start | bytes 393224 | tf_op jit(solution)/shard_map/ppermute | solution.py:32
  30.2 5.5 %collective-permute-start.2 = (bf16[2,128,256]{1,2,0:T(8,128)(2,1)S(1)}, bf16[2,128,256]{1,2,0:T(8,128)(2,1)S(1)}, u32[]{:S(2)}, u32[]{:S(2)}) collective-permute-start(bf16[2,128,256]{1,2,0:T(8,128)(2,1)S(1)} %get-tuple-element.42), channel_id=1, source_target_pairs={{0,3},{1,0},{2,1},{3,2},{4,7},{5,4},{6,5},{7,6},{8,11},{9,8},{10,9... | collective-permute-start | bytes 393224 | tf_op jit(solution)/shard_map/ppermute | solution.py:32
  35.7 1.6 slice.183
  39.1 1.4 collective-permute-done.1
  40.6 9.3 %collective-permute-done.2 = bf16[2,128,256]{1,2,0:T(8,128)(2,1)S(1)} collective-permute-done((bf16[2,128,256]{1,2,0:T(8,128)(2,1)S(1)}, bf16[2,128,256]{1,2,0:T(8,128)(2,1)S(1)}, u32[]{:S(2)}, u32[]{:S(2)}) %collective-permute-start.2) | collective-permute-done | bytes 131104 | tf_op jit(solution)/shard_map/ppermute | solution.py:32
  50.0 3.4 collective-permute-start.3
  53.4 3.0 collective-permute-start.4
  56.4 4.1 collective-permute-start.5
  60.8 6.9 %collective-permute-done.3 = bf16[4,2,128,256]{2,3,1,0:T(8,128)(2,1)S(1)} collective-permute-done((bf16[4,2,128,256]{2,3,1,0:T(8,128)(2,1)S(1)}, bf16[4,2,128,256]{2,3,1,0:T(8,128)(2,1)S(1)}, u32[]{:S(2)}, u32[]{:S(2)}) %collective-permute-start.3) | collective-permute-done | bytes 524320 | tf_op jit(solution)/shard_map/ppermute | solution.py:33
  67.8 3.9 collective-permute-done.4
  71.6 9.4 %collective-permute-done.5 = bf16[4,2,128,256]{2,3,1,0:T(8,128)(2,1)S(1)} collective-permute-done((bf16[4,2,128,256]{2,3,1,0:T(8,128)(2,1)S(1)}, bf16[4,2,128,256]{2,3,1,0:T(8,128)(2,1)S(1)}, u32[]{:S(2)}, u32[]{:S(2)}) %collective-permute-start.5) | collective-permute-done | bytes 524320 | tf_op jit(solution)/shard_map/ppermute | solution.py:33
  84.4 2.4 copy.43
  87.2 4.7 %fusion.95 = (f32[128,4]{0,1:T(4,128)S(1)}, f32[128,4,2048]{0,2,1:T(8,128)}) fusion(pred[128,2048]{0,1:T(8,128)(4,1)S(1)} %compare_and_fusion, bf16[128,4,128]{0,2,1:T(8,128)(2,1)} %bitcast.251, bf16[2048,256]{1,0:T(8,128)(2,1)} %bitcast.211), kind=kOutput, calls=%fused_computation.185 | convolution fusion | flops 273680384 | bytes 5376000 | tf_op jit(solution)/shard_map/sub | solution.py:150
  91.9 47.5 %all-gather.6.cloned.1.call-done = bf16[1,384,4096]{2,1,0:T(8,128)(2,1)} async-done(((bf16[1,384,256]{2,1,0:T(8,128)(2,1)}), bf16[1,384,4096]{2,1,0:T(8,128)(2,1)}) %all-gather.6.cloned.1.call-update) | async-done | bytes 3145744 | tf_op jit(solution)/shard_map/all_gather | solution.py:124
  139.4 2.9 fusion.41
  142.5 2.8 fusion.66
  147.0 8.2 %convolution_bitcast_fusion.1 = f32[2048,128]{0,1:T(8,128)} fusion(bf16[128,4,128]{0,2,1:T(8,128)(2,1)S(1)} %bitcast.252, f32[128,4,2048]{0,2,1:T(8,128)} %fusion.66, f32[128,4,2048]{0,2,1:T(8,128)} %get-tuple-element.48, f32[128,4]{0,1:T(4,128)S(1)} %get-tuple-element.47), kind=kOutput, calls=%fused_computation.29 | convolution fusion | flops 275778048 | bytes 9570304 | tf_op jit(solution)/shard_map/tgj,tgh->jh/dot_general | solution.py:162
  155.2 7.3 %fusion.38 = bf16[128,4,128]{0,2,1:T(8,128)(2,1)S(1)} fusion(f32[128,4,2048]{0,2,1:T(8,128)} %fusion.66, bf16[2048,256]{1,0:T(8,128)(2,1)} %bitcast.212, f32[128,4,2048]{0,2,1:T(8,128)} %get-tuple-element.48, f32[128,4]{0,1:T(4,128)S(1)} %get-tuple-element.47), kind=kOutput, calls=%fused_computation.61 | convolution fusion | flops 275843584 | bytes 17436672 | tf_op jit(solution)/shard_map/tgj,jh->tgh/dot_general | solution.py:158
  163.3 3.9 collective-permute-start.6
  167.2 6.9 %collective-permute-start.7 = (bf16[128,512]{1,0:T(8,128)(2,1)}, bf16[128,512]{1,0:T(8,128)(2,1)}, u32[]{:S(2)}, u32[]{:S(2)}) collective-permute-start(bf16[128,512]{1,0:T(8,128)(2,1)} %copy.52), channel_id=1, source_target_pairs={{0,2},{1,3},{2,0},{3,1},{4,6},{5,7},{6,4},{7,5},{8,10},{9,11},{10,... | collective-permute-start | bytes 393224 | tf_op jit(solution)/shard_map/ppermute | solution.py:32
  174.1 5.5 %collective-permute-start.8 = (bf16[128,512]{1,0:T(8,128)(2,1)}, bf16[128,512]{1,0:T(8,128)(2,1)}, u32[]{:S(2)}, u32[]{:S(2)}) collective-permute-start(bf16[128,512]{1,0:T(8,128)(2,1)} %copy.52), channel_id=1, source_target_pairs={{0,3},{1,0},{2,1},{3,2},{4,7},{5,4},{6,5},{7,6},{8,11},{9,8},{10,9... | collective-permute-start | bytes 393224 | tf_op jit(solution)/shard_map/ppermute | solution.py:32
  179.7 1.4 fusion.19
  181.9 1.8 copy.87
  183.7 1.9 collective-permute-start.18
  185.6 1.8 copy.88
  187.4 4.8 %collective-permute-start.19 = (bf16[4,128,256]{2,1,0:T(8,128)(2,1)}, bf16[4,128,256]{2,1,0:T(8,128)(2,1)}, u32[]{:S(2)}, u32[]{:S(2)}) collective-permute-start(bf16[4,128,256]{2,1,0:T(8,128)(2,1)} %bitcast.239), channel_id=1, source_target_pairs={{0,8},{1,9},{2,10},{3,11},{4,12},{5,13},{6,14},{7,15},{8,0},{9,1},... | collective-permute-start | bytes 786440 | tf_op jit(solution)/shard_map/ppermute | solution.py:40
  193.1 3.9 collective-permute-start.20
  198.1 2.7 reshape.309
  205.2 1.8 fusion.65
  208.4 2.2 fusion.89
  210.6 1.9 collective-permute-start.9
  212.5 4.2 collective-permute-start.10
  216.7 3.6 collective-permute-start.11
  220.4 1.9 fusion.91
  223.0 4.6 %collective-permute-start.21 = (bf16[128,256]{1,0:T(8,128)(2,1)S(1)}, bf16[128,256]{1,0:T(8,128)(2,1)S(1)}, u32[]{:S(2)}, u32[]{:S(2)}) collective-permute-start(bf16[128,256]{1,0:T(8,128)(2,1)S(1)} %get-tuple-element.38), channel_id=1, source_target_pairs={{0,3},{1,0},{2,1},{3,2},{4,7},{5,4},{6,5},{7,6},{8,11},{9,8},{10,9... | collective-permute-start | bytes 196616 | tf_op jit(solution)/shard_map/ppermute | solution.py:43
  229.0 7.8 %collective-permute-start.22 = (bf16[128,256]{1,0:T(8,128)(2,1)}, bf16[128,256]{1,0:T(8,128)(2,1)}, u32[]{:S(2)}, u32[]{:S(2)}) collective-permute-start(bf16[128,256]{1,0:T(8,128)(2,1)} %get-tuple-element.40), channel_id=1, source_target_pairs={{0,2},{1,3},{2,0},{3,1},{4,6},{5,7},{6,4},{7,5},{8,10},{9,11},{10,... | collective-permute-start | bytes 196616 | tf_op jit(solution)/shard_map/ppermute | solution.py:43
  236.8 4.6 %collective-permute-done.21 = bf16[128,256]{1,0:T(8,128)(2,1)S(1)} collective-permute-done((bf16[128,256]{1,0:T(8,128)(2,1)S(1)}, bf16[128,256]{1,0:T(8,128)(2,1)S(1)}, u32[]{:S(2)}, u32[]{:S(2)}) %collective-permute-start.21) | collective-permute-done | bytes 65568 | tf_op jit(solution)/shard_map/ppermute | solution.py:43
  241.4 4.2 collective-permute-start.23
  246.6 5.1 %collective-permute-done.22 = bf16[128,256]{1,0:T(8,128)(2,1)} collective-permute-done((bf16[128,256]{1,0:T(8,128)(2,1)}, bf16[128,256]{1,0:T(8,128)(2,1)}, u32[]{:S(2)}, u32[]{:S(2)}) %collective-permute-start.22) | collective-permute-done | bytes 65568 | tf_op jit(solution)/shard_map/ppermute | solution.py:43
  251.7 7.2 %collective-permute-done.23 = bf16[128,256]{1,0:T(8,128)(2,1)} collective-permute-done((bf16[128,256]{1,0:T(8,128)(2,1)}, bf16[128,256]{1,0:T(8,128)(2,1)}, u32[]{:S(2)}, u32[]{:S(2)}) %collective-permute-start.23) | collective-permute-done | bytes 65568 | tf_op jit(solution)/shard_map/ppermute | solution.py:43
  261.1 5.2 %collective-permute-start.25 = (bf16[5,128,256]{2,1,0:T(8,128)(2,1)S(1)}, bf16[5,128,256]{2,1,0:T(8,128)(2,1)S(1)}, u32[]{:S(2)}, u32[]{:S(2)}) collective-permute-start(bf16[5,128,256]{2,1,0:T(8,128)(2,1)S(1)} %get-tuple-element.44), channel_id=1, source_target_pairs={{0,1},{1,2},{2,3},{3,0},{4,5},{5,6},{6,7},{7,4},{8,9},{9,10},{10,1... | collective-permute-start | bytes 983048 | tf_op jit(solution)/shard_map/ppermute | solution.py:54
  266.4 4.5 %collective-permute-start.26 = (bf16[5,128,256]{2,1,0:T(8,128)(2,1)S(1)}, bf16[5,128,256]{2,1,0:T(8,128)(2,1)S(1)}, u32[]{:S(2)}, u32[]{:S(2)}) collective-permute-start(bf16[5,128,256]{2,1,0:T(8,128)(2,1)S(1)} %get-tuple-element.45), channel_id=1, source_target_pairs={{0,2},{1,3},{2,0},{3,1},{4,6},{5,7},{6,4},{7,5},{8,10},{9,11},{10,... | collective-permute-start | bytes 983048 | tf_op jit(solution)/shard_map/ppermute | solution.py:54
  270.9 6.4 %collective-permute-start.27 = (bf16[5,128,256]{2,1,0:T(8,128)(2,1)S(1)}, bf16[5,128,256]{2,1,0:T(8,128)(2,1)S(1)}, u32[]{:S(2)}, u32[]{:S(2)}) collective-permute-start(bf16[5,128,256]{2,1,0:T(8,128)(2,1)S(1)} %get-tuple-element.46), channel_id=1, source_target_pairs={{0,3},{1,0},{2,1},{3,2},{4,7},{5,4},{6,5},{7,6},{8,11},{9,8},{10,9... | collective-permute-start | bytes 983048 | tf_op jit(solution)/shard_map/ppermute | solution.py:54
  277.4 1.8 pad_maximum_fusion.2
  280.0 4.6 %collective-permute-start.12 = (bf16[4,128,256]{2,1,0:T(8,128)(2,1)S(1)}, bf16[4,128,256]{2,1,0:T(8,128)(2,1)S(1)}, u32[]{:S(2)}, u32[]{:S(2)}) collective-permute-start(bf16[4,128,256]{2,1,0:T(8,128)(2,1)S(1)} %bitcast.246), channel_id=1, source_target_pairs={{0,12},{1,13},{2,14},{3,15},{4,0},{5,1},{6,2},{7,3},{8,4},{9,5},{1... | collective-permute-start | bytes 786440 | tf_op jit(solution)/shard_map/ppermute | solution.py:72
  284.6 7.4 %collective-permute-start.13 = (bf16[4,128,256]{2,1,0:T(8,128)(2,1)S(1)}, bf16[4,128,256]{2,1,0:T(8,128)(2,1)S(1)}, u32[]{:S(2)}, u32[]{:S(2)}) collective-permute-start(bf16[4,128,256]{2,1,0:T(8,128)(2,1)S(1)} %bitcast.244), channel_id=1, source_target_pairs={{0,8},{1,9},{2,10},{3,11},{4,12},{5,13},{6,14},{7,15},{8,0},{9,1},... | collective-permute-start | bytes 786440 | tf_op jit(solution)/shard_map/ppermute | solution.py:72
  292.0 4.5 %collective-permute-start.14 = (bf16[4,128,256]{2,1,0:T(8,128)(2,1)S(1)}, bf16[4,128,256]{2,1,0:T(8,128)(2,1)S(1)}, u32[]{:S(2)}, u32[]{:S(2)}) collective-permute-start(bf16[4,128,256]{2,1,0:T(8,128)(2,1)S(1)} %bitcast.242), channel_id=1, source_target_pairs={{0,4},{1,5},{2,6},{3,7},{4,8},{5,9},{6,10},{7,11},{8,12},{9,13},{1... | collective-permute-start | bytes 786440 | tf_op jit(solution)/shard_map/ppermute | solution.py:72
  296.9 2.8 collective-permute-done.13
  299.7 2.5 collective-permute-done.14
  302.5 7.6 %collective-permute-start.15 = (bf16[4,128,256]{2,1,0:T(8,128)(2,1)S(1)}, bf16[4,128,256]{2,1,0:T(8,128)(2,1)S(1)}, u32[]{:S(2)}, u32[]{:S(2)}) collective-permute-start(bf16[4,128,256]{2,1,0:T(8,128)(2,1)S(1)} %get-tuple-element.18), channel_id=1, source_target_pairs={{0,3},{1,0},{2,1},{3,2},{4,7},{5,4},{6,5},{7,6},{8,11},{9,8},{10,9... | collective-permute-start | bytes 786440 | tf_op jit(solution)/shard_map/ppermute | solution.py:76
  310.0 2.8 collective-permute-start.16
  312.9 7.4 %collective-permute-start.17 = (bf16[4,128,256]{2,1,0:T(8,128)(2,1)S(1)}, bf16[4,128,256]{2,1,0:T(8,128)(2,1)S(1)}, u32[]{:S(2)}, u32[]{:S(2)}) collective-permute-start(bf16[4,128,256]{2,1,0:T(8,128)(2,1)S(1)} %get-tuple-element.17), channel_id=1, source_target_pairs={{0,1},{1,2},{2,3},{3,0},{4,5},{5,6},{6,7},{7,4},{8,9},{9,10},{10,1... | collective-permute-start | bytes 786440 | tf_op jit(solution)/shard_map/ppermute | solution.py:76
  322.0 7.6 %collective-permute-start.28 = (bf16[8,128,256]{2,1,0:T(8,128)(2,1)}, bf16[8,128,256]{2,1,0:T(8,128)(2,1)}, u32[]{:S(2)}, u32[]{:S(2)}) collective-permute-start(bf16[8,128,256]{2,1,0:T(8,128)(2,1)} %get-tuple-element.35), channel_id=1, source_target_pairs={{0,4},{1,5},{2,6},{3,7},{4,8},{5,9},{6,10},{7,11},{8,12},{9,13},{1... | collective-permute-start | bytes 1572872 | tf_op jit(solution)/shard_map/ppermute | solution.py:61
  329.6 19.3 %collective-permute-start.29 = (bf16[8,128,256]{2,1,0:T(8,128)(2,1)S(1)}, bf16[8,128,256]{2,1,0:T(8,128)(2,1)}, u32[]{:S(2)}, u32[]{:S(2)}) collective-permute-start(bf16[8,128,256]{2,1,0:T(8,128)(2,1)S(1)} %get-tuple-element.36), channel_id=1, source_target_pairs={{0,8},{1,9},{2,10},{3,11},{4,12},{5,13},{6,14},{7,15},{8,0},{9,1},... | collective-permute-start | bytes 1572872 | tf_op jit(solution)/shard_map/ppermute | solution.py:61
  349.0 1.9 collective-permute-start.30
  352.5 2.7 copy.59
  355.2 3.3 reshape.307
  358.5 3.1 multiply_reduce_fusion.1
  362.3 1.9 collective-permute-start.24
  368.9 2.4 fusion.35
  371.4 43.4 %collective-permute-start.31 = (bf16[256,768]{1,0:T(8,128)(2,1)S(1)}, bf16[256,768]{1,0:T(8,128)(2,1)S(1)}, u32[]{:S(2)}, u32[]{:S(2)}) collective-permute-start(bf16[256,768]{1,0:T(8,128)(2,1)S(1)} %fusion.35), channel_id=1, source_target_pairs={{0,496},{16,480},{32,464},{48,448},{64,432},{80,416},{96,400},{112... | collective-permute-start | bytes 1179656 | tf_op jit(solution)/shard_map/ppermute | solution.py:19
  414.8 15.9 %collective-permute-done.31 = bf16[256,768]{1,0:T(8,128)(2,1)S(1)} collective-permute-done((bf16[256,768]{1,0:T(8,128)(2,1)S(1)}, bf16[256,768]{1,0:T(8,128)(2,1)S(1)}, u32[]{:S(2)}, u32[]{:S(2)}) %collective-permute-start.31) | collective-permute-done | bytes 393248 | tf_op jit(solution)/shard_map/ppermute | solution.py:19
  (117 shorter events, 36.0 us)
Async XLA Ops:
  7.2 30.4 %copy-start = (bf16[1,128,4096]{2,1,0:T(8,128)(2,1)S(1)}, bf16[1,128,4096]{2,1,0:T(8,128)(2,1)}, u32[]{:S(2)}) copy-start(bf16[1,128,4096]{2,1,0:T(8,128)(2,1)} %param.8) | copy-start | bytes 3145732
  7.2 132.2 %all-gather.6.cloned.1.call-start = ((), (), s32[]{:S(2)}) async-start(), calls=%async_computation.1 | async-start | bytes 3342336 | tf_op jit(solution)/shard_map/all_gather | solution.py:124
  8.9 349.5 %all-gather.4.cloned.1.call-start = ((), (), s32[]{:S(2)}) async-start(), calls=%async_computation | async-start | bytes 2228224 | tf_op jit(solution)/shard_map/all_gather | solution.py:130
  10.9 49.6 %copy-start.12 = (s32[1,128]{1,0:T(1,128)S(1)}, s32[1,128]{1,0:T(1,128)}, u32[]{:S(2)}) copy-start(s32[1,128]{1,0:T(1,128)} %param.15) | copy-start | bytes 1540
  11.1 28.0 %collective-permute-start = (bf16[2,128,256]{1,2,0:T(8,128)(2,1)S(1)}, bf16[2,128,256]{1,2,0:T(8,128)(2,1)S(1)}, u32[]{:S(2)}, u32[]{:S(2)}) collective-permute-start(bf16[2,128,256]{1,2,0:T(8,128)(2,1)S(1)} %get-tuple-element.42), channel_id=1, source_target_pairs={{0,1},{1,2},{2,3},{3,0},{4,5},{5,6},{6,7},{7,4},{8,9},{9,10},{10,1... | collective-permute-start | bytes 393224 | tf_op jit(solution)/shard_map/ppermute | solution.py:32
  20.2 20.4 %collective-permute-start.1 = (bf16[2,128,256]{1,2,0:T(8,128)(2,1)S(1)}, bf16[2,128,256]{1,2,0:T(8,128)(2,1)S(1)}, u32[]{:S(2)}, u32[]{:S(2)}) collective-permute-start(bf16[2,128,256]{1,2,0:T(8,128)(2,1)S(1)} %get-tuple-element.42), channel_id=1, source_target_pairs={{0,2},{1,3},{2,0},{3,1},{4,6},{5,7},{6,4},{7,5},{8,10},{9,11},{10,... | collective-permute-start | bytes 393224 | tf_op jit(solution)/shard_map/ppermute | solution.py:32
  30.2 19.6 %collective-permute-start.2 = (bf16[2,128,256]{1,2,0:T(8,128)(2,1)S(1)}, bf16[2,128,256]{1,2,0:T(8,128)(2,1)S(1)}, u32[]{:S(2)}, u32[]{:S(2)}) collective-permute-start(bf16[2,128,256]{1,2,0:T(8,128)(2,1)S(1)} %get-tuple-element.42), channel_id=1, source_target_pairs={{0,3},{1,0},{2,1},{3,2},{4,7},{5,4},{6,5},{7,6},{8,11},{9,8},{10,9... | collective-permute-start | bytes 393224 | tf_op jit(solution)/shard_map/ppermute | solution.py:32
  50.0 17.8 %collective-permute-start.3 = (bf16[4,2,128,256]{2,3,1,0:T(8,128)(2,1)S(1)}, bf16[4,2,128,256]{2,3,1,0:T(8,128)(2,1)S(1)}, u32[]{:S(2)}, u32[]{:S(2)}) collective-permute-start(bf16[4,2,128,256]{2,3,1,0:T(8,128)(2,1)S(1)} %get-tuple-element.34), channel_id=1, source_target_pairs={{0,4},{1,5},{2,6},{3,7},{4,8},{5,9},{6,10},{7,11},{8,12},{9,13},{1... | collective-permute-start | bytes 1572872 | tf_op jit(solution)/shard_map/ppermute | solution.py:33
  53.4 18.3 %collective-permute-start.4 = (bf16[4,2,128,256]{2,3,1,0:T(8,128)(2,1)S(1)}, bf16[4,2,128,256]{2,3,1,0:T(8,128)(2,1)S(1)}, u32[]{:S(2)}, u32[]{:S(2)}) collective-permute-start(bf16[4,2,128,256]{2,3,1,0:T(8,128)(2,1)S(1)} %get-tuple-element.34), channel_id=1, source_target_pairs={{0,8},{1,9},{2,10},{3,11},{4,12},{5,13},{6,14},{7,15},{8,0},{9,1},... | collective-permute-start | bytes 1572872 | tf_op jit(solution)/shard_map/ppermute | solution.py:33
  56.4 24.6 %collective-permute-start.5 = (bf16[4,2,128,256]{2,3,1,0:T(8,128)(2,1)S(1)}, bf16[4,2,128,256]{2,3,1,0:T(8,128)(2,1)S(1)}, u32[]{:S(2)}, u32[]{:S(2)}) collective-permute-start(bf16[4,2,128,256]{2,3,1,0:T(8,128)(2,1)S(1)} %get-tuple-element.34), channel_id=1, source_target_pairs={{0,12},{1,13},{2,14},{3,15},{4,0},{5,1},{6,2},{7,3},{8,4},{9,5},{1... | collective-permute-start | bytes 1572872 | tf_op jit(solution)/shard_map/ppermute | solution.py:33
  84.3 2.5 copy-start.1
  91.9 50.6 %copy-start.3 = (bf16[4,4,1,128,256]{4,3,1,0,2:T(8,128)(2,1)S(1)}, bf16[4,4,1,128,256]{4,3,1,0,2:T(8,128)(2,1)}, u32[]{:S(2)}) copy-start(bf16[4,4,1,128,256]{4,3,1,0,2:T(8,128)(2,1)} %copy.43) | copy-start | bytes 3145732
  142.5 3.5 copy-start.13
  146.0 0.9 copy-start.7
  163.3 29.8 %collective-permute-start.6 = (bf16[128,512]{1,0:T(8,128)(2,1)}, bf16[128,512]{1,0:T(8,128)(2,1)}, u32[]{:S(2)}, u32[]{:S(2)}) collective-permute-start(bf16[128,512]{1,0:T(8,128)(2,1)} %copy.52), channel_id=1, source_target_pairs={{0,1},{1,2},{2,3},{3,0},{4,5},{5,6},{6,7},{7,4},{8,9},{9,10},{10,1... | collective-permute-start | bytes 393224 | tf_op jit(solution)/shard_map/ppermute | solution.py:32
  167.2 41.2 %collective-permute-start.7 = (bf16[128,512]{1,0:T(8,128)(2,1)}, bf16[128,512]{1,0:T(8,128)(2,1)}, u32[]{:S(2)}, u32[]{:S(2)}) collective-permute-start(bf16[128,512]{1,0:T(8,128)(2,1)} %copy.52), channel_id=1, source_target_pairs={{0,2},{1,3},{2,0},{3,1},{4,6},{5,7},{6,4},{7,5},{8,10},{9,11},{10,... | collective-permute-start | bytes 393224 | tf_op jit(solution)/shard_map/ppermute | solution.py:32
  174.1 34.2 %collective-permute-start.8 = (bf16[128,512]{1,0:T(8,128)(2,1)}, bf16[128,512]{1,0:T(8,128)(2,1)}, u32[]{:S(2)}, u32[]{:S(2)}) collective-permute-start(bf16[128,512]{1,0:T(8,128)(2,1)} %copy.52), channel_id=1, source_target_pairs={{0,3},{1,0},{2,1},{3,2},{4,7},{5,4},{6,5},{7,6},{8,11},{9,8},{10,9... | collective-permute-start | bytes 393224 | tf_op jit(solution)/shard_map/ppermute | solution.py:32
  183.7 33.0 %collective-permute-start.18 = (bf16[4,128,256]{2,1,0:T(8,128)(2,1)}, bf16[4,128,256]{2,1,0:T(8,128)(2,1)}, u32[]{:S(2)}, u32[]{:S(2)}) collective-permute-start(bf16[4,128,256]{2,1,0:T(8,128)(2,1)} %bitcast.240), channel_id=1, source_target_pairs={{0,12},{1,13},{2,14},{3,15},{4,0},{5,1},{6,2},{7,3},{8,4},{9,5},{1... | collective-permute-start | bytes 786440 | tf_op jit(solution)/shard_map/ppermute | solution.py:40
  185.6 15.7 %copy-start.8 = (f32[1,4096]{1,0:T(1,128)S(1)}, f32[1,4096]{1,0:T(1,128)}, u32[]{:S(2)}) copy-start(f32[1,4096]{1,0:T(1,128)} %param.13) | copy-start | bytes 49156
  187.4 33.0 %collective-permute-start.19 = (bf16[4,128,256]{2,1,0:T(8,128)(2,1)}, bf16[4,128,256]{2,1,0:T(8,128)(2,1)}, u32[]{:S(2)}, u32[]{:S(2)}) collective-permute-start(bf16[4,128,256]{2,1,0:T(8,128)(2,1)} %bitcast.239), channel_id=1, source_target_pairs={{0,8},{1,9},{2,10},{3,11},{4,12},{5,13},{6,14},{7,15},{8,0},{9,1},... | collective-permute-start | bytes 786440 | tf_op jit(solution)/shard_map/ppermute | solution.py:40
  193.1 27.3 %collective-permute-start.20 = (bf16[4,128,256]{2,1,0:T(8,128)(2,1)}, bf16[4,128,256]{2,1,0:T(8,128)(2,1)S(1)}, u32[]{:S(2)}, u32[]{:S(2)}) collective-permute-start(bf16[4,128,256]{2,1,0:T(8,128)(2,1)} %bitcast.241), channel_id=1, source_target_pairs={{0,4},{1,5},{2,6},{3,7},{4,8},{5,9},{6,10},{7,11},{8,12},{9,13},{1... | collective-permute-start | bytes 786440 | tf_op jit(solution)/shard_map/ppermute | solution.py:40
  208.3 19.2 %copy-start.2 = (f32[128,4,4,256]{3,2,1,0:T(4,128)S(1)}, f32[128,4,4,256]{3,2,1,0:T(4,128)}, u32[]{:S(2)}) copy-start(f32[128,4,4,256]{3,2,1,0:T(4,128)} %reshape.309) | copy-start | bytes 6291460
  208.3 19.2 %copy-start.9 = (f32[4,4,256]{2,0,1:T(4,128)S(1)}, f32[4,4,256]{2,0,1:T(4,128)}, u32[]{:S(2)}) copy-start(f32[4,4,256]{2,0,1:T(4,128)} %copy.68) | copy-start | bytes 49156
  208.3 19.2 %copy-start.11 = (f32[128]{0:T(128)S(1)}, f32[128]{0:T(128)}, u32[]{:S(2)}) copy-start(f32[128]{0:T(128)} %add_rsqrt_fusion) | copy-start | bytes 1540
  210.6 60.3 %collective-permute-start.9 = (bf16[4,128,512]{2,1,0:T(8,128)(2,1)}, bf16[4,128,512]{2,1,0:T(8,128)(2,1)}, u32[]{:S(2)}, u32[]{:S(2)}) collective-permute-start(bf16[4,128,512]{2,1,0:T(8,128)(2,1)} %get-tuple-element.32), channel_id=1, source_target_pairs={{0,4},{1,5},{2,6},{3,7},{4,8},{5,9},{6,10},{7,11},{8,12},{9,13},{1... | collective-permute-start | bytes 1572872 | tf_op jit(solution)/shard_map/ppermute | solution.py:33
  212.5 64.8 %collective-permute-start.10 = (bf16[4,128,512]{2,1,0:T(8,128)(2,1)}, bf16[4,128,512]{2,1,0:T(8,128)(2,1)}, u32[]{:S(2)}, u32[]{:S(2)}) collective-permute-start(bf16[4,128,512]{2,1,0:T(8,128)(2,1)} %get-tuple-element.32), channel_id=1, source_target_pairs={{0,8},{1,9},{2,10},{3,11},{4,12},{5,13},{6,14},{7,15},{8,0},{9,1},... | collective-permute-start | bytes 1572872 | tf_op jit(solution)/shard_map/ppermute | solution.py:33
  216.7 60.6 %collective-permute-start.11 = (bf16[4,128,512]{2,1,0:T(8,128)(2,1)}, bf16[4,128,512]{2,1,0:T(8,128)(2,1)}, u32[]{:S(2)}, u32[]{:S(2)}) collective-permute-start(bf16[4,128,512]{2,1,0:T(8,128)(2,1)} %get-tuple-element.32), channel_id=1, source_target_pairs={{0,12},{1,13},{2,14},{3,15},{4,0},{5,1},{6,2},{7,3},{8,4},{9,5},{1... | collective-permute-start | bytes 1572872 | tf_op jit(solution)/shard_map/ppermute | solution.py:33
  223.0 18.4 %collective-permute-start.21 = (bf16[128,256]{1,0:T(8,128)(2,1)S(1)}, bf16[128,256]{1,0:T(8,128)(2,1)S(1)}, u32[]{:S(2)}, u32[]{:S(2)}) collective-permute-start(bf16[128,256]{1,0:T(8,128)(2,1)S(1)} %get-tuple-element.38), channel_id=1, source_target_pairs={{0,3},{1,0},{2,1},{3,2},{4,7},{5,4},{6,5},{7,6},{8,11},{9,8},{10,9... | collective-permute-start | bytes 196616 | tf_op jit(solution)/shard_map/ppermute | solution.py:43
  229.0 22.7 %collective-permute-start.22 = (bf16[128,256]{1,0:T(8,128)(2,1)}, bf16[128,256]{1,0:T(8,128)(2,1)}, u32[]{:S(2)}, u32[]{:S(2)}) collective-permute-start(bf16[128,256]{1,0:T(8,128)(2,1)} %get-tuple-element.40), channel_id=1, source_target_pairs={{0,2},{1,3},{2,0},{3,1},{4,6},{5,7},{6,4},{7,5},{8,10},{9,11},{10,... | collective-permute-start | bytes 196616 | tf_op jit(solution)/shard_map/ppermute | solution.py:43
  241.4 17.5 %collective-permute-start.23 = (bf16[128,256]{1,0:T(8,128)(2,1)}, bf16[128,256]{1,0:T(8,128)(2,1)}, u32[]{:S(2)}, u32[]{:S(2)}) collective-permute-start(bf16[128,256]{1,0:T(8,128)(2,1)} %get-tuple-element.39), channel_id=1, source_target_pairs={{0,1},{1,2},{2,3},{3,0},{4,5},{5,6},{6,7},{7,4},{8,9},{9,10},{10,1... | collective-permute-start | bytes 196616 | tf_op jit(solution)/shard_map/ppermute | solution.py:43
  261.1 30.9 %collective-permute-start.25 = (bf16[5,128,256]{2,1,0:T(8,128)(2,1)S(1)}, bf16[5,128,256]{2,1,0:T(8,128)(2,1)S(1)}, u32[]{:S(2)}, u32[]{:S(2)}) collective-permute-start(bf16[5,128,256]{2,1,0:T(8,128)(2,1)S(1)} %get-tuple-element.44), channel_id=1, source_target_pairs={{0,1},{1,2},{2,3},{3,0},{4,5},{5,6},{6,7},{7,4},{8,9},{9,10},{10,1... | collective-permute-start | bytes 983048 | tf_op jit(solution)/shard_map/ppermute | solution.py:54
  266.4 30.2 %collective-permute-start.26 = (bf16[5,128,256]{2,1,0:T(8,128)(2,1)S(1)}, bf16[5,128,256]{2,1,0:T(8,128)(2,1)S(1)}, u32[]{:S(2)}, u32[]{:S(2)}) collective-permute-start(bf16[5,128,256]{2,1,0:T(8,128)(2,1)S(1)} %get-tuple-element.45), channel_id=1, source_target_pairs={{0,2},{1,3},{2,0},{3,1},{4,6},{5,7},{6,4},{7,5},{8,10},{9,11},{10,... | collective-permute-start | bytes 983048 | tf_op jit(solution)/shard_map/ppermute | solution.py:54
  270.9 25.7 %collective-permute-start.27 = (bf16[5,128,256]{2,1,0:T(8,128)(2,1)S(1)}, bf16[5,128,256]{2,1,0:T(8,128)(2,1)S(1)}, u32[]{:S(2)}, u32[]{:S(2)}) collective-permute-start(bf16[5,128,256]{2,1,0:T(8,128)(2,1)S(1)} %get-tuple-element.46), channel_id=1, source_target_pairs={{0,3},{1,0},{2,1},{3,2},{4,7},{5,4},{6,5},{7,6},{8,11},{9,8},{10,9... | collective-permute-start | bytes 983048 | tf_op jit(solution)/shard_map/ppermute | solution.py:54
  277.4 1.8 copy-start.10
  280.0 16.9 %collective-permute-start.12 = (bf16[4,128,256]{2,1,0:T(8,128)(2,1)S(1)}, bf16[4,128,256]{2,1,0:T(8,128)(2,1)S(1)}, u32[]{:S(2)}, u32[]{:S(2)}) collective-permute-start(bf16[4,128,256]{2,1,0:T(8,128)(2,1)S(1)} %bitcast.246), channel_id=1, source_target_pairs={{0,12},{1,13},{2,14},{3,15},{4,0},{5,1},{6,2},{7,3},{8,4},{9,5},{1... | collective-permute-start | bytes 786440 | tf_op jit(solution)/shard_map/ppermute | solution.py:72
  284.6 15.1 %collective-permute-start.13 = (bf16[4,128,256]{2,1,0:T(8,128)(2,1)S(1)}, bf16[4,128,256]{2,1,0:T(8,128)(2,1)S(1)}, u32[]{:S(2)}, u32[]{:S(2)}) collective-permute-start(bf16[4,128,256]{2,1,0:T(8,128)(2,1)S(1)} %bitcast.244), channel_id=1, source_target_pairs={{0,8},{1,9},{2,10},{3,11},{4,12},{5,13},{6,14},{7,15},{8,0},{9,1},... | collective-permute-start | bytes 786440 | tf_op jit(solution)/shard_map/ppermute | solution.py:72
  292.0 10.2 %collective-permute-start.14 = (bf16[4,128,256]{2,1,0:T(8,128)(2,1)S(1)}, bf16[4,128,256]{2,1,0:T(8,128)(2,1)S(1)}, u32[]{:S(2)}, u32[]{:S(2)}) collective-permute-start(bf16[4,128,256]{2,1,0:T(8,128)(2,1)S(1)} %bitcast.242), channel_id=1, source_target_pairs={{0,4},{1,5},{2,6},{3,7},{4,8},{5,9},{6,10},{7,11},{8,12},{9,13},{1... | collective-permute-start | bytes 786440 | tf_op jit(solution)/shard_map/ppermute | solution.py:72
  302.5 46.5 %collective-permute-start.15 = (bf16[4,128,256]{2,1,0:T(8,128)(2,1)S(1)}, bf16[4,128,256]{2,1,0:T(8,128)(2,1)S(1)}, u32[]{:S(2)}, u32[]{:S(2)}) collective-permute-start(bf16[4,128,256]{2,1,0:T(8,128)(2,1)S(1)} %get-tuple-element.18), channel_id=1, source_target_pairs={{0,3},{1,0},{2,1},{3,2},{4,7},{5,4},{6,5},{7,6},{8,11},{9,8},{10,9... | collective-permute-start | bytes 786440 | tf_op jit(solution)/shard_map/ppermute | solution.py:76
  310.0 40.9 %collective-permute-start.16 = (bf16[4,128,256]{2,1,0:T(8,128)(2,1)S(1)}, bf16[4,128,256]{2,1,0:T(8,128)(2,1)S(1)}, u32[]{:S(2)}, u32[]{:S(2)}) collective-permute-start(bf16[4,128,256]{2,1,0:T(8,128)(2,1)S(1)} %get-tuple-element.20), channel_id=1, source_target_pairs={{0,2},{1,3},{2,0},{3,1},{4,6},{5,7},{6,4},{7,5},{8,10},{9,11},{10,... | collective-permute-start | bytes 786440 | tf_op jit(solution)/shard_map/ppermute | solution.py:76
  312.9 38.0 %collective-permute-start.17 = (bf16[4,128,256]{2,1,0:T(8,128)(2,1)S(1)}, bf16[4,128,256]{2,1,0:T(8,128)(2,1)S(1)}, u32[]{:S(2)}, u32[]{:S(2)}) collective-permute-start(bf16[4,128,256]{2,1,0:T(8,128)(2,1)S(1)} %get-tuple-element.17), channel_id=1, source_target_pairs={{0,1},{1,2},{2,3},{3,0},{4,5},{5,6},{6,7},{7,4},{8,9},{9,10},{10,1... | collective-permute-start | bytes 786440 | tf_op jit(solution)/shard_map/ppermute | solution.py:76
  322.0 42.3 %collective-permute-start.28 = (bf16[8,128,256]{2,1,0:T(8,128)(2,1)}, bf16[8,128,256]{2,1,0:T(8,128)(2,1)}, u32[]{:S(2)}, u32[]{:S(2)}) collective-permute-start(bf16[8,128,256]{2,1,0:T(8,128)(2,1)} %get-tuple-element.35), channel_id=1, source_target_pairs={{0,4},{1,5},{2,6},{3,7},{4,8},{5,9},{6,10},{7,11},{8,12},{9,13},{1... | collective-permute-start | bytes 1572872 | tf_op jit(solution)/shard_map/ppermute | solution.py:61
  329.6 35.8 %collective-permute-start.29 = (bf16[8,128,256]{2,1,0:T(8,128)(2,1)S(1)}, bf16[8,128,256]{2,1,0:T(8,128)(2,1)}, u32[]{:S(2)}, u32[]{:S(2)}) collective-permute-start(bf16[8,128,256]{2,1,0:T(8,128)(2,1)S(1)} %get-tuple-element.36), channel_id=1, source_target_pairs={{0,8},{1,9},{2,10},{3,11},{4,12},{5,13},{6,14},{7,15},{8,0},{9,1},... | collective-permute-start | bytes 1572872 | tf_op jit(solution)/shard_map/ppermute | solution.py:61
  349.0 18.7 %collective-permute-start.30 = (bf16[8,128,256]{2,1,0:T(8,128)(2,1)S(1)}, bf16[8,128,256]{2,1,0:T(8,128)(2,1)}, u32[]{:S(2)}, u32[]{:S(2)}) collective-permute-start(bf16[8,128,256]{2,1,0:T(8,128)(2,1)S(1)} %get-tuple-element.37), channel_id=1, source_target_pairs={{0,12},{1,13},{2,14},{3,15},{4,0},{5,1},{6,2},{7,3},{8,4},{9,5},{1... | collective-permute-start | bytes 1572872 | tf_op jit(solution)/shard_map/ppermute | solution.py:61
  362.3 69.2 %collective-permute-start.24 = (bf16[128,4096]{1,0:T(8,128)(2,1)S(1)}, bf16[128,4096]{1,0:T(8,128)(2,1)S(1)}, u32[]{:S(2)}, u32[]{:S(2)}) collective-permute-start(bf16[128,4096]{1,0:T(8,128)(2,1)S(1)} %add_convert_fusion), channel_id=1, source_target_pairs={{0,16},{16,32},{32,48},{48,64},{64,80},{80,96},{96,112},{112,128},... | collective-permute-start | bytes 3145736 | tf_op jit(solution)/shard_map/ppermute | solution.py:14
  365.3 3.6 copy-start.4
  365.3 3.6 copy-start.6
  368.9 61.8 %copy-start.5 = (bf16[1,256,768]{2,1,0:T(8,128)(2,1)S(1)}, bf16[1,256,768]{2,1,0:T(8,128)(2,1)}, u32[]{:S(2)}) copy-start(bf16[1,256,768]{2,1,0:T(8,128)(2,1)} %param.14) | copy-start | bytes 1179652
  371.4 59.3 %collective-permute-start.31 = (bf16[256,768]{1,0:T(8,128)(2,1)S(1)}, bf16[256,768]{1,0:T(8,128)(2,1)S(1)}, u32[]{:S(2)}, u32[]{:S(2)}) collective-permute-start(bf16[256,768]{1,0:T(8,128)(2,1)S(1)} %fusion.35), channel_id=1, source_target_pairs={{0,496},{16,480},{32,464},{48,448},{64,432},{80,416},{96,400},{112... | collective-permute-start | bytes 1179656 | tf_op jit(solution)/shard_map/ppermute | solution.py:19
Sparse Core Ops, SparseCore 0:
  11.6 127.7 all-gather.5
  142.4 124.1 all-gather.3

commit v11 on v9

--- a/solution.py
+++ b/solution.py
@@ -77,6 +77,35 @@
     second = jnp.stack(second, axis=1)
     second = jnp.roll(jnp.roll(second, o, axis=0), i, axis=1)
     return second.transpose(2, 0, 1, 3).reshape(n, outer * INNER * w)
+
+
+def gather_scatter_return(x, cols, y, o, i):
+    outer = lax.axis_size("seq") // INNER
+    m, n, w = x.shape
+    parts = cols.reshape(n, outer, INNER, w).transpose(2, 1, 0, 3)
+    first = [jnp.concatenate([x, parts[i]])]
+    for k in range(1, INNER):
+        piece = lax.dynamic_index_in_dim(parts, (i + k) % INNER, 0, keepdims=False)
+        first.append(lax.ppermute(jnp.concatenate([x, piece]), "seq", seq_pairs(k, 0)))
+    first = jnp.stack(first, axis=1)
+    own, rest = first[:m], first[m:]
+    second = []
+    back = [y[0]] + [None] * (outer - 1)
+    for k in range(1, outer):
+        piece = lax.dynamic_index_in_dim(rest, (o + k) % outer, 0, keepdims=False)
+        payload = jnp.concatenate([own.reshape(m * INNER, n, w), piece, y[outer - k].astype(own.dtype)])
+        got = lax.ppermute(payload, "seq", seq_pairs(k, 1))
+        second.append(got[: (m + 1) * INNER])
+        back[outer - k] = got[(m + 1) * INNER :]
+    gathered = jnp.stack([own] + [s[: m * INNER].reshape(m, INNER, n, w) for s in second])
+    scattered = jnp.stack([lax.dynamic_index_in_dim(rest, o, 0, keepdims=False)] + [s[m * INNER :] for s in second])
+    back = jnp.stack(back, axis=1)
+    returned = [back[0]]
+    for k in range(1, INNER):
+        returned.append(lax.ppermute(back[k], "seq", seq_pairs(INNER - k, 0)))
+    returned = jnp.stack(returned, axis=1)
+    returned = jnp.roll(jnp.roll(returned, o, axis=0), i, axis=1)
+    return gathered, scattered, returned.transpose(2, 0, 1, 3).reshape(n, outer * INNER * w)
 
 
 def contract_last(left, right):
@@ -157,12 +186,13 @@
     kv_part = jnp.concatenate([key_part, value_part], axis=1).reshape(outer, INNER, count, 2 * HEAD)
     query_all = gather_blocks(query_grad)
     kv_grad = reduce_blocks(kv_part, jnp.bfloat16).astype(jnp.bfloat16)
-    kv_all, hidden_cols = gather_and_scatter(kv_grad[None], hidden, o, i)
+    block = contract_last(query_all.reshape(size * count, -1), up_input_weight[0][:, :width])
+    kv_all, hidden_cols, hidden_grad = gather_scatter_return(
+        kv_grad[None], hidden, block.astype(jnp.bfloat16).reshape(outer, INNER, count, -1), o, i
+    )
     hidden_cols = hidden_cols.reshape(size * count, -1)
     grad_all = jnp.concatenate([query_all, kv_all[:, 0]], axis=-1).reshape(size * count, -1)
     input_term = contract_first(hidden_cols, grad_all).astype(jnp.bfloat16)
-    block = contract_last(query_all.reshape(size * count, -1), up_input_weight[0][:, :width])
-    hidden_grad = gather_columns(block.astype(jnp.bfloat16).reshape(outer, INNER, count, -1), o, i)
     hidden_grad = hidden_grad.astype(jnp.float32) + contract_last(kv_grad, kv_weight_all)
     scaled = hidden_grad * upward_gain[0]
     input_grad = cotangent.astype(jnp.float32) + inverse_up * (

time: 439 us -> 513 us (1.17)
  the two profiles are of different devices: /device:TPU:25 before, /device:TPU:70 now
where the time goes in v11:
time: 513 us; the launch traced here: 512 us
  waiting for transfers between devices  266 us (52%)
  starting transfers between devices  144 us (28%)
  matrix products  37.1 us (7%)
  other arithmetic  25.6 us (5%)
  local copies, waits for them, and re-layouts  24.5 us (5%)
  between operations  14.9 us (3%)
    all_gather x1, waiting for transfers between devices, per_device(): lax.all_gather(up_output_weight[0], 'seq', axis=1, tiled=True)  77 us
    all_gather x1, waiting for transfers between devices, per_device(): lax.all_gather(up_input_weight[0][:, width:], 'seq', axis=0, tiled=True)  51.9 us
    ppermute x6, starting transfers between devices, gather_blocks(): lax.ppermute(x, 'seq', seq_pairs(k, 0))  41.5 us
    ppermute x3, waiting for transfers between devices, gather_scatter_return(): lax.ppermute(jnp.concatenate([x, piece]), 'seq', seq_pairs(k, 0))  37.2 us
    ppermute x3, waiting for transfers between devices, gather_scatter_return(): got = lax.ppermute(payload, 'seq', seq_pairs(k, 1))  35.3 us
    ppermute x1, waiting for transfers between devices, mirrored(): lax.ppermute(value, axis, [(source, count - 1 - source) for source in ran...  24.9 us
    ppermute x6, starting transfers between devices, gather_blocks(): lax.ppermute(first, 'seq', seq_pairs(k, 1))  22.5 us
    ppermute x3, waiting for transfers between devices, gather_scatter_return(): returned.append(lax.ppermute(back[k], 'seq', seq_pairs(INNER - k, 0)))  19.3 us
  transfers between devices with their start and end apart: 31, of which 15 were waited for; matrix products, arithmetic and copies ran while one was open for 11% of the time, Pallas kernels for 0%

profile of v11, /device:TPU:70, one launch (start us, length us, event | category | flops | bytes accessed | tf_op | source)
XLA Modules:
  0.0 511.9 jit_solution(13588178555546674633)
XLA Ops:
  9.1 9.1 %collective-permute-start = (bf16[128,256]{0,1:T(8,128)(2,1)S(1)}, bf16[128,256]{0,1:T(8,128)(2,1)S(1)}, u32[]{:S(2)}, u32[]{:S(2)}) collective-permute-start(bf16[128,256]{0,1:T(8,128)(2,1)S(1)} %get-tuple-element.43), channel_id=1, source_target_pairs={{0,1},{1,2},{2,3},{3,0},{4,5},{5,6},{6,7},{7,4},{8,9},{9,10},{10,1... | collective-permute-start | bytes 196616 | tf_op jit(solution)/shard_map/ppermute | solution.py:32
  18.2 9.1 %collective-permute-start.1 = (bf16[128,256]{0,1:T(8,128)(2,1)S(1)}, bf16[128,256]{0,1:T(8,128)(2,1)S(1)}, u32[]{:S(2)}, u32[]{:S(2)}) collective-permute-start(bf16[128,256]{0,1:T(8,128)(2,1)S(1)} %get-tuple-element.43), channel_id=1, source_target_pairs={{0,2},{1,3},{2,0},{3,1},{4,6},{5,7},{6,4},{7,5},{8,10},{9,11},{10,... | collective-permute-start | bytes 196616 | tf_op jit(solution)/shard_map/ppermute | solution.py:32
  27.3 5.5 %collective-permute-start.2 = (bf16[128,256]{0,1:T(8,128)(2,1)S(1)}, bf16[128,256]{0,1:T(8,128)(2,1)S(1)}, u32[]{:S(2)}, u32[]{:S(2)}) collective-permute-start(bf16[128,256]{0,1:T(8,128)(2,1)S(1)} %get-tuple-element.43), channel_id=1, source_target_pairs={{0,3},{1,0},{2,1},{3,2},{4,7},{5,4},{6,5},{7,6},{8,11},{9,8},{10,9... | collective-permute-start | bytes 196616 | tf_op jit(solution)/shard_map/ppermute | solution.py:32
  33.0 1.7 compare_and_fusion
  34.8 3.0 collective-permute-done.1
  37.7 5.6 %collective-permute-done.2 = bf16[128,256]{0,1:T(8,128)(2,1)S(1)} collective-permute-done((bf16[128,256]{0,1:T(8,128)(2,1)S(1)}, bf16[128,256]{0,1:T(8,128)(2,1)S(1)}, u32[]{:S(2)}, u32[]{:S(2)}) %collective-permute-start.2) | collective-permute-done | bytes 65568 | tf_op jit(solution)/shard_map/ppermute | solution.py:32
  44.0 1.9 collective-permute-start.3
  45.9 4.1 collective-permute-start.4
  50.1 1.9 collective-permute-start.5
  52.0 2.1 fusion.20
  54.1 1.7 reshape.210
  61.7 2.2 pad_maximum_fusion.8
  63.9 2.3 copy.41
  66.2 5.5 %fusion.91 = (f32[128,4]{0,1:T(4,128)}, f32[128,4,2048]{0,2,1:T(8,128)}) fusion(pred[128,2048]{0,1:T(8,128)(4,1)} %compare_and_fusion, bf16[128,4,128]{0,2,1:T(8,128)(2,1)S(1)} %bitcast.230, bf16[2048,256]{1,0:T(8,128)(2,1)} %bitcast.197), kind=kOutput, calls=%fused_computation.163 | convolution fusion | flops 273680384 | bytes 5376000 | tf_op jit(solution)/shard_map/sub | solution.py:172
  71.7 77.0 %all-gather.6.cloned.1.call-done = bf16[1,512,4096]{2,1,0:T(8,128)(2,1)} async-done(((bf16[1,512,256]{2,1,0:T(8,128)(2,1)}), bf16[1,512,4096]{2,1,0:T(8,128)(2,1)}) %all-gather.6.cloned.1.call-update) | async-done | bytes 4194320 | tf_op jit(solution)/shard_map/all_gather | solution.py:152
  148.6 4.0 fusion.38
  152.8 3.9 fusion.67
  156.7 1.8 convolution_bitcast_fusion
  158.5 8.2 %convolution_bitcast_fusion.1 = f32[2048,128]{0,1:T(8,128)} fusion(bf16[128,4,128]{0,2,1:T(8,128)(2,1)S(1)} %bitcast.231, f32[128,4,2048]{0,2,1:T(8,128)} %fusion.67, f32[128,4,2048]{0,2,1:T(8,128)} %get-tuple-element.49, f32[128,4]{0,1:T(4,128)S(1)} %copy-done.18), kind=kOutput, calls=%fused_computation.27 | convolution fusion | flops 275778048 | bytes 9570304 | tf_op jit(solution)/shard_map/tgj,tgh->jh/dot_general | solution.py:184
  166.8 1.7 fusion.19
  169.3 1.8 copy.82
  171.1 2.8 collective-permute-start.12
  173.9 1.8 copy.83
  175.7 2.9 collective-permute-start.13
  179.4 4.1 collective-permute-start.14
  183.6 2.2 fusion.22
  188.3 4.2 collective-permute-done.14
  193.7 4.9 collective-permute-start.15
  198.6 3.5 collective-permute-start.16
  202.1 7.3 %collective-permute-start.17 = (bf16[128,256]{1,0:T(8,128)(2,1)S(1)}, bf16[128,256]{1,0:T(8,128)(2,1)S(1)}, u32[]{:S(2)}, u32[]{:S(2)}) collective-permute-start(bf16[128,256]{1,0:T(8,128)(2,1)S(1)} %get-tuple-element.38), channel_id=1, source_target_pairs={{0,1},{1,2},{2,3},{3,0},{4,5},{5,6},{6,7},{7,4},{8,9},{9,10},{10,1... | collective-permute-start | bytes 196616 | tf_op jit(solution)/shard_map/ppermute | solution.py:43
  209.5 4.7 collective-permute-done.16
  215.3 6.2 %collective-permute-start.18 = (bf16[5,128,256]{2,1,0:T(8,128)(2,1)}, bf16[5,128,256]{2,1,0:T(8,128)(2,1)S(1)}, u32[]{:S(2)}, u32[]{:S(2)}) collective-permute-start(bf16[5,128,256]{2,1,0:T(8,128)(2,1)} %get-tuple-element.45), channel_id=1, source_target_pairs={{0,1},{1,2},{2,3},{3,0},{4,5},{5,6},{6,7},{7,4},{8,9},{9,10},{10,1... | collective-permute-start | bytes 983048 | tf_op jit(solution)/shard_map/ppermute | solution.py:89
  221.5 7.2 %fusion.41 = bf16[128,4,128]{0,2,1:T(8,128)(2,1)S(1)} fusion(f32[128,4,2048]{0,2,1:T(8,128)} %fusion.67, bf16[2048,256]{1,0:T(8,128)(2,1)S(1)} %bitcast.199, f32[128,4,2048]{0,2,1:T(8,128)} %get-tuple-element.49, f32[128,4]{0,1:T(4,128)} %get-tuple-element.48), kind=kOutput, calls=%fused_computation.58 | convolution fusion | flops 275843584 | bytes 17436672 | tf_op jit(solution)/shard_map/tgj,jh->tgh/dot_general | solution.py:180
  228.8 6.0 %collective-permute-start.6 = (bf16[128,512]{1,0:T(8,128)(2,1)S(1)}, bf16[128,512]{1,0:T(8,128)(2,1)S(1)}, u32[]{:S(2)}, u32[]{:S(2)}) collective-permute-start(bf16[128,512]{1,0:T(8,128)(2,1)S(1)} %copy.48), channel_id=1, source_target_pairs={{0,1},{1,2},{2,3},{3,0},{4,5},{5,6},{6,7},{7,4},{8,9},{9,10},{10,1... | collective-permute-start | bytes 393224 | tf_op jit(solution)/shard_map/ppermute | solution.py:32
  234.8 5.0 collective-permute-start.7
  239.8 6.8 %collective-permute-start.8 = (bf16[128,512]{1,0:T(8,128)(2,1)S(1)}, bf16[128,512]{1,0:T(8,128)(2,1)S(1)}, u32[]{:S(2)}, u32[]{:S(2)}) collective-permute-start(bf16[128,512]{1,0:T(8,128)(2,1)S(1)} %copy.48), channel_id=1, source_target_pairs={{0,3},{1,0},{2,1},{3,2},{4,7},{5,4},{6,5},{7,6},{8,11},{9,8},{10,9... | collective-permute-start | bytes 393224 | tf_op jit(solution)/shard_map/ppermute | solution.py:32
  246.6 6.5 %collective-permute-start.19 = (bf16[5,128,256]{2,1,0:T(8,128)(2,1)}, bf16[5,128,256]{2,1,0:T(8,128)(2,1)S(1)}, u32[]{:S(2)}, u32[]{:S(2)}) collective-permute-start(bf16[5,128,256]{2,1,0:T(8,128)(2,1)} %get-tuple-element.46), channel_id=1, source_target_pairs={{0,2},{1,3},{2,0},{3,1},{4,6},{5,7},{6,4},{7,5},{8,10},{9,11},{10,... | collective-permute-start | bytes 983048 | tf_op jit(solution)/shard_map/ppermute | solution.py:89
  253.2 3.7 collective-permute-start.20
  258.5 1.8 fusion.87
  260.3 9.8 %collective-permute-start.9 = (bf16[4,128,512]{2,1,0:T(8,128)(2,1)}, bf16[4,128,512]{2,1,0:T(8,128)(2,1)}, u32[]{:S(2)}, u32[]{:S(2)}) collective-permute-start(bf16[4,128,512]{2,1,0:T(8,128)(2,1)} %get-tuple-element.33), channel_id=1, source_target_pairs={{0,4},{1,5},{2,6},{3,7},{4,8},{5,9},{6,10},{7,11},{8,12},{9,13},{1... | collective-permute-start | bytes 1572872 | tf_op jit(solution)/shard_map/ppermute | solution.py:33
  270.1 1.9 collective-permute-start.10
  272.1 2.8 collective-permute-start.11
  274.8 1.6 slice.180
  276.5 6.2 %collective-permute-done.19 = bf16[5,128,256]{2,1,0:T(8,128)(2,1)S(1)} collective-permute-done((bf16[5,128,256]{2,1,0:T(8,128)(2,1)}, bf16[5,128,256]{2,1,0:T(8,128)(2,1)S(1)}, u32[]{:S(2)}, u32[]{:S(2)}) %collective-permute-start.19) | collective-permute-done | bytes 327712 | tf_op jit(solution)/shard_map/ppermute | solution.py:89
  282.7 31.1 %collective-permute-done.20 = bf16[5,128,256]{2,1,0:T(8,128)(2,1)S(1)} collective-permute-done((bf16[5,128,256]{2,1,0:T(8,128)(2,1)}, bf16[5,128,256]{2,1,0:T(8,128)(2,1)S(1)}, u32[]{:S(2)}, u32[]{:S(2)}) %collective-permute-start.20) | collective-permute-done | bytes 327712 | tf_op jit(solution)/shard_map/ppermute | solution.py:89
  314.1 1.6 pad_maximum_fusion.1
  316.7 9.6 %collective-permute-start.23 = (bf16[12,128,256]{2,1,0:T(8,128)(2,1)S(1)}, bf16[12,128,256]{2,1,0:T(8,128)(2,1)S(1)}, u32[]{:S(2)}, u32[]{:S(2)}) collective-permute-start(bf16[12,128,256]{2,1,0:T(8,128)(2,1)S(1)} %get-tuple-element.36), channel_id=1, source_target_pairs={{0,4},{1,5},{2,6},{3,7},{4,8},{5,9},{6,10},{7,11},{8,12},{9,13},{1... | collective-permute-start | bytes 2359304 | tf_op jit(solution)/shard_map/ppermute | solution.py:97
  326.3 1.9 collective-permute-start.22
  328.2 2.8 collective-permute-start.21
  331.0 31.2 %collective-permute-done.23 = bf16[12,128,256]{2,1,0:T(8,128)(2,1)S(1)} collective-permute-done((bf16[12,128,256]{2,1,0:T(8,128)(2,1)S(1)}, bf16[12,128,256]{2,1,0:T(8,128)(2,1)S(1)}, u32[]{:S(2)}, u32[]{:S(2)}) %collective-permute-start.23) | collective-permute-done | bytes 786464 | tf_op jit(solution)/shard_map/ppermute | solution.py:97
  363.8 4.1 collective-permute-done.21
  369.6 4.0 collective-permute-start.24
  373.6 6.7 %collective-permute-start.25 = (bf16[4,128,256]{2,1,0:T(8,128)(2,1)}, bf16[4,128,256]{2,1,0:T(8,128)(2,1)S(1)}, u32[]{:S(2)}, u32[]{:S(2)}) collective-permute-start(bf16[4,128,256]{2,1,0:T(8,128)(2,1)} %get-tuple-element.11), channel_id=1, source_target_pairs={{0,2},{1,3},{2,0},{3,1},{4,6},{5,7},{6,4},{7,5},{8,10},{9,11},{10,... | collective-permute-start | bytes 786440 | tf_op jit(solution)/shard_map/ppermute | solution.py:105
  380.4 5.6 %collective-permute-start.26 = (bf16[4,128,256]{2,1,0:T(8,128)(2,1)}, bf16[4,128,256]{2,1,0:T(8,128)(2,1)}, u32[]{:S(2)}, u32[]{:S(2)}) collective-permute-start(bf16[4,128,256]{2,1,0:T(8,128)(2,1)} %get-tuple-element.8), channel_id=1, source_target_pairs={{0,1},{1,2},{2,3},{3,0},{4,5},{5,6},{6,7},{7,4},{8,9},{9,10},{10,1... | collective-permute-start | bytes 786440 | tf_op jit(solution)/shard_map/ppermute | solution.py:105
  387.1 10.9 %collective-permute-done.25 = bf16[4,128,256]{2,1,0:T(8,128)(2,1)S(1)} collective-permute-done((bf16[4,128,256]{2,1,0:T(8,128)(2,1)}, bf16[4,128,256]{2,1,0:T(8,128)(2,1)S(1)}, u32[]{:S(2)}, u32[]{:S(2)}) %collective-permute-start.25) | collective-permute-done | bytes 262176 | tf_op jit(solution)/shard_map/ppermute | solution.py:105
  398.1 8.4 %collective-permute-done.26 = bf16[4,128,256]{2,1,0:T(8,128)(2,1)} collective-permute-done((bf16[4,128,256]{2,1,0:T(8,128)(2,1)}, bf16[4,128,256]{2,1,0:T(8,128)(2,1)}, u32[]{:S(2)}, u32[]{:S(2)}) %collective-permute-start.26) | collective-permute-done | bytes 262176 | tf_op jit(solution)/shard_map/ppermute | solution.py:105
  406.4 1.9 fusion.48
  410.2 2.1 reshape.211
  412.3 51.9 %all-gather.4.cloned.1.call-done = bf16[4096,256]{1,0:T(8,128)(2,1)} async-done(((bf16[256,256]{1,0:T(8,128)(2,1)}), bf16[4096,256]{1,0:T(8,128)(2,1)}) %all-gather.4.cloned.1.call-update) | async-done | bytes 2097168 | tf_op jit(solution)/shard_map/all_gather | solution.py:154
  464.2 3.2 multiply_reduce_fusion.1
  468.2 1.9 collective-permute-start.27
  470.1 2.4 fusion.35
  472.6 5.8 %collective-permute-start.28 = (bf16[256,768]{1,0:T(8,128)(2,1)S(1)}, bf16[256,768]{1,0:T(8,128)(2,1)S(1)}, u32[]{:S(2)}, u32[]{:S(2)}) collective-permute-start(bf16[256,768]{1,0:T(8,128)(2,1)S(1)} %fusion.35), channel_id=1, source_target_pairs={{0,496},{16,480},{32,464},{48,448},{64,432},{80,416},{96,400},{112... | collective-permute-start | bytes 1179656 | tf_op jit(solution)/shard_map/ppermute | solution.py:19
  478.3 24.9 %collective-permute-done.28 = bf16[256,768]{1,0:T(8,128)(2,1)S(1)} collective-permute-done((bf16[256,768]{1,0:T(8,128)(2,1)S(1)}, bf16[256,768]{1,0:T(8,128)(2,1)S(1)}, u32[]{:S(2)}, u32[]{:S(2)}) %collective-permute-start.28) | collective-permute-done | bytes 393248 | tf_op jit(solution)/shard_map/ppermute | solution.py:19
  (104 shorter events, 27.1 us)
Async XLA Ops:
  7.2 47.0 %copy-start = (bf16[1,128,4096]{2,1,0:T(8,128)(2,1)S(1)}, bf16[1,128,4096]{2,1,0:T(8,128)(2,1)}, u32[]{:S(2)}) copy-start(bf16[1,128,4096]{2,1,0:T(8,128)(2,1)} %param.8) | copy-start | bytes 3145732
  7.2 141.5 %all-gather.6.cloned.1.call-start = ((), (), s32[]{:S(2)}) async-start(), calls=%async_computation.1 | async-start | bytes 4456448 | tf_op jit(solution)/shard_map/all_gather | solution.py:152
  7.9 48.5 %copy-start.12 = (f32[1,4096]{1,0:T(1,128)S(1)}, f32[1,4096]{1,0:T(1,128)}, u32[]{:S(2)}) copy-start(f32[1,4096]{1,0:T(1,128)} %param.13) | copy-start | bytes 49156
  7.9 456.2 %all-gather.4.cloned.1.call-start = ((), (), s32[]{:S(2)}) async-start(), calls=%async_computation | async-start | bytes 2228224 | tf_op jit(solution)/shard_map/all_gather | solution.py:154
  9.1 25.7 %collective-permute-start = (bf16[128,256]{0,1:T(8,128)(2,1)S(1)}, bf16[128,256]{0,1:T(8,128)(2,1)S(1)}, u32[]{:S(2)}, u32[]{:S(2)}) collective-permute-start(bf16[128,256]{0,1:T(8,128)(2,1)S(1)} %get-tuple-element.43), channel_id=1, source_target_pairs={{0,1},{1,2},{2,3},{3,0},{4,5},{5,6},{6,7},{7,4},{8,9},{9,10},{10,1... | collective-permute-start | bytes 196616 | tf_op jit(solution)/shard_map/ppermute | solution.py:32
  18.2 19.5 %collective-permute-start.1 = (bf16[128,256]{0,1:T(8,128)(2,1)S(1)}, bf16[128,256]{0,1:T(8,128)(2,1)S(1)}, u32[]{:S(2)}, u32[]{:S(2)}) collective-permute-start(bf16[128,256]{0,1:T(8,128)(2,1)S(1)} %get-tuple-element.43), channel_id=1, source_target_pairs={{0,2},{1,3},{2,0},{3,1},{4,6},{5,7},{6,4},{7,5},{8,10},{9,11},{10,... | collective-permute-start | bytes 196616 | tf_op jit(solution)/shard_map/ppermute | solution.py:32
  27.3 16.0 %collective-permute-start.2 = (bf16[128,256]{0,1:T(8,128)(2,1)S(1)}, bf16[128,256]{0,1:T(8,128)(2,1)S(1)}, u32[]{:S(2)}, u32[]{:S(2)}) collective-permute-start(bf16[128,256]{0,1:T(8,128)(2,1)S(1)} %get-tuple-element.43), channel_id=1, source_target_pairs={{0,3},{1,0},{2,1},{3,2},{4,7},{5,4},{6,5},{7,6},{8,11},{9,8},{10,9... | collective-permute-start | bytes 196616 | tf_op jit(solution)/shard_map/ppermute | solution.py:32
  44.0 17.7 %collective-permute-start.3 = (bf16[4,128,256]{1,2,0:T(8,128)(2,1)}, bf16[4,128,256]{1,2,0:T(8,128)(2,1)}, u32[]{:S(2)}, u32[]{:S(2)}) collective-permute-start(bf16[4,128,256]{1,2,0:T(8,128)(2,1)} %get-tuple-element.41), channel_id=1, source_target_pairs={{0,4},{1,5},{2,6},{3,7},{4,8},{5,9},{6,10},{7,11},{8,12},{9,13},{1... | collective-permute-start | bytes 786440 | tf_op jit(solution)/shard_map/ppermute | solution.py:33
  45.9 15.8 %collective-permute-start.4 = (bf16[4,128,256]{1,2,0:T(8,128)(2,1)}, bf16[4,128,256]{1,2,0:T(8,128)(2,1)}, u32[]{:S(2)}, u32[]{:S(2)}) collective-permute-start(bf16[4,128,256]{1,2,0:T(8,128)(2,1)} %get-tuple-element.41), channel_id=1, source_target_pairs={{0,8},{1,9},{2,10},{3,11},{4,12},{5,13},{6,14},{7,15},{8,0},{9,1},... | collective-permute-start | bytes 786440 | tf_op jit(solution)/shard_map/ppermute | solution.py:33
  50.1 11.6 %collective-permute-start.5 = (bf16[4,128,256]{1,2,0:T(8,128)(2,1)}, bf16[4,128,256]{1,2,0:T(8,128)(2,1)}, u32[]{:S(2)}, u32[]{:S(2)}) collective-permute-start(bf16[4,128,256]{1,2,0:T(8,128)(2,1)} %get-tuple-element.41), channel_id=1, source_target_pairs={{0,12},{1,13},{2,14},{3,15},{4,0},{5,1},{6,2},{7,3},{8,4},{9,5},{1... | collective-permute-start | bytes 786440 | tf_op jit(solution)/shard_map/ppermute | solution.py:33
  152.8 3.9 copy-start.17
  152.8 3.9 copy-start.18
  166.8 16.8 %copy-start.13 = (f32[4,4,256]{2,0,1:T(4,128)S(1)}, f32[4,4,256]{2,0,1:T(4,128)}, u32[]{:S(2)}) copy-start(f32[4,4,256]{2,0,1:T(4,128)} %copy.60) | copy-start | bytes 49156
  166.8 16.8 %copy-start.15 = (f32[128]{0:T(128)S(1)}, f32[128]{0:T(128)}, u32[]{:S(2)}) copy-start(f32[128]{0:T(128)} %add_rsqrt_fusion) | copy-start | bytes 1540
  171.1 17.2 %collective-permute-start.12 = (bf16[4,128,256]{2,1,0:T(8,128)(2,1)}, bf16[4,128,256]{2,1,0:T(8,128)(2,1)}, u32[]{:S(2)}, u32[]{:S(2)}) collective-permute-start(bf16[4,128,256]{2,1,0:T(8,128)(2,1)} %bitcast.224), channel_id=1, source_target_pairs={{0,12},{1,13},{2,14},{3,15},{4,0},{5,1},{6,2},{7,3},{8,4},{9,5},{1... | collective-permute-start | bytes 786440 | tf_op jit(solution)/shard_map/ppermute | solution.py:40
  175.7 12.6 %collective-permute-start.13 = (bf16[4,128,256]{2,1,0:T(8,128)(2,1)}, bf16[4,128,256]{2,1,0:T(8,128)(2,1)}, u32[]{:S(2)}, u32[]{:S(2)}) collective-permute-start(bf16[4,128,256]{2,1,0:T(8,128)(2,1)} %bitcast.225), channel_id=1, source_target_pairs={{0,8},{1,9},{2,10},{3,11},{4,12},{5,13},{6,14},{7,15},{8,0},{9,1},... | collective-permute-start | bytes 786440 | tf_op jit(solution)/shard_map/ppermute | solution.py:40
  179.4 13.1 %collective-permute-start.14 = (bf16[4,128,256]{2,1,0:T(8,128)(2,1)}, bf16[4,128,256]{2,1,0:T(8,128)(2,1)S(1)}, u32[]{:S(2)}, u32[]{:S(2)}) collective-permute-start(bf16[4,128,256]{2,1,0:T(8,128)(2,1)} %bitcast.226), channel_id=1, source_target_pairs={{0,4},{1,5},{2,6},{3,7},{4,8},{5,9},{6,10},{7,11},{8,12},{9,13},{1... | collective-permute-start | bytes 786440 | tf_op jit(solution)/shard_map/ppermute | solution.py:40
  185.8 23.6 %copy-start.1 = (bf16[128,4,4,256]{3,0,1,2:T(8,128)(2,1)S(1)}, bf16[128,4,4,256]{3,0,1,2:T(8,128)(2,1)}, u32[]{:S(2)}) copy-start(bf16[128,4,4,256]{3,0,1,2:T(8,128)(2,1)} %fusion.22) | copy-start | bytes 3145732
  193.7 27.8 %copy-start.3 = (bf16[4,4,128,256]{3,2,1,0:T(8,128)(2,1)S(1)}, bf16[4,4,128,256]{3,2,1,0:T(8,128)(2,1)}, u32[]{:S(2)}) copy-start(bf16[4,4,128,256]{3,2,1,0:T(8,128)(2,1)} %copy.41) | copy-start | bytes 3145732
  193.7 15.8 %collective-permute-start.15 = (bf16[128,256]{1,0:T(8,128)(2,1)S(1)}, bf16[128,256]{1,0:T(8,128)(2,1)S(1)}, u32[]{:S(2)}, u32[]{:S(2)}) collective-permute-start(bf16[128,256]{1,0:T(8,128)(2,1)S(1)} %get-tuple-element.37), channel_id=1, source_target_pairs={{0,3},{1,0},{2,1},{3,2},{4,7},{5,4},{6,5},{7,6},{8,11},{9,8},{10,9... | collective-permute-start | bytes 196616 | tf_op jit(solution)/shard_map/ppermute | solution.py:43
  198.6 15.7 %collective-permute-start.16 = (bf16[128,256]{1,0:T(8,128)(2,1)S(1)}, bf16[128,256]{1,0:T(8,128)(2,1)S(1)}, u32[]{:S(2)}, u32[]{:S(2)}) collective-permute-start(bf16[128,256]{1,0:T(8,128)(2,1)S(1)} %get-tuple-element.39), channel_id=1, source_target_pairs={{0,2},{1,3},{2,0},{3,1},{4,6},{5,7},{6,4},{7,5},{8,10},{9,11},{10,... | collective-permute-start | bytes 196616 | tf_op jit(solution)/shard_map/ppermute | solution.py:43
  202.1 12.1 %collective-permute-start.17 = (bf16[128,256]{1,0:T(8,128)(2,1)S(1)}, bf16[128,256]{1,0:T(8,128)(2,1)S(1)}, u32[]{:S(2)}, u32[]{:S(2)}) collective-permute-start(bf16[128,256]{1,0:T(8,128)(2,1)S(1)} %get-tuple-element.38), channel_id=1, source_target_pairs={{0,1},{1,2},{2,3},{3,0},{4,5},{5,6},{6,7},{7,4},{8,9},{9,10},{10,1... | collective-permute-start | bytes 196616 | tf_op jit(solution)/shard_map/ppermute | solution.py:43
  215.3 56.8 %collective-permute-start.18 = (bf16[5,128,256]{2,1,0:T(8,128)(2,1)}, bf16[5,128,256]{2,1,0:T(8,128)(2,1)S(1)}, u32[]{:S(2)}, u32[]{:S(2)}) collective-permute-start(bf16[5,128,256]{2,1,0:T(8,128)(2,1)} %get-tuple-element.45), channel_id=1, source_target_pairs={{0,1},{1,2},{2,3},{3,0},{4,5},{5,6},{6,7},{7,4},{8,9},{9,10},{10,1... | collective-permute-start | bytes 983048 | tf_op jit(solution)/shard_map/ppermute | solution.py:89
  228.8 24.3 %collective-permute-start.6 = (bf16[128,512]{1,0:T(8,128)(2,1)S(1)}, bf16[128,512]{1,0:T(8,128)(2,1)S(1)}, u32[]{:S(2)}, u32[]{:S(2)}) collective-permute-start(bf16[128,512]{1,0:T(8,128)(2,1)S(1)} %copy.48), channel_id=1, source_target_pairs={{0,1},{1,2},{2,3},{3,0},{4,5},{5,6},{6,7},{7,4},{8,9},{9,10},{10,1... | collective-permute-start | bytes 393224 | tf_op jit(solution)/shard_map/ppermute | solution.py:32
  234.8 23.0 %collective-permute-start.7 = (bf16[128,512]{1,0:T(8,128)(2,1)S(1)}, bf16[128,512]{1,0:T(8,128)(2,1)S(1)}, u32[]{:S(2)}, u32[]{:S(2)}) collective-permute-start(bf16[128,512]{1,0:T(8,128)(2,1)S(1)} %copy.48), channel_id=1, source_target_pairs={{0,2},{1,3},{2,0},{3,1},{4,6},{5,7},{6,4},{7,5},{8,10},{9,11},{10,... | collective-permute-start | bytes 393224 | tf_op jit(solution)/shard_map/ppermute | solution.py:32
  239.8 18.0 %collective-permute-start.8 = (bf16[128,512]{1,0:T(8,128)(2,1)S(1)}, bf16[128,512]{1,0:T(8,128)(2,1)S(1)}, u32[]{:S(2)}, u32[]{:S(2)}) collective-permute-start(bf16[128,512]{1,0:T(8,128)(2,1)S(1)} %copy.48), channel_id=1, source_target_pairs={{0,3},{1,0},{2,1},{3,2},{4,7},{5,4},{6,5},{7,6},{8,11},{9,8},{10,9... | collective-permute-start | bytes 393224 | tf_op jit(solution)/shard_map/ppermute | solution.py:32
  246.6 36.0 %collective-permute-start.19 = (bf16[5,128,256]{2,1,0:T(8,128)(2,1)}, bf16[5,128,256]{2,1,0:T(8,128)(2,1)S(1)}, u32[]{:S(2)}, u32[]{:S(2)}) collective-permute-start(bf16[5,128,256]{2,1,0:T(8,128)(2,1)} %get-tuple-element.46), channel_id=1, source_target_pairs={{0,2},{1,3},{2,0},{3,1},{4,6},{5,7},{6,4},{7,5},{8,10},{9,11},{10,... | collective-permute-start | bytes 983048 | tf_op jit(solution)/shard_map/ppermute | solution.py:89
  253.2 60.5 %collective-permute-start.20 = (bf16[5,128,256]{2,1,0:T(8,128)(2,1)}, bf16[5,128,256]{2,1,0:T(8,128)(2,1)S(1)}, u32[]{:S(2)}, u32[]{:S(2)}) collective-permute-start(bf16[5,128,256]{2,1,0:T(8,128)(2,1)} %get-tuple-element.47), channel_id=1, source_target_pairs={{0,3},{1,0},{2,1},{3,2},{4,7},{5,4},{6,5},{7,6},{8,11},{9,8},{10,9... | collective-permute-start | bytes 983048 | tf_op jit(solution)/shard_map/ppermute | solution.py:89
  257.8 0.6 copy-start.11
  260.3 53.8 %copy-start.4 = (bf16[1,4,128,512]{3,2,1,0:T(8,128)(2,1)}, bf16[1,4,128,512]{3,2,1,0:T(8,128)(2,1)S(1)}, u32[]{:S(2)}) copy-start(bf16[1,4,128,512]{3,2,1,0:T(8,128)(2,1)S(1)} %get-tuple-element.32) | copy-start | bytes 1572868
  260.3 53.8 %collective-permute-start.9 = (bf16[4,128,512]{2,1,0:T(8,128)(2,1)}, bf16[4,128,512]{2,1,0:T(8,128)(2,1)}, u32[]{:S(2)}, u32[]{:S(2)}) collective-permute-start(bf16[4,128,512]{2,1,0:T(8,128)(2,1)} %get-tuple-element.33), channel_id=1, source_target_pairs={{0,4},{1,5},{2,6},{3,7},{4,8},{5,9},{6,10},{7,11},{8,12},{9,13},{1... | collective-permute-start | bytes 1572872 | tf_op jit(solution)/shard_map/ppermute | solution.py:33
  270.1 43.9 %collective-permute-start.10 = (bf16[4,128,512]{2,1,0:T(8,128)(2,1)}, bf16[4,128,512]{2,1,0:T(8,128)(2,1)}, u32[]{:S(2)}, u32[]{:S(2)}) collective-permute-start(bf16[4,128,512]{2,1,0:T(8,128)(2,1)} %get-tuple-element.33), channel_id=1, source_target_pairs={{0,8},{1,9},{2,10},{3,11},{4,12},{5,13},{6,14},{7,15},{8,0},{9,1},... | collective-permute-start | bytes 1572872 | tf_op jit(solution)/shard_map/ppermute | solution.py:33
  272.1 42.0 %collective-permute-start.11 = (bf16[4,128,512]{2,1,0:T(8,128)(2,1)}, bf16[4,128,512]{2,1,0:T(8,128)(2,1)}, u32[]{:S(2)}, u32[]{:S(2)}) collective-permute-start(bf16[4,128,512]{2,1,0:T(8,128)(2,1)} %get-tuple-element.33), channel_id=1, source_target_pairs={{0,12},{1,13},{2,14},{3,15},{4,0},{5,1},{6,2},{7,3},{8,4},{9,5},{1... | collective-permute-start | bytes 1572872 | tf_op jit(solution)/shard_map/ppermute | solution.py:33
  313.9 1.8 copy-start.14
  316.7 45.5 %collective-permute-start.23 = (bf16[12,128,256]{2,1,0:T(8,128)(2,1)S(1)}, bf16[12,128,256]{2,1,0:T(8,128)(2,1)S(1)}, u32[]{:S(2)}, u32[]{:S(2)}) collective-permute-start(bf16[12,128,256]{2,1,0:T(8,128)(2,1)S(1)} %get-tuple-element.36), channel_id=1, source_target_pairs={{0,4},{1,5},{2,6},{3,7},{4,8},{5,9},{6,10},{7,11},{8,12},{9,13},{1... | collective-permute-start | bytes 2359304 | tf_op jit(solution)/shard_map/ppermute | solution.py:97
  326.3 36.7 %collective-permute-start.22 = (bf16[12,128,256]{2,1,0:T(8,128)(2,1)S(1)}, bf16[12,128,256]{2,1,0:T(8,128)(2,1)S(1)}, u32[]{:S(2)}, u32[]{:S(2)}) collective-permute-start(bf16[12,128,256]{2,1,0:T(8,128)(2,1)S(1)} %get-tuple-element.35), channel_id=1, source_target_pairs={{0,8},{1,9},{2,10},{3,11},{4,12},{5,13},{6,14},{7,15},{8,0},{9,1},... | collective-permute-start | bytes 2359304 | tf_op jit(solution)/shard_map/ppermute | solution.py:97
  328.2 39.6 %collective-permute-start.21 = (bf16[12,128,256]{2,1,0:T(8,128)(2,1)S(1)}, bf16[12,128,256]{2,1,0:T(8,128)(2,1)S(1)}, u32[]{:S(2)}, u32[]{:S(2)}) collective-permute-start(bf16[12,128,256]{2,1,0:T(8,128)(2,1)S(1)} %get-tuple-element.34), channel_id=1, source_target_pairs={{0,12},{1,13},{2,14},{3,15},{4,0},{5,1},{6,2},{7,3},{8,4},{9,5},{1... | collective-permute-start | bytes 2359304 | tf_op jit(solution)/shard_map/ppermute | solution.py:97
  369.6 17.5 %collective-permute-start.24 = (bf16[4,128,256]{2,1,0:T(8,128)(2,1)}, bf16[4,128,256]{2,1,0:T(8,128)(2,1)S(1)}, u32[]{:S(2)}, u32[]{:S(2)}) collective-permute-start(bf16[4,128,256]{2,1,0:T(8,128)(2,1)} %get-tuple-element.9), channel_id=1, source_target_pairs={{0,3},{1,0},{2,1},{3,2},{4,7},{5,4},{6,5},{7,6},{8,11},{9,8},{10,9... | collective-permute-start | bytes 786440 | tf_op jit(solution)/shard_map/ppermute | solution.py:105
  373.6 24.4 %collective-permute-start.25 = (bf16[4,128,256]{2,1,0:T(8,128)(2,1)}, bf16[4,128,256]{2,1,0:T(8,128)(2,1)S(1)}, u32[]{:S(2)}, u32[]{:S(2)}) collective-permute-start(bf16[4,128,256]{2,1,0:T(8,128)(2,1)} %get-tuple-element.11), channel_id=1, source_target_pairs={{0,2},{1,3},{2,0},{3,1},{4,6},{5,7},{6,4},{7,5},{8,10},{9,11},{10,... | collective-permute-start | bytes 786440 | tf_op jit(solution)/shard_map/ppermute | solution.py:105
  380.4 26.1 %collective-permute-start.26 = (bf16[4,128,256]{2,1,0:T(8,128)(2,1)}, bf16[4,128,256]{2,1,0:T(8,128)(2,1)}, u32[]{:S(2)}, u32[]{:S(2)}) collective-permute-start(bf16[4,128,256]{2,1,0:T(8,128)(2,1)} %get-tuple-element.8), channel_id=1, source_target_pairs={{0,1},{1,2},{2,3},{3,0},{4,5},{5,6},{6,7},{7,4},{8,9},{9,10},{10,1... | collective-permute-start | bytes 786440 | tf_op jit(solution)/shard_map/ppermute | solution.py:105
  410.2 54.0 %copy-start.16 = (f32[128]{0:T(128)S(1)}, f32[128]{0:T(128)}, u32[]{:S(2)}) copy-start(f32[128]{0:T(128)} %add_rsqrt_fusion) | copy-start | bytes 1540
  464.2 3.3 copy-start.2
  467.4 2.7 copy-start.5
  467.4 2.7 copy-start.6
  467.4 2.7 copy-start.8
  467.4 2.7 copy-start.9
  467.4 2.7 copy-start.10
  468.2 35.9 %collective-permute-start.27 = (bf16[128,4096]{1,0:T(8,128)(2,1)S(1)}, bf16[128,4096]{1,0:T(8,128)(2,1)S(1)}, u32[]{:S(2)}, u32[]{:S(2)}) collective-permute-start(bf16[128,4096]{1,0:T(8,128)(2,1)S(1)} %add_convert_fusion), channel_id=1, source_target_pairs={{0,16},{16,32},{32,48},{48,64},{64,80},{80,96},{96,112},{112,128},... | collective-permute-start | bytes 3145736 | tf_op jit(solution)/shard_map/ppermute | solution.py:14
  470.1 33.1 %copy-start.7 = (bf16[1,256,768]{2,1,0:T(8,128)(2,1)S(1)}, bf16[1,256,768]{2,1,0:T(8,128)(2,1)}, u32[]{:S(2)}) copy-start(bf16[1,256,768]{2,1,0:T(8,128)(2,1)} %param.14) | copy-start | bytes 1179652
  472.6 30.7 %collective-permute-start.28 = (bf16[256,768]{1,0:T(8,128)(2,1)S(1)}, bf16[256,768]{1,0:T(8,128)(2,1)S(1)}, u32[]{:S(2)}, u32[]{:S(2)}) collective-permute-start(bf16[256,768]{1,0:T(8,128)(2,1)S(1)} %fusion.35), channel_id=1, source_target_pairs={{0,496},{16,480},{32,464},{48,448},{64,432},{80,416},{96,400},{112... | collective-permute-start | bytes 1179656 | tf_op jit(solution)/shard_map/ppermute | solution.py:19
Sparse Core Ops, SparseCore 0:
  11.0 137.6 all-gather.5
  276.5 187.5 all-gather.3

commit v12 on v9

--- a/solution.py
+++ b/solution.py
@@ -131,7 +131,6 @@
     ).reshape(size)
     key_positions = (sources[:, None] * count + jnp.arange(count, dtype=jnp.int32)[None, :]).reshape(-1)
     query = saved[:, :width].reshape(count, GROUP, HEAD)
-    attn_grad = contract_last(cotangent, output_weight).astype(jnp.bfloat16)
     positions = first + jnp.arange(count, dtype=jnp.int32)
     starts = doc_starts[0]
     visible = (key_positions[None, :] <= positions[:, None]) & (
@@ -143,6 +142,8 @@
     exps = jnp.where(visible[:, None, :], jnp.exp(scores - top), 0.0)
     probs = exps / jnp.sum(exps, axis=-1, keepdims=True)
     weights = probs.astype(jnp.bfloat16)
+    probs, weights, output_weight = lax.optimization_barrier((probs, weights, output_weight))
+    attn_grad = contract_last(cotangent, output_weight).astype(jnp.bfloat16)
     grad_heads = attn_grad.reshape(count, GROUP, HEAD)
     prob_grad = jnp.einsum("tgh,jh->tgj", grad_heads, values, preferred_element_type=jnp.float32)
     inner = jnp.sum(probs * prob_grad, axis=-1, keepdims=True)

time: 439 us -> 447 us (1.018)
  the two profiles are of different devices: /device:TPU:25 before, /device:TPU:89 now
where the time goes in v12:
time: 447 us; the launch traced here: 446 us
  starting transfers between devices  221 us (49%)
  waiting for transfers between devices  130 us (29%)
  matrix products  34.1 us (8%)
  local copies, waits for them, and re-layouts  26.9 us (6%)
  other arithmetic  18.6 us (4%)
  between operations  14.9 us (3%)
    all_gather x1, waiting for transfers between devices, per_device(): lax.all_gather(up_output_weight[0], 'seq', axis=1, tiled=True)  86.3 us
    ppermute x3, starting transfers between devices, gather_and_scatter(): second.append(lax.ppermute(payload, 'seq', seq_pairs(k, 1)))  39.7 us
    ppermute x1, starting transfers between devices, shifted(): lax.ppermute(value, axis, [(source, source + steps) for source in range(i...  38.7 us
    ppermute x6, starting transfers between devices, gather_blocks(): lax.ppermute(x, 'seq', seq_pairs(k, 0))  37.5 us
    ppermute x3, starting transfers between devices, reduce_blocks(): lax.ppermute(acc[k].astype(wire), 'seq', seq_pairs(INNER - k, 0))  22.3 us
    ppermute x6, starting transfers between devices, gather_blocks(): lax.ppermute(first, 'seq', seq_pairs(k, 1))  20 us
    ppermute x3, starting transfers between devices, gather_and_scatter(): lax.ppermute(jnp.concatenate([x, piece]), 'seq', seq_pairs(k, 0))  19.9 us
    ppermute x3, starting transfers between devices, gather_columns(): second.append(lax.ppermute(first[k], 'seq', seq_pairs(INNER - k, 0)))  18.4 us
  transfers between devices with their start and end apart: 34, of which 8 were waited for; matrix products, arithmetic and copies ran while one was open for 18% of the time, Pallas kernels for 0%

profile of v12, /device:TPU:89, one launch (start us, length us, event | category | flops | bytes accessed | tf_op | source)
XLA Modules:
  0.0 445.7 jit_solution(15292895751651644735)
XLA Ops:
  9.1 8.8 %collective-permute-start = (bf16[128,256]{0,1:T(8,128)(2,1)S(1)}, bf16[128,256]{0,1:T(8,128)(2,1)S(1)}, u32[]{:S(2)}, u32[]{:S(2)}) collective-permute-start(bf16[128,256]{0,1:T(8,128)(2,1)S(1)} %get-tuple-element.46), channel_id=1, source_target_pairs={{0,1},{1,2},{2,3},{3,0},{4,5},{5,6},{6,7},{7,4},{8,9},{9,10},{10,1... | collective-permute-start | bytes 196616 | tf_op jit(solution)/shard_map/ppermute | solution.py:32
  17.9 8.8 %collective-permute-start.1 = (bf16[128,256]{0,1:T(8,128)(2,1)S(1)}, bf16[128,256]{0,1:T(8,128)(2,1)S(1)}, u32[]{:S(2)}, u32[]{:S(2)}) collective-permute-start(bf16[128,256]{0,1:T(8,128)(2,1)S(1)} %get-tuple-element.46), channel_id=1, source_target_pairs={{0,2},{1,3},{2,0},{3,1},{4,6},{5,7},{6,4},{7,5},{8,10},{9,11},{10,... | collective-permute-start | bytes 196616 | tf_op jit(solution)/shard_map/ppermute | solution.py:32
  26.7 5.2 %collective-permute-start.2 = (bf16[128,256]{0,1:T(8,128)(2,1)S(1)}, bf16[128,256]{0,1:T(8,128)(2,1)S(1)}, u32[]{:S(2)}, u32[]{:S(2)}) collective-permute-start(bf16[128,256]{0,1:T(8,128)(2,1)S(1)} %get-tuple-element.46), channel_id=1, source_target_pairs={{0,3},{1,0},{2,1},{3,2},{4,7},{5,4},{6,5},{7,6},{8,11},{9,8},{10,9... | collective-permute-start | bytes 196616 | tf_op jit(solution)/shard_map/ppermute | solution.py:32
  31.9 1.6 slice.156
  33.8 5.7 %collective-permute-done.2 = bf16[128,256]{0,1:T(8,128)(2,1)S(1)} collective-permute-done((bf16[128,256]{0,1:T(8,128)(2,1)S(1)}, bf16[128,256]{0,1:T(8,128)(2,1)S(1)}, u32[]{:S(2)}, u32[]{:S(2)}) %collective-permute-start.2) | collective-permute-done | bytes 65568 | tf_op jit(solution)/shard_map/ppermute | solution.py:32
  39.6 3.1 collective-permute-start.3
  42.7 4.4 collective-permute-start.4
  47.1 3.1 collective-permute-start.5
  51.3 3.1 collective-permute-done.4
  54.5 1.9 collective-permute-done.5
  57.1 5.0 %fusion.84 = (bf16[128,4,2048]{0,2,1:T(8,128)(2,1)}, f32[128,4,2048]{0,2,1:T(8,128)}) fusion(pred[128,2048]{0,1:T(8,128)(4,1)S(1)} %compare_and_fusion, bf16[128,4,128]{0,2,1:T(8,128)(2,1)S(1)} %bitcast.231, bf16[2048,256]{1,0:T(8,128)(2,1)S(1)} %bitcast.194), kind=kOutput, calls=%fused_computation.153 | convolution fusion | flops 274732032 | bytes 7471104 | tf_op jit(solution)/shard_map/div | solution.py:143
  62.1 86.3 %all-gather.6.cloned.1.call-done = bf16[1,512,4096]{2,1,0:T(8,128)(2,1)} async-done(((bf16[1,512,256]{2,1,0:T(8,128)(2,1)}), bf16[1,512,4096]{2,1,0:T(8,128)(2,1)}) %all-gather.6.cloned.1.call-update) | async-done | bytes 4194320 | tf_op jit(solution)/shard_map/all_gather | solution.py:123
  148.4 3.4 convolution_convert_fusion.1
  151.8 2.6 fusion.60
  154.5 7.2 %convolution_bitcast_fusion.1 = f32[2048,128]{0,1:T(8,128)S(1)} fusion(bf16[128,4,128]{0,2,1:T(8,128)(2,1)S(1)} %bitcast.232, f32[128,4,2048]{0,2,1:T(8,128)} %get-tuple-element.5, f32[128,4,2048]{0,2,1:T(8,128)} %fusion.60), kind=kOutput, calls=%fused_computation.27 | convolution fusion | flops 273680896 | bytes 9568256 | tf_op jit(solution)/shard_map/tgj,tgh->jh/dot_general | solution.py:156
  161.7 7.0 %fusion.37 = bf16[128,4,128]{0,2,1:T(8,128)(2,1)S(1)} fusion(f32[128,4,2048]{0,2,1:T(8,128)} %get-tuple-element.5, f32[128,4,2048]{0,2,1:T(8,128)} %fusion.60, bf16[2048,256]{1,0:T(8,128)(2,1)S(1)} %bitcast.196), kind=kOutput, calls=%fused_computation.57 | convolution fusion | flops 273746432 | bytes 17432576 | tf_op jit(solution)/shard_map/tgj,jh->tgh/dot_general | solution.py:152
  169.5 1.9 collective-permute-start.6
  171.4 9.5 %collective-permute-start.7 = (bf16[128,512]{1,0:T(8,128)(2,1)}, bf16[128,512]{1,0:T(8,128)(2,1)}, u32[]{:S(2)}, u32[]{:S(2)}) collective-permute-start(bf16[128,512]{1,0:T(8,128)(2,1)} %copy.47), channel_id=1, source_target_pairs={{0,2},{1,3},{2,0},{3,1},{4,6},{5,7},{6,4},{7,5},{8,10},{9,11},{10,... | collective-permute-start | bytes 393224 | tf_op jit(solution)/shard_map/ppermute | solution.py:32
  180.9 3.2 collective-permute-start.8
  184.2 2.4 convolution_bitcast_fusion
  187.6 1.8 copy.81
  189.4 4.1 collective-permute-start.18
  193.5 1.8 copy.82
  195.2 2.7 collective-permute-start.19
  198.8 2.4 collective-permute-start.20
  202.3 2.7 reshape.212
  205.6 1.3 reduce.3
  206.8 1.3 mul.112
  208.2 1.3 copy.62
  210.3 1.2 copy.80
  211.7 2.1 fusion.80
  213.8 3.2 collective-permute-start.9
  217.0 3.9 collective-permute-start.10
  221.0 2.3 collective-permute-start.11
  223.3 1.9 fusion.81
  225.9 4.0 collective-permute-start.21
  230.0 1.3 fusion.22
  231.4 9.4 %collective-permute-start.22 = (bf16[128,256]{1,0:T(8,128)(2,1)}, bf16[128,256]{1,0:T(8,128)(2,1)S(1)}, u32[]{:S(2)}, u32[]{:S(2)}) collective-permute-start(bf16[128,256]{1,0:T(8,128)(2,1)} %get-tuple-element.42), channel_id=1, source_target_pairs={{0,2},{1,3},{2,0},{3,1},{4,6},{5,7},{6,4},{7,5},{8,10},{9,11},{10,... | collective-permute-start | bytes 196616 | tf_op jit(solution)/shard_map/ppermute | solution.py:43
  240.8 8.9 %collective-permute-start.23 = (bf16[128,256]{1,0:T(8,128)(2,1)}, bf16[128,256]{1,0:T(8,128)(2,1)}, u32[]{:S(2)}, u32[]{:S(2)}) collective-permute-start(bf16[128,256]{1,0:T(8,128)(2,1)} %get-tuple-element.41), channel_id=1, source_target_pairs={{0,1},{1,2},{2,3},{3,0},{4,5},{5,6},{6,7},{7,4},{8,9},{9,10},{10,1... | collective-permute-start | bytes 196616 | tf_op jit(solution)/shard_map/ppermute | solution.py:43
  250.5 4.1 collective-permute-done.23
  256.6 8.3 %collective-permute-start.25 = (bf16[5,128,256]{2,1,0:T(8,128)(2,1)S(1)}, bf16[5,128,256]{2,1,0:T(8,128)(2,1)S(1)}, u32[]{:S(2)}, u32[]{:S(2)}) collective-permute-start(bf16[5,128,256]{2,1,0:T(8,128)(2,1)S(1)} %get-tuple-element.48), channel_id=1, source_target_pairs={{0,1},{1,2},{2,3},{3,0},{4,5},{5,6},{6,7},{7,4},{8,9},{9,10},{10,1... | collective-permute-start | bytes 983048 | tf_op jit(solution)/shard_map/ppermute | solution.py:54
  264.9 4.3 collective-permute-start.26
  269.3 7.3 %collective-permute-start.27 = (bf16[5,128,256]{2,1,0:T(8,128)(2,1)S(1)}, bf16[5,128,256]{2,1,0:T(8,128)(2,1)S(1)}, u32[]{:S(2)}, u32[]{:S(2)}) collective-permute-start(bf16[5,128,256]{2,1,0:T(8,128)(2,1)S(1)} %get-tuple-element.50), channel_id=1, source_target_pairs={{0,3},{1,0},{2,1},{3,2},{4,7},{5,4},{6,5},{7,6},{8,11},{9,8},{10,9... | collective-permute-start | bytes 983048 | tf_op jit(solution)/shard_map/ppermute | solution.py:54
  276.6 1.7 pad_maximum_fusion.1
  279.1 3.4 collective-permute-start.12
  282.5 4.1 collective-permute-start.13
  286.6 2.2 collective-permute-done.25
  288.8 5.6 %collective-permute-start.14 = (bf16[4,128,256]{2,1,0:T(8,128)(2,1)S(1)}, bf16[4,128,256]{2,1,0:T(8,128)(2,1)S(1)}, u32[]{:S(2)}, u32[]{:S(2)}) collective-permute-start(bf16[4,128,256]{2,1,0:T(8,128)(2,1)S(1)} %bitcast.222), channel_id=1, source_target_pairs={{0,4},{1,5},{2,6},{3,7},{4,8},{5,9},{6,10},{7,11},{8,12},{9,13},{1... | collective-permute-start | bytes 786440 | tf_op jit(solution)/shard_map/ppermute | solution.py:72
  294.4 8.6 %collective-permute-done.26 = bf16[5,128,256]{2,1,0:T(8,128)(2,1)S(1)} collective-permute-done((bf16[5,128,256]{2,1,0:T(8,128)(2,1)S(1)}, bf16[5,128,256]{2,1,0:T(8,128)(2,1)S(1)}, u32[]{:S(2)}, u32[]{:S(2)}) %collective-permute-start.26) | collective-permute-done | bytes 327712 | tf_op jit(solution)/shard_map/ppermute | solution.py:54
  303.6 5.9 %collective-permute-start.15 = (bf16[4,128,256]{2,1,0:T(8,128)(2,1)S(1)}, bf16[4,128,256]{2,1,0:T(8,128)(2,1)S(1)}, u32[]{:S(2)}, u32[]{:S(2)}) collective-permute-start(bf16[4,128,256]{2,1,0:T(8,128)(2,1)S(1)} %get-tuple-element.22), channel_id=1, source_target_pairs={{0,3},{1,0},{2,1},{3,2},{4,7},{5,4},{6,5},{7,6},{8,11},{9,8},{10,9... | collective-permute-start | bytes 786440 | tf_op jit(solution)/shard_map/ppermute | solution.py:76
  309.5 10.6 %collective-permute-start.16 = (bf16[4,128,256]{2,1,0:T(8,128)(2,1)S(1)}, bf16[4,128,256]{2,1,0:T(8,128)(2,1)S(1)}, u32[]{:S(2)}, u32[]{:S(2)}) collective-permute-start(bf16[4,128,256]{2,1,0:T(8,128)(2,1)S(1)} %get-tuple-element.24), channel_id=1, source_target_pairs={{0,2},{1,3},{2,0},{3,1},{4,6},{5,7},{6,4},{7,5},{8,10},{9,11},{10,... | collective-permute-start | bytes 786440 | tf_op jit(solution)/shard_map/ppermute | solution.py:76
  320.1 1.9 collective-permute-start.17
  322.8 1.2 pad_maximum_fusion.7
  324.0 7.0 %collective-permute-start.28 = (bf16[8,128,256]{2,1,0:T(8,128)(2,1)}, bf16[8,128,256]{2,1,0:T(8,128)(2,1)}, u32[]{:S(2)}, u32[]{:S(2)}) collective-permute-start(bf16[8,128,256]{2,1,0:T(8,128)(2,1)} %get-tuple-element.37), channel_id=1, source_target_pairs={{0,4},{1,5},{2,6},{3,7},{4,8},{5,9},{6,10},{7,11},{8,12},{9,13},{1... | collective-permute-start | bytes 1572872 | tf_op jit(solution)/shard_map/ppermute | solution.py:61
  331.0 29.4 %collective-permute-start.29 = (bf16[8,128,256]{2,1,0:T(8,128)(2,1)}, bf16[8,128,256]{2,1,0:T(8,128)(2,1)}, u32[]{:S(2)}, u32[]{:S(2)}) collective-permute-start(bf16[8,128,256]{2,1,0:T(8,128)(2,1)} %get-tuple-element.38), channel_id=1, source_target_pairs={{0,8},{1,9},{2,10},{3,11},{4,12},{5,13},{6,14},{7,15},{8,0},{9,1},... | collective-permute-start | bytes 1572872 | tf_op jit(solution)/shard_map/ppermute | solution.py:61
  360.4 3.3 collective-permute-start.30
  365.3 1.4 copy.54
  366.7 2.1 reshape.210
  368.8 3.2 multiply_reduce_fusion.1
  372.7 38.7 %collective-permute-start.24 = (bf16[128,4096]{1,0:T(8,128)(2,1)S(1)}, bf16[128,4096]{1,0:T(8,128)(2,1)S(1)}, u32[]{:S(2)}, u32[]{:S(2)}) collective-permute-start(bf16[128,4096]{1,0:T(8,128)(2,1)S(1)} %add_convert_fusion), channel_id=1, source_target_pairs={{0,16},{16,32},{32,48},{48,64},{64,80},{80,96},{96,112},{112,128},... | collective-permute-start | bytes 3145736 | tf_op jit(solution)/shard_map/ppermute | solution.py:14
  412.6 1.1 slice_bitcast_fusion.13
  415.0 2.4 fusion.34
  417.4 1.9 collective-permute-start.31
  419.4 17.7 %collective-permute-done.31 = bf16[256,768]{1,0:T(8,128)(2,1)S(1)} collective-permute-done((bf16[256,768]{1,0:T(8,128)(2,1)S(1)}, bf16[256,768]{1,0:T(8,128)(2,1)S(1)}, u32[]{:S(2)}, u32[]{:S(2)}) %collective-permute-start.31) | collective-permute-done | bytes 393248 | tf_op jit(solution)/shard_map/ppermute | solution.py:19
  (102 shorter events, 21.2 us)
Async XLA Ops:
  7.2 43.0 %copy-start.14 = (s32[1,128]{1,0:T(1,128)S(1)}, s32[1,128]{1,0:T(1,128)}, u32[]{:S(2)}) copy-start(s32[1,128]{1,0:T(1,128)} %param.15) | copy-start | bytes 1540
  7.2 43.4 %copy-start = (bf16[1,128,4096]{2,1,0:T(8,128)(2,1)S(1)}, bf16[1,128,4096]{2,1,0:T(8,128)(2,1)}, u32[]{:S(2)}) copy-start(bf16[1,128,4096]{2,1,0:T(8,128)(2,1)} %param.8) | copy-start | bytes 3145732
  7.2 141.2 %all-gather.6.cloned.1.call-start = ((), (), s32[]{:S(2)}) async-start(), calls=%async_computation.1 | async-start | bytes 4456448 | tf_op jit(solution)/shard_map/all_gather | solution.py:123
  7.9 360.9 %all-gather.4.cloned.1.call-start = ((), (), s32[]{:S(2)}) async-start(), calls=%async_computation | async-start | bytes 2228224 | tf_op jit(solution)/shard_map/all_gather | solution.py:125
  9.1 24.8 %collective-permute-start = (bf16[128,256]{0,1:T(8,128)(2,1)S(1)}, bf16[128,256]{0,1:T(8,128)(2,1)S(1)}, u32[]{:S(2)}, u32[]{:S(2)}) collective-permute-start(bf16[128,256]{0,1:T(8,128)(2,1)S(1)} %get-tuple-element.46), channel_id=1, source_target_pairs={{0,1},{1,2},{2,3},{3,0},{4,5},{5,6},{6,7},{7,4},{8,9},{9,10},{10,1... | collective-permute-start | bytes 196616 | tf_op jit(solution)/shard_map/ppermute | solution.py:32
  17.9 15.9 %collective-permute-start.1 = (bf16[128,256]{0,1:T(8,128)(2,1)S(1)}, bf16[128,256]{0,1:T(8,128)(2,1)S(1)}, u32[]{:S(2)}, u32[]{:S(2)}) collective-permute-start(bf16[128,256]{0,1:T(8,128)(2,1)S(1)} %get-tuple-element.46), channel_id=1, source_target_pairs={{0,2},{1,3},{2,0},{3,1},{4,6},{5,7},{6,4},{7,5},{8,10},{9,11},{10,... | collective-permute-start | bytes 196616 | tf_op jit(solution)/shard_map/ppermute | solution.py:32
  26.7 12.8 %collective-permute-start.2 = (bf16[128,256]{0,1:T(8,128)(2,1)S(1)}, bf16[128,256]{0,1:T(8,128)(2,1)S(1)}, u32[]{:S(2)}, u32[]{:S(2)}) collective-permute-start(bf16[128,256]{0,1:T(8,128)(2,1)S(1)} %get-tuple-element.46), channel_id=1, source_target_pairs={{0,3},{1,0},{2,1},{3,2},{4,7},{5,4},{6,5},{7,6},{8,11},{9,8},{10,9... | collective-permute-start | bytes 196616 | tf_op jit(solution)/shard_map/ppermute | solution.py:32
  39.6 11.7 %collective-permute-start.3 = (bf16[4,128,256]{1,2,0:T(8,128)(2,1)S(1)}, bf16[4,128,256]{1,2,0:T(8,128)(2,1)S(1)}, u32[]{:S(2)}, u32[]{:S(2)}) collective-permute-start(bf16[4,128,256]{1,2,0:T(8,128)(2,1)S(1)} %get-tuple-element.44), channel_id=1, source_target_pairs={{0,4},{1,5},{2,6},{3,7},{4,8},{5,9},{6,10},{7,11},{8,12},{9,13},{1... | collective-permute-start | bytes 786440 | tf_op jit(solution)/shard_map/ppermute | solution.py:33
  42.7 11.7 %collective-permute-start.4 = (bf16[4,128,256]{1,2,0:T(8,128)(2,1)S(1)}, bf16[4,128,256]{1,2,0:T(8,128)(2,1)S(1)}, u32[]{:S(2)}, u32[]{:S(2)}) collective-permute-start(bf16[4,128,256]{1,2,0:T(8,128)(2,1)S(1)} %get-tuple-element.44), channel_id=1, source_target_pairs={{0,8},{1,9},{2,10},{3,11},{4,12},{5,13},{6,14},{7,15},{8,0},{9,1},... | collective-permute-start | bytes 786440 | tf_op jit(solution)/shard_map/ppermute | solution.py:33
  47.1 9.3 %collective-permute-start.5 = (bf16[4,128,256]{1,2,0:T(8,128)(2,1)S(1)}, bf16[4,128,256]{1,2,0:T(8,128)(2,1)S(1)}, u32[]{:S(2)}, u32[]{:S(2)}) collective-permute-start(bf16[4,128,256]{1,2,0:T(8,128)(2,1)S(1)} %get-tuple-element.44), channel_id=1, source_target_pairs={{0,12},{1,13},{2,14},{3,15},{4,0},{5,1},{6,2},{7,3},{8,4},{9,5},{1... | collective-permute-start | bytes 786440 | tf_op jit(solution)/shard_map/ppermute | solution.py:33
  57.1 91.3 %copy-start.4 = (bf16[1,128,4096]{2,1,0:T(8,128)(2,1)S(1)}, bf16[1,128,4096]{2,1,0:T(8,128)(2,1)}, u32[]{:S(2)}) copy-start(bf16[1,128,4096]{2,1,0:T(8,128)(2,1)} %param.10) | copy-start | bytes 3145732
  169.5 29.4 %collective-permute-start.6 = (bf16[128,512]{1,0:T(8,128)(2,1)}, bf16[128,512]{1,0:T(8,128)(2,1)}, u32[]{:S(2)}, u32[]{:S(2)}) collective-permute-start(bf16[128,512]{1,0:T(8,128)(2,1)} %copy.47), channel_id=1, source_target_pairs={{0,1},{1,2},{2,3},{3,0},{4,5},{5,6},{6,7},{7,4},{8,9},{9,10},{10,1... | collective-permute-start | bytes 393224 | tf_op jit(solution)/shard_map/ppermute | solution.py:32
  171.4 40.3 %collective-permute-start.7 = (bf16[128,512]{1,0:T(8,128)(2,1)}, bf16[128,512]{1,0:T(8,128)(2,1)}, u32[]{:S(2)}, u32[]{:S(2)}) collective-permute-start(bf16[128,512]{1,0:T(8,128)(2,1)} %copy.47), channel_id=1, source_target_pairs={{0,2},{1,3},{2,0},{3,1},{4,6},{5,7},{6,4},{7,5},{8,10},{9,11},{10,... | collective-permute-start | bytes 393224 | tf_op jit(solution)/shard_map/ppermute | solution.py:32
  180.9 30.8 %collective-permute-start.8 = (bf16[128,512]{1,0:T(8,128)(2,1)}, bf16[128,512]{1,0:T(8,128)(2,1)}, u32[]{:S(2)}, u32[]{:S(2)}) collective-permute-start(bf16[128,512]{1,0:T(8,128)(2,1)} %copy.47), channel_id=1, source_target_pairs={{0,3},{1,0},{2,1},{3,2},{4,7},{5,4},{6,5},{7,6},{8,11},{9,8},{10,9... | collective-permute-start | bytes 393224 | tf_op jit(solution)/shard_map/ppermute | solution.py:32
  189.4 31.6 %collective-permute-start.18 = (bf16[4,128,256]{2,1,0:T(8,128)(2,1)}, bf16[4,128,256]{2,1,0:T(8,128)(2,1)}, u32[]{:S(2)}, u32[]{:S(2)}) collective-permute-start(bf16[4,128,256]{2,1,0:T(8,128)(2,1)} %bitcast.220), channel_id=1, source_target_pairs={{0,12},{1,13},{2,14},{3,15},{4,0},{5,1},{6,2},{7,3},{8,4},{9,5},{1... | collective-permute-start | bytes 786440 | tf_op jit(solution)/shard_map/ppermute | solution.py:40
  193.4 12.1 %copy-start.8 = (f32[1,4096]{1,0:T(1,128)S(1)}, f32[1,4096]{1,0:T(1,128)}, u32[]{:S(2)}) copy-start(f32[1,4096]{1,0:T(1,128)} %param.13) | copy-start | bytes 49156
  195.2 28.0 %collective-permute-start.19 = (bf16[4,128,256]{2,1,0:T(8,128)(2,1)}, bf16[4,128,256]{2,1,0:T(8,128)(2,1)}, u32[]{:S(2)}, u32[]{:S(2)}) collective-permute-start(bf16[4,128,256]{2,1,0:T(8,128)(2,1)} %bitcast.219), channel_id=1, source_target_pairs={{0,8},{1,9},{2,10},{3,11},{4,12},{5,13},{6,14},{7,15},{8,0},{9,1},... | collective-permute-start | bytes 786440 | tf_op jit(solution)/shard_map/ppermute | solution.py:40
  198.8 24.5 %collective-permute-start.20 = (bf16[4,128,256]{2,1,0:T(8,128)(2,1)}, bf16[4,128,256]{2,1,0:T(8,128)(2,1)S(1)}, u32[]{:S(2)}, u32[]{:S(2)}) collective-permute-start(bf16[4,128,256]{2,1,0:T(8,128)(2,1)} %bitcast.221), channel_id=1, source_target_pairs={{0,4},{1,5},{2,6},{3,7},{4,8},{5,9},{6,10},{7,11},{8,12},{9,13},{1... | collective-permute-start | bytes 786440 | tf_op jit(solution)/shard_map/ppermute | solution.py:40
  211.7 18.3 %copy-start.1 = (f32[128,4,4,256]{3,2,1,0:T(4,128)S(1)}, f32[128,4,4,256]{3,2,1,0:T(4,128)}, u32[]{:S(2)}) copy-start(f32[128,4,4,256]{3,2,1,0:T(4,128)} %reshape.212) | copy-start | bytes 6291460
  211.7 18.3 %copy-start.9 = (f32[4,4,256]{2,0,1:T(4,128)S(1)}, f32[4,4,256]{2,0,1:T(4,128)}, u32[]{:S(2)}) copy-start(f32[4,4,256]{2,0,1:T(4,128)} %copy.62) | copy-start | bytes 49156
  211.7 18.3 %copy-start.12 = (f32[128]{0:T(128)S(1)}, f32[128]{0:T(128)}, u32[]{:S(2)}) copy-start(f32[128]{0:T(128)} %add_rsqrt_fusion) | copy-start | bytes 1540
  213.8 62.8 %copy-start.2 = (bf16[1,4,128,512]{3,2,1,0:T(8,128)(2,1)}, bf16[1,4,128,512]{3,2,1,0:T(8,128)(2,1)S(1)}, u32[]{:S(2)}) copy-start(bf16[1,4,128,512]{3,2,1,0:T(8,128)(2,1)S(1)} %get-tuple-element.35) | copy-start | bytes 1572868
  213.8 55.5 %collective-permute-start.9 = (bf16[4,128,512]{2,1,0:T(8,128)(2,1)}, bf16[4,128,512]{2,1,0:T(8,128)(2,1)}, u32[]{:S(2)}, u32[]{:S(2)}) collective-permute-start(bf16[4,128,512]{2,1,0:T(8,128)(2,1)} %get-tuple-element.36), channel_id=1, source_target_pairs={{0,4},{1,5},{2,6},{3,7},{4,8},{5,9},{6,10},{7,11},{8,12},{9,13},{1... | collective-permute-start | bytes 1572872 | tf_op jit(solution)/shard_map/ppermute | solution.py:33
  217.0 59.5 %collective-permute-start.10 = (bf16[4,128,512]{2,1,0:T(8,128)(2,1)}, bf16[4,128,512]{2,1,0:T(8,128)(2,1)}, u32[]{:S(2)}, u32[]{:S(2)}) collective-permute-start(bf16[4,128,512]{2,1,0:T(8,128)(2,1)} %get-tuple-element.36), channel_id=1, source_target_pairs={{0,8},{1,9},{2,10},{3,11},{4,12},{5,13},{6,14},{7,15},{8,0},{9,1},... | collective-permute-start | bytes 1572872 | tf_op jit(solution)/shard_map/ppermute | solution.py:33
  221.0 55.6 %collective-permute-start.11 = (bf16[4,128,512]{2,1,0:T(8,128)(2,1)}, bf16[4,128,512]{2,1,0:T(8,128)(2,1)}, u32[]{:S(2)}, u32[]{:S(2)}) collective-permute-start(bf16[4,128,512]{2,1,0:T(8,128)(2,1)} %get-tuple-element.36), channel_id=1, source_target_pairs={{0,12},{1,13},{2,14},{3,15},{4,0},{5,1},{6,2},{7,3},{8,4},{9,5},{1... | collective-permute-start | bytes 1572872 | tf_op jit(solution)/shard_map/ppermute | solution.py:33
  225.9 14.8 %collective-permute-start.21 = (bf16[128,256]{1,0:T(8,128)(2,1)S(1)}, bf16[128,256]{1,0:T(8,128)(2,1)S(1)}, u32[]{:S(2)}, u32[]{:S(2)}) collective-permute-start(bf16[128,256]{1,0:T(8,128)(2,1)S(1)} %get-tuple-element.40), channel_id=1, source_target_pairs={{0,3},{1,0},{2,1},{3,2},{4,7},{5,4},{6,5},{7,6},{8,11},{9,8},{10,9... | collective-permute-start | bytes 196616 | tf_op jit(solution)/shard_map/ppermute | solution.py:43
  231.4 19.1 %collective-permute-start.22 = (bf16[128,256]{1,0:T(8,128)(2,1)}, bf16[128,256]{1,0:T(8,128)(2,1)S(1)}, u32[]{:S(2)}, u32[]{:S(2)}) collective-permute-start(bf16[128,256]{1,0:T(8,128)(2,1)} %get-tuple-element.42), channel_id=1, source_target_pairs={{0,2},{1,3},{2,0},{3,1},{4,6},{5,7},{6,4},{7,5},{8,10},{9,11},{10,... | collective-permute-start | bytes 196616 | tf_op jit(solution)/shard_map/ppermute | solution.py:43
  240.8 13.8 %collective-permute-start.23 = (bf16[128,256]{1,0:T(8,128)(2,1)}, bf16[128,256]{1,0:T(8,128)(2,1)}, u32[]{:S(2)}, u32[]{:S(2)}) collective-permute-start(bf16[128,256]{1,0:T(8,128)(2,1)} %get-tuple-element.41), channel_id=1, source_target_pairs={{0,1},{1,2},{2,3},{3,0},{4,5},{5,6},{6,7},{7,4},{8,9},{9,10},{10,1... | collective-permute-start | bytes 196616 | tf_op jit(solution)/shard_map/ppermute | solution.py:43
  250.5 4.1 copy-start.10
  256.6 32.1 %collective-permute-start.25 = (bf16[5,128,256]{2,1,0:T(8,128)(2,1)S(1)}, bf16[5,128,256]{2,1,0:T(8,128)(2,1)S(1)}, u32[]{:S(2)}, u32[]{:S(2)}) collective-permute-start(bf16[5,128,256]{2,1,0:T(8,128)(2,1)S(1)} %get-tuple-element.48), channel_id=1, source_target_pairs={{0,1},{1,2},{2,3},{3,0},{4,5},{5,6},{6,7},{7,4},{8,9},{9,10},{10,1... | collective-permute-start | bytes 983048 | tf_op jit(solution)/shard_map/ppermute | solution.py:54
  264.9 38.1 %collective-permute-start.26 = (bf16[5,128,256]{2,1,0:T(8,128)(2,1)S(1)}, bf16[5,128,256]{2,1,0:T(8,128)(2,1)S(1)}, u32[]{:S(2)}, u32[]{:S(2)}) collective-permute-start(bf16[5,128,256]{2,1,0:T(8,128)(2,1)S(1)} %get-tuple-element.49), channel_id=1, source_target_pairs={{0,2},{1,3},{2,0},{3,1},{4,6},{5,7},{6,4},{7,5},{8,10},{9,11},{10,... | collective-permute-start | bytes 983048 | tf_op jit(solution)/shard_map/ppermute | solution.py:54
  269.3 33.7 %collective-permute-start.27 = (bf16[5,128,256]{2,1,0:T(8,128)(2,1)S(1)}, bf16[5,128,256]{2,1,0:T(8,128)(2,1)S(1)}, u32[]{:S(2)}, u32[]{:S(2)}) collective-permute-start(bf16[5,128,256]{2,1,0:T(8,128)(2,1)S(1)} %get-tuple-element.50), channel_id=1, source_target_pairs={{0,3},{1,0},{2,1},{3,2},{4,7},{5,4},{6,5},{7,6},{8,11},{9,8},{10,9... | collective-permute-start | bytes 983048 | tf_op jit(solution)/shard_map/ppermute | solution.py:54
  276.6 1.7 copy-start.11
  279.1 24.2 %collective-permute-start.12 = (bf16[4,128,256]{2,1,0:T(8,128)(2,1)S(1)}, bf16[4,128,256]{2,1,0:T(8,128)(2,1)S(1)}, u32[]{:S(2)}, u32[]{:S(2)}) collective-permute-start(bf16[4,128,256]{2,1,0:T(8,128)(2,1)S(1)} %bitcast.226), channel_id=1, source_target_pairs={{0,12},{1,13},{2,14},{3,15},{4,0},{5,1},{6,2},{7,3},{8,4},{9,5},{1... | collective-permute-start | bytes 786440 | tf_op jit(solution)/shard_map/ppermute | solution.py:72
  282.5 20.9 %collective-permute-start.13 = (bf16[4,128,256]{2,1,0:T(8,128)(2,1)S(1)}, bf16[4,128,256]{2,1,0:T(8,128)(2,1)S(1)}, u32[]{:S(2)}, u32[]{:S(2)}) collective-permute-start(bf16[4,128,256]{2,1,0:T(8,128)(2,1)S(1)} %bitcast.224), channel_id=1, source_target_pairs={{0,8},{1,9},{2,10},{3,11},{4,12},{5,13},{6,14},{7,15},{8,0},{9,1},... | collective-permute-start | bytes 786440 | tf_op jit(solution)/shard_map/ppermute | solution.py:72
  288.8 14.5 %collective-permute-start.14 = (bf16[4,128,256]{2,1,0:T(8,128)(2,1)S(1)}, bf16[4,128,256]{2,1,0:T(8,128)(2,1)S(1)}, u32[]{:S(2)}, u32[]{:S(2)}) collective-permute-start(bf16[4,128,256]{2,1,0:T(8,128)(2,1)S(1)} %bitcast.222), channel_id=1, source_target_pairs={{0,4},{1,5},{2,6},{3,7},{4,8},{5,9},{6,10},{7,11},{8,12},{9,13},{1... | collective-permute-start | bytes 786440 | tf_op jit(solution)/shard_map/ppermute | solution.py:72
  303.6 56.8 %collective-permute-start.15 = (bf16[4,128,256]{2,1,0:T(8,128)(2,1)S(1)}, bf16[4,128,256]{2,1,0:T(8,128)(2,1)S(1)}, u32[]{:S(2)}, u32[]{:S(2)}) collective-permute-start(bf16[4,128,256]{2,1,0:T(8,128)(2,1)S(1)} %get-tuple-element.22), channel_id=1, source_target_pairs={{0,3},{1,0},{2,1},{3,2},{4,7},{5,4},{6,5},{7,6},{8,11},{9,8},{10,9... | collective-permute-start | bytes 786440 | tf_op jit(solution)/shard_map/ppermute | solution.py:76
  309.5 54.3 %collective-permute-start.16 = (bf16[4,128,256]{2,1,0:T(8,128)(2,1)S(1)}, bf16[4,128,256]{2,1,0:T(8,128)(2,1)S(1)}, u32[]{:S(2)}, u32[]{:S(2)}) collective-permute-start(bf16[4,128,256]{2,1,0:T(8,128)(2,1)S(1)} %get-tuple-element.24), channel_id=1, source_target_pairs={{0,2},{1,3},{2,0},{3,1},{4,6},{5,7},{6,4},{7,5},{8,10},{9,11},{10,... | collective-permute-start | bytes 786440 | tf_op jit(solution)/shard_map/ppermute | solution.py:76
  320.1 43.7 %collective-permute-start.17 = (bf16[4,128,256]{2,1,0:T(8,128)(2,1)S(1)}, bf16[4,128,256]{2,1,0:T(8,128)(2,1)S(1)}, u32[]{:S(2)}, u32[]{:S(2)}) collective-permute-start(bf16[4,128,256]{2,1,0:T(8,128)(2,1)S(1)} %get-tuple-element.21), channel_id=1, source_target_pairs={{0,1},{1,2},{2,3},{3,0},{4,5},{5,6},{6,7},{7,4},{8,9},{9,10},{10,1... | collective-permute-start | bytes 786440 | tf_op jit(solution)/shard_map/ppermute | solution.py:76
  324.0 87.5 %collective-permute-start.28 = (bf16[8,128,256]{2,1,0:T(8,128)(2,1)}, bf16[8,128,256]{2,1,0:T(8,128)(2,1)}, u32[]{:S(2)}, u32[]{:S(2)}) collective-permute-start(bf16[8,128,256]{2,1,0:T(8,128)(2,1)} %get-tuple-element.37), channel_id=1, source_target_pairs={{0,4},{1,5},{2,6},{3,7},{4,8},{5,9},{6,10},{7,11},{8,12},{9,13},{1... | collective-permute-start | bytes 1572872 | tf_op jit(solution)/shard_map/ppermute | solution.py:61
  331.0 81.6 %collective-permute-start.29 = (bf16[8,128,256]{2,1,0:T(8,128)(2,1)}, bf16[8,128,256]{2,1,0:T(8,128)(2,1)}, u32[]{:S(2)}, u32[]{:S(2)}) collective-permute-start(bf16[8,128,256]{2,1,0:T(8,128)(2,1)} %get-tuple-element.38), channel_id=1, source_target_pairs={{0,8},{1,9},{2,10},{3,11},{4,12},{5,13},{6,14},{7,15},{8,0},{9,1},... | collective-permute-start | bytes 1572872 | tf_op jit(solution)/shard_map/ppermute | solution.py:61
  360.4 53.3 %collective-permute-start.30 = (bf16[8,128,256]{2,1,0:T(8,128)(2,1)}, bf16[8,128,256]{2,1,0:T(8,128)(2,1)}, u32[]{:S(2)}, u32[]{:S(2)}) collective-permute-start(bf16[8,128,256]{2,1,0:T(8,128)(2,1)} %get-tuple-element.39), channel_id=1, source_target_pairs={{0,12},{1,13},{2,14},{3,15},{4,0},{5,1},{6,2},{7,3},{8,4},{9,5},{1... | collective-permute-start | bytes 1572872 | tf_op jit(solution)/shard_map/ppermute | solution.py:61
  366.7 2.1 copy-start.13
  368.8 3.3 copy-start.5
  372.7 65.2 %collective-permute-start.24 = (bf16[128,4096]{1,0:T(8,128)(2,1)S(1)}, bf16[128,4096]{1,0:T(8,128)(2,1)S(1)}, u32[]{:S(2)}, u32[]{:S(2)}) collective-permute-start(bf16[128,4096]{1,0:T(8,128)(2,1)S(1)} %add_convert_fusion), channel_id=1, source_target_pairs={{0,16},{16,32},{32,48},{48,64},{64,80},{80,96},{96,112},{112,128},... | collective-permute-start | bytes 3145736 | tf_op jit(solution)/shard_map/ppermute | solution.py:14
  412.6 2.4 copy-start.3
  412.6 2.4 copy-start.7
  415.0 22.1 %copy-start.6 = (bf16[1,256,768]{2,1,0:T(8,128)(2,1)S(1)}, bf16[1,256,768]{2,1,0:T(8,128)(2,1)}, u32[]{:S(2)}) copy-start(bf16[1,256,768]{2,1,0:T(8,128)(2,1)} %param.14) | copy-start | bytes 1179652
  417.4 19.6 %collective-permute-start.31 = (bf16[256,768]{1,0:T(8,128)(2,1)S(1)}, bf16[256,768]{1,0:T(8,128)(2,1)S(1)}, u32[]{:S(2)}, u32[]{:S(2)}) collective-permute-start(bf16[256,768]{1,0:T(8,128)(2,1)S(1)} %fusion.34), channel_id=1, source_target_pairs={{0,496},{16,480},{32,464},{48,448},{64,432},{80,416},{96,400},{112... | collective-permute-start | bytes 1179656 | tf_op jit(solution)/shard_map/ppermute | solution.py:19
Sparse Core Ops, SparseCore 0:
  11.0 137.3 all-gather.5
  151.4 115.3 all-gather.3

commit v13 on v9

--- a/solution.py
+++ b/solution.py
@@ -156,7 +156,7 @@
     value_part = jnp.einsum("tgj,tgh->jh", weights, grad_heads, preferred_element_type=jnp.float32)
     kv_part = jnp.concatenate([key_part, value_part], axis=1).reshape(outer, INNER, count, 2 * HEAD)
     query_all = gather_blocks(query_grad)
-    kv_grad = reduce_blocks(kv_part, jnp.bfloat16).astype(jnp.bfloat16)
+    kv_grad = reduce_blocks(kv_part, jnp.float32).astype(jnp.bfloat16)
     kv_all, hidden_cols = gather_and_scatter(kv_grad[None], hidden, o, i)
     hidden_cols = hidden_cols.reshape(size * count, -1)
     grad_all = jnp.concatenate([query_all, kv_all[:, 0]], axis=-1).reshape(size * count, -1)

time: 439 us -> 473 us (1.077)
  the two profiles are of different devices: /device:TPU:25 before, /device:TPU:23 now
where the time goes in v13:
time: 473 us; the launch traced here: 472 us
  starting transfers between devices  234 us (49%)
  waiting for transfers between devices  137 us (29%)
  matrix products  35.8 us (8%)
  local copies, waits for them, and re-layouts  28.4 us (6%)
  other arithmetic  20.8 us (4%)
  between operations  14.9 us (3%)
    ppermute x1, starting transfers between devices, shifted(): lax.ppermute(value, axis, [(source, source + steps) for source in range(i...  92.7 us
    all_gather x1, waiting for transfers between devices, per_device(): lax.all_gather(up_output_weight[0], 'seq', axis=1, tiled=True)  77.9 us
    ppermute x6, starting transfers between devices, gather_blocks(): lax.ppermute(x, 'seq', seq_pairs(k, 0))  42 us
    ppermute x6, waiting for transfers between devices, gather_blocks(): lax.ppermute(x, 'seq', seq_pairs(k, 0))  28.7 us
    ppermute x3, starting transfers between devices, reduce_blocks(): lax.ppermute(acc[k].astype(wire), 'seq', seq_pairs(INNER - k, 0))  18.9 us
    ppermute x6, starting transfers between devices, gather_blocks(): lax.ppermute(first, 'seq', seq_pairs(k, 1))  18.1 us
    ppermute x3, starting transfers between devices, gather_columns(): second.append(lax.ppermute(first[k], 'seq', seq_pairs(INNER - k, 0)))  16.4 us
    ppermute x3, starting transfers between devices, gather_and_scatter(): lax.ppermute(jnp.concatenate([x, piece]), 'seq', seq_pairs(k, 0))  16 us
  transfers between devices with their start and end apart: 34, of which 8 were waited for; matrix products, arithmetic and copies ran while one was open for 18% of the time, Pallas kernels for 0%

profile of v13, /device:TPU:23, one launch (start us, length us, event | category | flops | bytes accessed | tf_op | source)
XLA Modules:
  0.0 471.6 jit_solution(18282582579677434936)
XLA Ops:
  9.1 8.8 %collective-permute-start = (bf16[128,256]{0,1:T(8,128)(2,1)S(1)}, bf16[128,256]{0,1:T(8,128)(2,1)S(1)}, u32[]{:S(2)}, u32[]{:S(2)}) collective-permute-start(bf16[128,256]{0,1:T(8,128)(2,1)S(1)} %get-tuple-element.39), channel_id=1, source_target_pairs={{0,1},{1,2},{2,3},{3,0},{4,5},{5,6},{6,7},{7,4},{8,9},{9,10},{10,1... | collective-permute-start | bytes 196616 | tf_op jit(solution)/shard_map/ppermute | solution.py:32
  17.9 10.6 %collective-permute-start.1 = (bf16[128,256]{0,1:T(8,128)(2,1)S(1)}, bf16[128,256]{0,1:T(8,128)(2,1)S(1)}, u32[]{:S(2)}, u32[]{:S(2)}) collective-permute-start(bf16[128,256]{0,1:T(8,128)(2,1)S(1)} %get-tuple-element.39), channel_id=1, source_target_pairs={{0,2},{1,3},{2,0},{3,1},{4,6},{5,7},{6,4},{7,5},{8,10},{9,11},{10,... | collective-permute-start | bytes 196616 | tf_op jit(solution)/shard_map/ppermute | solution.py:32
  28.5 5.2 %collective-permute-start.2 = (bf16[128,256]{0,1:T(8,128)(2,1)S(1)}, bf16[128,256]{0,1:T(8,128)(2,1)S(1)}, u32[]{:S(2)}, u32[]{:S(2)}) collective-permute-start(bf16[128,256]{0,1:T(8,128)(2,1)S(1)} %get-tuple-element.39), channel_id=1, source_target_pairs={{0,3},{1,0},{2,1},{3,2},{4,7},{5,4},{6,5},{7,6},{8,11},{9,8},{10,9... | collective-permute-start | bytes 196616 | tf_op jit(solution)/shard_map/ppermute | solution.py:32
  33.7 1.6 slice.151
  35.6 1.7 compare_and_fusion
  37.3 10.9 %collective-permute-done.2 = bf16[128,256]{0,1:T(8,128)(2,1)S(1)} collective-permute-done((bf16[128,256]{0,1:T(8,128)(2,1)S(1)}, bf16[128,256]{0,1:T(8,128)(2,1)S(1)}, u32[]{:S(2)}, u32[]{:S(2)}) %collective-permute-start.2) | collective-permute-done | bytes 65568 | tf_op jit(solution)/shard_map/ppermute | solution.py:32
  48.9 2.2 collective-permute-start.3
  51.1 4.0 collective-permute-start.4
  55.2 1.9 collective-permute-start.5
  58.0 1.7 reshape.206
  61.4 1.3 mul.112
  62.8 1.3 copy.64
  65.2 2.9 collective-permute-done.5
  68.1 2.2 pad_maximum_fusion.2
  70.3 2.3 copy.41
  72.6 5.3 %fusion.87 = (f32[128,4]{0,1:T(4,128)}, f32[128,4,2048]{0,2,1:T(8,128)}) fusion(pred[128,2048]{0,1:T(8,128)(4,1)S(1)} %copy-done.13, bf16[128,4,128]{0,2,1:T(8,128)(2,1)S(1)} %bitcast.235, bf16[2048,256]{1,0:T(8,128)(2,1)} %bitcast.194), kind=kOutput, calls=%fused_computation.158 | convolution fusion | flops 273680384 | bytes 5376000 | tf_op jit(solution)/shard_map/sub | solution.py:143
  78.0 77.9 %all-gather.6.cloned.1.call-done = bf16[1,512,4096]{2,1,0:T(8,128)(2,1)} async-done(((bf16[1,512,256]{2,1,0:T(8,128)(2,1)}), bf16[1,512,4096]{2,1,0:T(8,128)(2,1)}) %all-gather.6.cloned.1.call-update) | async-done | bytes 4194320 | tf_op jit(solution)/shard_map/all_gather | solution.py:123
  155.9 4.0 fusion.37
  160.1 3.9 fusion.65
  163.9 1.9 convolution_bitcast_fusion
  165.8 8.3 %convolution_bitcast_fusion.1 = f32[2048,128]{0,1:T(8,128)} fusion(bf16[128,4,128]{0,2,1:T(8,128)(2,1)S(1)} %bitcast.236, f32[128,4,2048]{0,2,1:T(8,128)} %fusion.65, f32[128,4,2048]{0,2,1:T(8,128)} %get-tuple-element.45, f32[128,4]{0,1:T(4,128)S(1)} %copy-done.20), kind=kOutput, calls=%fused_computation.30 | convolution fusion | flops 275778048 | bytes 9570304 | tf_op jit(solution)/shard_map/tgj,tgh->jh/dot_general | solution.py:155
  174.1 2.9 fusion.64
  177.0 2.1 copy.82
  179.1 1.9 collective-permute-start.18
  181.0 2.1 copy.83
  183.1 3.3 collective-permute-start.19
  186.4 2.1 copy.84
  188.5 3.3 collective-permute-start.20
  191.8 7.4 %fusion.40 = bf16[128,4,128]{0,2,1:T(8,128)(2,1)S(1)} fusion(f32[128,4,2048]{0,2,1:T(8,128)} %fusion.65, bf16[2048,256]{1,0:T(8,128)(2,1)} %bitcast.196, f32[128,4,2048]{0,2,1:T(8,128)} %get-tuple-element.45, f32[128,4]{0,1:T(4,128)S(1)} %copy-done.21), kind=kOutput, calls=%fused_computation.61 | convolution fusion | flops 275843584 | bytes 17436672 | tf_op jit(solution)/shard_map/tgj,jh->tgh/dot_general | solution.py:151
  200.0 7.6 %collective-permute-start.6 = (bf16[128,512]{1,0:T(8,128)(2,1)}, bf16[128,512]{1,0:T(8,128)(2,1)S(1)}, u32[]{:S(2)}, u32[]{:S(2)}) collective-permute-start(bf16[128,512]{1,0:T(8,128)(2,1)} %copy.48), channel_id=1, source_target_pairs={{0,1},{1,2},{2,3},{3,0},{4,5},{5,6},{6,7},{7,4},{8,9},{9,10},{10,1... | collective-permute-start | bytes 393224 | tf_op jit(solution)/shard_map/ppermute | solution.py:32
  207.6 2.2 fusion.21
  209.8 7.8 %collective-permute-start.7 = (bf16[128,512]{1,0:T(8,128)(2,1)}, bf16[128,512]{1,0:T(8,128)(2,1)}, u32[]{:S(2)}, u32[]{:S(2)}) collective-permute-start(bf16[128,512]{1,0:T(8,128)(2,1)} %copy.48), channel_id=1, source_target_pairs={{0,2},{1,3},{2,0},{3,1},{4,6},{5,7},{6,4},{7,5},{8,10},{9,11},{10,... | collective-permute-start | bytes 393224 | tf_op jit(solution)/shard_map/ppermute | solution.py:32
  217.6 1.9 collective-permute-start.8
  219.6 1.3 dynamic-slice_bitcast_fusion.6
  221.2 17.8 %collective-permute-done.7 = bf16[128,512]{1,0:T(8,128)(2,1)} collective-permute-done((bf16[128,512]{1,0:T(8,128)(2,1)}, bf16[128,512]{1,0:T(8,128)(2,1)}, u32[]{:S(2)}, u32[]{:S(2)}) %collective-permute-start.7) | collective-permute-done | bytes 131104 | tf_op jit(solution)/shard_map/ppermute | solution.py:32
  240.1 4.6 collective-permute-start.9
  244.7 2.5 collective-permute-start.10
  247.2 2.8 collective-permute-start.11
  250.0 1.5 add_add_fusion
  251.5 7.6 %collective-permute-start.21 = (f32[128,256]{1,0:T(8,128)S(1)}, f32[128,256]{1,0:T(8,128)S(1)}, u32[]{:S(2)}, u32[]{:S(2)}) collective-permute-start(f32[128,256]{1,0:T(8,128)S(1)} %get-tuple-element.28), channel_id=1, source_target_pairs={{0,3},{1,0},{2,1},{3,2},{4,7},{5,4},{6,5},{7,6},{8,11},{9,8},{10,9... | collective-permute-start | bytes 393224 | tf_op jit(solution)/shard_map/ppermute | solution.py:43
  259.1 4.9 %collective-permute-start.22 = (f32[128,256]{1,0:T(8,128)S(1)}, f32[128,256]{1,0:T(8,128)S(1)}, u32[]{:S(2)}, u32[]{:S(2)}) collective-permute-start(f32[128,256]{1,0:T(8,128)S(1)} %get-tuple-element.30), channel_id=1, source_target_pairs={{0,2},{1,3},{2,0},{3,1},{4,6},{5,7},{6,4},{7,5},{8,10},{9,11},{10,... | collective-permute-start | bytes 393224 | tf_op jit(solution)/shard_map/ppermute | solution.py:43
  264.1 6.5 %collective-permute-start.23 = (f32[128,256]{1,0:T(8,128)S(1)}, f32[128,256]{1,0:T(8,128)S(1)}, u32[]{:S(2)}, u32[]{:S(2)}) collective-permute-start(f32[128,256]{1,0:T(8,128)S(1)} %get-tuple-element.29), channel_id=1, source_target_pairs={{0,1},{1,2},{2,3},{3,0},{4,5},{5,6},{6,7},{7,4},{8,9},{9,10},{10,1... | collective-permute-start | bytes 393224 | tf_op jit(solution)/shard_map/ppermute | solution.py:43
  270.5 3.3 collective-permute-done.11
  275.9 1.9 collective-permute-start.12
  277.8 2.3 collective-permute-start.13
  280.2 4.1 collective-permute-start.14
  284.5 2.8 collective-permute-start.25
  287.3 11.3 %collective-permute-start.26 = (bf16[5,128,256]{2,1,0:T(8,128)(2,1)S(1)}, bf16[5,128,256]{2,1,0:T(8,128)(2,1)S(1)}, u32[]{:S(2)}, u32[]{:S(2)}) collective-permute-start(bf16[5,128,256]{2,1,0:T(8,128)(2,1)S(1)} %get-tuple-element.42), channel_id=1, source_target_pairs={{0,2},{1,3},{2,0},{3,1},{4,6},{5,7},{6,4},{7,5},{8,10},{9,11},{10,... | collective-permute-start | bytes 983048 | tf_op jit(solution)/shard_map/ppermute | solution.py:54
  298.6 1.9 collective-permute-start.27
  300.8 3.0 collective-permute-start.15
  303.8 11.3 %collective-permute-start.16 = (bf16[4,128,256]{2,1,0:T(8,128)(2,1)S(1)}, bf16[4,128,256]{2,1,0:T(8,128)(2,1)S(1)}, u32[]{:S(2)}, u32[]{:S(2)}) collective-permute-start(bf16[4,128,256]{2,1,0:T(8,128)(2,1)S(1)} %get-tuple-element.17), channel_id=1, source_target_pairs={{0,2},{1,3},{2,0},{3,1},{4,6},{5,7},{6,4},{7,5},{8,10},{9,11},{10,... | collective-permute-start | bytes 786440 | tf_op jit(solution)/shard_map/ppermute | solution.py:76
  315.1 2.2 collective-permute-start.17
  317.2 12.7 %collective-permute-done.26 = bf16[5,128,256]{2,1,0:T(8,128)(2,1)S(1)} collective-permute-done((bf16[5,128,256]{2,1,0:T(8,128)(2,1)S(1)}, bf16[5,128,256]{2,1,0:T(8,128)(2,1)S(1)}, u32[]{:S(2)}, u32[]{:S(2)}) %collective-permute-start.26) | collective-permute-done | bytes 327712 | tf_op jit(solution)/shard_map/ppermute | solution.py:54
  332.1 1.2 pad_maximum_fusion.6
  333.3 5.3 %collective-permute-start.28 = (bf16[8,128,256]{2,1,0:T(8,128)(2,1)}, bf16[8,128,256]{2,1,0:T(8,128)(2,1)}, u32[]{:S(2)}, u32[]{:S(2)}) collective-permute-start(bf16[8,128,256]{2,1,0:T(8,128)(2,1)} %get-tuple-element.33), channel_id=1, source_target_pairs={{0,4},{1,5},{2,6},{3,7},{4,8},{5,9},{6,10},{7,11},{8,12},{9,13},{1... | collective-permute-start | bytes 1572872 | tf_op jit(solution)/shard_map/ppermute | solution.py:61
  338.6 3.4 collective-permute-start.29
  342.0 2.8 collective-permute-start.30
  346.3 1.4 copy.55
  347.7 2.1 reshape.204
  349.8 3.2 multiply_reduce_fusion.1
  353.8 92.7 %collective-permute-start.24 = (bf16[128,4096]{1,0:T(8,128)(2,1)S(1)}, bf16[128,4096]{1,0:T(8,128)(2,1)S(1)}, u32[]{:S(2)}, u32[]{:S(2)}) collective-permute-start(bf16[128,4096]{1,0:T(8,128)(2,1)S(1)} %add_convert_fusion), channel_id=1, source_target_pairs={{0,16},{16,32},{32,48},{48,64},{64,80},{80,96},{96,112},{112,128},... | collective-permute-start | bytes 3145736 | tf_op jit(solution)/shard_map/ppermute | solution.py:14
  447.6 1.2 slice_bitcast_fusion.13
  451.2 1.9 collective-permute-start.31
  453.1 9.9 %collective-permute-done.31 = bf16[256,768]{1,0:T(8,128)(2,1)S(1)} collective-permute-done((bf16[256,768]{1,0:T(8,128)(2,1)S(1)}, bf16[256,768]{1,0:T(8,128)(2,1)S(1)}, u32[]{:S(2)}, u32[]{:S(2)}) %collective-permute-start.31) | collective-permute-done | bytes 393248 | tf_op jit(solution)/shard_map/ppermute | solution.py:19
  (115 shorter events, 20.8 us)
Async XLA Ops:
  7.2 50.0 %copy-start = (bf16[1,128,4096]{2,1,0:T(8,128)(2,1)S(1)}, bf16[1,128,4096]{2,1,0:T(8,128)(2,1)}, u32[]{:S(2)}) copy-start(bf16[1,128,4096]{2,1,0:T(8,128)(2,1)} %param.8) | copy-start | bytes 3145732
  7.2 148.7 %all-gather.6.cloned.1.call-start = ((), (), s32[]{:S(2)}) async-start(), calls=%async_computation.1 | async-start | bytes 4456448 | tf_op jit(solution)/shard_map/all_gather | solution.py:123
  7.9 341.9 %all-gather.4.cloned.1.call-start = ((), (), s32[]{:S(2)}) async-start(), calls=%async_computation | async-start | bytes 2228224 | tf_op jit(solution)/shard_map/all_gather | solution.py:125
  9.1 28.2 %collective-permute-start = (bf16[128,256]{0,1:T(8,128)(2,1)S(1)}, bf16[128,256]{0,1:T(8,128)(2,1)S(1)}, u32[]{:S(2)}, u32[]{:S(2)}) collective-permute-start(bf16[128,256]{0,1:T(8,128)(2,1)S(1)} %get-tuple-element.39), channel_id=1, source_target_pairs={{0,1},{1,2},{2,3},{3,0},{4,5},{5,6},{6,7},{7,4},{8,9},{9,10},{10,1... | collective-permute-start | bytes 196616 | tf_op jit(solution)/shard_map/ppermute | solution.py:32
  17.9 19.4 %collective-permute-start.1 = (bf16[128,256]{0,1:T(8,128)(2,1)S(1)}, bf16[128,256]{0,1:T(8,128)(2,1)S(1)}, u32[]{:S(2)}, u32[]{:S(2)}) collective-permute-start(bf16[128,256]{0,1:T(8,128)(2,1)S(1)} %get-tuple-element.39), channel_id=1, source_target_pairs={{0,2},{1,3},{2,0},{3,1},{4,6},{5,7},{6,4},{7,5},{8,10},{9,11},{10,... | collective-permute-start | bytes 196616 | tf_op jit(solution)/shard_map/ppermute | solution.py:32
  28.5 19.6 %collective-permute-start.2 = (bf16[128,256]{0,1:T(8,128)(2,1)S(1)}, bf16[128,256]{0,1:T(8,128)(2,1)S(1)}, u32[]{:S(2)}, u32[]{:S(2)}) collective-permute-start(bf16[128,256]{0,1:T(8,128)(2,1)S(1)} %get-tuple-element.39), channel_id=1, source_target_pairs={{0,3},{1,0},{2,1},{3,2},{4,7},{5,4},{6,5},{7,6},{8,11},{9,8},{10,9... | collective-permute-start | bytes 196616 | tf_op jit(solution)/shard_map/ppermute | solution.py:32
  48.9 11.3 %copy-start.14 = (f32[1,4096]{1,0:T(1,128)S(1)}, f32[1,4096]{1,0:T(1,128)}, u32[]{:S(2)}) copy-start(f32[1,4096]{1,0:T(1,128)} %param.13) | copy-start | bytes 49156
  48.9 16.3 %collective-permute-start.3 = (bf16[4,128,256]{1,2,0:T(8,128)(2,1)}, bf16[4,128,256]{1,2,0:T(8,128)(2,1)}, u32[]{:S(2)}, u32[]{:S(2)}) collective-permute-start(bf16[4,128,256]{1,2,0:T(8,128)(2,1)} %get-tuple-element.37), channel_id=1, source_target_pairs={{0,4},{1,5},{2,6},{3,7},{4,8},{5,9},{6,10},{7,11},{8,12},{9,13},{1... | collective-permute-start | bytes 786440 | tf_op jit(solution)/shard_map/ppermute | solution.py:33
  51.1 14.1 %collective-permute-start.4 = (bf16[4,128,256]{1,2,0:T(8,128)(2,1)}, bf16[4,128,256]{1,2,0:T(8,128)(2,1)}, u32[]{:S(2)}, u32[]{:S(2)}) collective-permute-start(bf16[4,128,256]{1,2,0:T(8,128)(2,1)} %get-tuple-element.37), channel_id=1, source_target_pairs={{0,8},{1,9},{2,10},{3,11},{4,12},{5,13},{6,14},{7,15},{8,0},{9,1},... | collective-permute-start | bytes 786440 | tf_op jit(solution)/shard_map/ppermute | solution.py:33
  55.2 12.9 %collective-permute-start.5 = (bf16[4,128,256]{1,2,0:T(8,128)(2,1)}, bf16[4,128,256]{1,2,0:T(8,128)(2,1)}, u32[]{:S(2)}, u32[]{:S(2)}) collective-permute-start(bf16[4,128,256]{1,2,0:T(8,128)(2,1)} %get-tuple-element.37), channel_id=1, source_target_pairs={{0,12},{1,13},{2,14},{3,15},{4,0},{5,1},{6,2},{7,3},{8,4},{9,5},{1... | collective-permute-start | bytes 786440 | tf_op jit(solution)/shard_map/ppermute | solution.py:33
  70.3 2.3 copy-start.13
  160.0 3.9 copy-start.19
  160.1 3.9 copy-start.20
  177.0 14.8 %copy-start.21 = (f32[128,4]{0,1:T(4,128)S(1)}, f32[128,4]{0,1:T(4,128)}, u32[]{:S(2)}) copy-start(f32[128,4]{0,1:T(4,128)} %get-tuple-element.44) | copy-start | bytes 6148
  179.1 68.1 %collective-permute-start.18 = (f32[4,128,256]{2,1,0:T(8,128)}, f32[4,128,256]{2,1,0:T(8,128)}, u32[]{:S(2)}, u32[]{:S(2)}) collective-permute-start(f32[4,128,256]{2,1,0:T(8,128)} %bitcast.215), channel_id=1, source_target_pairs={{0,12},{1,13},{2,14},{3,15},{4,0},{5,1},{6,2},{7,3},{8,4},{9,5},{1... | collective-permute-start | bytes 1572872 | tf_op jit(solution)/shard_map/ppermute | solution.py:40
  183.1 66.9 %collective-permute-start.19 = (f32[4,128,256]{2,1,0:T(8,128)}, f32[4,128,256]{2,1,0:T(8,128)}, u32[]{:S(2)}, u32[]{:S(2)}) collective-permute-start(f32[4,128,256]{2,1,0:T(8,128)} %bitcast.214), channel_id=1, source_target_pairs={{0,8},{1,9},{2,10},{3,11},{4,12},{5,13},{6,14},{7,15},{8,0},{9,1},... | collective-permute-start | bytes 1572872 | tf_op jit(solution)/shard_map/ppermute | solution.py:40
  188.5 19.1 %copy-start.15 = (f32[4,4,256]{2,0,1:T(4,128)S(1)}, f32[4,4,256]{2,0,1:T(4,128)}, u32[]{:S(2)}) copy-start(f32[4,4,256]{2,0,1:T(4,128)} %copy.64) | copy-start | bytes 49156
  188.5 19.1 %copy-start.17 = (f32[128]{0:T(128)S(1)}, f32[128]{0:T(128)}, u32[]{:S(2)}) copy-start(f32[128]{0:T(128)} %add_rsqrt_fusion) | copy-start | bytes 1540
  188.5 61.5 %collective-permute-start.20 = (f32[4,128,256]{2,1,0:T(8,128)}, f32[4,128,256]{2,1,0:T(8,128)}, u32[]{:S(2)}, u32[]{:S(2)}) collective-permute-start(f32[4,128,256]{2,1,0:T(8,128)} %bitcast.216), channel_id=1, source_target_pairs={{0,4},{1,5},{2,6},{3,7},{4,8},{5,9},{6,10},{7,11},{8,12},{9,13},{1... | collective-permute-start | bytes 1572872 | tf_op jit(solution)/shard_map/ppermute | solution.py:40
  200.0 17.7 %collective-permute-start.6 = (bf16[128,512]{1,0:T(8,128)(2,1)}, bf16[128,512]{1,0:T(8,128)(2,1)S(1)}, u32[]{:S(2)}, u32[]{:S(2)}) collective-permute-start(bf16[128,512]{1,0:T(8,128)(2,1)} %copy.48), channel_id=1, source_target_pairs={{0,1},{1,2},{2,3},{3,0},{4,5},{5,6},{6,7},{7,4},{8,9},{9,10},{10,1... | collective-permute-start | bytes 393224 | tf_op jit(solution)/shard_map/ppermute | solution.py:32
  209.8 11.0 %copy-start.4 = (f32[512,256]{0,1:T(8,128)S(1)}, f32[512,256]{0,1:T(8,128)}, u32[]{:S(2)}) copy-start(f32[512,256]{0,1:T(8,128)} %get-tuple-element.3) | copy-start | bytes 1572868
  209.8 29.2 %collective-permute-start.7 = (bf16[128,512]{1,0:T(8,128)(2,1)}, bf16[128,512]{1,0:T(8,128)(2,1)}, u32[]{:S(2)}, u32[]{:S(2)}) collective-permute-start(bf16[128,512]{1,0:T(8,128)(2,1)} %copy.48), channel_id=1, source_target_pairs={{0,2},{1,3},{2,0},{3,1},{4,6},{5,7},{6,4},{7,5},{8,10},{9,11},{10,... | collective-permute-start | bytes 393224 | tf_op jit(solution)/shard_map/ppermute | solution.py:32
  217.6 21.4 %collective-permute-start.8 = (bf16[128,512]{1,0:T(8,128)(2,1)}, bf16[128,512]{1,0:T(8,128)(2,1)}, u32[]{:S(2)}, u32[]{:S(2)}) collective-permute-start(bf16[128,512]{1,0:T(8,128)(2,1)} %copy.48), channel_id=1, source_target_pairs={{0,3},{1,0},{2,1},{3,2},{4,7},{5,4},{6,5},{7,6},{8,11},{9,8},{10,9... | collective-permute-start | bytes 393224 | tf_op jit(solution)/shard_map/ppermute | solution.py:32
  240.1 34.1 %copy-start.2 = (bf16[1,4,128,512]{3,2,1,0:T(8,128)(2,1)}, bf16[1,4,128,512]{3,2,1,0:T(8,128)(2,1)S(1)}, u32[]{:S(2)}) copy-start(bf16[1,4,128,512]{3,2,1,0:T(8,128)(2,1)S(1)} %get-tuple-element.31) | copy-start | bytes 1572868
  240.1 24.0 %collective-permute-start.9 = (bf16[4,128,512]{2,1,0:T(8,128)(2,1)S(1)}, bf16[4,128,512]{2,1,0:T(8,128)(2,1)S(1)}, u32[]{:S(2)}, u32[]{:S(2)}) collective-permute-start(bf16[4,128,512]{2,1,0:T(8,128)(2,1)S(1)} %get-tuple-element.32), channel_id=1, source_target_pairs={{0,4},{1,5},{2,6},{3,7},{4,8},{5,9},{6,10},{7,11},{8,12},{9,13},{1... | collective-permute-start | bytes 1572872 | tf_op jit(solution)/shard_map/ppermute | solution.py:33
  244.7 25.8 %collective-permute-start.10 = (bf16[4,128,512]{2,1,0:T(8,128)(2,1)S(1)}, bf16[4,128,512]{2,1,0:T(8,128)(2,1)S(1)}, u32[]{:S(2)}, u32[]{:S(2)}) collective-permute-start(bf16[4,128,512]{2,1,0:T(8,128)(2,1)S(1)} %get-tuple-element.32), channel_id=1, source_target_pairs={{0,8},{1,9},{2,10},{3,11},{4,12},{5,13},{6,14},{7,15},{8,0},{9,1},... | collective-permute-start | bytes 1572872 | tf_op jit(solution)/shard_map/ppermute | solution.py:33
  247.2 26.7 %collective-permute-start.11 = (bf16[4,128,512]{2,1,0:T(8,128)(2,1)S(1)}, bf16[4,128,512]{2,1,0:T(8,128)(2,1)S(1)}, u32[]{:S(2)}, u32[]{:S(2)}) collective-permute-start(bf16[4,128,512]{2,1,0:T(8,128)(2,1)S(1)} %get-tuple-element.32), channel_id=1, source_target_pairs={{0,12},{1,13},{2,14},{3,15},{4,0},{5,1},{6,2},{7,3},{8,4},{9,5},{1... | collective-permute-start | bytes 1572872 | tf_op jit(solution)/shard_map/ppermute | solution.py:33
  251.5 28.6 %collective-permute-start.21 = (f32[128,256]{1,0:T(8,128)S(1)}, f32[128,256]{1,0:T(8,128)S(1)}, u32[]{:S(2)}, u32[]{:S(2)}) collective-permute-start(f32[128,256]{1,0:T(8,128)S(1)} %get-tuple-element.28), channel_id=1, source_target_pairs={{0,3},{1,0},{2,1},{3,2},{4,7},{5,4},{6,5},{7,6},{8,11},{9,8},{10,9... | collective-permute-start | bytes 393224 | tf_op jit(solution)/shard_map/ppermute | solution.py:43
  259.1 25.2 %collective-permute-start.22 = (f32[128,256]{1,0:T(8,128)S(1)}, f32[128,256]{1,0:T(8,128)S(1)}, u32[]{:S(2)}, u32[]{:S(2)}) collective-permute-start(f32[128,256]{1,0:T(8,128)S(1)} %get-tuple-element.30), channel_id=1, source_target_pairs={{0,2},{1,3},{2,0},{3,1},{4,6},{5,7},{6,4},{7,5},{8,10},{9,11},{10,... | collective-permute-start | bytes 393224 | tf_op jit(solution)/shard_map/ppermute | solution.py:43
  264.0 10.1 %copy-start.5 = (bf16[4,128,512]{2,1,0:T(8,128)(2,1)}, bf16[4,128,512]{2,1,0:T(8,128)(2,1)S(1)}, u32[]{:S(2)}) copy-start(bf16[4,128,512]{2,1,0:T(8,128)(2,1)S(1)} %collective-permute-done.9) | copy-start | bytes 1572868
  264.1 20.3 %collective-permute-start.23 = (f32[128,256]{1,0:T(8,128)S(1)}, f32[128,256]{1,0:T(8,128)S(1)}, u32[]{:S(2)}, u32[]{:S(2)}) collective-permute-start(f32[128,256]{1,0:T(8,128)S(1)} %get-tuple-element.29), channel_id=1, source_target_pairs={{0,1},{1,2},{2,3},{3,0},{4,5},{5,6},{6,7},{7,4},{8,9},{9,10},{10,1... | collective-permute-start | bytes 393224 | tf_op jit(solution)/shard_map/ppermute | solution.py:43
  270.5 3.6 copy-start.7
  273.9 0.8 copy-start.9
  273.9 1.2 copy-start.16
  275.9 22.7 %collective-permute-start.12 = (bf16[4,128,256]{2,1,0:T(8,128)(2,1)S(1)}, bf16[4,128,256]{2,1,0:T(8,128)(2,1)S(1)}, u32[]{:S(2)}, u32[]{:S(2)}) collective-permute-start(bf16[4,128,256]{2,1,0:T(8,128)(2,1)S(1)} %bitcast.232), channel_id=1, source_target_pairs={{0,12},{1,13},{2,14},{3,15},{4,0},{5,1},{6,2},{7,3},{8,4},{9,5},{1... | collective-permute-start | bytes 786440 | tf_op jit(solution)/shard_map/ppermute | solution.py:72
  277.8 22.7 %collective-permute-start.13 = (bf16[4,128,256]{2,1,0:T(8,128)(2,1)S(1)}, bf16[4,128,256]{2,1,0:T(8,128)(2,1)S(1)}, u32[]{:S(2)}, u32[]{:S(2)}) collective-permute-start(bf16[4,128,256]{2,1,0:T(8,128)(2,1)S(1)} %bitcast.230), channel_id=1, source_target_pairs={{0,8},{1,9},{2,10},{3,11},{4,12},{5,13},{6,14},{7,15},{8,0},{9,1},... | collective-permute-start | bytes 786440 | tf_op jit(solution)/shard_map/ppermute | solution.py:72
  280.2 20.3 %collective-permute-start.14 = (bf16[4,128,256]{2,1,0:T(8,128)(2,1)S(1)}, bf16[4,128,256]{2,1,0:T(8,128)(2,1)S(1)}, u32[]{:S(2)}, u32[]{:S(2)}) collective-permute-start(bf16[4,128,256]{2,1,0:T(8,128)(2,1)S(1)} %bitcast.228), channel_id=1, source_target_pairs={{0,4},{1,5},{2,6},{3,7},{4,8},{5,9},{6,10},{7,11},{8,12},{9,13},{1... | collective-permute-start | bytes 786440 | tf_op jit(solution)/shard_map/ppermute | solution.py:72
  284.5 30.5 %collective-permute-start.25 = (bf16[5,128,256]{2,1,0:T(8,128)(2,1)S(1)}, bf16[5,128,256]{2,1,0:T(8,128)(2,1)S(1)}, u32[]{:S(2)}, u32[]{:S(2)}) collective-permute-start(bf16[5,128,256]{2,1,0:T(8,128)(2,1)S(1)} %get-tuple-element.41), channel_id=1, source_target_pairs={{0,1},{1,2},{2,3},{3,0},{4,5},{5,6},{6,7},{7,4},{8,9},{9,10},{10,1... | collective-permute-start | bytes 983048 | tf_op jit(solution)/shard_map/ppermute | solution.py:54
  287.3 42.6 %collective-permute-start.26 = (bf16[5,128,256]{2,1,0:T(8,128)(2,1)S(1)}, bf16[5,128,256]{2,1,0:T(8,128)(2,1)S(1)}, u32[]{:S(2)}, u32[]{:S(2)}) collective-permute-start(bf16[5,128,256]{2,1,0:T(8,128)(2,1)S(1)} %get-tuple-element.42), channel_id=1, source_target_pairs={{0,2},{1,3},{2,0},{3,1},{4,6},{5,7},{6,4},{7,5},{8,10},{9,11},{10,... | collective-permute-start | bytes 983048 | tf_op jit(solution)/shard_map/ppermute | solution.py:54
  298.6 32.4 %collective-permute-start.27 = (bf16[5,128,256]{2,1,0:T(8,128)(2,1)S(1)}, bf16[5,128,256]{2,1,0:T(8,128)(2,1)S(1)}, u32[]{:S(2)}, u32[]{:S(2)}) collective-permute-start(bf16[5,128,256]{2,1,0:T(8,128)(2,1)S(1)} %get-tuple-element.43), channel_id=1, source_target_pairs={{0,3},{1,0},{2,1},{3,2},{4,7},{5,4},{6,5},{7,6},{8,11},{9,8},{10,9... | collective-permute-start | bytes 983048 | tf_op jit(solution)/shard_map/ppermute | solution.py:54
  300.8 41.2 %collective-permute-start.15 = (bf16[4,128,256]{2,1,0:T(8,128)(2,1)S(1)}, bf16[4,128,256]{2,1,0:T(8,128)(2,1)S(1)}, u32[]{:S(2)}, u32[]{:S(2)}) collective-permute-start(bf16[4,128,256]{2,1,0:T(8,128)(2,1)S(1)} %get-tuple-element.15), channel_id=1, source_target_pairs={{0,3},{1,0},{2,1},{3,2},{4,7},{5,4},{6,5},{7,6},{8,11},{9,8},{10,9... | collective-permute-start | bytes 786440 | tf_op jit(solution)/shard_map/ppermute | solution.py:76
  303.8 41.0 %collective-permute-start.16 = (bf16[4,128,256]{2,1,0:T(8,128)(2,1)S(1)}, bf16[4,128,256]{2,1,0:T(8,128)(2,1)S(1)}, u32[]{:S(2)}, u32[]{:S(2)}) collective-permute-start(bf16[4,128,256]{2,1,0:T(8,128)(2,1)S(1)} %get-tuple-element.17), channel_id=1, source_target_pairs={{0,2},{1,3},{2,0},{3,1},{4,6},{5,7},{6,4},{7,5},{8,10},{9,11},{10,... | collective-permute-start | bytes 786440 | tf_op jit(solution)/shard_map/ppermute | solution.py:76
  315.1 29.7 %collective-permute-start.17 = (bf16[4,128,256]{2,1,0:T(8,128)(2,1)S(1)}, bf16[4,128,256]{2,1,0:T(8,128)(2,1)S(1)}, u32[]{:S(2)}, u32[]{:S(2)}) collective-permute-start(bf16[4,128,256]{2,1,0:T(8,128)(2,1)S(1)} %get-tuple-element.14), channel_id=1, source_target_pairs={{0,1},{1,2},{2,3},{3,0},{4,5},{5,6},{6,7},{7,4},{8,9},{9,10},{10,1... | collective-permute-start | bytes 786440 | tf_op jit(solution)/shard_map/ppermute | solution.py:76
  333.3 113.2 %collective-permute-start.28 = (bf16[8,128,256]{2,1,0:T(8,128)(2,1)}, bf16[8,128,256]{2,1,0:T(8,128)(2,1)}, u32[]{:S(2)}, u32[]{:S(2)}) collective-permute-start(bf16[8,128,256]{2,1,0:T(8,128)(2,1)} %get-tuple-element.33), channel_id=1, source_target_pairs={{0,4},{1,5},{2,6},{3,7},{4,8},{5,9},{6,10},{7,11},{8,12},{9,13},{1... | collective-permute-start | bytes 1572872 | tf_op jit(solution)/shard_map/ppermute | solution.py:61
  338.6 109.0 %collective-permute-start.29 = (bf16[8,128,256]{2,1,0:T(8,128)(2,1)}, bf16[8,128,256]{2,1,0:T(8,128)(2,1)}, u32[]{:S(2)}, u32[]{:S(2)}) collective-permute-start(bf16[8,128,256]{2,1,0:T(8,128)(2,1)} %get-tuple-element.34), channel_id=1, source_target_pairs={{0,8},{1,9},{2,10},{3,11},{4,12},{5,13},{6,14},{7,15},{8,0},{9,1},... | collective-permute-start | bytes 1572872 | tf_op jit(solution)/shard_map/ppermute | solution.py:61
  342.0 106.9 %collective-permute-start.30 = (bf16[8,128,256]{2,1,0:T(8,128)(2,1)}, bf16[8,128,256]{2,1,0:T(8,128)(2,1)}, u32[]{:S(2)}, u32[]{:S(2)}) collective-permute-start(bf16[8,128,256]{2,1,0:T(8,128)(2,1)} %get-tuple-element.35), channel_id=1, source_target_pairs={{0,12},{1,13},{2,14},{3,15},{4,0},{5,1},{6,2},{7,3},{8,4},{9,5},{1... | collective-permute-start | bytes 1572872 | tf_op jit(solution)/shard_map/ppermute | solution.py:61
  347.7 2.1 copy-start.18
  349.8 3.3 copy-start.1
  353.8 110.1 %collective-permute-start.24 = (bf16[128,4096]{1,0:T(8,128)(2,1)S(1)}, bf16[128,4096]{1,0:T(8,128)(2,1)S(1)}, u32[]{:S(2)}, u32[]{:S(2)}) collective-permute-start(bf16[128,4096]{1,0:T(8,128)(2,1)S(1)} %add_convert_fusion), channel_id=1, source_target_pairs={{0,16},{16,32},{32,48},{48,64},{64,80},{80,96},{96,112},{112,128},... | collective-permute-start | bytes 3145736 | tf_op jit(solution)/shard_map/ppermute | solution.py:14
  447.6 2.5 copy-start.3
  447.6 2.5 copy-start.6
  447.6 2.5 copy-start.8
  447.6 2.5 copy-start.10
  447.6 2.5 copy-start.12
  450.1 12.8 %copy-start.11 = (bf16[1,256,768]{2,1,0:T(8,128)(2,1)S(1)}, bf16[1,256,768]{2,1,0:T(8,128)(2,1)}, u32[]{:S(2)}) copy-start(bf16[1,256,768]{2,1,0:T(8,128)(2,1)} %param.14) | copy-start | bytes 1179652
  451.2 11.8 %collective-permute-start.31 = (bf16[256,768]{1,0:T(8,128)(2,1)S(1)}, bf16[256,768]{1,0:T(8,128)(2,1)S(1)}, u32[]{:S(2)}, u32[]{:S(2)}) collective-permute-start(bf16[256,768]{1,0:T(8,128)(2,1)S(1)} %fusion.34), channel_id=1, source_target_pairs={{0,496},{16,480},{32,464},{48,448},{64,432},{80,416},{96,400},{112... | collective-permute-start | bytes 1179656 | tf_op jit(solution)/shard_map/ppermute | solution.py:19
Sparse Core Ops, SparseCore 0:
  11.0 144.8 all-gather.5
  158.9 105.6 all-gather.3

commit v14 on v9

--- a/solution.py
+++ b/solution.py
@@ -121,7 +121,9 @@
     unit_up, inverse_up, normed_up = normalize(up_activation[0], upward_gain[0])
     hidden = normed_up.astype(jnp.bfloat16)
     output_weight = lax.all_gather(up_output_weight[0], "seq", axis=1, tiled=True)
-    key_value = gather_blocks(saved[:, width:]).reshape(size * count, 2 * HEAD)
+    key_value, hidden_cols = gather_and_scatter(saved[None, :, width:], hidden, o, i)
+    key_value = key_value[:, 0].reshape(size * count, 2 * HEAD)
+    hidden_cols = hidden_cols.reshape(size * count, -1)
     kv_weight_all = lax.all_gather(up_input_weight[0][:, width:], "seq", axis=0, tiled=True)
     keys = key_value[:, :HEAD]
     values = key_value[:, HEAD:]
@@ -157,9 +159,8 @@
     kv_part = jnp.concatenate([key_part, value_part], axis=1).reshape(outer, INNER, count, 2 * HEAD)
     query_all = gather_blocks(query_grad)
     kv_grad = reduce_blocks(kv_part, jnp.bfloat16).astype(jnp.bfloat16)
-    kv_all, hidden_cols = gather_and_scatter(kv_grad[None], hidden, o, i)
-    hidden_cols = hidden_cols.reshape(size * count, -1)
-    grad_all = jnp.concatenate([query_all, kv_all[:, 0]], axis=-1).reshape(size * count, -1)
+    kv_all = gather_blocks(kv_grad)
+    grad_all = jnp.concatenate([query_all, kv_all], axis=-1).reshape(size * count, -1)
     input_term = contract_first(hidden_cols, grad_all).astype(jnp.bfloat16)
     block = contract_last(query_all.reshape(size * count, -1), up_input_weight[0][:, :width])
     hidden_grad = gather_columns(block.astype(jnp.bfloat16).reshape(outer, INNER, count, -1), o, i)

time: 439 us -> 455 us (1.036)
  the two profiles are of different devices: /device:TPU:25 before, /device:TPU:66 now
where the time goes in v14:
time: 455 us; the launch traced here: 454 us
  waiting for transfers between devices  217 us (48%)
  starting transfers between devices  150 us (33%)
  matrix products  34.3 us (8%)
  local copies, waits for them, and re-layouts  23.6 us (5%)
  between operations  15 us (3%)
  other arithmetic  13.8 us (3%)
    ppermute x3, waiting for transfers between devices, gather_and_scatter(): lax.ppermute(jnp.concatenate([x, piece]), 'seq', seq_pairs(k, 0))  64.3 us
    ppermute x6, waiting for transfers between devices, gather_blocks(): lax.ppermute(x, 'seq', seq_pairs(k, 0))  51.1 us
    all_gather x1, waiting for transfers between devices, per_device(): lax.all_gather(up_output_weight[0], 'seq', axis=1, tiled=True)  45.8 us
    ppermute x6, starting transfers between devices, gather_blocks(): lax.ppermute(x, 'seq', seq_pairs(k, 0))  29.4 us
    ppermute x1, waiting for transfers between devices, mirrored(): lax.ppermute(value, axis, [(source, count - 1 - source) for source in ran...  24.7 us
    ppermute x3, starting transfers between devices, gather_and_scatter(): lax.ppermute(jnp.concatenate([x, piece]), 'seq', seq_pairs(k, 0))  23.7 us
    ppermute x6, starting transfers between devices, gather_blocks(): lax.ppermute(first, 'seq', seq_pairs(k, 1))  23 us
    ppermute x3, waiting for transfers between devices, gather_and_scatter(): second.append(lax.ppermute(payload, 'seq', seq_pairs(k, 1)))  22.1 us
  transfers between devices with their start and end apart: 34, of which 15 were waited for; matrix products, arithmetic and copies ran while one was open for 16% of the time, Pallas kernels for 0%

profile of v14, /device:TPU:66, one launch (start us, length us, event | category | flops | bytes accessed | tf_op | source)
XLA Modules:
  0.0 453.7 jit_solution(15707240313850290585)
XLA Ops:
  8.5 1.4 reduce.3
  11.1 3.8 reshape.206
  14.9 2.0 copy.39
  18.9 9.1 %collective-permute-start = (bf16[5,128,256]{1,2,0:T(8,128)(2,1)}, bf16[5,128,256]{1,2,0:T(8,128)(2,1)S(1)}, u32[]{:S(2)}, u32[]{:S(2)}) collective-permute-start(bf16[5,128,256]{1,2,0:T(8,128)(2,1)} %get-tuple-element.40), channel_id=1, source_target_pairs={{0,1},{1,2},{2,3},{3,0},{4,5},{5,6},{6,7},{7,4},{8,9},{9,10},{10,1... | collective-permute-start | bytes 983048 | tf_op jit(solution)/shard_map/ppermute | solution.py:54
  28.0 9.1 %collective-permute-start.1 = (bf16[5,128,256]{1,2,0:T(8,128)(2,1)S(1)}, bf16[5,128,256]{1,2,0:T(8,128)(2,1)S(1)}, u32[]{:S(2)}, u32[]{:S(2)}) collective-permute-start(bf16[5,128,256]{1,2,0:T(8,128)(2,1)S(1)} %get-tuple-element.41), channel_id=1, source_target_pairs={{0,2},{1,3},{2,0},{3,1},{4,6},{5,7},{6,4},{7,5},{8,10},{9,11},{10,... | collective-permute-start | bytes 983048 | tf_op jit(solution)/shard_map/ppermute | solution.py:54
  37.1 5.5 %collective-permute-start.2 = (bf16[5,128,256]{1,2,0:T(8,128)(2,1)S(1)}, bf16[5,128,256]{1,2,0:T(8,128)(2,1)S(1)}, u32[]{:S(2)}, u32[]{:S(2)}) collective-permute-start(bf16[5,128,256]{1,2,0:T(8,128)(2,1)S(1)} %get-tuple-element.42), channel_id=1, source_target_pairs={{0,3},{1,0},{2,1},{3,2},{4,7},{5,4},{6,5},{7,6},{8,11},{9,8},{10,9... | collective-permute-start | bytes 983048 | tf_op jit(solution)/shard_map/ppermute | solution.py:54
  42.6 1.6 slice.159
  44.4 41.5 %collective-permute-done = bf16[5,128,256]{1,2,0:T(8,128)(2,1)S(1)} collective-permute-done((bf16[5,128,256]{1,2,0:T(8,128)(2,1)}, bf16[5,128,256]{1,2,0:T(8,128)(2,1)S(1)}, u32[]{:S(2)}, u32[]{:S(2)}) %collective-permute-start) | collective-permute-done | bytes 327712 | tf_op jit(solution)/shard_map/ppermute | solution.py:54
  85.9 14.3 %collective-permute-done.1 = bf16[5,128,256]{1,2,0:T(8,128)(2,1)S(1)} collective-permute-done((bf16[5,128,256]{1,2,0:T(8,128)(2,1)S(1)}, bf16[5,128,256]{1,2,0:T(8,128)(2,1)S(1)}, u32[]{:S(2)}, u32[]{:S(2)}) %collective-permute-start.1) | collective-permute-done | bytes 327712 | tf_op jit(solution)/shard_map/ppermute | solution.py:54
  100.2 8.5 %collective-permute-done.2 = bf16[5,128,256]{1,2,0:T(8,128)(2,1)S(1)} collective-permute-done((bf16[5,128,256]{1,2,0:T(8,128)(2,1)S(1)}, bf16[5,128,256]{1,2,0:T(8,128)(2,1)S(1)}, u32[]{:S(2)}, u32[]{:S(2)}) %collective-permute-start.2) | collective-permute-done | bytes 327712 | tf_op jit(solution)/shard_map/ppermute | solution.py:54
  109.8 3.3 collective-permute-start.3
  113.1 4.9 %collective-permute-start.4 = (bf16[8,128,256]{1,2,0:T(8,128)(2,1)S(1)}, bf16[8,128,256]{1,2,0:T(8,128)(2,1)S(1)}, u32[]{:S(2)}, u32[]{:S(2)}) collective-permute-start(bf16[8,128,256]{1,2,0:T(8,128)(2,1)S(1)} %get-tuple-element.37), channel_id=1, source_target_pairs={{0,8},{1,9},{2,10},{3,11},{4,12},{5,13},{6,14},{7,15},{8,0},{9,1},... | collective-permute-start | bytes 1572872 | tf_op jit(solution)/shard_map/ppermute | solution.py:61
  117.9 4.0 collective-permute-start.5
  123.1 4.2 collective-permute-done.3
  128.0 7.6 %collective-permute-done.4 = bf16[8,128,256]{1,2,0:T(8,128)(2,1)S(1)} collective-permute-done((bf16[8,128,256]{1,2,0:T(8,128)(2,1)S(1)}, bf16[8,128,256]{1,2,0:T(8,128)(2,1)S(1)}, u32[]{:S(2)}, u32[]{:S(2)}) %collective-permute-start.4) | collective-permute-done | bytes 524320 | tf_op jit(solution)/shard_map/ppermute | solution.py:61
  136.3 10.3 %collective-permute-done.5 = bf16[8,128,256]{1,2,0:T(8,128)(2,1)S(1)} collective-permute-done((bf16[8,128,256]{1,2,0:T(8,128)(2,1)S(1)}, bf16[8,128,256]{1,2,0:T(8,128)(2,1)S(1)}, u32[]{:S(2)}, u32[]{:S(2)}) %collective-permute-start.5) | collective-permute-done | bytes 524320 | tf_op jit(solution)/shard_map/ppermute | solution.py:61
  148.1 3.8 fusion.92
  151.8 45.8 %all-gather.6.cloned.1.call-done = bf16[1,512,4096]{2,1,0:T(8,128)(2,1)} async-done(((bf16[1,512,256]{2,1,0:T(8,128)(2,1)}), bf16[1,512,4096]{2,1,0:T(8,128)(2,1)}) %all-gather.6.cloned.1.call-update) | async-done | bytes 4194320 | tf_op jit(solution)/shard_map/all_gather | solution.py:123
  197.7 3.7 fusion.42
  201.5 2.7 fusion.68
  204.2 7.2 %fusion.45 = bf16[128,4,128]{0,2,1:T(8,128)(2,1)S(1)} fusion(f32[128,4,2048]{0,2,1:T(8,128)} %fusion.68, bf16[2048,256]{1,0:T(8,128)(2,1)S(1)} %bitcast.188, f32[128,4,2048]{0,2,1:T(8,128)} %get-tuple-element.44, f32[128,4]{0,1:T(4,128)S(1)} %get-tuple-element.43), kind=kOutput, calls=%fused_computation.62 | convolution fusion | flops 275843584 | bytes 17436672 | tf_op jit(solution)/shard_map/tgj,jh->tgh/dot_general | solution.py:153
  212.1 4.8 %collective-permute-start.8 = (bf16[128,512]{1,0:T(8,128)(2,1)}, bf16[128,512]{1,0:T(8,128)(2,1)S(1)}, u32[]{:S(2)}, u32[]{:S(2)}) collective-permute-start(bf16[128,512]{1,0:T(8,128)(2,1)} %copy.51), channel_id=1, source_target_pairs={{0,3},{1,0},{2,1},{3,2},{4,7},{5,4},{6,5},{7,6},{8,11},{9,8},{10,9... | collective-permute-start | bytes 393224 | tf_op jit(solution)/shard_map/ppermute | solution.py:32
  216.9 3.4 collective-permute-start.7
  220.3 7.2 %collective-permute-start.6 = (bf16[128,512]{1,0:T(8,128)(2,1)}, bf16[128,512]{1,0:T(8,128)(2,1)}, u32[]{:S(2)}, u32[]{:S(2)}) collective-permute-start(bf16[128,512]{1,0:T(8,128)(2,1)} %copy.51), channel_id=1, source_target_pairs={{0,1},{1,2},{2,3},{3,0},{4,5},{5,6},{6,7},{7,4},{8,9},{9,10},{10,1... | collective-permute-start | bytes 393224 | tf_op jit(solution)/shard_map/ppermute | solution.py:32
  227.7 3.0 convolution_bitcast_fusion
  230.7 7.3 %convolution_bitcast_fusion.1 = f32[2048,128]{0,1:T(8,128)S(1)} fusion(bf16[128,4,128]{0,2,1:T(8,128)(2,1)} %bitcast.222, f32[128,4,2048]{0,2,1:T(8,128)} %fusion.68, f32[128,4,2048]{0,2,1:T(8,128)} %get-tuple-element.44, f32[128,4]{0,1:T(4,128)S(1)} %get-tuple-element.43), kind=kOutput, calls=%fused_computation.33 | convolution fusion | flops 275778048 | bytes 9570304 | tf_op jit(solution)/shard_map/tgj,tgh->jh/dot_general | solution.py:157
  238.1 2.1 collective-permute-done.7
  240.2 2.9 collective-permute-done.6
  243.0 2.0 fusion.88
  245.0 4.1 collective-permute-start.10
  249.1 1.9 collective-permute-start.9
  251.1 4.1 collective-permute-start.11
  256.2 1.8 copy.75
  258.9 1.3 copy.74
  261.4 3.4 collective-permute-start.19
  264.8 4.5 collective-permute-start.20
  269.4 1.9 collective-permute-start.18
  271.3 5.8 %collective-permute-done.9 = bf16[4,128,512]{2,1,0:T(8,128)(2,1)} collective-permute-done((bf16[4,128,512]{2,1,0:T(8,128)(2,1)}, bf16[4,128,512]{2,1,0:T(8,128)(2,1)}, u32[]{:S(2)}, u32[]{:S(2)}) %collective-permute-start.9) | collective-permute-done | bytes 524320 | tf_op jit(solution)/shard_map/ppermute | solution.py:33
  277.2 1.8 pad_maximum_fusion.1
  279.8 2.3 collective-permute-start.14
  282.1 3.2 collective-permute-start.13
  285.4 4.2 collective-permute-start.12
  289.6 2.4 collective-permute-done.20
  292.2 7.0 %collective-permute-start.21 = (bf16[128,256]{1,0:T(8,128)(2,1)S(1)}, bf16[128,256]{1,0:T(8,128)(2,1)S(1)}, u32[]{:S(2)}, u32[]{:S(2)}) collective-permute-start(bf16[128,256]{1,0:T(8,128)(2,1)S(1)} %get-tuple-element.33), channel_id=1, source_target_pairs={{0,3},{1,0},{2,1},{3,2},{4,7},{5,4},{6,5},{7,6},{8,11},{9,8},{10,9... | collective-permute-start | bytes 196616 | tf_op jit(solution)/shard_map/ppermute | solution.py:43
  299.2 2.8 collective-permute-start.23
  302.0 7.4 %collective-permute-start.22 = (bf16[128,256]{1,0:T(8,128)(2,1)S(1)}, bf16[128,256]{1,0:T(8,128)(2,1)S(1)}, u32[]{:S(2)}, u32[]{:S(2)}) collective-permute-start(bf16[128,256]{1,0:T(8,128)(2,1)S(1)} %get-tuple-element.35), channel_id=1, source_target_pairs={{0,2},{1,3},{2,0},{3,1},{4,6},{5,7},{6,4},{7,5},{8,10},{9,11},{10,... | collective-permute-start | bytes 196616 | tf_op jit(solution)/shard_map/ppermute | solution.py:43
  309.6 6.9 %collective-permute-start.17 = (bf16[4,128,256]{2,1,0:T(8,128)(2,1)S(1)}, bf16[4,128,256]{2,1,0:T(8,128)(2,1)S(1)}, u32[]{:S(2)}, u32[]{:S(2)}) collective-permute-start(bf16[4,128,256]{2,1,0:T(8,128)(2,1)S(1)} %get-tuple-element.11), channel_id=1, source_target_pairs={{0,1},{1,2},{2,3},{3,0},{4,5},{5,6},{6,7},{7,4},{8,9},{9,10},{10,1... | collective-permute-start | bytes 786440 | tf_op jit(solution)/shard_map/ppermute | solution.py:76
  316.5 2.9 collective-permute-start.15
  319.4 7.2 %collective-permute-start.16 = (bf16[4,128,256]{2,1,0:T(8,128)(2,1)S(1)}, bf16[4,128,256]{2,1,0:T(8,128)(2,1)S(1)}, u32[]{:S(2)}, u32[]{:S(2)}) collective-permute-start(bf16[4,128,256]{2,1,0:T(8,128)(2,1)S(1)} %get-tuple-element.14), channel_id=1, source_target_pairs={{0,2},{1,3},{2,0},{3,1},{4,6},{5,7},{6,4},{7,5},{8,10},{9,11},{10,... | collective-permute-start | bytes 786440 | tf_op jit(solution)/shard_map/ppermute | solution.py:76
  327.0 6.7 %collective-permute-start.27 = (bf16[128,256]{1,0:T(8,128)(2,1)S(1)}, bf16[128,256]{1,0:T(8,128)(2,1)S(1)}, u32[]{:S(2)}, u32[]{:S(2)}) collective-permute-start(bf16[128,256]{1,0:T(8,128)(2,1)S(1)} %fusion.76), channel_id=1, source_target_pairs={{0,3},{1,0},{2,1},{3,2},{4,7},{5,4},{6,5},{7,6},{8,11},{9,8},{10,9... | collective-permute-start | bytes 196616 | tf_op jit(solution)/shard_map/ppermute | solution.py:32
  333.6 4.9 %collective-permute-start.26 = (bf16[128,256]{1,0:T(8,128)(2,1)S(1)}, bf16[128,256]{1,0:T(8,128)(2,1)S(1)}, u32[]{:S(2)}, u32[]{:S(2)}) collective-permute-start(bf16[128,256]{1,0:T(8,128)(2,1)S(1)} %fusion.76), channel_id=1, source_target_pairs={{0,2},{1,3},{2,0},{3,1},{4,6},{5,7},{6,4},{7,5},{8,10},{9,11},{10,... | collective-permute-start | bytes 196616 | tf_op jit(solution)/shard_map/ppermute | solution.py:32
  338.5 37.3 %collective-permute-done.27 = bf16[128,256]{1,0:T(8,128)(2,1)S(1)} collective-permute-done((bf16[128,256]{1,0:T(8,128)(2,1)S(1)}, bf16[128,256]{1,0:T(8,128)(2,1)S(1)}, u32[]{:S(2)}, u32[]{:S(2)}) %collective-permute-start.27) | collective-permute-done | bytes 65568 | tf_op jit(solution)/shard_map/ppermute | solution.py:32
  375.9 2.4 collective-permute-start.25
  378.4 8.8 %collective-permute-done.25 = bf16[128,256]{1,0:T(8,128)(2,1)S(1)} collective-permute-done((bf16[128,256]{1,0:T(8,128)(2,1)S(1)}, bf16[128,256]{1,0:T(8,128)(2,1)S(1)}, u32[]{:S(2)}, u32[]{:S(2)}) %collective-permute-start.25) | collective-permute-done | bytes 65568 | tf_op jit(solution)/shard_map/ppermute | solution.py:32
  387.9 7.1 %collective-permute-start.29 = (bf16[4,128,256]{2,1,0:T(8,128)(2,1)}, bf16[4,128,256]{2,1,0:T(8,128)(2,1)}, u32[]{:S(2)}, u32[]{:S(2)}) collective-permute-start(bf16[4,128,256]{2,1,0:T(8,128)(2,1)} %get-tuple-element.32), channel_id=1, source_target_pairs={{0,8},{1,9},{2,10},{3,11},{4,12},{5,13},{6,14},{7,15},{8,0},{9,1},... | collective-permute-start | bytes 786440 | tf_op jit(solution)/shard_map/ppermute | solution.py:33
  395.0 2.0 collective-permute-start.28
  397.0 3.9 collective-permute-start.30
  402.5 1.4 copy.58
  403.8 2.1 reshape.207
  405.9 3.2 multiply_reduce_fusion.1
  409.9 1.9 collective-permute-start.24
  412.0 2.6 fusion.39
  414.6 5.7 %collective-permute-start.31 = (bf16[256,768]{1,0:T(8,128)(2,1)S(1)}, bf16[256,768]{1,0:T(8,128)(2,1)S(1)}, u32[]{:S(2)}, u32[]{:S(2)}) collective-permute-start(bf16[256,768]{1,0:T(8,128)(2,1)S(1)} %fusion.39), channel_id=1, source_target_pairs={{0,496},{16,480},{32,464},{48,448},{64,432},{80,416},{96,400},{112... | collective-permute-start | bytes 1179656 | tf_op jit(solution)/shard_map/ppermute | solution.py:19
  420.4 24.7 %collective-permute-done.31 = bf16[256,768]{1,0:T(8,128)(2,1)S(1)} collective-permute-done((bf16[256,768]{1,0:T(8,128)(2,1)S(1)}, bf16[256,768]{1,0:T(8,128)(2,1)S(1)}, u32[]{:S(2)}, u32[]{:S(2)}) %collective-permute-start.31) | collective-permute-done | bytes 393248 | tf_op jit(solution)/shard_map/ppermute | solution.py:19
  (100 shorter events, 20.3 us)
Async XLA Ops:
  7.2 190.5 %all-gather.6.cloned.1.call-start = ((), (), s32[]{:S(2)}) async-start(), calls=%async_computation.1 | async-start | bytes 4456448 | tf_op jit(solution)/shard_map/all_gather | solution.py:123
  7.9 398.0 %all-gather.4.cloned.1.call-start = ((), (), s32[]{:S(2)}) async-start(), calls=%async_computation | async-start | bytes 2228224 | tf_op jit(solution)/shard_map/all_gather | solution.py:127
  11.1 5.9 %copy-start = (bf16[1,128,4096]{2,1,0:T(8,128)(2,1)S(1)}, bf16[1,128,4096]{2,1,0:T(8,128)(2,1)}, u32[]{:S(2)}) copy-start(bf16[1,128,4096]{2,1,0:T(8,128)(2,1)} %param.8) | copy-start | bytes 3145732
  18.9 67.0 %collective-permute-start = (bf16[5,128,256]{1,2,0:T(8,128)(2,1)}, bf16[5,128,256]{1,2,0:T(8,128)(2,1)S(1)}, u32[]{:S(2)}, u32[]{:S(2)}) collective-permute-start(bf16[5,128,256]{1,2,0:T(8,128)(2,1)} %get-tuple-element.40), channel_id=1, source_target_pairs={{0,1},{1,2},{2,3},{3,0},{4,5},{5,6},{6,7},{7,4},{8,9},{9,10},{10,1... | collective-permute-start | bytes 983048 | tf_op jit(solution)/shard_map/ppermute | solution.py:54
  28.0 72.3 %collective-permute-start.1 = (bf16[5,128,256]{1,2,0:T(8,128)(2,1)S(1)}, bf16[5,128,256]{1,2,0:T(8,128)(2,1)S(1)}, u32[]{:S(2)}, u32[]{:S(2)}) collective-permute-start(bf16[5,128,256]{1,2,0:T(8,128)(2,1)S(1)} %get-tuple-element.41), channel_id=1, source_target_pairs={{0,2},{1,3},{2,0},{3,1},{4,6},{5,7},{6,4},{7,5},{8,10},{9,11},{10,... | collective-permute-start | bytes 983048 | tf_op jit(solution)/shard_map/ppermute | solution.py:54
  37.1 71.6 %collective-permute-start.2 = (bf16[5,128,256]{1,2,0:T(8,128)(2,1)S(1)}, bf16[5,128,256]{1,2,0:T(8,128)(2,1)S(1)}, u32[]{:S(2)}, u32[]{:S(2)}) collective-permute-start(bf16[5,128,256]{1,2,0:T(8,128)(2,1)S(1)} %get-tuple-element.42), channel_id=1, source_target_pairs={{0,3},{1,0},{2,1},{3,2},{4,7},{5,4},{6,5},{7,6},{8,11},{9,8},{10,9... | collective-permute-start | bytes 983048 | tf_op jit(solution)/shard_map/ppermute | solution.py:54
  108.7 13.2 %copy-start.13 = (s32[1,128]{1,0:T(1,128)S(1)}, s32[1,128]{1,0:T(1,128)}, u32[]{:S(2)}) copy-start(s32[1,128]{1,0:T(1,128)} %param.15) | copy-start | bytes 1540
  109.8 17.5 %collective-permute-start.3 = (bf16[8,128,256]{1,2,0:T(8,128)(2,1)S(1)}, bf16[8,128,256]{1,2,0:T(8,128)(2,1)S(1)}, u32[]{:S(2)}, u32[]{:S(2)}) collective-permute-start(bf16[8,128,256]{1,2,0:T(8,128)(2,1)S(1)} %get-tuple-element.36), channel_id=1, source_target_pairs={{0,4},{1,5},{2,6},{3,7},{4,8},{5,9},{6,10},{7,11},{8,12},{9,13},{1... | collective-permute-start | bytes 1572872 | tf_op jit(solution)/shard_map/ppermute | solution.py:61
  113.1 22.5 %collective-permute-start.4 = (bf16[8,128,256]{1,2,0:T(8,128)(2,1)S(1)}, bf16[8,128,256]{1,2,0:T(8,128)(2,1)S(1)}, u32[]{:S(2)}, u32[]{:S(2)}) collective-permute-start(bf16[8,128,256]{1,2,0:T(8,128)(2,1)S(1)} %get-tuple-element.37), channel_id=1, source_target_pairs={{0,8},{1,9},{2,10},{3,11},{4,12},{5,13},{6,14},{7,15},{8,0},{9,1},... | collective-permute-start | bytes 1572872 | tf_op jit(solution)/shard_map/ppermute | solution.py:61
  117.9 28.7 %collective-permute-start.5 = (bf16[8,128,256]{1,2,0:T(8,128)(2,1)S(1)}, bf16[8,128,256]{1,2,0:T(8,128)(2,1)S(1)}, u32[]{:S(2)}, u32[]{:S(2)}) collective-permute-start(bf16[8,128,256]{1,2,0:T(8,128)(2,1)S(1)} %get-tuple-element.38), channel_id=1, source_target_pairs={{0,12},{1,13},{2,14},{3,15},{4,0},{5,1},{6,2},{7,3},{8,4},{9,5},{1... | collective-permute-start | bytes 1572872 | tf_op jit(solution)/shard_map/ppermute | solution.py:61
  123.0 25.0 %copy-start.10 = (bf16[128,512]{0,1:T(8,128)(2,1)}, bf16[128,512]{0,1:T(8,128)(2,1)S(1)}, u32[]{:S(2)}) copy-start(bf16[128,512]{0,1:T(8,128)(2,1)S(1)} %slice.139) | copy-start | bytes 393220
  128.0 20.0 %copy-start.6 = (pred[128,2048]{0,1:T(8,128)(4,1)S(1)}, pred[128,2048]{0,1:T(8,128)(4,1)}, u32[]{:S(2)}) copy-start(pred[128,2048]{0,1:T(8,128)(4,1)} %compare_and_fusion) | copy-start | bytes 786436
  148.0 49.6 %copy-start.1 = (bf16[1,128,4096]{2,1,0:T(8,128)(2,1)S(1)}, bf16[1,128,4096]{2,1,0:T(8,128)(2,1)}, u32[]{:S(2)}) copy-start(bf16[1,128,4096]{2,1,0:T(8,128)(2,1)} %param.10) | copy-start | bytes 3145732
  212.1 25.9 %collective-permute-start.8 = (bf16[128,512]{1,0:T(8,128)(2,1)}, bf16[128,512]{1,0:T(8,128)(2,1)S(1)}, u32[]{:S(2)}, u32[]{:S(2)}) collective-permute-start(bf16[128,512]{1,0:T(8,128)(2,1)} %copy.51), channel_id=1, source_target_pairs={{0,3},{1,0},{2,1},{3,2},{4,7},{5,4},{6,5},{7,6},{8,11},{9,8},{10,9... | collective-permute-start | bytes 393224 | tf_op jit(solution)/shard_map/ppermute | solution.py:32
  216.9 23.2 %collective-permute-start.7 = (bf16[128,512]{1,0:T(8,128)(2,1)}, bf16[128,512]{1,0:T(8,128)(2,1)}, u32[]{:S(2)}, u32[]{:S(2)}) collective-permute-start(bf16[128,512]{1,0:T(8,128)(2,1)} %copy.51), channel_id=1, source_target_pairs={{0,2},{1,3},{2,0},{3,1},{4,6},{5,7},{6,4},{7,5},{8,10},{9,11},{10,... | collective-permute-start | bytes 393224 | tf_op jit(solution)/shard_map/ppermute | solution.py:32
  220.3 22.7 %collective-permute-start.6 = (bf16[128,512]{1,0:T(8,128)(2,1)}, bf16[128,512]{1,0:T(8,128)(2,1)}, u32[]{:S(2)}, u32[]{:S(2)}) collective-permute-start(bf16[128,512]{1,0:T(8,128)(2,1)} %copy.51), channel_id=1, source_target_pairs={{0,1},{1,2},{2,3},{3,0},{4,5},{5,6},{6,7},{7,4},{8,9},{9,10},{10,1... | collective-permute-start | bytes 393224 | tf_op jit(solution)/shard_map/ppermute | solution.py:32
  245.0 24.3 %collective-permute-start.10 = (bf16[4,128,512]{2,1,0:T(8,128)(2,1)}, bf16[4,128,512]{2,1,0:T(8,128)(2,1)}, u32[]{:S(2)}, u32[]{:S(2)}) collective-permute-start(bf16[4,128,512]{2,1,0:T(8,128)(2,1)} %get-tuple-element.30), channel_id=1, source_target_pairs={{0,8},{1,9},{2,10},{3,11},{4,12},{5,13},{6,14},{7,15},{8,0},{9,1},... | collective-permute-start | bytes 1572872 | tf_op jit(solution)/shard_map/ppermute | solution.py:33
  249.1 28.0 %collective-permute-start.9 = (bf16[4,128,512]{2,1,0:T(8,128)(2,1)}, bf16[4,128,512]{2,1,0:T(8,128)(2,1)}, u32[]{:S(2)}, u32[]{:S(2)}) collective-permute-start(bf16[4,128,512]{2,1,0:T(8,128)(2,1)} %get-tuple-element.30), channel_id=1, source_target_pairs={{0,4},{1,5},{2,6},{3,7},{4,8},{5,9},{6,10},{7,11},{8,12},{9,13},{1... | collective-permute-start | bytes 1572872 | tf_op jit(solution)/shard_map/ppermute | solution.py:33
  251.1 26.1 %collective-permute-start.11 = (bf16[4,128,512]{2,1,0:T(8,128)(2,1)}, bf16[4,128,512]{2,1,0:T(8,128)(2,1)}, u32[]{:S(2)}, u32[]{:S(2)}) collective-permute-start(bf16[4,128,512]{2,1,0:T(8,128)(2,1)} %get-tuple-element.30), channel_id=1, source_target_pairs={{0,12},{1,13},{2,14},{3,15},{4,0},{5,1},{6,2},{7,3},{8,4},{9,5},{1... | collective-permute-start | bytes 1572872 | tf_op jit(solution)/shard_map/ppermute | solution.py:33
  258.9 20.0 %copy-start.12 = (bf16[1,256,768]{2,1,0:T(8,128)(2,1)S(1)}, bf16[1,256,768]{2,1,0:T(8,128)(2,1)}, u32[]{:S(2)}) copy-start(bf16[1,256,768]{2,1,0:T(8,128)(2,1)} %param.11) | copy-start | bytes 1179652
  261.4 23.9 %collective-permute-start.19 = (bf16[4,128,256]{2,1,0:T(8,128)(2,1)S(1)}, bf16[4,128,256]{2,1,0:T(8,128)(2,1)S(1)}, u32[]{:S(2)}, u32[]{:S(2)}) collective-permute-start(bf16[4,128,256]{2,1,0:T(8,128)(2,1)S(1)} %bitcast.213), channel_id=1, source_target_pairs={{0,8},{1,9},{2,10},{3,11},{4,12},{5,13},{6,14},{7,15},{8,0},{9,1},... | collective-permute-start | bytes 786440 | tf_op jit(solution)/shard_map/ppermute | solution.py:40
  264.8 27.1 %collective-permute-start.20 = (bf16[4,128,256]{2,1,0:T(8,128)(2,1)S(1)}, bf16[4,128,256]{2,1,0:T(8,128)(2,1)S(1)}, u32[]{:S(2)}, u32[]{:S(2)}) collective-permute-start(bf16[4,128,256]{2,1,0:T(8,128)(2,1)S(1)} %bitcast.212), channel_id=1, source_target_pairs={{0,4},{1,5},{2,6},{3,7},{4,8},{5,9},{6,10},{7,11},{8,12},{9,13},{1... | collective-permute-start | bytes 786440 | tf_op jit(solution)/shard_map/ppermute | solution.py:40
  269.4 22.6 %collective-permute-start.18 = (bf16[4,128,256]{2,1,0:T(8,128)(2,1)}, bf16[4,128,256]{2,1,0:T(8,128)(2,1)S(1)}, u32[]{:S(2)}, u32[]{:S(2)}) collective-permute-start(bf16[4,128,256]{2,1,0:T(8,128)(2,1)} %bitcast.211), channel_id=1, source_target_pairs={{0,12},{1,13},{2,14},{3,15},{4,0},{5,1},{6,2},{7,3},{8,4},{9,5},{1... | collective-permute-start | bytes 786440 | tf_op jit(solution)/shard_map/ppermute | solution.py:40
  279.8 22.2 %collective-permute-start.14 = (bf16[4,128,256]{2,1,0:T(8,128)(2,1)S(1)}, bf16[4,128,256]{2,1,0:T(8,128)(2,1)S(1)}, u32[]{:S(2)}, u32[]{:S(2)}) collective-permute-start(bf16[4,128,256]{2,1,0:T(8,128)(2,1)S(1)} %bitcast.219), channel_id=1, source_target_pairs={{0,4},{1,5},{2,6},{3,7},{4,8},{5,9},{6,10},{7,11},{8,12},{9,13},{1... | collective-permute-start | bytes 786440 | tf_op jit(solution)/shard_map/ppermute | solution.py:72
  282.1 27.3 %collective-permute-start.13 = (bf16[4,128,256]{2,1,0:T(8,128)(2,1)S(1)}, bf16[4,128,256]{2,1,0:T(8,128)(2,1)S(1)}, u32[]{:S(2)}, u32[]{:S(2)}) collective-permute-start(bf16[4,128,256]{2,1,0:T(8,128)(2,1)S(1)} %bitcast.216), channel_id=1, source_target_pairs={{0,8},{1,9},{2,10},{3,11},{4,12},{5,13},{6,14},{7,15},{8,0},{9,1},... | collective-permute-start | bytes 786440 | tf_op jit(solution)/shard_map/ppermute | solution.py:72
  285.4 24.0 %collective-permute-start.12 = (bf16[4,128,256]{2,1,0:T(8,128)(2,1)S(1)}, bf16[4,128,256]{2,1,0:T(8,128)(2,1)S(1)}, u32[]{:S(2)}, u32[]{:S(2)}) collective-permute-start(bf16[4,128,256]{2,1,0:T(8,128)(2,1)S(1)} %bitcast.214), channel_id=1, source_target_pairs={{0,12},{1,13},{2,14},{3,15},{4,0},{5,1},{6,2},{7,3},{8,4},{9,5},{1... | collective-permute-start | bytes 786440 | tf_op jit(solution)/shard_map/ppermute | solution.py:72
  292.2 27.2 %collective-permute-start.21 = (bf16[128,256]{1,0:T(8,128)(2,1)S(1)}, bf16[128,256]{1,0:T(8,128)(2,1)S(1)}, u32[]{:S(2)}, u32[]{:S(2)}) collective-permute-start(bf16[128,256]{1,0:T(8,128)(2,1)S(1)} %get-tuple-element.33), channel_id=1, source_target_pairs={{0,3},{1,0},{2,1},{3,2},{4,7},{5,4},{6,5},{7,6},{8,11},{9,8},{10,9... | collective-permute-start | bytes 196616 | tf_op jit(solution)/shard_map/ppermute | solution.py:43
  299.2 27.4 %collective-permute-start.23 = (bf16[128,256]{1,0:T(8,128)(2,1)S(1)}, bf16[128,256]{1,0:T(8,128)(2,1)S(1)}, u32[]{:S(2)}, u32[]{:S(2)}) collective-permute-start(bf16[128,256]{1,0:T(8,128)(2,1)S(1)} %get-tuple-element.34), channel_id=1, source_target_pairs={{0,1},{1,2},{2,3},{3,0},{4,5},{5,6},{6,7},{7,4},{8,9},{9,10},{10,1... | collective-permute-start | bytes 196616 | tf_op jit(solution)/shard_map/ppermute | solution.py:43
  302.0 25.0 %collective-permute-start.22 = (bf16[128,256]{1,0:T(8,128)(2,1)S(1)}, bf16[128,256]{1,0:T(8,128)(2,1)S(1)}, u32[]{:S(2)}, u32[]{:S(2)}) collective-permute-start(bf16[128,256]{1,0:T(8,128)(2,1)S(1)} %get-tuple-element.35), channel_id=1, source_target_pairs={{0,2},{1,3},{2,0},{3,1},{4,6},{5,7},{6,4},{7,5},{8,10},{9,11},{10,... | collective-permute-start | bytes 196616 | tf_op jit(solution)/shard_map/ppermute | solution.py:43
  309.6 87.4 %collective-permute-start.17 = (bf16[4,128,256]{2,1,0:T(8,128)(2,1)S(1)}, bf16[4,128,256]{2,1,0:T(8,128)(2,1)S(1)}, u32[]{:S(2)}, u32[]{:S(2)}) collective-permute-start(bf16[4,128,256]{2,1,0:T(8,128)(2,1)S(1)} %get-tuple-element.11), channel_id=1, source_target_pairs={{0,1},{1,2},{2,3},{3,0},{4,5},{5,6},{6,7},{7,4},{8,9},{9,10},{10,1... | collective-permute-start | bytes 786440 | tf_op jit(solution)/shard_map/ppermute | solution.py:76
  316.5 84.4 %collective-permute-start.15 = (bf16[4,128,256]{2,1,0:T(8,128)(2,1)S(1)}, bf16[4,128,256]{2,1,0:T(8,128)(2,1)S(1)}, u32[]{:S(2)}, u32[]{:S(2)}) collective-permute-start(bf16[4,128,256]{2,1,0:T(8,128)(2,1)S(1)} %get-tuple-element.12), channel_id=1, source_target_pairs={{0,3},{1,0},{2,1},{3,2},{4,7},{5,4},{6,5},{7,6},{8,11},{9,8},{10,9... | collective-permute-start | bytes 786440 | tf_op jit(solution)/shard_map/ppermute | solution.py:76
  319.4 81.5 %collective-permute-start.16 = (bf16[4,128,256]{2,1,0:T(8,128)(2,1)S(1)}, bf16[4,128,256]{2,1,0:T(8,128)(2,1)S(1)}, u32[]{:S(2)}, u32[]{:S(2)}) collective-permute-start(bf16[4,128,256]{2,1,0:T(8,128)(2,1)S(1)} %get-tuple-element.14), channel_id=1, source_target_pairs={{0,2},{1,3},{2,0},{3,1},{4,6},{5,7},{6,4},{7,5},{8,10},{9,11},{10,... | collective-permute-start | bytes 786440 | tf_op jit(solution)/shard_map/ppermute | solution.py:76
  327.0 48.9 %collective-permute-start.27 = (bf16[128,256]{1,0:T(8,128)(2,1)S(1)}, bf16[128,256]{1,0:T(8,128)(2,1)S(1)}, u32[]{:S(2)}, u32[]{:S(2)}) collective-permute-start(bf16[128,256]{1,0:T(8,128)(2,1)S(1)} %fusion.76), channel_id=1, source_target_pairs={{0,3},{1,0},{2,1},{3,2},{4,7},{5,4},{6,5},{7,6},{8,11},{9,8},{10,9... | collective-permute-start | bytes 196616 | tf_op jit(solution)/shard_map/ppermute | solution.py:32
  333.6 44.7 %collective-permute-start.26 = (bf16[128,256]{1,0:T(8,128)(2,1)S(1)}, bf16[128,256]{1,0:T(8,128)(2,1)S(1)}, u32[]{:S(2)}, u32[]{:S(2)}) collective-permute-start(bf16[128,256]{1,0:T(8,128)(2,1)S(1)} %fusion.76), channel_id=1, source_target_pairs={{0,2},{1,3},{2,0},{3,1},{4,6},{5,7},{6,4},{7,5},{8,10},{9,11},{10,... | collective-permute-start | bytes 196616 | tf_op jit(solution)/shard_map/ppermute | solution.py:32
  375.9 11.3 %collective-permute-start.25 = (bf16[128,256]{1,0:T(8,128)(2,1)S(1)}, bf16[128,256]{1,0:T(8,128)(2,1)S(1)}, u32[]{:S(2)}, u32[]{:S(2)}) collective-permute-start(bf16[128,256]{1,0:T(8,128)(2,1)S(1)} %fusion.76), channel_id=1, source_target_pairs={{0,1},{1,2},{2,3},{3,0},{4,5},{5,6},{6,7},{7,4},{8,9},{9,10},{10,1... | collective-permute-start | bytes 196616 | tf_op jit(solution)/shard_map/ppermute | solution.py:32
  387.9 24.0 %collective-permute-start.29 = (bf16[4,128,256]{2,1,0:T(8,128)(2,1)}, bf16[4,128,256]{2,1,0:T(8,128)(2,1)}, u32[]{:S(2)}, u32[]{:S(2)}) collective-permute-start(bf16[4,128,256]{2,1,0:T(8,128)(2,1)} %get-tuple-element.32), channel_id=1, source_target_pairs={{0,8},{1,9},{2,10},{3,11},{4,12},{5,13},{6,14},{7,15},{8,0},{9,1},... | collective-permute-start | bytes 786440 | tf_op jit(solution)/shard_map/ppermute | solution.py:33
  395.0 16.9 %collective-permute-start.28 = (bf16[4,128,256]{2,1,0:T(8,128)(2,1)}, bf16[4,128,256]{2,1,0:T(8,128)(2,1)}, u32[]{:S(2)}, u32[]{:S(2)}) collective-permute-start(bf16[4,128,256]{2,1,0:T(8,128)(2,1)} %get-tuple-element.32), channel_id=1, source_target_pairs={{0,4},{1,5},{2,6},{3,7},{4,8},{5,9},{6,10},{7,11},{8,12},{9,13},{1... | collective-permute-start | bytes 786440 | tf_op jit(solution)/shard_map/ppermute | solution.py:33
  397.0 14.9 %collective-permute-start.30 = (bf16[4,128,256]{2,1,0:T(8,128)(2,1)}, bf16[4,128,256]{2,1,0:T(8,128)(2,1)}, u32[]{:S(2)}, u32[]{:S(2)}) collective-permute-start(bf16[4,128,256]{2,1,0:T(8,128)(2,1)} %get-tuple-element.32), channel_id=1, source_target_pairs={{0,12},{1,13},{2,14},{3,15},{4,0},{5,1},{6,2},{7,3},{8,4},{9,5},{1... | collective-permute-start | bytes 786440 | tf_op jit(solution)/shard_map/ppermute | solution.py:33
  403.8 2.1 copy-start.11
  405.9 3.3 copy-start.2
  409.2 2.7 copy-start.3
  409.2 2.7 copy-start.5
  409.2 2.7 copy-start.7
  409.2 2.7 copy-start.8
  409.2 2.7 copy-start.9
  409.9 35.9 %collective-permute-start.24 = (bf16[128,4096]{1,0:T(8,128)(2,1)S(1)}, bf16[128,4096]{1,0:T(8,128)(2,1)S(1)}, u32[]{:S(2)}, u32[]{:S(2)}) collective-permute-start(bf16[128,4096]{1,0:T(8,128)(2,1)S(1)} %add_convert_fusion), channel_id=1, source_target_pairs={{0,16},{16,32},{32,48},{48,64},{64,80},{80,96},{96,112},{112,128},... | collective-permute-start | bytes 3145736 | tf_op jit(solution)/shard_map/ppermute | solution.py:14
  411.9 33.1 %copy-start.4 = (bf16[1,256,768]{2,1,0:T(8,128)(2,1)S(1)}, bf16[1,256,768]{2,1,0:T(8,128)(2,1)}, u32[]{:S(2)}) copy-start(bf16[1,256,768]{2,1,0:T(8,128)(2,1)} %param.14) | copy-start | bytes 1179652
  414.6 30.4 %collective-permute-start.31 = (bf16[256,768]{1,0:T(8,128)(2,1)S(1)}, bf16[256,768]{1,0:T(8,128)(2,1)S(1)}, u32[]{:S(2)}, u32[]{:S(2)}) collective-permute-start(bf16[256,768]{1,0:T(8,128)(2,1)S(1)} %fusion.39), channel_id=1, source_target_pairs={{0,496},{16,480},{32,464},{48,448},{64,432},{80,416},{96,400},{112... | collective-permute-start | bytes 1179656 | tf_op jit(solution)/shard_map/ppermute | solution.py:19
Sparse Core Ops, SparseCore 0:
  11.0 186.6 all-gather.5
  200.7 114.0 all-gather.3
